TPU v7x, 32 devices: a whole 2x2x4 slice. The times are simulated.
32 devices in a mesh: leaf: 8 (over z, x), panel: 4 (over y, core).
Axes of the slice: x: 2, y: 2, z: 4, core: 2. Of those that a mesh axis runs over, the one named last changes fastest.
Arguments:
- upper_rhs: float32 [8, 512, 128], P('leaf'), may hold values from -6 to 6
- upper_panel: float32 [8, 1024, 512], P('leaf', 'panel'), may hold values from -0.25 to 0.25
- upper_inverse: float32 [8, 512, 512], P('leaf'), as said below
- top_index: int32 [8, 1024], P('leaf', 'panel'), may hold values from 0 to 511
- top_solution: float32 [512, 128], P(('leaf', 'panel')), may hold values from -6 to 6
- owner_map: int32 [8], replicated, may hold values from 0 to 7, each once
- parent_list: int32 [256], P(('leaf', 'panel')), may hold values from 0 to 7, as said below
- lower_index: int32 [256, 256], P(('leaf', 'panel')), may hold values from 0 to 511
- lower_panel: float32 [256, 256, 256], P(('leaf', 'panel')), may hold values from -0.5 to 0.5
- lower_rhs: float32 [256, 256, 128], P(('leaf', 'panel')), may hold values from -6 to 6
- lower_inverse: float32 [256, 256, 256], P(('leaf', 'panel')), as said below
Outputs:
- upper_solution: float32 [8, 512, 128], P('leaf', 'panel')
- lower_solution: float32 [256, 256, 128], P(('leaf', 'panel'))
Inputs may be any that keep to these rules, and one draw needn't show every extreme that they name: `owner_map`: each leaf index holds exactly one upper supernode. `parent_list`: the 8 lower supernodes of one device have pairwise different parents. `upper_inverse`: lower triangular with a positive diagonal. `lower_inverse`: lower triangular with a positive diagonal.
All inputs are finite; a program needn't handle non-finite values.
Results may differ from a plain program's by a relative error of at most 0.00007.
Values sent between devices are 32-bit elements; how exact they have to be, the bound alone decides.
No kernel may reach another device: no remote copies, remote signals or barrier semaphores. Data moves between devices by JAX's collectives and lax.ppermute only.
A program may use at most 64 MiB of HBM per device.

v0:
```python
import jax
import jax.numpy as jnp
from jax import lax
from jax.sharding import PartitionSpec as P


def local(
    upper_rhs,
    upper_panel,
    upper_inverse,
    top_index,
    top_solution,
    owner_map,
    parent_list,
    lower_index,
    lower_panel,
    lower_rhs,
    lower_inverse,
):
    highest = lax.Precision.HIGHEST
    panels = lax.axis_size("panel")
    panel_index = lax.axis_index("panel")
    width_upper = upper_rhs.shape[1]
    share = width_upper // panels
    begin = panel_index * share
    top_whole = lax.all_gather(top_solution, ("leaf", "panel"), axis=0, tiled=True)
    gathered = top_whole[top_index[0]]
    panel_rows = upper_panel[0]
    partial_update = jnp.einsum("kw,kr->wr", panel_rows, gathered, precision=highest)
    update = lax.psum(partial_update, "panel")
    reduced = upper_rhs[0] - update
    full_solution = jnp.einsum("kw,kr->wr", upper_inverse[0], reduced, precision=highest)
    own_rows = lax.dynamic_slice_in_dim(full_solution, begin, share, 0)
    position = owner_map[parent_list]
    all_upper = lax.all_gather(full_solution[None], "leaf", axis=0, tiled=True)
    parent_rows = all_upper[position[:, None], lower_index]
    lower_update = jnp.einsum("skw,skr->swr", lower_panel, parent_rows, precision=highest)
    lower_solution = jnp.einsum(
        "skw,skr->swr", lower_inverse, lower_rhs - lower_update, precision=highest
    )
    return (own_rows[None], lower_solution)


def solution(mesh):
    placed = (
        P("leaf", None, None),
        P("leaf", "panel", None),
        P("leaf", None, None),
        P("leaf", "panel"),
        P(("leaf", "panel"), None),
        P(),
        P(("leaf", "panel")),
        P(("leaf", "panel"), None),
        P(("leaf", "panel"), None, None),
        P(("leaf", "panel"), None, None),
        P(("leaf", "panel"), None, None),
    )
    return jax.shard_map(
        local,
        mesh=mesh,
        in_specs=placed,
        out_specs=(P("leaf", "panel", None), P(("leaf", "panel"), None, None)),
        check_vma=False,
    )
```

profile of v0, /device:TPU:0, one launch (start us, length us, event | category | flops | bytes accessed | tf_op | source)
XLA Modules:
  0.0 174.9 jit_solution(9198700522070792228)
XLA Ops:
  7.2 0.0 copy-start
  7.2 0.0 all-reduce.2.cloned.1.call-start
  7.2 44.3 %all_gather.6 = f32[512,128]{1,0:T(8,128)S(1)} all-gather(f32[16,128]{1,0:T(8,128)} %param.15), channel_id=1, replica_groups=mesh['leaf'=8,'panel'=4] {'leaf','panel'}, dimensions={0}, use_global_device_ids=true | all-gather | bytes 270336 | tf_op jit(solution)/shard_map/all_gather | solution.py:26
  51.5 0.7 compare_select_fusion.1
  52.2 0.0 copy-start.1
  52.3 0.7 gather_fusion
  53.0 0.0 copy-start.4
  53.0 2.8 %convolution_bitcast_fusion.2 = f32[512,128]{1,0:T(8,128)} fusion(f32[256,128]{1,0:T(8,128)S(1)} %gather_fusion, f32[1,256,512]{2,1,0:T(8,128)} %param.12), kind=kOutput, calls=%fused_computation.6 | convolution fusion | flops 201326592 | bytes 917504 | tf_op jit(solution)/shard_map/kw,kr->wr/dot_general | solution.py:29
  55.7 0.0 all-reduce.2.cloned.1.call-update
  55.8 0.0 all-gather.3.cloned.1.call-start
  55.8 28.2 %all-reduce.2.cloned.1.call-done = f32[512,128]{1,0:T(8,128)} async-done(((f32[512,128]{1,0:T(8,128)}), f32[512,128]{1,0:T(8,128)}) %all-reduce.2.cloned.1.call-update) | async-done | bytes 262160 | tf_op jit(solution)/shard_map/psum | solution.py:30
  84.0 2.5 %fusion.1 = f32[128,512]{1,0:T(8,128)} fusion(f32[1,512,512]{2,1,0:T(8,128)S(1)} %copy-done.3, f32[512,128]{1,0:T(8,128)} %all-reduce.2.cloned.1.call-done, f32[1,512,128]{2,1,0:T(8,128)} %param.11), kind=kOutput, calls=%fused_computation.7 | convolution fusion | flops 402718720 | bytes 1835008 | tf_op jit(solution)/shard_map/kw,kr->wr/dot_general | solution.py:32
  86.5 0.0 all-gather.3.cloned.1.call-update
  86.6 0.6 gather_fusion.1
  87.3 0.1 fusion.8
  87.3 0.8 dynamic-slice_bitcast_fusion
  88.2 0.7 copy.19
  88.9 47.4 %all-gather.3.cloned.1.call-done = f32[4096,128]{0,1:T(8,128)} async-done(((f32[512,128]{0,1:T(8,128)}), f32[4096,128]{0,1:T(8,128)}) %all-gather.3.cloned.1.call-update) | async-done | bytes 2097168 | tf_op jit(solution)/shard_map/all_gather | solution.py:35
  136.3 2.9 %copy.22 = f32[4096,128]{1,0:T(8,128)} copy(f32[4096,128]{0,1:T(8,128)} %all-gather.3.cloned.1.call-done) | data formatting | bytes 4194304 | tf_op jit(solution)/shard_map/all_gather | solution.py:35
  139.2 20.6 %gather_fusion.2 = f32[2048,128]{1,0:T(8,128)S(1)} fusion(f32[8,512,128]{2,1,0:T(8,128)} %bitcast.43, s32[2048]{0:T(1024)S(1)} %bitcast.42), kind=kCustom, calls=%fused_computation.2 | custom fusion | bytes 2113536 | tf_op jit(solution)/shard_map/gather | solution.py:36
  159.8 0.0 copy-start.2
  159.8 4.9 %fusion = f32[8,256,128]{2,1,0:T(8,128)S(1)} fusion(f32[8,256,128]{2,1,0:T(8,128)} %param.20, f32[8,256,128]{2,1,0:T(8,128)S(1)} %bitcast.44, f32[8,256,256]{2,1,0:T(8,128)S(1)} %copy-done), kind=kOutput, calls=%fused_computation.5 | convolution fusion | flops 805568512 | bytes 5242880 | tf_op jit(solution)/shard_map/skw,skr->swr/dot_general | solution.py:37
  164.7 2.0 %convolution_bitcast_fusion = f32[8,256,128]{1,2,0:T(8,128)S(1)} fusion(f32[8,256,128]{2,1,0:T(8,128)S(1)} %fusion, f32[8,256,256]{2,1,0:T(8,128)S(1)} %copy-done.2), kind=kOutput, calls=%fused_computation.3 | convolution fusion | flops 805306368 | bytes 4194304 | tf_op jit(solution)/shard_map/skw,skr->swr/dot_general | solution.py:38
  166.7 1.3 copy.20
  (13 shorter events, 0.1 us)
Async XLA Ops:
  7.2 152.6 %copy-start = (f32[8,256,256]{2,1,0:T(8,128)S(1)}, f32[8,256,256]{2,1,0:T(8,128)}, u32[]{:S(2)}) copy-start(f32[8,256,256]{2,1,0:T(8,128)} %param.19) | copy-start | bytes 6291460
  7.2 76.8 %copy-start.3 = (f32[1,512,512]{2,1,0:T(8,128)S(1)}, f32[1,512,512]{2,1,0:T(8,128)}, u32[]{:S(2)}) copy-start(f32[1,512,512]{2,1,0:T(8,128)} %param.13) | copy-start | bytes 3145732
  7.2 76.8 %all-reduce.2.cloned.1.call-start = ((), (), s32[]{:S(2)}) async-start(), calls=%async_computation | async-start | bytes 524288 | tf_op jit(solution)/shard_map/psum | solution.py:30
  52.2 34.3 %copy-start.5 = (s32[8]{0:T(128)S(1)}, s32[8]{0:T(128)}, u32[]{:S(2)}) copy-start(s32[8]{0:T(128)} %param.17) | copy-start | bytes 100
  52.2 34.3 %copy-start.1 = (s32[8]{0:T(128)S(1)}, s32[8]{0:T(128)}, u32[]{:S(2)}) copy-start(s32[8]{0:T(128)} %param.16) | copy-start | bytes 100
  53.0 34.3 %copy-start.4 = (s32[8,256]{1,0:T(8,128)S(1)}, s32[8,256]{1,0:T(8,128)}, u32[]{:S(2)}) copy-start(s32[8,256]{1,0:T(8,128)} %param.18) | copy-start | bytes 24580
  55.8 80.5 %all-gather.3.cloned.1.call-start = ((), (), s32[]{:S(2)}) async-start(), calls=%async_computation.1 | async-start | bytes 2359296 | tf_op jit(solution)/shard_map/all_gather | solution.py:35
  159.8 4.9 %copy-start.2 = (f32[8,256,256]{2,1,0:T(8,128)S(1)}, f32[8,256,256]{2,1,0:T(8,128)}, u32[]{:S(2)}) copy-start(f32[8,256,256]{2,1,0:T(8,128)} %param.21) | copy-start | bytes 6291460
Sparse Core Ops, SparseCore 0:
  55.9 28.0 all-reduce.1
  87.0 49.2 all-gather.2
where the time goes:
time: 175 us
  waiting for transfers between devices  75.6 us (43%)
  blocking collectives  44.3 us (25%)
  local copies, waits for them, and re-layouts  27.8 us (16%)
  between operations  14.2 us (8%)
  matrix products  12.2 us (7%)
    all_gather x1, waiting for transfers between devices, local(): all_upper = lax.all_gather(full_solution[None], 'leaf', axis=0, tiled=True)  47.4 us
    all_gather x1, blocking collectives, local(): lax.all_gather(top_solution, ('leaf', 'panel'), axis=0, tiled=True)  44.3 us
    psum x1, waiting for transfers between devices, local(): update = lax.psum(partial_update, 'panel')  28.2 us
    gather x1, local copies, waits for them, and re-layouts, local(): parent_rows = all_upper[position[:, None], lower_index]  20.6 us
    dot_general x1, matrix products, local(): jnp.einsum('skw,skr->swr', lower_panel, parent_rows, precision=highest)  4.89 us
  transfers between devices with their start and end apart: 2, of which 2 were waited for; matrix products, arithmetic and copies ran while one was open for 1% of the time, Pallas kernels for 0%

commit v1 on v0

--- a/solution.py
+++ b/solution.py
@@ -2,6 +2,34 @@
 import jax.numpy as jnp
 from jax import lax
 from jax.sharding import PartitionSpec as P
+
+
+def doubling_gather(block, axes, count):
+    bits = count.bit_length() - 1
+    if (1 << bits) != count:
+        return lax.all_gather(block, axes, axis=0, tiled=True)
+    index = lax.axis_index(axes)
+    held = block[None]
+    for bit in reversed(range(bits)):
+        pairs = [(i, i ^ (1 << bit)) for i in range(count)]
+        received = lax.ppermute(held, axes, pairs)
+        upper = ((index >> bit) & 1) == 1
+        held = jnp.where(upper, jnp.concatenate([received, held], 0), jnp.concatenate([held, received], 0))
+    shape = held.shape[1:]
+    held = held.reshape((2,) * bits + shape)
+    held = jnp.transpose(held, tuple(reversed(range(bits))) + tuple(range(bits, bits + len(shape))))
+    held = held.reshape((count,) + shape)
+    return held.reshape((count * shape[0],) + shape[1:])
+
+
+def butterfly_sum(value, axis, count):
+    bits = count.bit_length() - 1
+    if (1 << bits) != count:
+        return lax.psum(value, axis)
+    for bit in range(bits):
+        pairs = [(i, i ^ (1 << bit)) for i in range(count)]
+        value = value + lax.ppermute(value, axis, pairs)
+    return value
 
 
 def local(
@@ -18,22 +46,27 @@
     lower_inverse,
 ):
     highest = lax.Precision.HIGHEST
+    leaves = lax.axis_size("leaf")
     panels = lax.axis_size("panel")
     panel_index = lax.axis_index("panel")
     width_upper = upper_rhs.shape[1]
     share = width_upper // panels
     begin = panel_index * share
-    top_whole = lax.all_gather(top_solution, ("leaf", "panel"), axis=0, tiled=True)
+    both = ("leaf", "panel")
+    top_whole = doubling_gather(top_solution, both, leaves * panels)
     gathered = top_whole[top_index[0]]
-    panel_rows = upper_panel[0]
-    partial_update = jnp.einsum("kw,kr->wr", panel_rows, gathered, precision=highest)
-    update = lax.psum(partial_update, "panel")
+    partial_update = jnp.einsum("kw,kr->wr", upper_panel[0], gathered, precision=highest)
+    update = butterfly_sum(partial_update, "panel", panels)
     reduced = upper_rhs[0] - update
     full_solution = jnp.einsum("kw,kr->wr", upper_inverse[0], reduced, precision=highest)
     own_rows = lax.dynamic_slice_in_dim(full_solution, begin, share, 0)
+    all_upper = doubling_gather(own_rows, both, leaves * panels)
+    all_upper = all_upper.reshape(leaves, width_upper, all_upper.shape[-1])
     position = owner_map[parent_list]
-    all_upper = lax.all_gather(full_solution[None], "leaf", axis=0, tiled=True)
-    parent_rows = all_upper[position[:, None], lower_index]
+    slabs = all_upper[position]
+    columns = lax.broadcasted_iota(jnp.int32, lower_index.shape + (width_upper,), 2)
+    pick = (lower_index[:, :, None] == columns).astype(jnp.float32)
+    parent_rows = jnp.einsum("skj,sjr->skr", pick, slabs, precision=highest)
     lower_update = jnp.einsum("skw,skr->swr", lower_panel, parent_rows, precision=highest)
     lower_solution = jnp.einsum(
         "skw,skr->swr", lower_inverse, lower_rhs - lower_update, precision=highest

time: 175 us -> 85.6 us (0.49)
  blocking collectives: 44.3 us -> 0 us
  waiting for transfers between devices: 75.6 us -> 35.5 us
  starting transfers between devices: 0.08 us -> 19.6 us
  local copies, waits for them, and re-layouts: 27.8 us -> 11.8 us
  between operations: 14.2 us -> 0.85 us
  other arithmetic: 0.78 us -> 4.91 us
    all_gather x1 -> x0, waiting for transfers between devices: 47.4 us -> none  [local(): all_upper = lax.all_gather(full_solution[None], 'leaf', axis=0, tiled=True)]
    all_gather x1 -> x0, blocking collectives: 44.3 us -> none  [local(): lax.all_gather(top_solution, ('leaf', 'panel'), axis=0, tiled=True)]
    ppermute x0 -> x12, waiting for transfers between devices: none -> 35.5 us  [the longest x10 29.2 us: doubling_gather(): received = lax.ppermute(held, axes, pairs)]
    psum x1 -> x0, waiting for transfers between devices: 28.2 us -> none  [local(): update = lax.psum(partial_update, 'panel')]
    ppermute x0 -> x12, starting transfers between devices: none -> 19.6 us  [the longest x10 17.5 us: doubling_gather(): received = lax.ppermute(held, axes, pairs)]
    gather x1, local copies, waits for them, and re-layouts: 20.6 us -> 3.62 us  [local(): slabs = all_upper[position]]
    select_n x0 -> x11, other arithmetic: none -> 4.17 us  [the longest x10 4.16 us: doubling_gather(): jnp.where(upper, jnp.concatenate([received, held], 0), jnp.concatenate([h...]
    select_n x0 -> x2, local copies, waits for them, and re-layouts: none -> 2.93 us  [doubling_gather(): jnp.where(upper, jnp.concatenate([received, held], 0), jnp.concatenate([h...]
  transfers between devices with their start and end apart: 2 -> 12, of which waited for: 2 -> 12; matrix products, arithmetic and copies ran while one was open for 1% -> 5% of each run, Pallas kernels for 0% -> 0%
where the time goes in v1:
time: 85.6 us; the launch traced here: 85.3 us
  waiting for transfers between devices  35.5 us (41%)
  starting transfers between devices  19.6 us (23%)
  matrix products  12.6 us (15%)
  local copies, waits for them, and re-layouts  11.8 us (14%)
  other arithmetic  4.91 us (6%)
    ppermute x10, waiting for transfers between devices, doubling_gather(): received = lax.ppermute(held, axes, pairs)  29.2 us
    ppermute x10, starting transfers between devices, doubling_gather(): received = lax.ppermute(held, axes, pairs)  17.5 us
    ppermute x2, waiting for transfers between devices, butterfly_sum(): value = value + lax.ppermute(value, axis, pairs)  6.32 us
    select_n x10, other arithmetic, doubling_gather(): jnp.where(upper, jnp.concatenate([received, held], 0), jnp.concatenate([h...  4.16 us
    unnamed x17, local copies, waits for them, and re-layouts  3.87 us
    dot_general x1, matrix products, local(): parent_rows = jnp.einsum('skj,sjr->skr', pick, slabs, precision=highest)  3.78 us
    gather x1, local copies, waits for them, and re-layouts, local(): slabs = all_upper[position]  3.62 us
    dot_general x1, matrix products, local(): jnp.einsum('skw,skr->swr', lower_panel, parent_rows, precision=highest)  3.52 us
  transfers between devices with their start and end apart: 12, of which 12 were waited for; matrix products, arithmetic and copies ran while one was open for 5% of the time, Pallas kernels for 0%

profile of v1, /device:TPU:0, one launch (start us, length us, event | category | flops | bytes accessed | tf_op | source)
XLA Modules:
  0.0 85.3 jit_solution(2135024166521942520)
XLA Ops:
  0.6 4.1 %collective-permute-start = (f32[1,16,128]{2,1,0:T(8,128)}, f32[1,16,128]{2,1,0:T(8,128)S(1)}, u32[]{:S(2)}, u32[]{:S(2)}) collective-permute-start(f32[1,16,128]{2,1,0:T(8,128)} %bitcast.47), channel_id=1, source_target_pairs={{0,16},{1,17},{2,18},{3,19},{4,20},{5,21},{6,22},{7,23},{8,24},{9,... | collective-permute-start | bytes 24584 | tf_op jit(solution)/shard_map/ppermute | solution.py:15
  4.7 1.8 %collective-permute-done = f32[1,16,128]{2,1,0:T(8,128)S(1)} collective-permute-done((f32[1,16,128]{2,1,0:T(8,128)}, f32[1,16,128]{2,1,0:T(8,128)S(1)}, u32[]{:S(2)}, u32[]{:S(2)}) %collective-permute-start) | collective-permute-done | bytes 8224 | tf_op jit(solution)/shard_map/ppermute | solution.py:15
  7.4 1.9 %collective-permute-start.1 = (f32[2,16,128]{2,1,0:T(8,128)S(1)}, f32[2,16,128]{2,1,0:T(8,128)S(1)}, u32[]{:S(2)}, u32[]{:S(2)}) collective-permute-start(f32[2,16,128]{2,1,0:T(8,128)S(1)} %maximum_select_fusion.9), channel_id=1, source_target_pairs={{0,8},{1,9},{2,10},{3,11},{4,12},{5,13},{6,14},{7,15},{8,0},{9,1},... | collective-permute-start | bytes 49160 | tf_op jit(solution)/shard_map/ppermute | solution.py:15
  9.3 1.8 %collective-permute-done.1 = f32[2,16,128]{2,1,0:T(8,128)S(1)} collective-permute-done((f32[2,16,128]{2,1,0:T(8,128)S(1)}, f32[2,16,128]{2,1,0:T(8,128)S(1)}, u32[]{:S(2)}, u32[]{:S(2)}) %collective-permute-start.1) | collective-permute-done | bytes 16416 | tf_op jit(solution)/shard_map/ppermute | solution.py:15
  11.1 1.8 %collective-permute-start.2 = (f32[4,16,128]{2,1,0:T(8,128)S(1)}, f32[4,16,128]{2,1,0:T(8,128)S(1)}, u32[]{:S(2)}, u32[]{:S(2)}) collective-permute-start(f32[4,16,128]{2,1,0:T(8,128)S(1)} %maximum_select_fusion.8), channel_id=1, source_target_pairs={{0,4},{1,5},{2,6},{3,7},{4,0},{5,1},{6,2},{7,3},{8,12},{9,13},{10,... | collective-permute-start | bytes 98312 | tf_op jit(solution)/shard_map/ppermute | solution.py:15
  12.9 2.1 %collective-permute-done.2 = f32[4,16,128]{2,1,0:T(8,128)S(1)} collective-permute-done((f32[4,16,128]{2,1,0:T(8,128)S(1)}, f32[4,16,128]{2,1,0:T(8,128)S(1)}, u32[]{:S(2)}, u32[]{:S(2)}) %collective-permute-start.2) | collective-permute-done | bytes 32800 | tf_op jit(solution)/shard_map/ppermute | solution.py:15
  15.0 1.9 %collective-permute-start.3 = (f32[8,16,128]{2,1,0:T(8,128)S(1)}, f32[8,16,128]{2,1,0:T(8,128)S(1)}, u32[]{:S(2)}, u32[]{:S(2)}) collective-permute-start(f32[8,16,128]{2,1,0:T(8,128)S(1)} %maximum_select_fusion.7), channel_id=1, source_target_pairs={{0,2},{1,3},{2,0},{3,1},{4,6},{5,7},{6,4},{7,5},{8,10},{9,11},{10,... | collective-permute-start | bytes 196616 | tf_op jit(solution)/shard_map/ppermute | solution.py:15
  17.0 2.4 %collective-permute-done.3 = f32[8,16,128]{2,1,0:T(8,128)S(1)} collective-permute-done((f32[8,16,128]{2,1,0:T(8,128)S(1)}, f32[8,16,128]{2,1,0:T(8,128)S(1)}, u32[]{:S(2)}, u32[]{:S(2)}) %collective-permute-start.3) | collective-permute-done | bytes 65568 | tf_op jit(solution)/shard_map/ppermute | solution.py:15
  24.7 1.9 %collective-permute-start.6 = (f32[512,128]{0,1:T(8,128)S(1)}, f32[512,128]{0,1:T(8,128)}, u32[]{:S(2)}, u32[]{:S(2)}) collective-permute-start(f32[512,128]{0,1:T(8,128)S(1)} %add.42), channel_id=1, source_target_pairs={{0,2},{1,3},{2,0},{3,1},{4,6},{5,7},{6,4},{7,5},{8,10},{9,11},{10,... | collective-permute-start | bytes 786440 | tf_op jit(solution)/shard_map/ppermute | solution.py:31
  26.6 1.8 %copy.18 = f32[1,512,128]{1,2,0:T(8,128)} copy(f32[1,512,128]{2,1,0:T(8,128)} %param.11) | data formatting | bytes 524288 | tf_op args[0]
  28.4 4.9 %collective-permute-done.6 = f32[512,128]{0,1:T(8,128)} collective-permute-done((f32[512,128]{0,1:T(8,128)S(1)}, f32[512,128]{0,1:T(8,128)}, u32[]{:S(2)}, u32[]{:S(2)}) %collective-permute-start.6) | collective-permute-done | bytes 262176 | tf_op jit(solution)/shard_map/ppermute | solution.py:31
  33.4 1.8 %fusion.3 = f32[128,512]{1,0:T(8,128)S(1)} fusion(f32[1,512,512]{2,1,0:T(8,128)S(1)} %copy-done.4, f32[1,512,128]{1,2,0:T(8,128)} %copy.18, f32[512,128]{0,1:T(8,128)S(1)} %add.42, f32[512,128]{0,1:T(8,128)} %collective-permute-done.6), kind=kOutput, calls=%fused_computation.12 | convolution fusion | flops 402784256 | bytes 2097152 | tf_op jit(solution)/shard_map/kw,kr->wr/dot_general | solution.py:61
  35.2 2.9 %collective-permute-start.7 = (f32[1,128,128]{1,2,0:T(8,128)S(1)}, f32[1,128,128]{1,2,0:T(8,128)S(1)}, u32[]{:S(2)}, u32[]{:S(2)}) collective-permute-start(f32[1,128,128]{1,2,0:T(8,128)S(1)} %dynamic-slice_bitcast_fusion), channel_id=1, source_target_pairs={{0,16},{1,17},{2,18},{3,19},{4,20},{5,21},{6,22},{7,23},{8,24},{9,... | collective-permute-start | bytes 196616 | tf_op jit(solution)/shard_map/ppermute | solution.py:15
  38.1 2.6 %collective-permute-done.7 = f32[1,128,128]{1,2,0:T(8,128)S(1)} collective-permute-done((f32[1,128,128]{1,2,0:T(8,128)S(1)}, f32[1,128,128]{1,2,0:T(8,128)S(1)}, u32[]{:S(2)}, u32[]{:S(2)}) %collective-permute-start.7) | collective-permute-done | bytes 65568 | tf_op jit(solution)/shard_map/ppermute | solution.py:15
  42.3 3.5 %collective-permute-done.8 = f32[2,128,128]{1,2,0:T(8,128)S(1)} collective-permute-done((f32[2,128,128]{1,2,0:T(8,128)S(1)}, f32[2,128,128]{1,2,0:T(8,128)S(1)}, u32[]{:S(2)}, u32[]{:S(2)}) %collective-permute-start.8) | collective-permute-done | bytes 131104 | tf_op jit(solution)/shard_map/ppermute | solution.py:15
  47.3 4.9 %collective-permute-done.9 = f32[4,128,128]{1,2,0:T(8,128)S(1)} collective-permute-done((f32[4,128,128]{1,2,0:T(8,128)S(1)}, f32[4,128,128]{1,2,0:T(8,128)S(1)}, u32[]{:S(2)}, u32[]{:S(2)}) %collective-permute-start.9) | collective-permute-done | bytes 262176 | tf_op jit(solution)/shard_map/ppermute | solution.py:15
  52.3 1.6 %collective-permute-start.10 = (f32[8,128,128]{1,2,0:T(8,128)S(1)}, f32[8,128,128]{1,2,0:T(8,128)S(1)}, u32[]{:S(2)}, u32[]{:S(2)}) collective-permute-start(f32[8,128,128]{1,2,0:T(8,128)S(1)} %maximum_select_fusion.2), channel_id=1, source_target_pairs={{0,2},{1,3},{2,0},{3,1},{4,6},{5,7},{6,4},{7,5},{8,10},{9,11},{10,... | collective-permute-start | bytes 1572872 | tf_op jit(solution)/shard_map/ppermute | solution.py:15
  53.8 8.1 %collective-permute-done.10 = f32[8,128,128]{1,2,0:T(8,128)S(1)} collective-permute-done((f32[8,128,128]{1,2,0:T(8,128)S(1)}, f32[8,128,128]{1,2,0:T(8,128)S(1)}, u32[]{:S(2)}, u32[]{:S(2)}) %collective-permute-start.10) | collective-permute-done | bytes 524320 | tf_op jit(solution)/shard_map/ppermute | solution.py:15
  64.9 3.2 %maximum_select_fusion = f32[32,128,128]{1,2,0:T(8,128)} fusion(f32[16,128,128]{1,2,0:T(8,128)S(1)} %maximum_select_fusion.1, f32[16,128,128]{1,2,0:T(8,128)} %collective-permute-done.11, pred[]{:T(512)S(6)} %eq.28), kind=kLoop, calls=%fused_computation.5 | loop fusion | flops 1572864 | bytes 4194305 | tf_op jit(solution)/shard_map/jit(_where)/select_n | solution.py:17
  68.0 2.9 %copy.20 = f32[2,2,2,2,2,128,128]{6,5,0,1,2,3,4:T(8,128)} copy(f32[2,2,2,2,2,128,128]{5,6,4,3,2,1,0:T(8,128)} %bitcast.43) | data formatting | bytes 4194304 | tf_op jit(solution)/shard_map/jit(_where)/select_n | solution.py:17
  71.0 3.6 %gather_fusion.2 = f32[8,512,128]{2,1,0:T(8,128)} fusion(f32[8,512,128]{2,1,0:T(8,128)} %bitcast.44, s32[1024]{0:T(1024)S(1)} %pad_clamp_fusion), kind=kCustom, calls=%fused_computation.2 | custom fusion | bytes 4194336 | tf_op jit(solution)/shard_map/gather | solution.py:66
  74.6 3.8 %fusion = f32[8,256,128]{2,1,0:T(8,128)S(1)} fusion(f32[8,512,128]{2,1,0:T(8,128)} %gather_fusion.2, s32[8,256]{1,0:T(8,128)S(1)} %copy-done.5), kind=kOutput, calls=%fused_computation.4 | convolution fusion | flops 1611661312 | bytes 3153920 | tf_op jit(solution)/shard_map/skj,sjr->skr/dot_general | solution.py:69
  78.4 3.5 %fusion.2 = f32[8,256,128]{2,1,0:T(8,128)S(1)} fusion(f32[8,256,128]{2,1,0:T(8,128)S(1)} %copy-done.3, f32[8,256,128]{2,1,0:T(8,128)S(1)} %fusion, f32[8,256,256]{2,1,0:T(8,128)S(1)} %copy-done), kind=kOutput, calls=%fused_computation.9 | convolution fusion | flops 805568512 | bytes 5242880 | tf_op jit(solution)/shard_map/skw,skr->swr/dot_general | solution.py:70
  82.0 2.0 %convolution_bitcast_fusion = f32[8,256,128]{1,2,0:T(8,128)S(1)} fusion(f32[8,256,128]{2,1,0:T(8,128)S(1)} %fusion.2, f32[8,256,256]{2,1,0:T(8,128)S(1)} %copy-done.2), kind=kOutput, calls=%fused_computation.7 | convolution fusion | flops 805306368 | bytes 4194304 | tf_op jit(solution)/shard_map/skw,skr->swr/dot_general | solution.py:71
  (45 shorter events, 13.6 us)
Async XLA Ops:
  0.6 77.8 %copy-start = (f32[8,256,256]{2,1,0:T(8,128)S(1)}, f32[8,256,256]{2,1,0:T(8,128)}, u32[]{:S(2)}) copy-start(f32[8,256,256]{2,1,0:T(8,128)} %param.19) | copy-start | bytes 6291460
  0.6 5.9 %collective-permute-start = (f32[1,16,128]{2,1,0:T(8,128)}, f32[1,16,128]{2,1,0:T(8,128)S(1)}, u32[]{:S(2)}, u32[]{:S(2)}) collective-permute-start(f32[1,16,128]{2,1,0:T(8,128)} %bitcast.47), channel_id=1, source_target_pairs={{0,16},{1,17},{2,18},{3,19},{4,20},{5,21},{6,22},{7,23},{8,24},{9,... | collective-permute-start | bytes 24584 | tf_op jit(solution)/shard_map/ppermute | solution.py:15
  7.4 3.7 %collective-permute-start.1 = (f32[2,16,128]{2,1,0:T(8,128)S(1)}, f32[2,16,128]{2,1,0:T(8,128)S(1)}, u32[]{:S(2)}, u32[]{:S(2)}) collective-permute-start(f32[2,16,128]{2,1,0:T(8,128)S(1)} %maximum_select_fusion.9), channel_id=1, source_target_pairs={{0,8},{1,9},{2,10},{3,11},{4,12},{5,13},{6,14},{7,15},{8,0},{9,1},... | collective-permute-start | bytes 49160 | tf_op jit(solution)/shard_map/ppermute | solution.py:15
  11.1 3.9 %collective-permute-start.2 = (f32[4,16,128]{2,1,0:T(8,128)S(1)}, f32[4,16,128]{2,1,0:T(8,128)S(1)}, u32[]{:S(2)}, u32[]{:S(2)}) collective-permute-start(f32[4,16,128]{2,1,0:T(8,128)S(1)} %maximum_select_fusion.8), channel_id=1, source_target_pairs={{0,4},{1,5},{2,6},{3,7},{4,0},{5,1},{6,2},{7,3},{8,12},{9,13},{10,... | collective-permute-start | bytes 98312 | tf_op jit(solution)/shard_map/ppermute | solution.py:15
  15.0 4.3 %collective-permute-start.3 = (f32[8,16,128]{2,1,0:T(8,128)S(1)}, f32[8,16,128]{2,1,0:T(8,128)S(1)}, u32[]{:S(2)}, u32[]{:S(2)}) collective-permute-start(f32[8,16,128]{2,1,0:T(8,128)S(1)} %maximum_select_fusion.7), channel_id=1, source_target_pairs={{0,2},{1,3},{2,0},{3,1},{4,6},{5,7},{6,4},{7,5},{8,10},{9,11},{10,... | collective-permute-start | bytes 196616 | tf_op jit(solution)/shard_map/ppermute | solution.py:15
  19.4 1.4 %collective-permute-start.4 = (f32[16,16,128]{2,1,0:T(8,128)S(1)}, f32[16,16,128]{2,1,0:T(8,128)S(1)}, u32[]{:S(2)}, u32[]{:S(2)}) collective-permute-start(f32[16,16,128]{2,1,0:T(8,128)S(1)} %maximum_select_fusion.5), channel_id=1, source_target_pairs={{0,1},{1,0},{2,3},{3,2},{4,5},{5,4},{6,7},{7,6},{8,9},{9,8},{10,11... | collective-permute-start | bytes 393224 | tf_op jit(solution)/shard_map/ppermute | solution.py:15
  20.8 12.6 %copy-start.4 = (f32[1,512,512]{2,1,0:T(8,128)S(1)}, f32[1,512,512]{2,1,0:T(8,128)}, u32[]{:S(2)}) copy-start(f32[1,512,512]{2,1,0:T(8,128)} %param.13) | copy-start | bytes 3145732
  23.1 1.6 %collective-permute-start.5 = (f32[512,128]{0,1:T(8,128)S(1)}, f32[512,128]{0,1:T(8,128)S(1)}, u32[]{:S(2)}, u32[]{:S(2)}) collective-permute-start(f32[512,128]{0,1:T(8,128)S(1)} %convolution_bitcast_fusion.2), channel_id=1, source_target_pairs={{0,1},{1,0},{2,3},{3,2},{4,5},{5,4},{6,7},{7,6},{8,9},{9,8},{10,11... | collective-permute-start | bytes 786440 | tf_op jit(solution)/shard_map/ppermute | solution.py:31
  24.7 8.6 %collective-permute-start.6 = (f32[512,128]{0,1:T(8,128)S(1)}, f32[512,128]{0,1:T(8,128)}, u32[]{:S(2)}, u32[]{:S(2)}) collective-permute-start(f32[512,128]{0,1:T(8,128)S(1)} %add.42), channel_id=1, source_target_pairs={{0,2},{1,3},{2,0},{3,1},{4,6},{5,7},{6,4},{7,5},{8,10},{9,11},{10,... | collective-permute-start | bytes 786440 | tf_op jit(solution)/shard_map/ppermute | solution.py:31
  35.1 27.0 %copy-start.6 = (s32[8]{0:T(128)S(1)}, s32[8]{0:T(128)}, u32[]{:S(2)}) copy-start(s32[8]{0:T(128)} %param.17) | copy-start | bytes 100
  35.1 27.0 %copy-start.1 = (s32[8]{0:T(128)S(1)}, s32[8]{0:T(128)}, u32[]{:S(2)}) copy-start(s32[8]{0:T(128)} %param.16) | copy-start | bytes 100
  35.2 5.5 %collective-permute-start.7 = (f32[1,128,128]{1,2,0:T(8,128)S(1)}, f32[1,128,128]{1,2,0:T(8,128)S(1)}, u32[]{:S(2)}, u32[]{:S(2)}) collective-permute-start(f32[1,128,128]{1,2,0:T(8,128)S(1)} %dynamic-slice_bitcast_fusion), channel_id=1, source_target_pairs={{0,16},{1,17},{2,18},{3,19},{4,20},{5,21},{6,22},{7,23},{8,24},{9,... | collective-permute-start | bytes 196616 | tf_op jit(solution)/shard_map/ppermute | solution.py:15
  40.7 5.0 %collective-permute-start.8 = (f32[2,128,128]{1,2,0:T(8,128)S(1)}, f32[2,128,128]{1,2,0:T(8,128)S(1)}, u32[]{:S(2)}, u32[]{:S(2)}) collective-permute-start(f32[2,128,128]{1,2,0:T(8,128)S(1)} %maximum_select_fusion.6), channel_id=1, source_target_pairs={{0,8},{1,9},{2,10},{3,11},{4,12},{5,13},{6,14},{7,15},{8,0},{9,1},... | collective-permute-start | bytes 393224 | tf_op jit(solution)/shard_map/ppermute | solution.py:15
  45.8 6.4 %collective-permute-start.9 = (f32[4,128,128]{1,2,0:T(8,128)S(1)}, f32[4,128,128]{1,2,0:T(8,128)S(1)}, u32[]{:S(2)}, u32[]{:S(2)}) collective-permute-start(f32[4,128,128]{1,2,0:T(8,128)S(1)} %maximum_select_fusion.4), channel_id=1, source_target_pairs={{0,4},{1,5},{2,6},{3,7},{4,0},{5,1},{6,2},{7,3},{8,12},{9,13},{10,... | collective-permute-start | bytes 786440 | tf_op jit(solution)/shard_map/ppermute | solution.py:15
  52.3 9.7 %collective-permute-start.10 = (f32[8,128,128]{1,2,0:T(8,128)S(1)}, f32[8,128,128]{1,2,0:T(8,128)S(1)}, u32[]{:S(2)}, u32[]{:S(2)}) collective-permute-start(f32[8,128,128]{1,2,0:T(8,128)S(1)} %maximum_select_fusion.2), channel_id=1, source_target_pairs={{0,2},{1,3},{2,0},{3,1},{4,6},{5,7},{6,4},{7,5},{8,10},{9,11},{10,... | collective-permute-start | bytes 1572872 | tf_op jit(solution)/shard_map/ppermute | solution.py:15
  62.0 2.9 %collective-permute-start.11 = (f32[16,128,128]{1,2,0:T(8,128)S(1)}, f32[16,128,128]{1,2,0:T(8,128)}, u32[]{:S(2)}, u32[]{:S(2)}) collective-permute-start(f32[16,128,128]{1,2,0:T(8,128)S(1)} %maximum_select_fusion.1), channel_id=1, source_target_pairs={{0,1},{1,0},{2,3},{3,2},{4,5},{5,4},{6,7},{7,6},{8,9},{9,8},{10,11... | collective-permute-start | bytes 3145736 | tf_op jit(solution)/shard_map/ppermute | solution.py:15
  71.0 3.6 %copy-start.5 = (s32[8,256]{1,0:T(8,128)S(1)}, s32[8,256]{1,0:T(8,128)}, u32[]{:S(2)}) copy-start(s32[8,256]{1,0:T(8,128)} %param.18) | copy-start | bytes 24580
  74.6 3.8 %copy-start.3 = (f32[8,256,128]{2,1,0:T(8,128)S(1)}, f32[8,256,128]{2,1,0:T(8,128)}, u32[]{:S(2)}) copy-start(f32[8,256,128]{2,1,0:T(8,128)} %param.20) | copy-start | bytes 3145732
  78.4 3.5 %copy-start.2 = (f32[8,256,256]{2,1,0:T(8,128)S(1)}, f32[8,256,256]{2,1,0:T(8,128)}, u32[]{:S(2)}) copy-start(f32[8,256,256]{2,1,0:T(8,128)} %param.21) | copy-start | bytes 6291460

commit v2 on v0

v2 whole, which is shorter than its diff:
```python
import jax
import jax.numpy as jnp
from jax import lax
from jax.sharding import PartitionSpec as P


def xor_gather(block, axes, count, groups):
    held = block[None]
    for bits in groups:
        parts = [held]
        for k in range(1, 1 << len(bits)):
            v = sum(((k >> t) & 1) << b for t, b in enumerate(bits))
            parts.append(lax.ppermute(held, axes, [(i, i ^ v) for i in range(count)]))
        held = jnp.concatenate(parts, 0)
    return held


def xor_position(offset, groups):
    position = jnp.zeros_like(offset)
    stride = 1
    for bits in groups:
        k = sum(((offset >> b) & 1) << t for t, b in enumerate(bits))
        position = position + k * stride
        stride *= 1 << len(bits)
    return position


def log2(count):
    bits = count.bit_length() - 1
    assert (1 << bits) == count
    return bits


def local(
    upper_rhs,
    upper_panel,
    upper_inverse,
    top_index,
    top_solution,
    owner_map,
    parent_list,
    lower_index,
    lower_panel,
    lower_rhs,
    lower_inverse,
):
    highest = lax.Precision.HIGHEST
    leaves = lax.axis_size("leaf")
    panels = lax.axis_size("panel")
    count = leaves * panels
    both = ("leaf", "panel")
    me = lax.axis_index(both)
    panel_index = lax.axis_index("panel")
    width_upper = upper_rhs.shape[1]
    share = width_upper // panels
    begin = panel_index * share

    panel_bits = list(range(log2(panels)))
    leaf_bits = list(range(log2(panels), log2(count)))
    high_first = leaf_bits[::-1]
    leaf_groups = []
    if len(high_first) % 2:
        leaf_groups.append([high_first[0]])
        high_first = high_first[1:]
    leaf_groups += [high_first[i : i + 2] for i in range(0, len(high_first), 2)]
    top_groups = [panel_bits] + leaf_groups
    spread_groups = leaf_groups + [[b] for b in panel_bits[::-1]]

    top_rows = top_solution.shape[0]
    top_held = xor_gather(top_solution, both, count, top_groups)
    top_held = top_held.reshape(count * top_rows, top_solution.shape[1])
    wanted = top_index[0]
    source = wanted // top_rows
    slot = xor_position(source ^ me, top_groups) * top_rows + wanted % top_rows
    gathered = top_held[slot]

    folded = jnp.einsum("kv,vw->kw", upper_panel[0], upper_inverse[0], precision=highest)
    own_inverse = lax.dynamic_slice_in_dim(upper_inverse[0], begin, share, 1)
    own_base = jnp.einsum("kw,kr->wr", own_inverse, upper_rhs[0], precision=highest)
    term = jnp.einsum("kw,kr->wr", folded, gathered, precision=highest)
    total = lax.dynamic_slice_in_dim(term, begin, share, 0)
    for v in range(1, panels):
        outgoing = lax.dynamic_slice_in_dim(term, (panel_index ^ v) * share, share, 0)
        total = total + lax.ppermute(outgoing, "panel", [(i, i ^ v) for i in range(panels)])
    own_rows = own_base - total

    lower_base = jnp.einsum("skw,skr->swr", lower_inverse, lower_rhs, precision=highest)
    chained = jnp.einsum("skv,svw->skw", lower_panel, lower_inverse, precision=highest)
    columns = lax.broadcasted_iota(jnp.int32, lower_index.shape + (width_upper,), 2)
    pick = (lower_index[:, :, None] == columns).astype(jnp.float32)
    spread = jnp.einsum("skj,skw->sjw", pick, chained, precision=highest)

    held = xor_gather(own_rows, both, count, spread_groups)
    position = owner_map[parent_list]
    sources = position[:, None] * panels + jnp.arange(panels, dtype=jnp.int32)[None, :]
    slabs = held[xor_position(sources ^ me, spread_groups)]
    slabs = slabs.reshape(position.shape[0], width_upper, own_rows.shape[1])
    lower_update = jnp.einsum("sjw,sjr->swr", spread, slabs, precision=highest)
    lower_solution = lower_base - lower_update
    return (own_rows[None], lower_solution)


def solution(mesh):
    placed = (
        P("leaf", None, None),
        P("leaf", "panel", None),
        P("leaf", None, None),
        P("leaf", "panel"),
        P(("leaf", "panel"), None),
        P(),
        P(("leaf", "panel")),
        P(("leaf", "panel"), None),
        P(("leaf", "panel"), None, None),
        P(("leaf", "panel"), None, None),
        P(("leaf", "panel"), None, None),
    )
    return jax.shard_map(
        local,
        mesh=mesh,
        in_specs=placed,
        out_specs=(P("leaf", "panel", None), P(("leaf", "panel"), None, None)),
        check_vma=False,
    )
```

time: 175 us -> 84.5 us (0.48)
  waiting for transfers between devices: 75.6 us -> 27.5 us
  blocking collectives: 44.3 us -> 0 us
  starting transfers between devices: 0.08 us -> 19.5 us
  local copies, waits for them, and re-layouts: 27.8 us -> 11.1 us
  between operations: 14.2 us -> 0.89 us
  matrix products: 12.2 us -> 24.7 us
    all_gather x1 -> x0, waiting for transfers between devices: 47.4 us -> none  [local(): all_upper = lax.all_gather(full_solution[None], 'leaf', axis=0, tiled=True)]
    all_gather x1 -> x0, blocking collectives: 44.3 us -> none  [local(): lax.all_gather(top_solution, ('leaf', 'panel'), axis=0, tiled=True)]
    psum x1 -> x0, waiting for transfers between devices: 28.2 us -> none  [local(): update = lax.psum(partial_update, 'panel')]
    ppermute x0 -> x16, waiting for transfers between devices: none -> 27.5 us  [the longest x13 23.8 us: xor_gather(): parts.append(lax.ppermute(held, axes, [(i, i ^ v) for i in range(count)]))]
    ppermute x0 -> x16, starting transfers between devices: none -> 19.5 us  [the longest x13 17.5 us: xor_gather(): parts.append(lax.ppermute(held, axes, [(i, i ^ v) for i in range(count)]))]
    gather x2, local copies, waits for them, and re-layouts: 21.3 us -> 4.4 us  [the longest x1 3.67 us: local(): slabs = held[xor_position(sources ^ me, spread_groups)]]
    dot_general x4 -> x7, matrix products: 12.2 us -> 24.7 us  [the longest x1 7.6 us: local(): lower_update = jnp.einsum('sjw,sjr->swr', spread, slabs, precision=highest)]
    all_gather x1 -> x0, local copies, waits for them, and re-layouts: 2.9 us -> none  [local(): all_upper = lax.all_gather(full_solution[None], 'leaf', axis=0, tiled=True)]
  transfers between devices with their start and end apart: 2 -> 16, of which waited for: 2 -> 10; matrix products, arithmetic and copies ran while one was open for 1% -> 21% of each run, Pallas kernels for 0% -> 0%
where the time goes in v2:
time: 84.5 us; the launch traced here: 83.8 us
  waiting for transfers between devices  27.5 us (33%)
  matrix products  24.7 us (29%)
  starting transfers between devices  19.5 us (23%)
  local copies, waits for them, and re-layouts  11.1 us (13%)
  between operations  0.89 us (1%)
    ppermute x13, waiting for transfers between devices, xor_gather(): parts.append(lax.ppermute(held, axes, [(i, i ^ v) for i in range(count)]))  23.8 us
    ppermute x13, starting transfers between devices, xor_gather(): parts.append(lax.ppermute(held, axes, [(i, i ^ v) for i in range(count)]))  17.5 us
    dot_general x1, matrix products, local(): lower_update = jnp.einsum('sjw,sjr->swr', spread, slabs, precision=highest)  7.6 us
    dot_general x1, matrix products, local(): jnp.einsum('skw,skr->swr', lower_inverse, lower_rhs, precision=highest)  4.84 us
    dot_general x1, matrix products, local(): spread = jnp.einsum('skj,skw->sjw', pick, chained, precision=highest)  4.39 us
    ppermute x3, waiting for transfers between devices, local(): lax.ppermute(outgoing, 'panel', [(i, i ^ v) for i in range(panels)])  3.77 us
    unnamed x28, local copies, waits for them, and re-layouts  3.76 us
    gather x1, local copies, waits for them, and re-layouts, local(): slabs = held[xor_position(sources ^ me, spread_groups)]  3.67 us
  transfers between devices with their start and end apart: 16, of which 10 were waited for; matrix products, arithmetic and copies ran while one was open for 21% of the time, Pallas kernels for 0%

profile of v2, /device:TPU:0, one launch (start us, length us, event | category | flops | bytes accessed | tf_op | source)
XLA Modules:
  0.0 83.8 jit_solution(15535347354524358484)
XLA Ops:
  1.2 2.6 %collective-permute-start.1 = (f32[1,16,128]{2,1,0:T(8,128)}, f32[1,16,128]{2,1,0:T(8,128)S(1)}, u32[]{:S(2)}, u32[]{:S(2)}) collective-permute-start(f32[1,16,128]{2,1,0:T(8,128)} %bitcast.57), channel_id=1, source_target_pairs={{0,2},{1,3},{2,0},{3,1},{4,6},{5,7},{6,4},{7,5},{8,10},{9,11},{10,... | collective-permute-start | bytes 24584 | tf_op jit(solution)/shard_map/ppermute | solution.py:13
  4.6 2.4 %fusion.2 = f32[256,512]{1,0:T(8,128)S(1)} fusion(f32[1,512,512]{2,1,0:T(8,128)} %param.13, f32[1,256,512]{2,1,0:T(8,128)} %param.12), kind=kOutput, calls=%fused_computation.7 | convolution fusion | flops 805306368 | bytes 2097152 | tf_op jit(solution)/shard_map/kv,vw->kw/dot_general | solution.py:77
  7.2 2.9 %collective-permute-start.3 = (f32[4,16,128]{2,1,0:T(8,128)S(1)}, f32[4,16,128]{2,1,0:T(8,128)S(1)}, u32[]{:S(2)}, u32[]{:S(2)}) collective-permute-start(f32[4,16,128]{2,1,0:T(8,128)S(1)} %pad_maximum_fusion.1), channel_id=1, source_target_pairs={{0,16},{1,17},{2,18},{3,19},{4,20},{5,21},{6,22},{7,23},{8,24},{9,... | collective-permute-start | bytes 98312 | tf_op jit(solution)/shard_map/ppermute | solution.py:13
  10.0 2.0 %collective-permute-done.3 = f32[4,16,128]{2,1,0:T(8,128)S(1)} collective-permute-done((f32[4,16,128]{2,1,0:T(8,128)S(1)}, f32[4,16,128]{2,1,0:T(8,128)S(1)}, u32[]{:S(2)}, u32[]{:S(2)}) %collective-permute-start.3) | collective-permute-done | bytes 32800 | tf_op jit(solution)/shard_map/ppermute | solution.py:13
  12.1 1.8 %collective-permute-start.4 = (f32[8,16,128]{2,1,0:T(8,128)S(1)}, f32[8,16,128]{2,1,0:T(8,128)S(1)}, u32[]{:S(2)}, u32[]{:S(2)}) collective-permute-start(f32[8,16,128]{2,1,0:T(8,128)S(1)} %get-tuple-element.22), channel_id=1, source_target_pairs={{0,8},{1,9},{2,10},{3,11},{4,12},{5,13},{6,14},{7,15},{8,0},{9,1},... | collective-permute-start | bytes 196616 | tf_op jit(solution)/shard_map/ppermute | solution.py:13
  13.8 1.5 %collective-permute-start.5 = (f32[8,16,128]{2,1,0:T(8,128)S(1)}, f32[8,16,128]{2,1,0:T(8,128)S(1)}, u32[]{:S(2)}, u32[]{:S(2)}) collective-permute-start(f32[8,16,128]{2,1,0:T(8,128)S(1)} %get-tuple-element.22), channel_id=1, source_target_pairs={{0,4},{1,5},{2,6},{3,7},{4,0},{5,1},{6,2},{7,3},{8,12},{9,13},{10,... | collective-permute-start | bytes 196616 | tf_op jit(solution)/shard_map/ppermute | solution.py:13
  16.3 2.5 %collective-permute-done.5 = f32[8,16,128]{2,1,0:T(8,128)S(1)} collective-permute-done((f32[8,16,128]{2,1,0:T(8,128)S(1)}, f32[8,16,128]{2,1,0:T(8,128)S(1)}, u32[]{:S(2)}, u32[]{:S(2)}) %collective-permute-start.5) | collective-permute-done | bytes 65568 | tf_op jit(solution)/shard_map/ppermute | solution.py:13
  18.8 1.7 %collective-permute-done.6 = f32[8,16,128]{2,1,0:T(8,128)S(1)} collective-permute-done((f32[8,16,128]{2,1,0:T(8,128)S(1)}, f32[8,16,128]{2,1,0:T(8,128)S(1)}, u32[]{:S(2)}, u32[]{:S(2)}) %collective-permute-start.6) | collective-permute-done | bytes 65568 | tf_op jit(solution)/shard_map/ppermute | solution.py:13
  22.3 1.6 %collective-permute-start.8 = (f32[128,128]{1,0:T(8,128)S(1)}, f32[128,128]{1,0:T(8,128)S(1)}, u32[]{:S(2)}, u32[]{:S(2)}) collective-permute-start(f32[128,128]{1,0:T(8,128)S(1)} %get-tuple-element.6), channel_id=1, source_target_pairs={{0,2},{1,3},{2,0},{3,1},{4,6},{5,7},{6,4},{7,5},{8,10},{9,11},{10,... | collective-permute-start | bytes 196616 | tf_op jit(solution)/shard_map/ppermute | solution.py:84
  24.2 2.6 %collective-permute-done.8 = f32[128,128]{1,0:T(8,128)S(1)} collective-permute-done((f32[128,128]{1,0:T(8,128)S(1)}, f32[128,128]{1,0:T(8,128)S(1)}, u32[]{:S(2)}, u32[]{:S(2)}) %collective-permute-start.8) | collective-permute-done | bytes 65568 | tf_op jit(solution)/shard_map/ppermute | solution.py:84
  26.9 1.1 %collective-permute-done.9 = f32[128,128]{1,0:T(8,128)S(1)} collective-permute-done((f32[128,128]{1,0:T(8,128)S(1)}, f32[128,128]{1,0:T(8,128)S(1)}, u32[]{:S(2)}, u32[]{:S(2)}) %collective-permute-start.9) | collective-permute-done | bytes 65568 | tf_op jit(solution)/shard_map/ppermute | solution.py:84
  28.0 2.2 %constant_dynamic-update-slice_fusion.23 = (f32[16,128,128]{2,1,0:T(8,128)}, f32[32,128,128]{2,1,0:T(8,128)}, f32[8,128,128]{2,1,0:T(8,128)}, f32[1,128,128]{2,1,0:T(8,128)S(1)}) fusion(f32[128,128]{1,0:T(8,128)S(1)} %collective-permute-done.9, f32[128,128]{1,0:T(8,128)S(1)} %collective-permute-done.8, f32[128,128]{1,0:T(8,128)S(1)} %collective-permute-done.7, ...), kind=kOutput, calls=%fused_computation.39 | convolution fusion | flops 100728832 | bytes 1049600 | tf_op jit(solution)/shard_map/kw,kr->wr/dot_general | solution.py:79
  30.2 2.9 %collective-permute-start.10 = (f32[1,128,128]{2,1,0:T(8,128)S(1)}, f32[1,128,128]{2,1,0:T(8,128)S(1)}, u32[]{:S(2)}, u32[]{:S(2)}) collective-permute-start(f32[1,128,128]{2,1,0:T(8,128)S(1)} %get-tuple-element.32), channel_id=1, source_target_pairs={{0,16},{1,17},{2,18},{3,19},{4,20},{5,21},{6,22},{7,23},{8,24},{9,... | collective-permute-start | bytes 196616 | tf_op jit(solution)/shard_map/ppermute | solution.py:13
  33.1 3.4 %collective-permute-done.10 = f32[1,128,128]{2,1,0:T(8,128)S(1)} collective-permute-done((f32[1,128,128]{2,1,0:T(8,128)S(1)}, f32[1,128,128]{2,1,0:T(8,128)S(1)}, u32[]{:S(2)}, u32[]{:S(2)}) %collective-permute-start.10) | collective-permute-done | bytes 65568 | tf_op jit(solution)/shard_map/ppermute | solution.py:13
  37.9 2.9 %collective-permute-start.13 = (f32[2,128,128]{2,1,0:T(8,128)S(1)}, f32[2,128,128]{2,1,0:T(8,128)S(1)}, u32[]{:S(2)}, u32[]{:S(2)}) collective-permute-start(f32[2,128,128]{2,1,0:T(8,128)S(1)} %pad_maximum_fusion), channel_id=1, source_target_pairs={{0,12},{1,13},{2,14},{3,15},{4,8},{5,9},{6,10},{7,11},{8,4},{9,5},... | collective-permute-start | bytes 393224 | tf_op jit(solution)/shard_map/ppermute | solution.py:13
  41.5 1.4 %collective-permute-done.11 = f32[2,128,128]{2,1,0:T(8,128)S(1)} collective-permute-done((f32[2,128,128]{2,1,0:T(8,128)S(1)}, f32[2,128,128]{2,1,0:T(8,128)S(1)}, u32[]{:S(2)}, u32[]{:S(2)}) %collective-permute-start.11) | collective-permute-done | bytes 131104 | tf_op jit(solution)/shard_map/ppermute | solution.py:13
  43.7 1.9 %collective-permute-done.12 = f32[2,128,128]{2,1,0:T(8,128)S(1)} collective-permute-done((f32[2,128,128]{2,1,0:T(8,128)S(1)}, f32[2,128,128]{2,1,0:T(8,128)S(1)}, u32[]{:S(2)}, u32[]{:S(2)}) %collective-permute-start.12) | collective-permute-done | bytes 131104 | tf_op jit(solution)/shard_map/ppermute | solution.py:13
  47.1 1.5 %collective-permute-start.14 = (f32[8,128,128]{2,1,0:T(8,128)}, f32[8,128,128]{2,1,0:T(8,128)S(1)}, u32[]{:S(2)}, u32[]{:S(2)}) collective-permute-start(f32[8,128,128]{2,1,0:T(8,128)} %get-tuple-element.9), channel_id=1, source_target_pairs={{0,2},{1,3},{2,0},{3,1},{4,6},{5,7},{6,4},{7,5},{8,10},{9,11},{10,... | collective-permute-start | bytes 1572872 | tf_op jit(solution)/shard_map/ppermute | solution.py:13
  48.8 10.0 %collective-permute-done.14 = f32[8,128,128]{2,1,0:T(8,128)S(1)} collective-permute-done((f32[8,128,128]{2,1,0:T(8,128)}, f32[8,128,128]{2,1,0:T(8,128)S(1)}, u32[]{:S(2)}, u32[]{:S(2)}) %collective-permute-start.14) | collective-permute-done | bytes 524320 | tf_op jit(solution)/shard_map/ppermute | solution.py:13
  60.0 4.8 %fusion.16 = f32[8,256,128]{2,1,0:T(8,128)S(1)} fusion(f32[8,256,256]{2,1,0:T(8,128)S(1)} %copy-done, f32[8,256,128]{2,1,0:T(8,128)} %param.20), kind=kOutput, calls=%fused_computation.67 | convolution fusion | flops 805306368 | bytes 4194304 | tf_op jit(solution)/shard_map/skw,skr->swr/dot_general | solution.py:87
  64.9 2.2 %fusion.17 = f32[8,256,256]{2,1,0:T(8,128)S(1)} fusion(f32[8,256,256]{2,1,0:T(8,128)S(1)} %copy-done.2, f32[8,256,256]{2,1,0:T(8,128)S(1)} %copy-done), kind=kOutput, calls=%fused_computation.68 | convolution fusion | flops 1610612736 | bytes 6291456 | tf_op jit(solution)/shard_map/skv,svw->skw/dot_general | solution.py:88
  67.1 4.4 %fusion = f32[8,512,256]{1,2,0:T(8,128)} fusion(f32[8,256,256]{2,1,0:T(8,128)S(1)} %fusion.17, s32[8,256]{1,0:T(8,128)S(1)} %copy-done.6), kind=kOutput, calls=%fused_computation.4 | convolution fusion | flops 3222274048 | bytes 6299648 | tf_op jit(solution)/shard_map/skj,skw->sjw/dot_general | solution.py:91
  72.5 3.7 %gather_fusion.2 = f32[32,128,128]{2,1,0:T(8,128)} fusion(f32[32,128,128]{2,1,0:T(8,128)} %constant_dynamic-update-slice_fusion.24, s32[1024]{0:T(1024)S(1)} %pad_clamp_fusion), kind=kCustom, calls=%fused_computation.2 | custom fusion | bytes 4194432 | tf_op jit(solution)/shard_map/gather | solution.py:96
  76.2 7.6 %convolution_subtract_fusion = f32[8,256,128]{2,1,0:T(8,128)} fusion(f32[8,256,128]{2,1,0:T(8,128)S(1)} %fusion.16, f32[8,512,256]{1,2,0:T(8,128)} %fusion, f32[8,512,128]{2,1,0:T(8,128)} %bitcast.54), kind=kOutput, calls=%fused_computation.6 | convolution fusion | flops 1610874880 | bytes 8388608 | tf_op jit(solution)/shard_map/sjw,sjr->swr/dot_general | solution.py:98
  (61 shorter events, 11.2 us)
Async XLA Ops:
  0.6 59.4 %copy-start = (f32[8,256,256]{2,1,0:T(8,128)S(1)}, f32[8,256,256]{2,1,0:T(8,128)}, u32[]{:S(2)}) copy-start(f32[8,256,256]{2,1,0:T(8,128)} %param.21) | copy-start | bytes 6291460
  0.6 6.5 %copy-start.5 = (f32[16,128]{1,0:T(8,128)S(1)}, f32[16,128]{1,0:T(8,128)}, u32[]{:S(2)}) copy-start(f32[16,128]{1,0:T(8,128)} %param.15) | copy-start | bytes 24580
  0.7 6.4 %copy-start.7 = (s32[1,256]{1,0:T(1,128)S(1)}, s32[1,256]{1,0:T(1,128)}, u32[]{:S(2)}) copy-start(s32[1,256]{1,0:T(1,128)} %param.14) | copy-start | bytes 3076
  0.7 6.4 %collective-permute-start = (f32[1,16,128]{2,1,0:T(8,128)}, f32[1,16,128]{2,1,0:T(8,128)S(1)}, u32[]{:S(2)}, u32[]{:S(2)}) collective-permute-start(f32[1,16,128]{2,1,0:T(8,128)} %bitcast.56), channel_id=1, source_target_pairs={{0,1},{1,0},{2,3},{3,2},{4,5},{5,4},{6,7},{7,6},{8,9},{9,8},{10,11... | collective-permute-start | bytes 24584 | tf_op jit(solution)/shard_map/ppermute | solution.py:13
  1.2 5.9 %collective-permute-start.1 = (f32[1,16,128]{2,1,0:T(8,128)}, f32[1,16,128]{2,1,0:T(8,128)S(1)}, u32[]{:S(2)}, u32[]{:S(2)}) collective-permute-start(f32[1,16,128]{2,1,0:T(8,128)} %bitcast.57), channel_id=1, source_target_pairs={{0,2},{1,3},{2,0},{3,1},{4,6},{5,7},{6,4},{7,5},{8,10},{9,11},{10,... | collective-permute-start | bytes 24584 | tf_op jit(solution)/shard_map/ppermute | solution.py:13
  3.8 3.4 %collective-permute-start.2 = (f32[1,16,128]{2,1,0:T(8,128)}, f32[1,16,128]{2,1,0:T(8,128)S(1)}, u32[]{:S(2)}, u32[]{:S(2)}) collective-permute-start(f32[1,16,128]{2,1,0:T(8,128)} %bitcast.58), channel_id=1, source_target_pairs={{0,3},{1,2},{2,1},{3,0},{4,7},{5,6},{6,5},{7,4},{8,11},{9,10},{10,... | collective-permute-start | bytes 24584 | tf_op jit(solution)/shard_map/ppermute | solution.py:13
  7.0 20.9 %copy-start.3 = (f32[1,512,128]{2,1,0:T(8,128)S(1)}, f32[1,512,128]{2,1,0:T(8,128)}, u32[]{:S(2)}) copy-start(f32[1,512,128]{2,1,0:T(8,128)} %param.11) | copy-start | bytes 786436
  7.1 26.0 %copy-start.8 = (s32[8]{0:T(128)S(1)}, s32[8]{0:T(128)}, u32[]{:S(2)}) copy-start(s32[8]{0:T(128)} %param.17) | copy-start | bytes 100
  7.2 4.9 %collective-permute-start.3 = (f32[4,16,128]{2,1,0:T(8,128)S(1)}, f32[4,16,128]{2,1,0:T(8,128)S(1)}, u32[]{:S(2)}, u32[]{:S(2)}) collective-permute-start(f32[4,16,128]{2,1,0:T(8,128)S(1)} %pad_maximum_fusion.1), channel_id=1, source_target_pairs={{0,16},{1,17},{2,18},{3,19},{4,20},{5,21},{6,22},{7,23},{8,24},{9,... | collective-permute-start | bytes 98312 | tf_op jit(solution)/shard_map/ppermute | solution.py:13
  12.1 4.3 %collective-permute-start.4 = (f32[8,16,128]{2,1,0:T(8,128)S(1)}, f32[8,16,128]{2,1,0:T(8,128)S(1)}, u32[]{:S(2)}, u32[]{:S(2)}) collective-permute-start(f32[8,16,128]{2,1,0:T(8,128)S(1)} %get-tuple-element.22), channel_id=1, source_target_pairs={{0,8},{1,9},{2,10},{3,11},{4,12},{5,13},{6,14},{7,15},{8,0},{9,1},... | collective-permute-start | bytes 196616 | tf_op jit(solution)/shard_map/ppermute | solution.py:13
  13.8 5.0 %collective-permute-start.5 = (f32[8,16,128]{2,1,0:T(8,128)S(1)}, f32[8,16,128]{2,1,0:T(8,128)S(1)}, u32[]{:S(2)}, u32[]{:S(2)}) collective-permute-start(f32[8,16,128]{2,1,0:T(8,128)S(1)} %get-tuple-element.22), channel_id=1, source_target_pairs={{0,4},{1,5},{2,6},{3,7},{4,0},{5,1},{6,2},{7,3},{8,12},{9,13},{10,... | collective-permute-start | bytes 196616 | tf_op jit(solution)/shard_map/ppermute | solution.py:13
  15.3 5.2 %collective-permute-start.6 = (f32[8,16,128]{2,1,0:T(8,128)S(1)}, f32[8,16,128]{2,1,0:T(8,128)S(1)}, u32[]{:S(2)}, u32[]{:S(2)}) collective-permute-start(f32[8,16,128]{2,1,0:T(8,128)S(1)} %get-tuple-element.22), channel_id=1, source_target_pairs={{0,12},{1,13},{2,14},{3,15},{4,8},{5,9},{6,10},{7,11},{8,4},{9,5},... | collective-permute-start | bytes 196616 | tf_op jit(solution)/shard_map/ppermute | solution.py:13
  16.3 20.4 %copy-start.1 = (s32[8]{0:T(128)S(1)}, s32[8]{0:T(128)}, u32[]{:S(2)}) copy-start(s32[8]{0:T(128)} %param.16) | copy-start | bytes 100
  22.3 1.9 %collective-permute-start.7 = (f32[128,128]{1,0:T(8,128)S(1)}, f32[128,128]{1,0:T(8,128)S(1)}, u32[]{:S(2)}, u32[]{:S(2)}) collective-permute-start(f32[128,128]{1,0:T(8,128)S(1)} %get-tuple-element.4), channel_id=1, source_target_pairs={{0,1},{1,0},{2,3},{3,2},{4,5},{5,4},{6,7},{7,6},{8,9},{9,8},{10,11... | collective-permute-start | bytes 196616 | tf_op jit(solution)/shard_map/ppermute | solution.py:84
  22.3 4.5 %collective-permute-start.8 = (f32[128,128]{1,0:T(8,128)S(1)}, f32[128,128]{1,0:T(8,128)S(1)}, u32[]{:S(2)}, u32[]{:S(2)}) collective-permute-start(f32[128,128]{1,0:T(8,128)S(1)} %get-tuple-element.6), channel_id=1, source_target_pairs={{0,2},{1,3},{2,0},{3,1},{4,6},{5,7},{6,4},{7,5},{8,10},{9,11},{10,... | collective-permute-start | bytes 196616 | tf_op jit(solution)/shard_map/ppermute | solution.py:84
  23.9 4.0 %collective-permute-start.9 = (f32[128,128]{1,0:T(8,128)S(1)}, f32[128,128]{1,0:T(8,128)S(1)}, u32[]{:S(2)}, u32[]{:S(2)}) collective-permute-start(f32[128,128]{1,0:T(8,128)S(1)} %get-tuple-element.5), channel_id=1, source_target_pairs={{0,3},{1,2},{2,1},{3,0},{4,7},{5,6},{6,5},{7,4},{8,11},{9,10},{10,... | collective-permute-start | bytes 196616 | tf_op jit(solution)/shard_map/ppermute | solution.py:84
  30.2 29.8 %copy-start.4 = (f32[1,128,128]{2,1,0:T(8,128)}, f32[1,128,128]{2,1,0:T(8,128)S(1)}, u32[]{:S(2)}) copy-start(f32[1,128,128]{2,1,0:T(8,128)S(1)} %get-tuple-element.32) | copy-start | bytes 196612
  30.2 6.4 %collective-permute-start.10 = (f32[1,128,128]{2,1,0:T(8,128)S(1)}, f32[1,128,128]{2,1,0:T(8,128)S(1)}, u32[]{:S(2)}, u32[]{:S(2)}) collective-permute-start(f32[1,128,128]{2,1,0:T(8,128)S(1)} %get-tuple-element.32), channel_id=1, source_target_pairs={{0,16},{1,17},{2,18},{3,19},{4,20},{5,21},{6,22},{7,23},{8,24},{9,... | collective-permute-start | bytes 196616 | tf_op jit(solution)/shard_map/ppermute | solution.py:13
  36.6 6.4 %collective-permute-start.11 = (f32[2,128,128]{2,1,0:T(8,128)S(1)}, f32[2,128,128]{2,1,0:T(8,128)S(1)}, u32[]{:S(2)}, u32[]{:S(2)}) collective-permute-start(f32[2,128,128]{2,1,0:T(8,128)S(1)} %pad_maximum_fusion), channel_id=1, source_target_pairs={{0,8},{1,9},{2,10},{3,11},{4,12},{5,13},{6,14},{7,15},{8,0},{9,1},... | collective-permute-start | bytes 393224 | tf_op jit(solution)/shard_map/ppermute | solution.py:13
  37.3 8.3 %collective-permute-start.12 = (f32[2,128,128]{2,1,0:T(8,128)S(1)}, f32[2,128,128]{2,1,0:T(8,128)S(1)}, u32[]{:S(2)}, u32[]{:S(2)}) collective-permute-start(f32[2,128,128]{2,1,0:T(8,128)S(1)} %pad_maximum_fusion), channel_id=1, source_target_pairs={{0,4},{1,5},{2,6},{3,7},{4,0},{5,1},{6,2},{7,3},{8,12},{9,13},{10,... | collective-permute-start | bytes 393224 | tf_op jit(solution)/shard_map/ppermute | solution.py:13
  37.9 8.5 %collective-permute-start.13 = (f32[2,128,128]{2,1,0:T(8,128)S(1)}, f32[2,128,128]{2,1,0:T(8,128)S(1)}, u32[]{:S(2)}, u32[]{:S(2)}) collective-permute-start(f32[2,128,128]{2,1,0:T(8,128)S(1)} %pad_maximum_fusion), channel_id=1, source_target_pairs={{0,12},{1,13},{2,14},{3,15},{4,8},{5,9},{6,10},{7,11},{8,4},{9,5},... | collective-permute-start | bytes 393224 | tf_op jit(solution)/shard_map/ppermute | solution.py:13
  47.1 11.7 %collective-permute-start.14 = (f32[8,128,128]{2,1,0:T(8,128)}, f32[8,128,128]{2,1,0:T(8,128)S(1)}, u32[]{:S(2)}, u32[]{:S(2)}) collective-permute-start(f32[8,128,128]{2,1,0:T(8,128)} %get-tuple-element.9), channel_id=1, source_target_pairs={{0,2},{1,3},{2,0},{3,1},{4,6},{5,7},{6,4},{7,5},{8,10},{9,11},{10,... | collective-permute-start | bytes 1572872 | tf_op jit(solution)/shard_map/ppermute | solution.py:13
  60.0 4.9 %copy-start.2 = (f32[8,256,256]{2,1,0:T(8,128)S(1)}, f32[8,256,256]{2,1,0:T(8,128)}, u32[]{:S(2)}) copy-start(f32[8,256,256]{2,1,0:T(8,128)} %param.19) | copy-start | bytes 6291460
  60.0 11.5 %collective-permute-start.15 = (f32[16,128,128]{2,1,0:T(8,128)}, f32[16,128,128]{2,1,0:T(8,128)S(1)}, u32[]{:S(2)}, u32[]{:S(2)}) collective-permute-start(f32[16,128,128]{2,1,0:T(8,128)} %get-tuple-element.2), channel_id=1, source_target_pairs={{0,1},{1,0},{2,3},{3,2},{4,5},{5,4},{6,7},{7,6},{8,9},{9,8},{10,11... | collective-permute-start | bytes 3145736 | tf_op jit(solution)/shard_map/ppermute | solution.py:13
  (1 other events, 2.2 us)

commit v3 on v2

--- a/solution.py
+++ b/solution.py
@@ -21,6 +21,34 @@
     for bits in groups:
         k = sum(((offset >> b) & 1) << t for t, b in enumerate(bits))
         position = position + k * stride
+        stride *= 1 << len(bits)
+    return position
+
+
+def xor_offset(position, groups):
+    offset = jnp.zeros_like(position)
+    stride = 1
+    for bits in groups:
+        k = (position // stride) % (1 << len(bits))
+        for t, b in enumerate(bits):
+            offset = offset | (((k >> t) & 1) << b)
+        stride *= 1 << len(bits)
+    return offset
+
+
+def static_offset(position, groups):
+    offset, stride = 0, 1
+    for bits in groups:
+        k = (position // stride) % (1 << len(bits))
+        offset |= sum(((k >> t) & 1) << b for t, b in enumerate(bits))
+        stride *= 1 << len(bits)
+    return offset
+
+
+def static_position(offset, groups):
+    position, stride = 0, 1
+    for bits in groups:
+        position += sum(((offset >> b) & 1) << t for t, b in enumerate(bits)) * stride
         stride *= 1 << len(bits)
     return position
 
@@ -66,36 +94,38 @@
     top_groups = [panel_bits] + leaf_groups
     spread_groups = leaf_groups + [[b] for b in panel_bits[::-1]]
 
-    top_rows = top_solution.shape[0]
-    top_held = xor_gather(top_solution, both, count, top_groups)
-    top_held = top_held.reshape(count * top_rows, top_solution.shape[1])
-    wanted = top_index[0]
-    source = wanted // top_rows
-    slot = xor_position(source ^ me, top_groups) * top_rows + wanted % top_rows
-    gathered = top_held[slot]
-
+    top_rows, rhs = top_solution.shape
+    places = lax.broadcasted_iota(jnp.int32, (count, top_rows), 0)
+    within = lax.broadcasted_iota(jnp.int32, (count, top_rows), 1)
+    natural = ((me ^ xor_offset(places, top_groups)) * top_rows + within).reshape(-1)
+    pick_top = (top_index[0][:, None] == natural[None, :]).astype(jnp.float32)
     folded = jnp.einsum("kv,vw->kw", upper_panel[0], upper_inverse[0], precision=highest)
+    weights = jnp.einsum("kj,kw->wj", pick_top, folded, precision=highest)
+    total = lax.dynamic_slice_in_dim(weights, begin, share, 0)
+    for v in range(1, panels):
+        outgoing = lax.dynamic_slice_in_dim(weights, (panel_index ^ v) * share, share, 0)
+        order = [static_position(static_offset(h, top_groups) ^ v, top_groups) for h in range(count)]
+        outgoing = outgoing.reshape(share, count, top_rows)[:, jnp.array(order), :]
+        outgoing = outgoing.reshape(share, count * top_rows)
+        total = total + lax.ppermute(outgoing, "panel", [(i, i ^ v) for i in range(panels)])
     own_inverse = lax.dynamic_slice_in_dim(upper_inverse[0], begin, share, 1)
     own_base = jnp.einsum("kw,kr->wr", own_inverse, upper_rhs[0], precision=highest)
-    term = jnp.einsum("kw,kr->wr", folded, gathered, precision=highest)
-    total = lax.dynamic_slice_in_dim(term, begin, share, 0)
-    for v in range(1, panels):
-        outgoing = lax.dynamic_slice_in_dim(term, (panel_index ^ v) * share, share, 0)
-        total = total + lax.ppermute(outgoing, "panel", [(i, i ^ v) for i in range(panels)])
-    own_rows = own_base - total
 
     lower_base = jnp.einsum("skw,skr->swr", lower_inverse, lower_rhs, precision=highest)
     chained = jnp.einsum("skv,svw->skw", lower_panel, lower_inverse, precision=highest)
     columns = lax.broadcasted_iota(jnp.int32, lower_index.shape + (width_upper,), 2)
     pick = (lower_index[:, :, None] == columns).astype(jnp.float32)
-    spread = jnp.einsum("skj,skw->sjw", pick, chained, precision=highest)
+    spread = jnp.einsum("skw,skj->swj", chained, pick, precision=highest)
+
+    top_held = xor_gather(top_solution, both, count, top_groups).reshape(count * top_rows, rhs)
+    own_rows = own_base - jnp.einsum("wj,jr->wr", total, top_held, precision=highest)
 
     held = xor_gather(own_rows, both, count, spread_groups)
     position = owner_map[parent_list]
     sources = position[:, None] * panels + jnp.arange(panels, dtype=jnp.int32)[None, :]
     slabs = held[xor_position(sources ^ me, spread_groups)]
     slabs = slabs.reshape(position.shape[0], width_upper, own_rows.shape[1])
-    lower_update = jnp.einsum("sjw,sjr->swr", spread, slabs, precision=highest)
+    lower_update = jnp.einsum("swj,sjr->swr", spread, slabs, precision=highest)
     lower_solution = lower_base - lower_update
     return (own_rows[None], lower_solution)
 

time: 84.5 us -> 80.7 us (0.955)
  waiting for transfers between devices: 27.5 us -> 18.1 us
  starting transfers between devices: 19.5 us -> 21.7 us
  local copies, waits for them, and re-layouts: 11.1 us -> 12.7 us
  matrix products: 24.7 us -> 26.2 us
    ppermute x13, waiting for transfers between devices: 23.8 us -> 18.1 us  [xor_gather(): parts.append(lax.ppermute(held, axes, [(i, i ^ v) for i in range(count)]))]
    ppermute x3, waiting for transfers between devices: 3.77 us -> 0.01 us  [local(): lax.ppermute(outgoing, 'panel', [(i, i ^ v) for i in range(panels)])]
    dot_general x3 -> x4, matrix products: 13 us -> 15.1 us  [the longest x1 7.6 us: local(): lower_update = jnp.einsum('swj,sjr->swr', spread, slabs, precision=highest)]
    ppermute x13, starting transfers between devices: 17.5 us -> 19.3 us  [xor_gather(): parts.append(lax.ppermute(held, axes, [(i, i ^ v) for i in range(count)]))]
    gather x1 -> x3, local copies, waits for them, and re-layouts: 0.73 us -> 1.75 us  [local(): outgoing = outgoing.reshape(share, count, top_rows)[:, jnp.array(order), :]]
    unnamed x28 -> x32, local copies, waits for them, and re-layouts: 3.76 us -> 3.88 us
  transfers between devices with their start and end apart: 16 -> 16, of which waited for: 10 -> 8; matrix products, arithmetic and copies ran while one was open for 21% -> 28% of each run, Pallas kernels for 0% -> 0%
where the time goes in v3:
time: 80.7 us; the launch traced here: 80.5 us
  matrix products  26.2 us (32%)
  starting transfers between devices  21.7 us (27%)
  waiting for transfers between devices  18.1 us (22%)
  local copies, waits for them, and re-layouts  12.7 us (16%)
  other arithmetic  0.97 us (1%)
  between operations  0.91 us (1%)
    ppermute x13, starting transfers between devices, xor_gather(): parts.append(lax.ppermute(held, axes, [(i, i ^ v) for i in range(count)]))  19.3 us
    ppermute x13, waiting for transfers between devices, xor_gather(): parts.append(lax.ppermute(held, axes, [(i, i ^ v) for i in range(count)]))  18.1 us
    dot_general x1, matrix products, local(): lower_update = jnp.einsum('swj,sjr->swr', spread, slabs, precision=highest)  7.6 us
    dot_general x1, matrix products, local(): jnp.einsum('skw,skr->swr', lower_inverse, lower_rhs, precision=highest)  4.84 us
    dot_general x1, matrix products, local(): spread = jnp.einsum('skw,skj->swj', chained, pick, precision=highest)  4.39 us
    unnamed x32, local copies, waits for them, and re-layouts  3.88 us
    gather x1, local copies, waits for them, and re-layouts, local(): slabs = held[xor_position(sources ^ me, spread_groups)]  3.67 us
    dot_general x1, matrix products, local(): jnp.einsum('kv,vw->kw', upper_panel[0], upper_inverse[0], precision=highest)  2.44 us
  transfers between devices with their start and end apart: 16, of which 8 were waited for; matrix products, arithmetic and copies ran while one was open for 28% of the time, Pallas kernels for 0%

profile of v3, /device:TPU:0, one launch (start us, length us, event | category | flops | bytes accessed | tf_op | source)
XLA Modules:
  0.0 80.5 jit_solution(3747198466241273975)
XLA Ops:
  1.2 2.6 %collective-permute-start.4 = (f32[1,16,128]{2,1,0:T(8,128)}, f32[1,16,128]{2,1,0:T(8,128)S(1)}, u32[]{:S(2)}, u32[]{:S(2)}) collective-permute-start(f32[1,16,128]{2,1,0:T(8,128)} %bitcast.52), channel_id=1, source_target_pairs={{0,2},{1,3},{2,0},{3,1},{4,6},{5,7},{6,4},{7,5},{8,10},{9,11},{10,... | collective-permute-start | bytes 24584 | tf_op jit(solution)/shard_map/ppermute | solution.py:13
  5.1 2.4 %fusion.3 = f32[256,512]{1,0:T(8,128)S(1)} fusion(f32[1,512,512]{2,1,0:T(8,128)} %param.16, f32[1,256,512]{2,1,0:T(8,128)} %param.15), kind=kOutput, calls=%fused_computation.11 | convolution fusion | flops 805306368 | bytes 2097152 | tf_op jit(solution)/shard_map/kv,vw->kw/dot_general | solution.py:102
  9.8 1.7 %collective-permute-start.2 = (f32[128,512]{0,1:T(8,128)S(1)}, f32[128,512]{0,1:T(8,128)}, u32[]{:S(2)}, u32[]{:S(2)}) collective-permute-start(f32[128,512]{0,1:T(8,128)S(1)} %bitcast.46), channel_id=1, source_target_pairs={{0,3},{1,2},{2,1},{3,0},{4,7},{5,6},{6,5},{7,4},{8,11},{9,10},{10,... | collective-permute-start | bytes 786440 | tf_op jit(solution)/shard_map/ppermute | solution.py:110
  13.4 2.9 %collective-permute-start.6 = (f32[4,16,128]{2,1,0:T(8,128)S(1)}, f32[4,16,128]{2,1,0:T(8,128)S(1)}, u32[]{:S(2)}, u32[]{:S(2)}) collective-permute-start(f32[4,16,128]{2,1,0:T(8,128)S(1)} %pad_maximum_fusion.1), channel_id=1, source_target_pairs={{0,16},{1,17},{2,18},{3,19},{4,20},{5,21},{6,22},{7,23},{8,24},{9,... | collective-permute-start | bytes 98312 | tf_op jit(solution)/shard_map/ppermute | solution.py:13
  16.3 2.0 %collective-permute-done.6 = f32[4,16,128]{2,1,0:T(8,128)S(1)} collective-permute-done((f32[4,16,128]{2,1,0:T(8,128)S(1)}, f32[4,16,128]{2,1,0:T(8,128)S(1)}, u32[]{:S(2)}, u32[]{:S(2)}) %collective-permute-start.6) | collective-permute-done | bytes 32800 | tf_op jit(solution)/shard_map/ppermute | solution.py:13
  18.3 1.8 %collective-permute-start.7 = (f32[8,16,128]{2,1,0:T(8,128)S(1)}, f32[8,16,128]{2,1,0:T(8,128)S(1)}, u32[]{:S(2)}, u32[]{:S(2)}) collective-permute-start(f32[8,16,128]{2,1,0:T(8,128)S(1)} %get-tuple-element.22), channel_id=1, source_target_pairs={{0,8},{1,9},{2,10},{3,11},{4,12},{5,13},{6,14},{7,15},{8,0},{9,1},... | collective-permute-start | bytes 196616 | tf_op jit(solution)/shard_map/ppermute | solution.py:13
  20.1 1.6 %fusion.8 = f32[128,128]{1,0:T(8,128)S(1)} fusion(f32[1,512,128]{2,1,0:T(8,128)} %param.14, f32[1,512,512]{2,1,0:T(8,128)} %param.16, s32[]{:T(128)S(6)} %select_n.86), kind=kOutput, calls=%fused_computation.16 | convolution fusion | flops 100663296 | bytes 589828 | tf_op jit(solution)/shard_map/kw,kr->wr/dot_general | solution.py:112
  21.7 1.6 %collective-permute-start.8 = (f32[8,16,128]{2,1,0:T(8,128)S(1)}, f32[8,16,128]{2,1,0:T(8,128)S(1)}, u32[]{:S(2)}, u32[]{:S(2)}) collective-permute-start(f32[8,16,128]{2,1,0:T(8,128)S(1)} %get-tuple-element.22), channel_id=1, source_target_pairs={{0,4},{1,5},{2,6},{3,7},{4,0},{5,1},{6,2},{7,3},{8,12},{9,13},{10,... | collective-permute-start | bytes 196616 | tf_op jit(solution)/shard_map/ppermute | solution.py:13
  23.3 2.0 %collective-permute-start.9 = (f32[8,16,128]{2,1,0:T(8,128)S(1)}, f32[8,16,128]{2,1,0:T(8,128)S(1)}, u32[]{:S(2)}, u32[]{:S(2)}) collective-permute-start(f32[8,16,128]{2,1,0:T(8,128)S(1)} %get-tuple-element.22), channel_id=1, source_target_pairs={{0,12},{1,13},{2,14},{3,15},{4,8},{5,9},{6,10},{7,11},{8,4},{9,5},... | collective-permute-start | bytes 196616 | tf_op jit(solution)/shard_map/ppermute | solution.py:13
  25.3 1.3 %collective-permute-done.8 = f32[8,16,128]{2,1,0:T(8,128)S(1)} collective-permute-done((f32[8,16,128]{2,1,0:T(8,128)S(1)}, f32[8,16,128]{2,1,0:T(8,128)S(1)}, u32[]{:S(2)}, u32[]{:S(2)}) %collective-permute-start.8) | collective-permute-done | bytes 65568 | tf_op jit(solution)/shard_map/ppermute | solution.py:13
  26.6 1.8 %collective-permute-done.9 = f32[8,16,128]{2,1,0:T(8,128)S(1)} collective-permute-done((f32[8,16,128]{2,1,0:T(8,128)S(1)}, f32[8,16,128]{2,1,0:T(8,128)S(1)}, u32[]{:S(2)}, u32[]{:S(2)}) %collective-permute-start.9) | collective-permute-done | bytes 65568 | tf_op jit(solution)/shard_map/ppermute | solution.py:13
  28.5 2.4 %constant_dynamic-update-slice_fusion.23 = (f32[16,128,128]{2,1,0:T(8,128)}, f32[32,128,128]{2,1,0:T(8,128)}, f32[8,128,128]{2,1,0:T(8,128)}, f32[1,128,128]{2,1,0:T(8,128)S(1)}) fusion(f32[128,128]{1,0:T(8,128)S(1)} %fusion.8, f32[512,128]{1,0:T(8,128)S(1)} %bitcast.50, f32[128,512]{0,1:T(8,128)} %collective-permute-done.2, ...), kind=kOutput, calls=%fused_computation.50 | convolution fusion | flops 100876288 | bytes 1638404 | tf_op jit(solution)/shard_map/wj,jr->wr/dot_general | solution.py:121
  30.9 2.8 %collective-permute-start.10 = (f32[1,128,128]{2,1,0:T(8,128)S(1)}, f32[1,128,128]{2,1,0:T(8,128)S(1)}, u32[]{:S(2)}, u32[]{:S(2)}) collective-permute-start(f32[1,128,128]{2,1,0:T(8,128)S(1)} %get-tuple-element.32), channel_id=1, source_target_pairs={{0,16},{1,17},{2,18},{3,19},{4,20},{5,21},{6,22},{7,23},{8,24},{9,... | collective-permute-start | bytes 196616 | tf_op jit(solution)/shard_map/ppermute | solution.py:13
  33.7 3.1 %collective-permute-done.10 = f32[1,128,128]{2,1,0:T(8,128)S(1)} collective-permute-done((f32[1,128,128]{2,1,0:T(8,128)S(1)}, f32[1,128,128]{2,1,0:T(8,128)S(1)}, u32[]{:S(2)}, u32[]{:S(2)}) %collective-permute-start.10) | collective-permute-done | bytes 65568 | tf_op jit(solution)/shard_map/ppermute | solution.py:13
  38.0 1.6 %collective-permute-start.12 = (f32[2,128,128]{2,1,0:T(8,128)S(1)}, f32[2,128,128]{2,1,0:T(8,128)S(1)}, u32[]{:S(2)}, u32[]{:S(2)}) collective-permute-start(f32[2,128,128]{2,1,0:T(8,128)S(1)} %pad_maximum_fusion), channel_id=1, source_target_pairs={{0,4},{1,5},{2,6},{3,7},{4,0},{5,1},{6,2},{7,3},{8,12},{9,13},{10,... | collective-permute-start | bytes 393224 | tf_op jit(solution)/shard_map/ppermute | solution.py:13
  39.5 1.6 %collective-permute-start.13 = (f32[2,128,128]{2,1,0:T(8,128)S(1)}, f32[2,128,128]{2,1,0:T(8,128)S(1)}, u32[]{:S(2)}, u32[]{:S(2)}) collective-permute-start(f32[2,128,128]{2,1,0:T(8,128)S(1)} %pad_maximum_fusion), channel_id=1, source_target_pairs={{0,12},{1,13},{2,14},{3,15},{4,8},{5,9},{6,10},{7,11},{8,4},{9,5},... | collective-permute-start | bytes 393224 | tf_op jit(solution)/shard_map/ppermute | solution.py:13
  43.8 1.6 %collective-permute-done.13 = f32[2,128,128]{2,1,0:T(8,128)S(1)} collective-permute-done((f32[2,128,128]{2,1,0:T(8,128)S(1)}, f32[2,128,128]{2,1,0:T(8,128)S(1)}, u32[]{:S(2)}, u32[]{:S(2)}) %collective-permute-start.13) | collective-permute-done | bytes 131104 | tf_op jit(solution)/shard_map/ppermute | solution.py:13
  46.1 1.5 %collective-permute-start.14 = (f32[8,128,128]{2,1,0:T(8,128)}, f32[8,128,128]{2,1,0:T(8,128)S(1)}, u32[]{:S(2)}, u32[]{:S(2)}) collective-permute-start(f32[8,128,128]{2,1,0:T(8,128)} %get-tuple-element.9), channel_id=1, source_target_pairs={{0,2},{1,3},{2,0},{3,1},{4,6},{5,7},{6,4},{7,5},{8,10},{9,11},{10,... | collective-permute-start | bytes 1572872 | tf_op jit(solution)/shard_map/ppermute | solution.py:13
  47.8 7.7 %collective-permute-done.14 = f32[8,128,128]{2,1,0:T(8,128)S(1)} collective-permute-done((f32[8,128,128]{2,1,0:T(8,128)}, f32[8,128,128]{2,1,0:T(8,128)S(1)}, u32[]{:S(2)}, u32[]{:S(2)}) %collective-permute-start.14) | collective-permute-done | bytes 524320 | tf_op jit(solution)/shard_map/ppermute | solution.py:13
  56.7 4.8 %fusion.30 = f32[8,256,128]{2,1,0:T(8,128)S(1)} fusion(f32[8,256,256]{2,1,0:T(8,128)S(1)} %copy-done, f32[8,256,128]{2,1,0:T(8,128)} %param.23), kind=kOutput, calls=%fused_computation.103 | convolution fusion | flops 805306368 | bytes 4194304 | tf_op jit(solution)/shard_map/skw,skr->swr/dot_general | solution.py:114
  61.5 2.2 %fusion.31 = f32[8,256,256]{2,1,0:T(8,128)S(1)} fusion(f32[8,256,256]{2,1,0:T(8,128)S(1)} %copy-done.3, f32[8,256,256]{2,1,0:T(8,128)S(1)} %copy-done), kind=kOutput, calls=%fused_computation.104 | convolution fusion | flops 1610612736 | bytes 6291456 | tf_op jit(solution)/shard_map/skv,svw->skw/dot_general | solution.py:115
  63.7 4.4 %fusion = f32[8,256,512]{2,1,0:T(8,128)} fusion(f32[8,256,256]{2,1,0:T(8,128)S(1)} %fusion.31, s32[8,256]{1,0:T(8,128)S(1)} %copy-done.6), kind=kOutput, calls=%fused_computation.6 | convolution fusion | flops 3222274048 | bytes 6299648 | tf_op jit(solution)/shard_map/skw,skj->swj/dot_general | solution.py:118
  69.2 3.7 %gather_fusion.4 = f32[32,128,128]{2,1,0:T(8,128)} fusion(f32[32,128,128]{2,1,0:T(8,128)} %constant_dynamic-update-slice_fusion.24, s32[1024]{0:T(1024)S(1)} %pad_clamp_fusion), kind=kCustom, calls=%fused_computation.4 | custom fusion | bytes 4194432 | tf_op jit(solution)/shard_map/gather | solution.py:126
  72.9 7.6 %convolution_subtract_fusion = f32[8,256,128]{2,1,0:T(8,128)} fusion(f32[8,256,128]{2,1,0:T(8,128)S(1)} %fusion.30, f32[8,256,512]{2,1,0:T(8,128)} %fusion, f32[8,512,128]{2,1,0:T(8,128)} %bitcast.49), kind=kOutput, calls=%fused_computation.8 | convolution fusion | flops 1610874880 | bytes 8388608 | tf_op jit(solution)/shard_map/swj,sjr->swr/dot_general | solution.py:128
  (79 shorter events, 12.7 us)
Async XLA Ops:
  0.6 56.0 %copy-start = (f32[8,256,256]{2,1,0:T(8,128)S(1)}, f32[8,256,256]{2,1,0:T(8,128)}, u32[]{:S(2)}) copy-start(f32[8,256,256]{2,1,0:T(8,128)} %param.24) | copy-start | bytes 6291460
  0.6 6.9 %copy-start.10 = (s32[32]{0:T(128)S(1)}, s32[32]{0:T(128)}, u32[]{:S(2)}) copy-start(s32[32]{0:T(128)} %constant.136) | copy-start | bytes 388
  0.7 6.9 %copy-start.7 = (s32[1,256]{1,0:T(1,128)S(1)}, s32[1,256]{1,0:T(1,128)}, u32[]{:S(2)}) copy-start(s32[1,256]{1,0:T(1,128)} %param.17) | copy-start | bytes 3076
  0.7 12.4 %collective-permute-start.3 = (f32[1,16,128]{2,1,0:T(8,128)}, f32[1,16,128]{2,1,0:T(8,128)S(1)}, u32[]{:S(2)}, u32[]{:S(2)}) collective-permute-start(f32[1,16,128]{2,1,0:T(8,128)} %bitcast.51), channel_id=1, source_target_pairs={{0,1},{1,0},{2,3},{3,2},{4,5},{5,4},{6,7},{7,6},{8,9},{9,8},{10,11... | collective-permute-start | bytes 24584 | tf_op jit(solution)/shard_map/ppermute | solution.py:13
  1.2 12.2 %collective-permute-start.4 = (f32[1,16,128]{2,1,0:T(8,128)}, f32[1,16,128]{2,1,0:T(8,128)S(1)}, u32[]{:S(2)}, u32[]{:S(2)}) collective-permute-start(f32[1,16,128]{2,1,0:T(8,128)} %bitcast.52), channel_id=1, source_target_pairs={{0,2},{1,3},{2,0},{3,1},{4,6},{5,7},{6,4},{7,5},{8,10},{9,11},{10,... | collective-permute-start | bytes 24584 | tf_op jit(solution)/shard_map/ppermute | solution.py:13
  3.8 9.6 %collective-permute-start.5 = (f32[1,16,128]{2,1,0:T(8,128)}, f32[1,16,128]{2,1,0:T(8,128)S(1)}, u32[]{:S(2)}, u32[]{:S(2)}) collective-permute-start(f32[1,16,128]{2,1,0:T(8,128)} %bitcast.53), channel_id=1, source_target_pairs={{0,3},{1,2},{2,1},{3,0},{4,7},{5,6},{6,5},{7,4},{8,11},{9,10},{10,... | collective-permute-start | bytes 24584 | tf_op jit(solution)/shard_map/ppermute | solution.py:13
  9.2 2.3 %copy-start.8 = (s32[32]{0:T(128)S(1)}, s32[32]{0:T(128)}, u32[]{:S(2)}) copy-start(s32[32]{0:T(128)} %constant.134) | copy-start | bytes 388
  9.2 2.3 %copy-start.9 = (s32[32]{0:T(128)S(1)}, s32[32]{0:T(128)}, u32[]{:S(2)}) copy-start(s32[32]{0:T(128)} %constant.135) | copy-start | bytes 388
  9.8 18.6 %collective-permute-start.2 = (f32[128,512]{0,1:T(8,128)S(1)}, f32[128,512]{0,1:T(8,128)}, u32[]{:S(2)}, u32[]{:S(2)}) collective-permute-start(f32[128,512]{0,1:T(8,128)S(1)} %bitcast.46), channel_id=1, source_target_pairs={{0,3},{1,2},{2,1},{3,0},{4,7},{5,6},{6,5},{7,4},{8,11},{9,10},{10,... | collective-permute-start | bytes 786440 | tf_op jit(solution)/shard_map/ppermute | solution.py:110
  12.2 16.3 %collective-permute-start = (f32[128,512]{0,1:T(8,128)S(1)}, f32[128,512]{0,1:T(8,128)}, u32[]{:S(2)}, u32[]{:S(2)}) collective-permute-start(f32[128,512]{0,1:T(8,128)S(1)} %bitcast.47), channel_id=1, source_target_pairs={{0,1},{1,0},{2,3},{3,2},{4,5},{5,4},{6,7},{7,6},{8,9},{9,8},{10,11... | collective-permute-start | bytes 786440 | tf_op jit(solution)/shard_map/ppermute | solution.py:110
  13.0 24.3 %copy-start.1 = (s32[8]{0:T(128)S(1)}, s32[8]{0:T(128)}, u32[]{:S(2)}) copy-start(s32[8]{0:T(128)} %param.19) | copy-start | bytes 100
  13.1 15.4 %collective-permute-start.1 = (f32[128,512]{0,1:T(8,128)S(1)}, f32[128,512]{0,1:T(8,128)S(1)}, u32[]{:S(2)}, u32[]{:S(2)}) collective-permute-start(f32[128,512]{0,1:T(8,128)S(1)} %bitcast.48), channel_id=1, source_target_pairs={{0,2},{1,3},{2,0},{3,1},{4,6},{5,7},{6,4},{7,5},{8,10},{9,11},{10,... | collective-permute-start | bytes 786440 | tf_op jit(solution)/shard_map/ppermute | solution.py:110
  13.4 4.9 %collective-permute-start.6 = (f32[4,16,128]{2,1,0:T(8,128)S(1)}, f32[4,16,128]{2,1,0:T(8,128)S(1)}, u32[]{:S(2)}, u32[]{:S(2)}) collective-permute-start(f32[4,16,128]{2,1,0:T(8,128)S(1)} %pad_maximum_fusion.1), channel_id=1, source_target_pairs={{0,16},{1,17},{2,18},{3,19},{4,20},{5,21},{6,22},{7,23},{8,24},{9,... | collective-permute-start | bytes 98312 | tf_op jit(solution)/shard_map/ppermute | solution.py:13
  18.3 5.0 %collective-permute-start.7 = (f32[8,16,128]{2,1,0:T(8,128)S(1)}, f32[8,16,128]{2,1,0:T(8,128)S(1)}, u32[]{:S(2)}, u32[]{:S(2)}) collective-permute-start(f32[8,16,128]{2,1,0:T(8,128)S(1)} %get-tuple-element.22), channel_id=1, source_target_pairs={{0,8},{1,9},{2,10},{3,11},{4,12},{5,13},{6,14},{7,15},{8,0},{9,1},... | collective-permute-start | bytes 196616 | tf_op jit(solution)/shard_map/ppermute | solution.py:13
  21.7 4.9 %collective-permute-start.8 = (f32[8,16,128]{2,1,0:T(8,128)S(1)}, f32[8,16,128]{2,1,0:T(8,128)S(1)}, u32[]{:S(2)}, u32[]{:S(2)}) collective-permute-start(f32[8,16,128]{2,1,0:T(8,128)S(1)} %get-tuple-element.22), channel_id=1, source_target_pairs={{0,4},{1,5},{2,6},{3,7},{4,0},{5,1},{6,2},{7,3},{8,12},{9,13},{10,... | collective-permute-start | bytes 196616 | tf_op jit(solution)/shard_map/ppermute | solution.py:13
  23.3 5.2 %collective-permute-start.9 = (f32[8,16,128]{2,1,0:T(8,128)S(1)}, f32[8,16,128]{2,1,0:T(8,128)S(1)}, u32[]{:S(2)}, u32[]{:S(2)}) collective-permute-start(f32[8,16,128]{2,1,0:T(8,128)S(1)} %get-tuple-element.22), channel_id=1, source_target_pairs={{0,12},{1,13},{2,14},{3,15},{4,8},{5,9},{6,10},{7,11},{8,4},{9,5},... | collective-permute-start | bytes 196616 | tf_op jit(solution)/shard_map/ppermute | solution.py:13
  30.9 25.7 %copy-start.4 = (f32[1,128,128]{2,1,0:T(8,128)}, f32[1,128,128]{2,1,0:T(8,128)S(1)}, u32[]{:S(2)}) copy-start(f32[1,128,128]{2,1,0:T(8,128)S(1)} %get-tuple-element.32) | copy-start | bytes 196612
  30.9 6.0 %collective-permute-start.10 = (f32[1,128,128]{2,1,0:T(8,128)S(1)}, f32[1,128,128]{2,1,0:T(8,128)S(1)}, u32[]{:S(2)}, u32[]{:S(2)}) collective-permute-start(f32[1,128,128]{2,1,0:T(8,128)S(1)} %get-tuple-element.32), channel_id=1, source_target_pairs={{0,16},{1,17},{2,18},{3,19},{4,20},{5,21},{6,22},{7,23},{8,24},{9,... | collective-permute-start | bytes 196616 | tf_op jit(solution)/shard_map/ppermute | solution.py:13
  36.9 5.0 %collective-permute-start.11 = (f32[2,128,128]{2,1,0:T(8,128)S(1)}, f32[2,128,128]{2,1,0:T(8,128)S(1)}, u32[]{:S(2)}, u32[]{:S(2)}) collective-permute-start(f32[2,128,128]{2,1,0:T(8,128)S(1)} %pad_maximum_fusion), channel_id=1, source_target_pairs={{0,8},{1,9},{2,10},{3,11},{4,12},{5,13},{6,14},{7,15},{8,0},{9,1},... | collective-permute-start | bytes 393224 | tf_op jit(solution)/shard_map/ppermute | solution.py:13
  38.0 5.0 %collective-permute-start.12 = (f32[2,128,128]{2,1,0:T(8,128)S(1)}, f32[2,128,128]{2,1,0:T(8,128)S(1)}, u32[]{:S(2)}, u32[]{:S(2)}) collective-permute-start(f32[2,128,128]{2,1,0:T(8,128)S(1)} %pad_maximum_fusion), channel_id=1, source_target_pairs={{0,4},{1,5},{2,6},{3,7},{4,0},{5,1},{6,2},{7,3},{8,12},{9,13},{10,... | collective-permute-start | bytes 393224 | tf_op jit(solution)/shard_map/ppermute | solution.py:13
  39.5 5.9 %collective-permute-start.13 = (f32[2,128,128]{2,1,0:T(8,128)S(1)}, f32[2,128,128]{2,1,0:T(8,128)S(1)}, u32[]{:S(2)}, u32[]{:S(2)}) collective-permute-start(f32[2,128,128]{2,1,0:T(8,128)S(1)} %pad_maximum_fusion), channel_id=1, source_target_pairs={{0,12},{1,13},{2,14},{3,15},{4,8},{5,9},{6,10},{7,11},{8,4},{9,5},... | collective-permute-start | bytes 393224 | tf_op jit(solution)/shard_map/ppermute | solution.py:13
  46.1 9.4 %collective-permute-start.14 = (f32[8,128,128]{2,1,0:T(8,128)}, f32[8,128,128]{2,1,0:T(8,128)S(1)}, u32[]{:S(2)}, u32[]{:S(2)}) collective-permute-start(f32[8,128,128]{2,1,0:T(8,128)} %get-tuple-element.9), channel_id=1, source_target_pairs={{0,2},{1,3},{2,0},{3,1},{4,6},{5,7},{6,4},{7,5},{8,10},{9,11},{10,... | collective-permute-start | bytes 1572872 | tf_op jit(solution)/shard_map/ppermute | solution.py:13
  56.6 4.9 %copy-start.3 = (f32[8,256,256]{2,1,0:T(8,128)S(1)}, f32[8,256,256]{2,1,0:T(8,128)}, u32[]{:S(2)}) copy-start(f32[8,256,256]{2,1,0:T(8,128)} %param.22) | copy-start | bytes 6291460
  56.6 11.5 %collective-permute-start.15 = (f32[16,128,128]{2,1,0:T(8,128)}, f32[16,128,128]{2,1,0:T(8,128)S(1)}, u32[]{:S(2)}, u32[]{:S(2)}) collective-permute-start(f32[16,128,128]{2,1,0:T(8,128)} %get-tuple-element.5), channel_id=1, source_target_pairs={{0,1},{1,0},{2,3},{3,2},{4,5},{5,4},{6,7},{7,6},{8,9},{9,8},{10,11... | collective-permute-start | bytes 3145736 | tf_op jit(solution)/shard_map/ppermute | solution.py:13
  (3 other events, 4.0 us)

commit v4 on v3

--- a/solution.py
+++ b/solution.py
@@ -7,12 +7,16 @@
 def xor_gather(block, axes, count, groups):
     held = block[None]
     for bits in groups:
-        parts = [held]
-        for k in range(1, 1 << len(bits)):
-            v = sum(((k >> t) & 1) << b for t, b in enumerate(bits))
-            parts.append(lax.ppermute(held, axes, [(i, i ^ v) for i in range(count)]))
-        held = jnp.concatenate(parts, 0)
+        held = xor_gather_step(held, axes, count, bits)
     return held
+
+
+def xor_gather_step(held, axes, count, bits):
+    parts = [held]
+    for k in range(1, 1 << len(bits)):
+        v = sum(((k >> t) & 1) << b for t, b in enumerate(bits))
+        parts.append(lax.ppermute(held, axes, [(i, i ^ v) for i in range(count)]))
+    return jnp.concatenate(parts, 0)
 
 
 def xor_position(offset, groups):
@@ -118,14 +122,26 @@
     spread = jnp.einsum("skw,skj->swj", chained, pick, precision=highest)
 
     top_held = xor_gather(top_solution, both, count, top_groups).reshape(count * top_rows, rhs)
+    top_held, spread, lower_base = lax.optimization_barrier((top_held, spread, lower_base))
     own_rows = own_base - jnp.einsum("wj,jr->wr", total, top_held, precision=highest)
 
-    held = xor_gather(own_rows, both, count, spread_groups)
     position = owner_map[parent_list]
-    sources = position[:, None] * panels + jnp.arange(panels, dtype=jnp.int32)[None, :]
-    slabs = held[xor_position(sources ^ me, spread_groups)]
-    slabs = slabs.reshape(position.shape[0], width_upper, own_rows.shape[1])
-    lower_update = jnp.einsum("swj,sjr->swr", spread, slabs, precision=highest)
+    held = xor_gather(own_rows, both, count, leaf_groups)
+    present = [0]
+    lower_update = None
+    for step in [None] + [[b] for b in panel_bits[::-1]]:
+        if step is None:
+            fresh = present
+        else:
+            held = xor_gather_step(held, both, count, step)
+            fresh = [o ^ (1 << step[0]) for o in present]
+            present = present + fresh
+        for o in fresh:
+            quarter = panel_index ^ o
+            blocks = held[xor_position((position * panels + quarter) ^ me, spread_groups)]
+            part = lax.dynamic_slice_in_dim(spread, quarter * share, share, 2)
+            term = jnp.einsum("swj,sjr->swr", part, blocks, precision=highest)
+            lower_update = term if lower_update is None else lower_update + term
     lower_solution = lower_base - lower_update
     return (own_rows[None], lower_solution)
 

time: 80.7 us -> 94.3 us (1.17)
  local copies, waits for them, and re-layouts: 12.7 us -> 20.1 us
  matrix products: 26.2 us -> 31.7 us
    gather x1 -> x4, local copies, waits for them, and re-layouts: 3.67 us -> 10 us  [local(): blocks = held[xor_position(position * panels + quarter ^ me, spread_groups)]]
    dot_general x1 -> x4, matrix products: 7.6 us -> 10.9 us  [local(): term = jnp.einsum('swj,sjr->swr', part, blocks, precision=highest)]
    dot_general x1, matrix products: 2.17 us -> 5.18 us  [local(): jnp.einsum('skv,svw->skw', lower_panel, lower_inverse, precision=highest)]
    concatenate x4, local copies, waits for them, and re-layouts: 2.19 us -> 3.41 us  [xor_gather_step(): return jnp.concatenate(parts, 0)]
    sub x0 -> x1, other arithmetic: none -> 1.08 us  [local(): lower_solution = lower_base - lower_update]
    unnamed x32 -> x40, local copies, waits for them, and re-layouts: 3.88 us -> 3.84 us
  transfers between devices with their start and end apart: 16 -> 16, of which waited for: 8 -> 7; matrix products, arithmetic and copies ran while one was open for 28% -> 32% of each run, Pallas kernels for 0% -> 0%
where the time goes in v4:
time: 94.3 us; the launch traced here: 93.9 us
  matrix products  31.7 us (34%)
  starting transfers between devices  21.7 us (23%)
  local copies, waits for them, and re-layouts  20.1 us (21%)
  waiting for transfers between devices  17.9 us (19%)
  other arithmetic  1.35 us (1%)
  between operations  1.03 us (1%)
    ppermute x13, starting transfers between devices, xor_gather_step(): parts.append(lax.ppermute(held, axes, [(i, i ^ v) for i in range(count)]))  19.7 us
    ppermute x13, waiting for transfers between devices, xor_gather_step(): parts.append(lax.ppermute(held, axes, [(i, i ^ v) for i in range(count)]))  17.9 us
    dot_general x4, matrix products, local(): term = jnp.einsum('swj,sjr->swr', part, blocks, precision=highest)  10.9 us
    gather x4, local copies, waits for them, and re-layouts, local(): blocks = held[xor_position(position * panels + quarter ^ me, spread_groups)]  10 us
    dot_general x1, matrix products, local(): jnp.einsum('skv,svw->skw', lower_panel, lower_inverse, precision=highest)  5.18 us
    dot_general x1, matrix products, local(): jnp.einsum('skw,skr->swr', lower_inverse, lower_rhs, precision=highest)  4.48 us
    dot_general x1, matrix products, local(): spread = jnp.einsum('skw,skj->swj', chained, pick, precision=highest)  3.97 us
    unnamed x40, local copies, waits for them, and re-layouts  3.84 us
  transfers between devices with their start and end apart: 16, of which 7 were waited for; matrix products, arithmetic and copies ran while one was open for 32% of the time, Pallas kernels for 0%

profile of v4, /device:TPU:0, one launch (start us, length us, event | category | flops | bytes accessed | tf_op | source)
XLA Modules:
  0.0 93.9 jit_solution(170483633941622263)
XLA Ops:
  1.2 2.6 %collective-permute-start.4 = (f32[1,16,128]{2,1,0:T(8,128)}, f32[1,16,128]{2,1,0:T(8,128)S(1)}, u32[]{:S(2)}, u32[]{:S(2)}) collective-permute-start(f32[1,16,128]{2,1,0:T(8,128)} %bitcast.66), channel_id=1, source_target_pairs={{0,2},{1,3},{2,0},{3,1},{4,6},{5,7},{6,4},{7,5},{8,10},{9,11},{10,... | collective-permute-start | bytes 24584 | tf_op jit(solution)/shard_map/ppermute | solution.py:18
  4.4 2.4 %fusion.5 = f32[256,512]{1,0:T(8,128)S(1)} fusion(f32[1,512,512]{2,1,0:T(8,128)} %param.16, f32[1,256,512]{2,1,0:T(8,128)} %param.15), kind=kOutput, calls=%fused_computation.16 | convolution fusion | flops 805306368 | bytes 2097152 | tf_op jit(solution)/shard_map/kv,vw->kw/dot_general | solution.py:106
  9.2 1.7 %collective-permute-start.2 = (f32[128,512]{0,1:T(8,128)S(1)}, f32[128,512]{0,1:T(8,128)}, u32[]{:S(2)}, u32[]{:S(2)}) collective-permute-start(f32[128,512]{0,1:T(8,128)S(1)} %bitcast.61), channel_id=1, source_target_pairs={{0,3},{1,2},{2,1},{3,0},{4,7},{5,6},{6,5},{7,4},{8,11},{9,10},{10,... | collective-permute-start | bytes 786440 | tf_op jit(solution)/shard_map/ppermute | solution.py:114
  11.8 5.2 %fusion.47 = f32[8,256,256]{1,2,0:T(8,128)S(1)} fusion(f32[8,256,256]{2,1,0:T(8,128)} %param.22, f32[8,256,256]{2,1,0:T(8,128)S(1)} %copy-done), kind=kOutput, calls=%fused_computation.129 | convolution fusion | flops 1610612736 | bytes 6291456 | tf_op jit(solution)/shard_map/skv,svw->skw/dot_general | solution.py:119
  17.0 4.5 %fusion.48 = f32[8,256,128]{2,1,0:T(8,128)} fusion(f32[8,256,256]{2,1,0:T(8,128)S(1)} %copy-done, f32[8,256,128]{2,1,0:T(8,128)S(1)} %copy-done.6), kind=kOutput, calls=%fused_computation.130 | convolution fusion | flops 805306368 | bytes 4194304 | tf_op jit(solution)/shard_map/skw,skr->swr/dot_general | solution.py:118
  21.4 4.0 %fusion = f32[8,256,512]{2,1,0:T(8,128)} fusion(f32[8,256,256]{1,2,0:T(8,128)S(1)} %fusion.47, s32[8,256]{1,0:T(8,128)S(1)} %copy-done.9), kind=kOutput, calls=%fused_computation.9 | convolution fusion | flops 3222274048 | bytes 6299648 | tf_op jit(solution)/shard_map/skw,skj->swj/dot_general | solution.py:122
  26.2 3.0 %collective-permute-start.6 = (f32[4,16,128]{2,1,0:T(8,128)S(1)}, f32[4,16,128]{2,1,0:T(8,128)S(1)}, u32[]{:S(2)}, u32[]{:S(2)}) collective-permute-start(f32[4,16,128]{2,1,0:T(8,128)S(1)} %pad_maximum_fusion.1), channel_id=1, source_target_pairs={{0,16},{1,17},{2,18},{3,19},{4,20},{5,21},{6,22},{7,23},{8,24},{9,... | collective-permute-start | bytes 98312 | tf_op jit(solution)/shard_map/ppermute | solution.py:18
  29.2 2.0 %collective-permute-done.6 = f32[4,16,128]{2,1,0:T(8,128)S(1)} collective-permute-done((f32[4,16,128]{2,1,0:T(8,128)S(1)}, f32[4,16,128]{2,1,0:T(8,128)S(1)}, u32[]{:S(2)}, u32[]{:S(2)}) %collective-permute-start.6) | collective-permute-done | bytes 32800 | tf_op jit(solution)/shard_map/ppermute | solution.py:18
  31.2 1.8 %collective-permute-start.7 = (f32[8,16,128]{2,1,0:T(8,128)S(1)}, f32[8,16,128]{2,1,0:T(8,128)S(1)}, u32[]{:S(2)}, u32[]{:S(2)}) collective-permute-start(f32[8,16,128]{2,1,0:T(8,128)S(1)} %get-tuple-element.28), channel_id=1, source_target_pairs={{0,8},{1,9},{2,10},{3,11},{4,12},{5,13},{6,14},{7,15},{8,0},{9,1},... | collective-permute-start | bytes 196616 | tf_op jit(solution)/shard_map/ppermute | solution.py:18
  33.0 1.6 %fusion.17 = f32[128,128]{1,0:T(8,128)S(1)} fusion(f32[1,512,128]{2,1,0:T(8,128)} %param.14, f32[1,512,512]{2,1,0:T(8,128)} %param.16, s32[]{:T(128)S(6)} %select_n.120), kind=kOutput, calls=%fused_computation.28 | convolution fusion | flops 100663296 | bytes 589828 | tf_op jit(solution)/shard_map/kw,kr->wr/dot_general | solution.py:116
  36.2 2.0 %collective-permute-start.9 = (f32[8,16,128]{2,1,0:T(8,128)S(1)}, f32[8,16,128]{2,1,0:T(8,128)S(1)}, u32[]{:S(2)}, u32[]{:S(2)}) collective-permute-start(f32[8,16,128]{2,1,0:T(8,128)S(1)} %get-tuple-element.28), channel_id=1, source_target_pairs={{0,12},{1,13},{2,14},{3,15},{4,8},{5,9},{6,10},{7,11},{8,4},{9,5},... | collective-permute-start | bytes 196616 | tf_op jit(solution)/shard_map/ppermute | solution.py:18
  39.7 1.7 %collective-permute-done.9 = f32[8,16,128]{2,1,0:T(8,128)S(1)} collective-permute-done((f32[8,16,128]{2,1,0:T(8,128)S(1)}, f32[8,16,128]{2,1,0:T(8,128)S(1)}, u32[]{:S(2)}, u32[]{:S(2)}) %collective-permute-start.9) | collective-permute-done | bytes 65568 | tf_op jit(solution)/shard_map/ppermute | solution.py:18
  41.4 2.4 %constant_dynamic-update-slice_fusion.23 = (f32[16,128,128]{2,1,0:T(8,128)}, f32[32,128,128]{2,1,0:T(8,128)}, f32[8,128,128]{2,1,0:T(8,128)S(1)}, f32[1,128,128]{2,1,0:T(8,128)S(1)}) fusion(f32[128,128]{1,0:T(8,128)S(1)} %fusion.17, f32[512,128]{1,0:T(8,128)S(1)} %bitcast.64, f32[128,512]{0,1:T(8,128)} %collective-permute-done.2, ...), kind=kOutput, calls=%fused_computation.62 | convolution fusion | flops 100876288 | bytes 1638404 | tf_op jit(solution)/shard_map/wj,jr->wr/dot_general | solution.py:126
  43.8 3.1 %collective-permute-start.10 = (f32[1,128,128]{2,1,0:T(8,128)S(1)}, f32[1,128,128]{2,1,0:T(8,128)S(1)}, u32[]{:S(2)}, u32[]{:S(2)}) collective-permute-start(f32[1,128,128]{2,1,0:T(8,128)S(1)} %get-tuple-element.42), channel_id=1, source_target_pairs={{0,16},{1,17},{2,18},{3,19},{4,20},{5,21},{6,22},{7,23},{8,24},{9,... | collective-permute-start | bytes 196616 | tf_op jit(solution)/shard_map/ppermute | solution.py:18
  46.9 2.9 %collective-permute-done.10 = f32[1,128,128]{2,1,0:T(8,128)S(1)} collective-permute-done((f32[1,128,128]{2,1,0:T(8,128)S(1)}, f32[1,128,128]{2,1,0:T(8,128)S(1)}, u32[]{:S(2)}, u32[]{:S(2)}) %collective-permute-start.10) | collective-permute-done | bytes 65568 | tf_op jit(solution)/shard_map/ppermute | solution.py:18
  59.9 7.7 %collective-permute-done.14 = f32[8,128,128]{2,1,0:T(8,128)S(1)} collective-permute-done((f32[8,128,128]{2,1,0:T(8,128)S(1)}, f32[8,128,128]{2,1,0:T(8,128)S(1)}, u32[]{:S(2)}, u32[]{:S(2)}) %collective-permute-start.14) | collective-permute-done | bytes 524320 | tf_op jit(solution)/shard_map/ppermute | solution.py:18
  70.8 2.6 %gather_fusion.5 = f32[8,128,128]{2,1,0:T(8,128)} fusion(f32[16,128,128]{2,1,0:T(8,128)} %get-tuple-element.11, s32[1024]{0:T(1024)S(1)} %pad_clamp_fusion.2), kind=kCustom, calls=%fused_computation.5 | custom fusion | bytes 1048608 | tf_op jit(solution)/shard_map/gather | solution.py:141
  73.4 2.4 %fusion.11 = f32[8,256,128]{2,1,0:T(8,128)S(1)} fusion(f32[8,128,128]{2,1,0:T(8,128)} %gather_fusion.5, f32[8,256,512]{2,1,0:T(8,128)} %fusion, s32[]{:T(128)S(6)} %select_n.130), kind=kOutput, calls=%fused_computation.22 | convolution fusion | flops 402653184 | bytes 2621444 | tf_op jit(solution)/shard_map/swj,sjr->swr/dot_general | solution.py:143
  75.9 2.3 %constant_dynamic-update-slice_fusion.24 = f32[32,128,128]{2,1,0:T(8,128)} fusion(f32[32,128,128]{2,1,0:T(8,128)} %get-tuple-element.12, f32[16,128,128]{2,1,0:T(8,128)} %collective-permute-done.15), kind=kLoop, calls=%fused_computation.63 | loop fusion | bytes 2097152 | tf_op jit(solution)/shard_map/concatenate | solution.py:19
  78.2 3.0 %gather_fusion.7 = f32[8,128,128]{2,1,0:T(8,128)} fusion(f32[32,128,128]{2,1,0:T(8,128)} %constant_dynamic-update-slice_fusion.24, s32[1024]{0:T(1024)S(1)} %get-tuple-element.49), kind=kCustom, calls=%fused_computation.7 | custom fusion | bytes 1048608 | tf_op jit(solution)/shard_map/gather | solution.py:141
  81.2 3.4 %fusion.7 = f32[8,256,128]{2,1,0:T(8,128)} fusion(f32[8,128,128]{2,1,0:T(8,128)} %gather_fusion.7, f32[8,256,512]{2,1,0:T(8,128)} %fusion, s32[]{:T(128)S(6)} %select_n.132), kind=kOutput, calls=%fused_computation.18 | convolution fusion | flops 402653184 | bytes 2621444 | tf_op jit(solution)/shard_map/swj,sjr->swr/dot_general | solution.py:143
  84.6 3.0 %gather_fusion.6 = f32[8,128,128]{2,1,0:T(8,128)} fusion(f32[32,128,128]{2,1,0:T(8,128)} %constant_dynamic-update-slice_fusion.24, s32[1024]{0:T(1024)S(1)} %get-tuple-element.50), kind=kCustom, calls=%fused_computation.6 | custom fusion | bytes 1048608 | tf_op jit(solution)/shard_map/gather | solution.py:141
  87.6 2.5 %fusion.9 = f32[8,256,128]{2,1,0:T(8,128)S(1)} fusion(f32[8,128,128]{2,1,0:T(8,128)} %gather_fusion.6, f32[8,256,512]{2,1,0:T(8,128)} %fusion, s32[]{:T(128)S(6)} %select_n.128), kind=kOutput, calls=%fused_computation.20 | convolution fusion | flops 402653184 | bytes 2621444 | tf_op jit(solution)/shard_map/swj,sjr->swr/dot_general | solution.py:143
  90.2 2.6 %fusion.3 = f32[8,256,128]{2,1,0:T(8,128)S(1)} fusion(f32[8,256,128]{2,1,0:T(8,128)S(1)} %copy-done.4, f32[8,256,128]{2,1,0:T(8,128)S(1)} %fusion.9, f32[8,256,128]{2,1,0:T(8,128)S(1)} %fusion.11, f32[8,128,128]{2,1,0:T(8,128)S(1)} %copy-done.5, f32[8,256,512]{2,1,0:T(8,128)} %fusion, s32[]{:T(128)S(6)} %select_n.120), kind=kOutput, calls=%fused_computation.13 | convolution fusion | flops 403439616 | bytes 5767172 | tf_op jit(solution)/shard_map/swj,sjr->swr/dot_general | solution.py:143
  (95 shorter events, 22.4 us)
Async XLA Ops:
  0.6 11.1 %copy-start = (f32[8,256,256]{2,1,0:T(8,128)S(1)}, f32[8,256,256]{2,1,0:T(8,128)}, u32[]{:S(2)}) copy-start(f32[8,256,256]{2,1,0:T(8,128)} %param.24) | copy-start | bytes 6291460
  0.6 6.2 %copy-start.12 = (s32[32]{0:T(128)S(1)}, s32[32]{0:T(128)}, u32[]{:S(2)}) copy-start(s32[32]{0:T(128)} %constant.133) | copy-start | bytes 388
  0.7 6.2 %copy-start.13 = (s32[32]{0:T(128)S(1)}, s32[32]{0:T(128)}, u32[]{:S(2)}) copy-start(s32[32]{0:T(128)} %constant.132) | copy-start | bytes 388
  0.7 6.3 %copy-start.10 = (s32[1,256]{1,0:T(1,128)S(1)}, s32[1,256]{1,0:T(1,128)}, u32[]{:S(2)}) copy-start(s32[1,256]{1,0:T(1,128)} %param.17) | copy-start | bytes 3076
  0.7 25.4 %collective-permute-start.3 = (f32[1,16,128]{2,1,0:T(8,128)}, f32[1,16,128]{2,1,0:T(8,128)S(1)}, u32[]{:S(2)}, u32[]{:S(2)}) collective-permute-start(f32[1,16,128]{2,1,0:T(8,128)} %bitcast.65), channel_id=1, source_target_pairs={{0,1},{1,0},{2,3},{3,2},{4,5},{5,4},{6,7},{7,6},{8,9},{9,8},{10,11... | collective-permute-start | bytes 24584 | tf_op jit(solution)/shard_map/ppermute | solution.py:18
  1.2 25.0 %collective-permute-start.4 = (f32[1,16,128]{2,1,0:T(8,128)}, f32[1,16,128]{2,1,0:T(8,128)S(1)}, u32[]{:S(2)}, u32[]{:S(2)}) collective-permute-start(f32[1,16,128]{2,1,0:T(8,128)} %bitcast.66), channel_id=1, source_target_pairs={{0,2},{1,3},{2,0},{3,1},{4,6},{5,7},{6,4},{7,5},{8,10},{9,11},{10,... | collective-permute-start | bytes 24584 | tf_op jit(solution)/shard_map/ppermute | solution.py:18
  3.8 22.4 %collective-permute-start.5 = (f32[1,16,128]{2,1,0:T(8,128)}, f32[1,16,128]{2,1,0:T(8,128)S(1)}, u32[]{:S(2)}, u32[]{:S(2)}) collective-permute-start(f32[1,16,128]{2,1,0:T(8,128)} %bitcast.67), channel_id=1, source_target_pairs={{0,3},{1,2},{2,1},{3,0},{4,7},{5,6},{6,5},{7,4},{8,11},{9,10},{10,... | collective-permute-start | bytes 24584 | tf_op jit(solution)/shard_map/ppermute | solution.py:18
  9.2 32.1 %collective-permute-start.2 = (f32[128,512]{0,1:T(8,128)S(1)}, f32[128,512]{0,1:T(8,128)}, u32[]{:S(2)}, u32[]{:S(2)}) collective-permute-start(f32[128,512]{0,1:T(8,128)S(1)} %bitcast.61), channel_id=1, source_target_pairs={{0,3},{1,2},{2,1},{3,0},{4,7},{5,6},{6,5},{7,4},{8,11},{9,10},{10,... | collective-permute-start | bytes 786440 | tf_op jit(solution)/shard_map/ppermute | solution.py:114
  11.6 29.8 %collective-permute-start.1 = (f32[128,512]{0,1:T(8,128)S(1)}, f32[128,512]{0,1:T(8,128)}, u32[]{:S(2)}, u32[]{:S(2)}) collective-permute-start(f32[128,512]{0,1:T(8,128)S(1)} %bitcast.62), channel_id=1, source_target_pairs={{0,2},{1,3},{2,0},{3,1},{4,6},{5,7},{6,4},{7,5},{8,10},{9,11},{10,... | collective-permute-start | bytes 786440 | tf_op jit(solution)/shard_map/ppermute | solution.py:114
  11.7 5.2 %copy-start.6 = (f32[8,256,128]{2,1,0:T(8,128)S(1)}, f32[8,256,128]{2,1,0:T(8,128)}, u32[]{:S(2)}) copy-start(f32[8,256,128]{2,1,0:T(8,128)} %param.23) | copy-start | bytes 3145732
  26.0 15.3 %collective-permute-start = (f32[128,512]{0,1:T(8,128)S(1)}, f32[128,512]{0,1:T(8,128)S(1)}, u32[]{:S(2)}, u32[]{:S(2)}) collective-permute-start(f32[128,512]{0,1:T(8,128)S(1)} %bitcast.63), channel_id=1, source_target_pairs={{0,1},{1,0},{2,3},{3,2},{4,5},{5,4},{6,7},{7,6},{8,9},{9,8},{10,11... | collective-permute-start | bytes 786440 | tf_op jit(solution)/shard_map/ppermute | solution.py:114
  26.2 5.0 %collective-permute-start.6 = (f32[4,16,128]{2,1,0:T(8,128)S(1)}, f32[4,16,128]{2,1,0:T(8,128)S(1)}, u32[]{:S(2)}, u32[]{:S(2)}) collective-permute-start(f32[4,16,128]{2,1,0:T(8,128)S(1)} %pad_maximum_fusion.1), channel_id=1, source_target_pairs={{0,16},{1,17},{2,18},{3,19},{4,20},{5,21},{6,22},{7,23},{8,24},{9,... | collective-permute-start | bytes 98312 | tf_op jit(solution)/shard_map/ppermute | solution.py:18
  31.2 5.0 %collective-permute-start.7 = (f32[8,16,128]{2,1,0:T(8,128)S(1)}, f32[8,16,128]{2,1,0:T(8,128)S(1)}, u32[]{:S(2)}, u32[]{:S(2)}) collective-permute-start(f32[8,16,128]{2,1,0:T(8,128)S(1)} %get-tuple-element.28), channel_id=1, source_target_pairs={{0,8},{1,9},{2,10},{3,11},{4,12},{5,13},{6,14},{7,15},{8,0},{9,1},... | collective-permute-start | bytes 196616 | tf_op jit(solution)/shard_map/ppermute | solution.py:18
  34.6 5.0 %collective-permute-start.8 = (f32[8,16,128]{2,1,0:T(8,128)S(1)}, f32[8,16,128]{2,1,0:T(8,128)S(1)}, u32[]{:S(2)}, u32[]{:S(2)}) collective-permute-start(f32[8,16,128]{2,1,0:T(8,128)S(1)} %get-tuple-element.28), channel_id=1, source_target_pairs={{0,4},{1,5},{2,6},{3,7},{4,0},{5,1},{6,2},{7,3},{8,12},{9,13},{10,... | collective-permute-start | bytes 196616 | tf_op jit(solution)/shard_map/ppermute | solution.py:18
  36.2 5.2 %collective-permute-start.9 = (f32[8,16,128]{2,1,0:T(8,128)S(1)}, f32[8,16,128]{2,1,0:T(8,128)S(1)}, u32[]{:S(2)}, u32[]{:S(2)}) collective-permute-start(f32[8,16,128]{2,1,0:T(8,128)S(1)} %get-tuple-element.28), channel_id=1, source_target_pairs={{0,12},{1,13},{2,14},{3,15},{4,8},{5,9},{6,10},{7,11},{8,4},{9,5},... | collective-permute-start | bytes 196616 | tf_op jit(solution)/shard_map/ppermute | solution.py:18
  43.8 25.6 %copy-start.7 = (f32[1,128,128]{2,1,0:T(8,128)}, f32[1,128,128]{2,1,0:T(8,128)S(1)}, u32[]{:S(2)}) copy-start(f32[1,128,128]{2,1,0:T(8,128)S(1)} %get-tuple-element.42) | copy-start | bytes 196612
  43.8 24.9 %copy-start.14 = (s32[8]{0:T(128)S(1)}, s32[8]{0:T(128)}, u32[]{:S(2)}) copy-start(s32[8]{0:T(128)} %param.20) | copy-start | bytes 100
  43.8 24.9 %copy-start.1 = (s32[8]{0:T(128)S(1)}, s32[8]{0:T(128)}, u32[]{:S(2)}) copy-start(s32[8]{0:T(128)} %param.19) | copy-start | bytes 100
  43.8 6.0 %collective-permute-start.10 = (f32[1,128,128]{2,1,0:T(8,128)S(1)}, f32[1,128,128]{2,1,0:T(8,128)S(1)}, u32[]{:S(2)}, u32[]{:S(2)}) collective-permute-start(f32[1,128,128]{2,1,0:T(8,128)S(1)} %get-tuple-element.42), channel_id=1, source_target_pairs={{0,16},{1,17},{2,18},{3,19},{4,20},{5,21},{6,22},{7,23},{8,24},{9,... | collective-permute-start | bytes 196616 | tf_op jit(solution)/shard_map/ppermute | solution.py:18
  49.8 5.0 %collective-permute-start.11 = (f32[2,128,128]{2,1,0:T(8,128)S(1)}, f32[2,128,128]{2,1,0:T(8,128)S(1)}, u32[]{:S(2)}, u32[]{:S(2)}) collective-permute-start(f32[2,128,128]{2,1,0:T(8,128)S(1)} %pad_maximum_fusion), channel_id=1, source_target_pairs={{0,8},{1,9},{2,10},{3,11},{4,12},{5,13},{6,14},{7,15},{8,0},{9,1},... | collective-permute-start | bytes 393224 | tf_op jit(solution)/shard_map/ppermute | solution.py:18
  50.4 5.3 %collective-permute-start.12 = (f32[2,128,128]{2,1,0:T(8,128)S(1)}, f32[2,128,128]{2,1,0:T(8,128)S(1)}, u32[]{:S(2)}, u32[]{:S(2)}) collective-permute-start(f32[2,128,128]{2,1,0:T(8,128)S(1)} %pad_maximum_fusion), channel_id=1, source_target_pairs={{0,4},{1,5},{2,6},{3,7},{4,0},{5,1},{6,2},{7,3},{8,12},{9,13},{10,... | collective-permute-start | bytes 393224 | tf_op jit(solution)/shard_map/ppermute | solution.py:18
  51.8 5.9 %collective-permute-start.13 = (f32[2,128,128]{2,1,0:T(8,128)S(1)}, f32[2,128,128]{2,1,0:T(8,128)S(1)}, u32[]{:S(2)}, u32[]{:S(2)}) collective-permute-start(f32[2,128,128]{2,1,0:T(8,128)S(1)} %pad_maximum_fusion), channel_id=1, source_target_pairs={{0,12},{1,13},{2,14},{3,15},{4,8},{5,9},{6,10},{7,11},{8,4},{9,5},... | collective-permute-start | bytes 393224 | tf_op jit(solution)/shard_map/ppermute | solution.py:18
  58.4 9.2 %collective-permute-start.14 = (f32[8,128,128]{2,1,0:T(8,128)S(1)}, f32[8,128,128]{2,1,0:T(8,128)S(1)}, u32[]{:S(2)}, u32[]{:S(2)}) collective-permute-start(f32[8,128,128]{2,1,0:T(8,128)S(1)} %get-tuple-element.15), channel_id=1, source_target_pairs={{0,2},{1,3},{2,0},{3,1},{4,6},{5,7},{6,4},{7,5},{8,10},{9,11},{10,... | collective-permute-start | bytes 1572872 | tf_op jit(solution)/shard_map/ppermute | solution.py:18
  68.7 7.2 %collective-permute-start.15 = (f32[16,128,128]{2,1,0:T(8,128)}, f32[16,128,128]{2,1,0:T(8,128)}, u32[]{:S(2)}, u32[]{:S(2)}) collective-permute-start(f32[16,128,128]{2,1,0:T(8,128)} %get-tuple-element.11), channel_id=1, source_target_pairs={{0,1},{1,0},{2,3},{3,2},{4,5},{5,4},{6,7},{7,6},{8,9},{9,8},{10,11... | collective-permute-start | bytes 3145736 | tf_op jit(solution)/shard_map/ppermute | solution.py:18
  (7 other events, 17.9 us)

commit v5 on v3

--- a/solution.py
+++ b/solution.py
@@ -111,22 +111,28 @@
     own_inverse = lax.dynamic_slice_in_dim(upper_inverse[0], begin, share, 1)
     own_base = jnp.einsum("kw,kr->wr", own_inverse, upper_rhs[0], precision=highest)
 
-    lower_base = jnp.einsum("skw,skr->swr", lower_inverse, lower_rhs, precision=highest)
-    chained = jnp.einsum("skv,svw->skw", lower_panel, lower_inverse, precision=highest)
-    columns = lax.broadcasted_iota(jnp.int32, lower_index.shape + (width_upper,), 2)
-    pick = (lower_index[:, :, None] == columns).astype(jnp.float32)
-    spread = jnp.einsum("skw,skj->swj", chained, pick, precision=highest)
-
     top_held = xor_gather(top_solution, both, count, top_groups).reshape(count * top_rows, rhs)
     own_rows = own_base - jnp.einsum("wj,jr->wr", total, top_held, precision=highest)
 
     held = xor_gather(own_rows, both, count, spread_groups)
     position = owner_map[parent_list]
     sources = position[:, None] * panels + jnp.arange(panels, dtype=jnp.int32)[None, :]
-    slabs = held[xor_position(sources ^ me, spread_groups)]
-    slabs = slabs.reshape(position.shape[0], width_upper, own_rows.shape[1])
-    lower_update = jnp.einsum("swj,sjr->swr", spread, slabs, precision=highest)
-    lower_solution = lower_base - lower_update
+    places = xor_position(sources ^ me, spread_groups)
+    slabs = jnp.stack(
+        [
+            jnp.concatenate([held[places[s, q]] for q in range(panels)], 0)
+            for s in range(position.shape[0])
+        ]
+    )
+
+    columns = lax.broadcasted_iota(jnp.int32, lower_index.shape + (width_upper,), 2)
+    pick = (lower_index[:, :, None] == columns).astype(jnp.float32)
+    parent_rows = jnp.einsum("skj,sjr->skr", pick, slabs, precision=highest)
+
+    lower_update = jnp.einsum("skw,skr->swr", lower_panel, parent_rows, precision=highest)
+    lower_solution = jnp.einsum(
+        "skw,skr->swr", lower_inverse, lower_rhs - lower_update, precision=highest
+    )
     return (own_rows[None], lower_solution)
 
 

time: 80.7 us -> 132 us (1.64)
  between operations: 0.91 us -> 60.6 us
  matrix products: 26.2 us -> 15 us
  local copies, waits for them, and re-layouts: 12.7 us -> 14.3 us
    dot_general x4 -> x3, matrix products: 19 us -> 7.84 us  [the longest x1 3.51 us: local(): jnp.einsum('skw,skr->swr', lower_panel, parent_rows, precision=highest)]
    gather x1 -> x0, local copies, waits for them, and re-layouts: 3.67 us -> none  [local(): slabs = held[xor_position(sources ^ me, spread_groups)]]
    squeeze x0 -> x2, local copies, waits for them, and re-layouts: none -> 2.73 us  [local(): held[places[s, q]]]
    slice x0 -> x2, local copies, waits for them, and re-layouts: none -> 1.42 us  [local(): places[s, q]]
    unnamed x32 -> x35, local copies, waits for them, and re-layouts: 3.88 us -> 5.1 us
  transfers between devices with their start and end apart: 16 -> 16, of which waited for: 8 -> 7; matrix products, arithmetic and copies ran while one was open for 28% -> 9% of each run, Pallas kernels for 0% -> 0%
where the time goes in v5:
time: 132 us; the launch traced here: 131 us
  between operations  60.6 us (46%)
  starting transfers between devices  21.7 us (16%)
  waiting for transfers between devices  18.3 us (14%)
  matrix products  15 us (11%)
  local copies, waits for them, and re-layouts  14.3 us (11%)
    ppermute x13, starting transfers between devices, xor_gather(): parts.append(lax.ppermute(held, axes, [(i, i ^ v) for i in range(count)]))  19.6 us
    ppermute x13, waiting for transfers between devices, xor_gather(): parts.append(lax.ppermute(held, axes, [(i, i ^ v) for i in range(count)]))  18.3 us
    unnamed x35, local copies, waits for them, and re-layouts  5.1 us
    dot_general x1, matrix products, local(): jnp.einsum('skw,skr->swr', lower_panel, parent_rows, precision=highest)  3.51 us
    squeeze x2, local copies, waits for them, and re-layouts, local(): held[places[s, q]]  2.73 us
  transfers between devices with their start and end apart: 16, of which 7 were waited for; matrix products, arithmetic and copies ran while one was open for 9% of the time, Pallas kernels for 0%

profile of v5, /device:TPU:0, one launch (start us, length us, event | category | flops | bytes accessed | tf_op | source)
XLA Modules:
  0.0 131.1 jit_solution(15074576555069831565)
XLA Ops:
  1.2 2.6 %collective-permute-start.4 = (f32[1,16,128]{2,1,0:T(8,128)}, f32[1,16,128]{2,1,0:T(8,128)S(1)}, u32[]{:S(2)}, u32[]{:S(2)}) collective-permute-start(f32[1,16,128]{2,1,0:T(8,128)} %bitcast.180), channel_id=1, source_target_pairs={{0,2},{1,3},{2,0},{3,1},{4,6},{5,7},{6,4},{7,5},{8,10},{9,11},{10,... | collective-permute-start | bytes 24584 | tf_op jit(solution)/shard_map/ppermute | solution.py:13
  5.1 2.4 %fusion.4 = f32[256,512]{1,0:T(8,128)S(1)} fusion(f32[1,512,512]{2,1,0:T(8,128)} %param.16, f32[1,256,512]{2,1,0:T(8,128)} %param.15), kind=kOutput, calls=%fused_computation.12 | convolution fusion | flops 805306368 | bytes 2097152 | tf_op jit(solution)/shard_map/kv,vw->kw/dot_general | solution.py:102
  9.9 1.7 %collective-permute-start.2 = (f32[128,512]{0,1:T(8,128)S(1)}, f32[128,512]{0,1:T(8,128)}, u32[]{:S(2)}, u32[]{:S(2)}) collective-permute-start(f32[128,512]{0,1:T(8,128)S(1)} %bitcast.175), channel_id=1, source_target_pairs={{0,3},{1,2},{2,1},{3,0},{4,7},{5,6},{6,5},{7,4},{8,11},{9,10},{10,... | collective-permute-start | bytes 786440 | tf_op jit(solution)/shard_map/ppermute | solution.py:110
  13.2 3.0 %collective-permute-start.6 = (f32[4,16,128]{2,1,0:T(8,128)S(1)}, f32[4,16,128]{2,1,0:T(8,128)S(1)}, u32[]{:S(2)}, u32[]{:S(2)}) collective-permute-start(f32[4,16,128]{2,1,0:T(8,128)S(1)} %pad_maximum_fusion.1), channel_id=1, source_target_pairs={{0,16},{1,17},{2,18},{3,19},{4,20},{5,21},{6,22},{7,23},{8,24},{9,... | collective-permute-start | bytes 98312 | tf_op jit(solution)/shard_map/ppermute | solution.py:13
  16.2 2.0 %collective-permute-done.6 = f32[4,16,128]{2,1,0:T(8,128)S(1)} collective-permute-done((f32[4,16,128]{2,1,0:T(8,128)S(1)}, f32[4,16,128]{2,1,0:T(8,128)S(1)}, u32[]{:S(2)}, u32[]{:S(2)}) %collective-permute-start.6) | collective-permute-done | bytes 32800 | tf_op jit(solution)/shard_map/ppermute | solution.py:13
  18.2 1.8 %collective-permute-start.7 = (f32[8,16,128]{2,1,0:T(8,128)S(1)}, f32[8,16,128]{2,1,0:T(8,128)S(1)}, u32[]{:S(2)}, u32[]{:S(2)}) collective-permute-start(f32[8,16,128]{2,1,0:T(8,128)S(1)} %get-tuple-element.58), channel_id=1, source_target_pairs={{0,8},{1,9},{2,10},{3,11},{4,12},{5,13},{6,14},{7,15},{8,0},{9,1},... | collective-permute-start | bytes 196616 | tf_op jit(solution)/shard_map/ppermute | solution.py:13
  20.0 1.6 %fusion.17 = f32[128,128]{1,0:T(8,128)S(1)} fusion(f32[1,512,128]{2,1,0:T(8,128)} %param.14, f32[1,512,512]{2,1,0:T(8,128)} %param.16, s32[]{:T(128)S(6)} %select_n.172), kind=kOutput, calls=%fused_computation.33 | convolution fusion | flops 100663296 | bytes 589828 | tf_op jit(solution)/shard_map/kw,kr->wr/dot_general | solution.py:112
  21.6 1.6 %collective-permute-start.8 = (f32[8,16,128]{2,1,0:T(8,128)S(1)}, f32[8,16,128]{2,1,0:T(8,128)S(1)}, u32[]{:S(2)}, u32[]{:S(2)}) collective-permute-start(f32[8,16,128]{2,1,0:T(8,128)S(1)} %get-tuple-element.58), channel_id=1, source_target_pairs={{0,4},{1,5},{2,6},{3,7},{4,0},{5,1},{6,2},{7,3},{8,12},{9,13},{10,... | collective-permute-start | bytes 196616 | tf_op jit(solution)/shard_map/ppermute | solution.py:13
  23.2 2.0 %collective-permute-start.9 = (f32[8,16,128]{2,1,0:T(8,128)S(1)}, f32[8,16,128]{2,1,0:T(8,128)S(1)}, u32[]{:S(2)}, u32[]{:S(2)}) collective-permute-start(f32[8,16,128]{2,1,0:T(8,128)S(1)} %get-tuple-element.58), channel_id=1, source_target_pairs={{0,12},{1,13},{2,14},{3,15},{4,8},{5,9},{6,10},{7,11},{8,4},{9,5},... | collective-permute-start | bytes 196616 | tf_op jit(solution)/shard_map/ppermute | solution.py:13
  25.2 1.5 %collective-permute-done.8 = f32[8,16,128]{2,1,0:T(8,128)S(1)} collective-permute-done((f32[8,16,128]{2,1,0:T(8,128)S(1)}, f32[8,16,128]{2,1,0:T(8,128)S(1)}, u32[]{:S(2)}, u32[]{:S(2)}) %collective-permute-start.8) | collective-permute-done | bytes 65568 | tf_op jit(solution)/shard_map/ppermute | solution.py:13
  26.6 1.7 %collective-permute-done.9 = f32[8,16,128]{2,1,0:T(8,128)S(1)} collective-permute-done((f32[8,16,128]{2,1,0:T(8,128)S(1)}, f32[8,16,128]{2,1,0:T(8,128)S(1)}, u32[]{:S(2)}, u32[]{:S(2)}) %collective-permute-start.9) | collective-permute-done | bytes 65568 | tf_op jit(solution)/shard_map/ppermute | solution.py:13
  28.4 2.4 %constant_dynamic-update-slice_fusion.23 = (f32[16,128,128]{2,1,0:T(8,128)}, f32[32,128,128]{2,1,0:T(8,128)}, f32[8,128,128]{2,1,0:T(8,128)S(1)}, f32[1,128,128]{2,1,0:T(8,128)S(1)}) fusion(f32[128,128]{1,0:T(8,128)S(1)} %fusion.17, f32[512,128]{1,0:T(8,128)S(1)} %bitcast.178, f32[128,512]{0,1:T(8,128)} %collective-permute-done.2, ...), kind=kOutput, calls=%fused_computation.67 | convolution fusion | flops 100876288 | bytes 1638404 | tf_op jit(solution)/shard_map/wj,jr->wr/dot_general | solution.py:115
  30.8 3.0 %collective-permute-start.10 = (f32[1,128,128]{2,1,0:T(8,128)S(1)}, f32[1,128,128]{2,1,0:T(8,128)S(1)}, u32[]{:S(2)}, u32[]{:S(2)}) collective-permute-start(f32[1,128,128]{2,1,0:T(8,128)S(1)} %get-tuple-element.100), channel_id=1, source_target_pairs={{0,16},{1,17},{2,18},{3,19},{4,20},{5,21},{6,22},{7,23},{8,24},{9,... | collective-permute-start | bytes 196616 | tf_op jit(solution)/shard_map/ppermute | solution.py:13
  33.8 2.9 %collective-permute-done.10 = f32[1,128,128]{2,1,0:T(8,128)S(1)} collective-permute-done((f32[1,128,128]{2,1,0:T(8,128)S(1)}, f32[1,128,128]{2,1,0:T(8,128)S(1)}, u32[]{:S(2)}, u32[]{:S(2)}) %collective-permute-start.10) | collective-permute-done | bytes 65568 | tf_op jit(solution)/shard_map/ppermute | solution.py:13
  37.3 1.4 %collective-permute-start.12 = (f32[2,128,128]{2,1,0:T(8,128)S(1)}, f32[2,128,128]{2,1,0:T(8,128)S(1)}, u32[]{:S(2)}, u32[]{:S(2)}) collective-permute-start(f32[2,128,128]{2,1,0:T(8,128)S(1)} %pad_maximum_fusion), channel_id=1, source_target_pairs={{0,4},{1,5},{2,6},{3,7},{4,0},{5,1},{6,2},{7,3},{8,12},{9,13},{10,... | collective-permute-start | bytes 393224 | tf_op jit(solution)/shard_map/ppermute | solution.py:13
  38.7 1.6 %collective-permute-start.13 = (f32[2,128,128]{2,1,0:T(8,128)S(1)}, f32[2,128,128]{2,1,0:T(8,128)S(1)}, u32[]{:S(2)}, u32[]{:S(2)}) collective-permute-start(f32[2,128,128]{2,1,0:T(8,128)S(1)} %pad_maximum_fusion), channel_id=1, source_target_pairs={{0,12},{1,13},{2,14},{3,15},{4,8},{5,9},{6,10},{7,11},{8,4},{9,5},... | collective-permute-start | bytes 393224 | tf_op jit(solution)/shard_map/ppermute | solution.py:13
  43.3 1.3 collective-permute-done.13
  45.3 1.5 %collective-permute-start.14 = (f32[8,128,128]{2,1,0:T(8,128)S(1)}, f32[8,128,128]{2,1,0:T(8,128)S(1)}, u32[]{:S(2)}, u32[]{:S(2)}) collective-permute-start(f32[8,128,128]{2,1,0:T(8,128)S(1)} %get-tuple-element.45), channel_id=1, source_target_pairs={{0,2},{1,3},{2,0},{3,1},{4,6},{5,7},{6,4},{7,5},{8,10},{9,11},{10,... | collective-permute-start | bytes 1572872 | tf_op jit(solution)/shard_map/ppermute | solution.py:13
  46.8 8.1 %collective-permute-done.14 = f32[8,128,128]{2,1,0:T(8,128)S(1)} collective-permute-done((f32[8,128,128]{2,1,0:T(8,128)S(1)}, f32[8,128,128]{2,1,0:T(8,128)S(1)}, u32[]{:S(2)}, u32[]{:S(2)}) %collective-permute-start.14) | collective-permute-done | bytes 524320 | tf_op jit(solution)/shard_map/ppermute | solution.py:13
  120.2 1.5 %dynamic-slice_bitcast_fusion.3 = (f32[128,128]{1,0:T(8,128)S(1)}, f32[128,128]{1,0:T(8,128)S(1)}, f32[128,128]{1,0:T(8,128)S(1)}, f32[128,128]{1,0:T(8,128)S(1)...) fusion(f32[32,128,128]{2,1,0:T(8,128)} %constant_dynamic-update, ...), kind=kLoop, calls=%fused_computation.78 | loop fusion | bytes 2359368 | tf_op jit(solution)/shard_map/squeeze | solution.py:123
  121.9 2.3 %fusion = f32[8,256,128]{2,1,0:T(8,128)S(1)} fusion(f32[8,512,128]{2,1,0:T(8,128)S(1)} %fusion.16, s32[8,256]{1,0:T(8,128)S(1)} %copy-done.7), kind=kOutput, calls=%fused_computation.5 | convolution fusion | flops 1611661312 | bytes 3153920 | tf_op jit(solution)/shard_map/skj,sjr->skr/dot_general | solution.py:130
  124.2 3.5 %fusion.2 = f32[8,256,128]{2,1,0:T(8,128)S(1)} fusion(f32[8,256,128]{2,1,0:T(8,128)S(1)} %copy-done.4, f32[8,256,128]{2,1,0:T(8,128)S(1)} %fusion, f32[8,256,256]{2,1,0:T(8,128)S(1)} %copy-done), kind=kOutput, calls=%fused_computation.9 | convolution fusion | flops 805568512 | bytes 5242880 | tf_op jit(solution)/shard_map/skw,skr->swr/dot_general | solution.py:132
  127.8 2.0 %convolution_bitcast_fusion = f32[8,256,128]{1,2,0:T(8,128)S(1)} fusion(f32[8,256,128]{2,1,0:T(8,128)S(1)} %fusion.2, f32[8,256,256]{2,1,0:T(8,128)S(1)} %copy-done.3), kind=kOutput, calls=%fused_computation.7 | convolution fusion | flops 805306368 | bytes 4194304 | tf_op jit(solution)/shard_map/skw,skr->swr/dot_general | solution.py:133
  129.8 1.3 copy.19
  (90 shorter events, 15.7 us)
Async XLA Ops:
  0.6 123.6 %copy-start = (f32[8,256,256]{2,1,0:T(8,128)S(1)}, f32[8,256,256]{2,1,0:T(8,128)}, u32[]{:S(2)}) copy-start(f32[8,256,256]{2,1,0:T(8,128)} %param.22) | copy-start | bytes 6291460
  0.6 6.9 %copy-start.11 = (s32[32]{0:T(128)S(1)}, s32[32]{0:T(128)}, u32[]{:S(2)}) copy-start(s32[32]{0:T(128)} %constant.136) | copy-start | bytes 388
  0.7 6.9 %copy-start.8 = (s32[1,256]{1,0:T(1,128)S(1)}, s32[1,256]{1,0:T(1,128)}, u32[]{:S(2)}) copy-start(s32[1,256]{1,0:T(1,128)} %param.17) | copy-start | bytes 3076
  0.7 12.3 %collective-permute-start.3 = (f32[1,16,128]{2,1,0:T(8,128)}, f32[1,16,128]{2,1,0:T(8,128)S(1)}, u32[]{:S(2)}, u32[]{:S(2)}) collective-permute-start(f32[1,16,128]{2,1,0:T(8,128)} %bitcast.179), channel_id=1, source_target_pairs={{0,1},{1,0},{2,3},{3,2},{4,5},{5,4},{6,7},{7,6},{8,9},{9,8},{10,11... | collective-permute-start | bytes 24584 | tf_op jit(solution)/shard_map/ppermute | solution.py:13
  1.2 12.0 %collective-permute-start.4 = (f32[1,16,128]{2,1,0:T(8,128)}, f32[1,16,128]{2,1,0:T(8,128)S(1)}, u32[]{:S(2)}, u32[]{:S(2)}) collective-permute-start(f32[1,16,128]{2,1,0:T(8,128)} %bitcast.180), channel_id=1, source_target_pairs={{0,2},{1,3},{2,0},{3,1},{4,6},{5,7},{6,4},{7,5},{8,10},{9,11},{10,... | collective-permute-start | bytes 24584 | tf_op jit(solution)/shard_map/ppermute | solution.py:13
  3.8 9.4 %collective-permute-start.5 = (f32[1,16,128]{2,1,0:T(8,128)}, f32[1,16,128]{2,1,0:T(8,128)S(1)}, u32[]{:S(2)}, u32[]{:S(2)}) collective-permute-start(f32[1,16,128]{2,1,0:T(8,128)} %bitcast.181), channel_id=1, source_target_pairs={{0,3},{1,2},{2,1},{3,0},{4,7},{5,6},{6,5},{7,4},{8,11},{9,10},{10,... | collective-permute-start | bytes 24584 | tf_op jit(solution)/shard_map/ppermute | solution.py:13
  9.3 2.3 %copy-start.10 = (s32[32]{0:T(128)S(1)}, s32[32]{0:T(128)}, u32[]{:S(2)}) copy-start(s32[32]{0:T(128)} %constant.134) | copy-start | bytes 388
  9.9 18.5 %collective-permute-start.2 = (f32[128,512]{0,1:T(8,128)S(1)}, f32[128,512]{0,1:T(8,128)}, u32[]{:S(2)}, u32[]{:S(2)}) collective-permute-start(f32[128,512]{0,1:T(8,128)S(1)} %bitcast.175), channel_id=1, source_target_pairs={{0,3},{1,2},{2,1},{3,0},{4,7},{5,6},{6,5},{7,4},{8,11},{9,10},{10,... | collective-permute-start | bytes 786440 | tf_op jit(solution)/shard_map/ppermute | solution.py:110
  12.2 16.1 %collective-permute-start.1 = (f32[128,512]{0,1:T(8,128)S(1)}, f32[128,512]{0,1:T(8,128)}, u32[]{:S(2)}, u32[]{:S(2)}) collective-permute-start(f32[128,512]{0,1:T(8,128)S(1)} %bitcast.176), channel_id=1, source_target_pairs={{0,2},{1,3},{2,0},{3,1},{4,6},{5,7},{6,4},{7,5},{8,10},{9,11},{10,... | collective-permute-start | bytes 786440 | tf_op jit(solution)/shard_map/ppermute | solution.py:110
  13.0 15.3 %collective-permute-start = (f32[128,512]{0,1:T(8,128)S(1)}, f32[128,512]{0,1:T(8,128)S(1)}, u32[]{:S(2)}, u32[]{:S(2)}) collective-permute-start(f32[128,512]{0,1:T(8,128)S(1)} %bitcast.177), channel_id=1, source_target_pairs={{0,1},{1,0},{2,3},{3,2},{4,5},{5,4},{6,7},{7,6},{8,9},{9,8},{10,11... | collective-permute-start | bytes 786440 | tf_op jit(solution)/shard_map/ppermute | solution.py:110
  13.2 5.0 %collective-permute-start.6 = (f32[4,16,128]{2,1,0:T(8,128)S(1)}, f32[4,16,128]{2,1,0:T(8,128)S(1)}, u32[]{:S(2)}, u32[]{:S(2)}) collective-permute-start(f32[4,16,128]{2,1,0:T(8,128)S(1)} %pad_maximum_fusion.1), channel_id=1, source_target_pairs={{0,16},{1,17},{2,18},{3,19},{4,20},{5,21},{6,22},{7,23},{8,24},{9,... | collective-permute-start | bytes 98312 | tf_op jit(solution)/shard_map/ppermute | solution.py:13
  18.2 5.0 %collective-permute-start.7 = (f32[8,16,128]{2,1,0:T(8,128)S(1)}, f32[8,16,128]{2,1,0:T(8,128)S(1)}, u32[]{:S(2)}, u32[]{:S(2)}) collective-permute-start(f32[8,16,128]{2,1,0:T(8,128)S(1)} %get-tuple-element.58), channel_id=1, source_target_pairs={{0,8},{1,9},{2,10},{3,11},{4,12},{5,13},{6,14},{7,15},{8,0},{9,1},... | collective-permute-start | bytes 196616 | tf_op jit(solution)/shard_map/ppermute | solution.py:13
  21.6 5.0 %collective-permute-start.8 = (f32[8,16,128]{2,1,0:T(8,128)S(1)}, f32[8,16,128]{2,1,0:T(8,128)S(1)}, u32[]{:S(2)}, u32[]{:S(2)}) collective-permute-start(f32[8,16,128]{2,1,0:T(8,128)S(1)} %get-tuple-element.58), channel_id=1, source_target_pairs={{0,4},{1,5},{2,6},{3,7},{4,0},{5,1},{6,2},{7,3},{8,12},{9,13},{10,... | collective-permute-start | bytes 196616 | tf_op jit(solution)/shard_map/ppermute | solution.py:13
  23.2 5.2 %collective-permute-start.9 = (f32[8,16,128]{2,1,0:T(8,128)S(1)}, f32[8,16,128]{2,1,0:T(8,128)S(1)}, u32[]{:S(2)}, u32[]{:S(2)}) collective-permute-start(f32[8,16,128]{2,1,0:T(8,128)S(1)} %get-tuple-element.58), channel_id=1, source_target_pairs={{0,12},{1,13},{2,14},{3,15},{4,8},{5,9},{6,10},{7,11},{8,4},{9,5},... | collective-permute-start | bytes 196616 | tf_op jit(solution)/shard_map/ppermute | solution.py:13
  30.8 25.9 %copy-start.5 = (f32[1,128,128]{2,1,0:T(8,128)}, f32[1,128,128]{2,1,0:T(8,128)S(1)}, u32[]{:S(2)}) copy-start(f32[1,128,128]{2,1,0:T(8,128)S(1)} %get-tuple-element.100) | copy-start | bytes 196612
  30.8 25.3 %copy-start.1 = (s32[8]{0:T(128)S(1)}, s32[8]{0:T(128)}, u32[]{:S(2)}) copy-start(s32[8]{0:T(128)} %param.19) | copy-start | bytes 100
  30.8 6.0 %collective-permute-start.10 = (f32[1,128,128]{2,1,0:T(8,128)S(1)}, f32[1,128,128]{2,1,0:T(8,128)S(1)}, u32[]{:S(2)}, u32[]{:S(2)}) collective-permute-start(f32[1,128,128]{2,1,0:T(8,128)S(1)} %get-tuple-element.100), channel_id=1, source_target_pairs={{0,16},{1,17},{2,18},{3,19},{4,20},{5,21},{6,22},{7,23},{8,24},{9,... | collective-permute-start | bytes 196616 | tf_op jit(solution)/shard_map/ppermute | solution.py:13
  36.8 5.0 %collective-permute-start.11 = (f32[2,128,128]{2,1,0:T(8,128)S(1)}, f32[2,128,128]{2,1,0:T(8,128)S(1)}, u32[]{:S(2)}, u32[]{:S(2)}) collective-permute-start(f32[2,128,128]{2,1,0:T(8,128)S(1)} %pad_maximum_fusion), channel_id=1, source_target_pairs={{0,8},{1,9},{2,10},{3,11},{4,12},{5,13},{6,14},{7,15},{8,0},{9,1},... | collective-permute-start | bytes 393224 | tf_op jit(solution)/shard_map/ppermute | solution.py:13
  37.3 5.2 %collective-permute-start.12 = (f32[2,128,128]{2,1,0:T(8,128)S(1)}, f32[2,128,128]{2,1,0:T(8,128)S(1)}, u32[]{:S(2)}, u32[]{:S(2)}) collective-permute-start(f32[2,128,128]{2,1,0:T(8,128)S(1)} %pad_maximum_fusion), channel_id=1, source_target_pairs={{0,4},{1,5},{2,6},{3,7},{4,0},{5,1},{6,2},{7,3},{8,12},{9,13},{10,... | collective-permute-start | bytes 393224 | tf_op jit(solution)/shard_map/ppermute | solution.py:13
  38.7 5.9 %collective-permute-start.13 = (f32[2,128,128]{2,1,0:T(8,128)S(1)}, f32[2,128,128]{2,1,0:T(8,128)S(1)}, u32[]{:S(2)}, u32[]{:S(2)}) collective-permute-start(f32[2,128,128]{2,1,0:T(8,128)S(1)} %pad_maximum_fusion), channel_id=1, source_target_pairs={{0,12},{1,13},{2,14},{3,15},{4,8},{5,9},{6,10},{7,11},{8,4},{9,5},... | collective-permute-start | bytes 393224 | tf_op jit(solution)/shard_map/ppermute | solution.py:13
  45.3 9.6 %collective-permute-start.14 = (f32[8,128,128]{2,1,0:T(8,128)S(1)}, f32[8,128,128]{2,1,0:T(8,128)S(1)}, u32[]{:S(2)}, u32[]{:S(2)}) collective-permute-start(f32[8,128,128]{2,1,0:T(8,128)S(1)} %get-tuple-element.45), channel_id=1, source_target_pairs={{0,2},{1,3},{2,0},{3,1},{4,6},{5,7},{6,4},{7,5},{8,10},{9,11},{10,... | collective-permute-start | bytes 1572872 | tf_op jit(solution)/shard_map/ppermute | solution.py:13
  56.0 61.7 %collective-permute-start.15 = (f32[16,128,128]{2,1,0:T(8,128)}, f32[16,128,128]{2,1,0:T(8,128)S(1)}, u32[]{:S(2)}, u32[]{:S(2)}) collective-permute-start(f32[16,128,128]{2,1,0:T(8,128)} %get-tuple-element.41), channel_id=1, source_target_pairs={{0,1},{1,0},{2,3},{3,2},{4,5},{5,4},{6,7},{7,6},{8,9},{9,8},{10,11... | collective-permute-start | bytes 3145736 | tf_op jit(solution)/shard_map/ppermute | solution.py:13
  121.8 2.4 %copy-start.4 = (f32[8,256,128]{2,1,0:T(8,128)S(1)}, f32[8,256,128]{2,1,0:T(8,128)}, u32[]{:S(2)}) copy-start(f32[8,256,128]{2,1,0:T(8,128)} %param.23) | copy-start | bytes 3145732
  124.2 3.5 %copy-start.3 = (f32[8,256,256]{2,1,0:T(8,128)S(1)}, f32[8,256,256]{2,1,0:T(8,128)}, u32[]{:S(2)}) copy-start(f32[8,256,256]{2,1,0:T(8,128)} %param.24) | copy-start | bytes 6291460
  (4 other events, 5.7 us)

commit v6 on v5

--- a/solution.py
+++ b/solution.py
@@ -118,12 +118,7 @@
     position = owner_map[parent_list]
     sources = position[:, None] * panels + jnp.arange(panels, dtype=jnp.int32)[None, :]
     places = xor_position(sources ^ me, spread_groups)
-    slabs = jnp.stack(
-        [
-            jnp.concatenate([held[places[s, q]] for q in range(panels)], 0)
-            for s in range(position.shape[0])
-        ]
-    )
+    slabs = held[places].reshape(position.shape[0], width_upper, own_rows.shape[1])
 
     columns = lax.broadcasted_iota(jnp.int32, lower_index.shape + (width_upper,), 2)
     pick = (lower_index[:, :, None] == columns).astype(jnp.float32)

time: 132 us -> 74.5 us (0.56)
  between operations: 60.6 us -> 0.94 us
  waiting for transfers between devices: 18.3 us -> 20.4 us
  matrix products: 15 us -> 16.5 us
    gather x0 -> x1, local copies, waits for them, and re-layouts: none -> 3.6 us  [local(): held[places].reshape(position.shape[0], width_upper, own_rows.shape[1])]
    squeeze x2 -> x0, local copies, waits for them, and re-layouts: 2.73 us -> none  [local(): held[places[s, q]]]
    ppermute x13, waiting for transfers between devices: 18.3 us -> 20.3 us  [xor_gather(): parts.append(lax.ppermute(held, axes, [(i, i ^ v) for i in range(count)]))]
    dot_general x1, matrix products: 2.32 us -> 3.79 us  [local(): parent_rows = jnp.einsum('skj,sjr->skr', pick, slabs, precision=highest)]
    slice x2 -> x0, local copies, waits for them, and re-layouts: 1.42 us -> none  [local(): places[s, q]]
  transfers between devices with their start and end apart: 16 -> 16, of which waited for: 7 -> 8; matrix products, arithmetic and copies ran while one was open for 9% -> 15% of each run, Pallas kernels for 0% -> 0%
where the time goes in v6:
time: 74.5 us; the launch traced here: 74.2 us
  starting transfers between devices  21.7 us (29%)
  waiting for transfers between devices  20.4 us (27%)
  matrix products  16.5 us (22%)
  local copies, waits for them, and re-layouts  13.8 us (19%)
  other arithmetic  0.98 us (1%)
  between operations  0.94 us (1%)
    ppermute x13, waiting for transfers between devices, xor_gather(): parts.append(lax.ppermute(held, axes, [(i, i ^ v) for i in range(count)]))  20.3 us
    ppermute x13, starting transfers between devices, xor_gather(): parts.append(lax.ppermute(held, axes, [(i, i ^ v) for i in range(count)]))  19.6 us
    unnamed x35, local copies, waits for them, and re-layouts  5.09 us
    dot_general x1, matrix products, local(): parent_rows = jnp.einsum('skj,sjr->skr', pick, slabs, precision=highest)  3.79 us
    gather x1, local copies, waits for them, and re-layouts, local(): held[places].reshape(position.shape[0], width_upper, own_rows.shape[1])  3.6 us
    dot_general x1, matrix products, local(): jnp.einsum('skw,skr->swr', lower_panel, parent_rows, precision=highest)  3.52 us
    dot_general x1, matrix products, local(): jnp.einsum('kv,vw->kw', upper_panel[0], upper_inverse[0], precision=highest)  2.44 us
    dot_general x1, matrix products, local(): jnp.einsum('wj,jr->wr', total, top_held, precision=highest)  2.4 us
  transfers between devices with their start and end apart: 16, of which 8 were waited for; matrix products, arithmetic and copies ran while one was open for 15% of the time, Pallas kernels for 0%

profile of v6, /device:TPU:0, one launch (start us, length us, event | category | flops | bytes accessed | tf_op | source)
XLA Modules:
  0.0 74.2 jit_solution(14534052671573055485)
XLA Ops:
  1.2 2.6 %collective-permute-start.4 = (f32[1,16,128]{2,1,0:T(8,128)}, f32[1,16,128]{2,1,0:T(8,128)S(1)}, u32[]{:S(2)}, u32[]{:S(2)}) collective-permute-start(f32[1,16,128]{2,1,0:T(8,128)} %bitcast.56), channel_id=1, source_target_pairs={{0,2},{1,3},{2,0},{3,1},{4,6},{5,7},{6,4},{7,5},{8,10},{9,11},{10,... | collective-permute-start | bytes 24584 | tf_op jit(solution)/shard_map/ppermute | solution.py:13
  5.1 2.4 %fusion.4 = f32[256,512]{1,0:T(8,128)S(1)} fusion(f32[1,512,512]{2,1,0:T(8,128)} %param.16, f32[1,256,512]{2,1,0:T(8,128)} %param.15), kind=kOutput, calls=%fused_computation.13 | convolution fusion | flops 805306368 | bytes 2097152 | tf_op jit(solution)/shard_map/kv,vw->kw/dot_general | solution.py:102
  9.9 1.7 %collective-permute-start.2 = (f32[128,512]{0,1:T(8,128)S(1)}, f32[128,512]{0,1:T(8,128)}, u32[]{:S(2)}, u32[]{:S(2)}) collective-permute-start(f32[128,512]{0,1:T(8,128)S(1)} %bitcast.50), channel_id=1, source_target_pairs={{0,3},{1,2},{2,1},{3,0},{4,7},{5,6},{6,5},{7,4},{8,11},{9,10},{10,... | collective-permute-start | bytes 786440 | tf_op jit(solution)/shard_map/ppermute | solution.py:110
  13.2 3.0 %collective-permute-start.6 = (f32[4,16,128]{2,1,0:T(8,128)S(1)}, f32[4,16,128]{2,1,0:T(8,128)S(1)}, u32[]{:S(2)}, u32[]{:S(2)}) collective-permute-start(f32[4,16,128]{2,1,0:T(8,128)S(1)} %pad_maximum_fusion.1), channel_id=1, source_target_pairs={{0,16},{1,17},{2,18},{3,19},{4,20},{5,21},{6,22},{7,23},{8,24},{9,... | collective-permute-start | bytes 98312 | tf_op jit(solution)/shard_map/ppermute | solution.py:13
  16.2 2.0 %collective-permute-done.6 = f32[4,16,128]{2,1,0:T(8,128)S(1)} collective-permute-done((f32[4,16,128]{2,1,0:T(8,128)S(1)}, f32[4,16,128]{2,1,0:T(8,128)S(1)}, u32[]{:S(2)}, u32[]{:S(2)}) %collective-permute-start.6) | collective-permute-done | bytes 32800 | tf_op jit(solution)/shard_map/ppermute | solution.py:13
  18.2 1.8 %collective-permute-start.7 = (f32[8,16,128]{2,1,0:T(8,128)S(1)}, f32[8,16,128]{2,1,0:T(8,128)S(1)}, u32[]{:S(2)}, u32[]{:S(2)}) collective-permute-start(f32[8,16,128]{2,1,0:T(8,128)S(1)} %get-tuple-element.26), channel_id=1, source_target_pairs={{0,8},{1,9},{2,10},{3,11},{4,12},{5,13},{6,14},{7,15},{8,0},{9,1},... | collective-permute-start | bytes 196616 | tf_op jit(solution)/shard_map/ppermute | solution.py:13
  20.0 1.6 %fusion.9 = f32[128,128]{1,0:T(8,128)S(1)} fusion(f32[1,512,128]{2,1,0:T(8,128)} %param.14, f32[1,512,512]{2,1,0:T(8,128)} %param.16, s32[]{:T(128)S(6)} %select_n.86), kind=kOutput, calls=%fused_computation.18 | convolution fusion | flops 100663296 | bytes 589828 | tf_op jit(solution)/shard_map/kw,kr->wr/dot_general | solution.py:112
  21.6 1.6 %collective-permute-start.8 = (f32[8,16,128]{2,1,0:T(8,128)S(1)}, f32[8,16,128]{2,1,0:T(8,128)S(1)}, u32[]{:S(2)}, u32[]{:S(2)}) collective-permute-start(f32[8,16,128]{2,1,0:T(8,128)S(1)} %get-tuple-element.26), channel_id=1, source_target_pairs={{0,4},{1,5},{2,6},{3,7},{4,0},{5,1},{6,2},{7,3},{8,12},{9,13},{10,... | collective-permute-start | bytes 196616 | tf_op jit(solution)/shard_map/ppermute | solution.py:13
  23.2 2.0 %collective-permute-start.9 = (f32[8,16,128]{2,1,0:T(8,128)S(1)}, f32[8,16,128]{2,1,0:T(8,128)S(1)}, u32[]{:S(2)}, u32[]{:S(2)}) collective-permute-start(f32[8,16,128]{2,1,0:T(8,128)S(1)} %get-tuple-element.26), channel_id=1, source_target_pairs={{0,12},{1,13},{2,14},{3,15},{4,8},{5,9},{6,10},{7,11},{8,4},{9,5},... | collective-permute-start | bytes 196616 | tf_op jit(solution)/shard_map/ppermute | solution.py:13
  25.2 1.5 %collective-permute-done.8 = f32[8,16,128]{2,1,0:T(8,128)S(1)} collective-permute-done((f32[8,16,128]{2,1,0:T(8,128)S(1)}, f32[8,16,128]{2,1,0:T(8,128)S(1)}, u32[]{:S(2)}, u32[]{:S(2)}) %collective-permute-start.8) | collective-permute-done | bytes 65568 | tf_op jit(solution)/shard_map/ppermute | solution.py:13
  26.6 1.7 %collective-permute-done.9 = f32[8,16,128]{2,1,0:T(8,128)S(1)} collective-permute-done((f32[8,16,128]{2,1,0:T(8,128)S(1)}, f32[8,16,128]{2,1,0:T(8,128)S(1)}, u32[]{:S(2)}, u32[]{:S(2)}) %collective-permute-start.9) | collective-permute-done | bytes 65568 | tf_op jit(solution)/shard_map/ppermute | solution.py:13
  28.4 2.4 %constant_dynamic-update-slice_fusion.23 = (f32[16,128,128]{2,1,0:T(8,128)}, f32[32,128,128]{2,1,0:T(8,128)}, f32[8,128,128]{2,1,0:T(8,128)S(1)}, f32[1,128,128]{2,1,0:T(8,128)S(1)}) fusion(f32[128,128]{1,0:T(8,128)S(1)} %fusion.9, f32[512,128]{1,0:T(8,128)S(1)} %bitcast.54, f32[128,512]{0,1:T(8,128)} %collective-permute-done.2, ...), kind=kOutput, calls=%fused_computation.52 | convolution fusion | flops 100876288 | bytes 1638404 | tf_op jit(solution)/shard_map/wj,jr->wr/dot_general | solution.py:115
  30.8 3.0 %collective-permute-start.10 = (f32[1,128,128]{2,1,0:T(8,128)S(1)}, f32[1,128,128]{2,1,0:T(8,128)S(1)}, u32[]{:S(2)}, u32[]{:S(2)}) collective-permute-start(f32[1,128,128]{2,1,0:T(8,128)S(1)} %get-tuple-element.36), channel_id=1, source_target_pairs={{0,16},{1,17},{2,18},{3,19},{4,20},{5,21},{6,22},{7,23},{8,24},{9,... | collective-permute-start | bytes 196616 | tf_op jit(solution)/shard_map/ppermute | solution.py:13
  33.8 2.9 %collective-permute-done.10 = f32[1,128,128]{2,1,0:T(8,128)S(1)} collective-permute-done((f32[1,128,128]{2,1,0:T(8,128)S(1)}, f32[1,128,128]{2,1,0:T(8,128)S(1)}, u32[]{:S(2)}, u32[]{:S(2)}) %collective-permute-start.10) | collective-permute-done | bytes 65568 | tf_op jit(solution)/shard_map/ppermute | solution.py:13
  37.3 1.4 %collective-permute-start.12 = (f32[2,128,128]{2,1,0:T(8,128)S(1)}, f32[2,128,128]{2,1,0:T(8,128)S(1)}, u32[]{:S(2)}, u32[]{:S(2)}) collective-permute-start(f32[2,128,128]{2,1,0:T(8,128)S(1)} %pad_maximum_fusion), channel_id=1, source_target_pairs={{0,4},{1,5},{2,6},{3,7},{4,0},{5,1},{6,2},{7,3},{8,12},{9,13},{10,... | collective-permute-start | bytes 393224 | tf_op jit(solution)/shard_map/ppermute | solution.py:13
  38.7 1.6 %collective-permute-start.13 = (f32[2,128,128]{2,1,0:T(8,128)S(1)}, f32[2,128,128]{2,1,0:T(8,128)S(1)}, u32[]{:S(2)}, u32[]{:S(2)}) collective-permute-start(f32[2,128,128]{2,1,0:T(8,128)S(1)} %pad_maximum_fusion), channel_id=1, source_target_pairs={{0,12},{1,13},{2,14},{3,15},{4,8},{5,9},{6,10},{7,11},{8,4},{9,5},... | collective-permute-start | bytes 393224 | tf_op jit(solution)/shard_map/ppermute | solution.py:13
  45.3 1.5 %collective-permute-start.14 = (f32[8,128,128]{2,1,0:T(8,128)S(1)}, f32[8,128,128]{2,1,0:T(8,128)S(1)}, u32[]{:S(2)}, u32[]{:S(2)}) collective-permute-start(f32[8,128,128]{2,1,0:T(8,128)S(1)} %get-tuple-element.13), channel_id=1, source_target_pairs={{0,2},{1,3},{2,0},{3,1},{4,6},{5,7},{6,4},{7,5},{8,10},{9,11},{10,... | collective-permute-start | bytes 1572872 | tf_op jit(solution)/shard_map/ppermute | solution.py:13
  46.8 8.1 %collective-permute-done.14 = f32[8,128,128]{2,1,0:T(8,128)S(1)} collective-permute-done((f32[8,128,128]{2,1,0:T(8,128)S(1)}, f32[8,128,128]{2,1,0:T(8,128)S(1)}, u32[]{:S(2)}, u32[]{:S(2)}) %collective-permute-start.14) | collective-permute-done | bytes 524320 | tf_op jit(solution)/shard_map/ppermute | solution.py:13
  56.8 2.0 %collective-permute-done.15 = f32[16,128,128]{2,1,0:T(8,128)S(1)} collective-permute-done((f32[16,128,128]{2,1,0:T(8,128)}, f32[16,128,128]{2,1,0:T(8,128)S(1)}, u32[]{:S(2)}, u32[]{:S(2)}) %collective-permute-start.15) | collective-permute-done | bytes 1048608 | tf_op jit(solution)/shard_map/ppermute | solution.py:13
  59.9 3.6 %gather_fusion.4 = f32[32,128,128]{2,1,0:T(8,128)} fusion(f32[32,128,128]{2,1,0:T(8,128)} %constant_dynamic-update-slice_fusion.24, s32[1024]{0:T(1024)S(1)} %pad_clamp_fusion), kind=kCustom, calls=%fused_computation.4 | custom fusion | bytes 4194432 | tf_op jit(solution)/shard_map/gather | solution.py:121
  63.5 3.8 %fusion = f32[8,256,128]{2,1,0:T(8,128)S(1)} fusion(f32[8,512,128]{2,1,0:T(8,128)} %bitcast.53, s32[8,256]{1,0:T(8,128)S(1)} %copy-done.7), kind=kOutput, calls=%fused_computation.6 | convolution fusion | flops 1611661312 | bytes 3153920 | tf_op jit(solution)/shard_map/skj,sjr->skr/dot_general | solution.py:125
  67.4 3.5 %fusion.2 = f32[8,256,128]{2,1,0:T(8,128)S(1)} fusion(f32[8,256,128]{2,1,0:T(8,128)S(1)} %copy-done.4, f32[8,256,128]{2,1,0:T(8,128)S(1)} %fusion, f32[8,256,256]{2,1,0:T(8,128)S(1)} %copy-done), kind=kOutput, calls=%fused_computation.10 | convolution fusion | flops 805568512 | bytes 5242880 | tf_op jit(solution)/shard_map/skw,skr->swr/dot_general | solution.py:127
  70.9 2.0 %convolution_bitcast_fusion = f32[8,256,128]{1,2,0:T(8,128)S(1)} fusion(f32[8,256,128]{2,1,0:T(8,128)S(1)} %fusion.2, f32[8,256,256]{2,1,0:T(8,128)S(1)} %copy-done.3), kind=kOutput, calls=%fused_computation.8 | convolution fusion | flops 805306368 | bytes 4194304 | tf_op jit(solution)/shard_map/skw,skr->swr/dot_general | solution.py:128
  72.9 1.3 %copy.19 = f32[8,256,128]{2,1,0:T(8,128)} copy(f32[8,256,128]{1,2,0:T(8,128)S(1)} %convolution_bitcast_fusion) | data formatting | bytes 2097152
  (81 shorter events, 14.2 us)
Async XLA Ops:
  0.6 66.7 %copy-start = (f32[8,256,256]{2,1,0:T(8,128)S(1)}, f32[8,256,256]{2,1,0:T(8,128)}, u32[]{:S(2)}) copy-start(f32[8,256,256]{2,1,0:T(8,128)} %param.22) | copy-start | bytes 6291460
  0.6 6.9 %copy-start.11 = (s32[32]{0:T(128)S(1)}, s32[32]{0:T(128)}, u32[]{:S(2)}) copy-start(s32[32]{0:T(128)} %constant.136) | copy-start | bytes 388
  0.7 6.9 %copy-start.8 = (s32[1,256]{1,0:T(1,128)S(1)}, s32[1,256]{1,0:T(1,128)}, u32[]{:S(2)}) copy-start(s32[1,256]{1,0:T(1,128)} %param.17) | copy-start | bytes 3076
  0.7 12.3 %collective-permute-start.3 = (f32[1,16,128]{2,1,0:T(8,128)}, f32[1,16,128]{2,1,0:T(8,128)S(1)}, u32[]{:S(2)}, u32[]{:S(2)}) collective-permute-start(f32[1,16,128]{2,1,0:T(8,128)} %bitcast.55), channel_id=1, source_target_pairs={{0,1},{1,0},{2,3},{3,2},{4,5},{5,4},{6,7},{7,6},{8,9},{9,8},{10,11... | collective-permute-start | bytes 24584 | tf_op jit(solution)/shard_map/ppermute | solution.py:13
  1.2 12.0 %collective-permute-start.4 = (f32[1,16,128]{2,1,0:T(8,128)}, f32[1,16,128]{2,1,0:T(8,128)S(1)}, u32[]{:S(2)}, u32[]{:S(2)}) collective-permute-start(f32[1,16,128]{2,1,0:T(8,128)} %bitcast.56), channel_id=1, source_target_pairs={{0,2},{1,3},{2,0},{3,1},{4,6},{5,7},{6,4},{7,5},{8,10},{9,11},{10,... | collective-permute-start | bytes 24584 | tf_op jit(solution)/shard_map/ppermute | solution.py:13
  3.8 9.4 %collective-permute-start.5 = (f32[1,16,128]{2,1,0:T(8,128)}, f32[1,16,128]{2,1,0:T(8,128)S(1)}, u32[]{:S(2)}, u32[]{:S(2)}) collective-permute-start(f32[1,16,128]{2,1,0:T(8,128)} %bitcast.57), channel_id=1, source_target_pairs={{0,3},{1,2},{2,1},{3,0},{4,7},{5,6},{6,5},{7,4},{8,11},{9,10},{10,... | collective-permute-start | bytes 24584 | tf_op jit(solution)/shard_map/ppermute | solution.py:13
  9.9 18.5 %collective-permute-start.2 = (f32[128,512]{0,1:T(8,128)S(1)}, f32[128,512]{0,1:T(8,128)}, u32[]{:S(2)}, u32[]{:S(2)}) collective-permute-start(f32[128,512]{0,1:T(8,128)S(1)} %bitcast.50), channel_id=1, source_target_pairs={{0,3},{1,2},{2,1},{3,0},{4,7},{5,6},{6,5},{7,4},{8,11},{9,10},{10,... | collective-permute-start | bytes 786440 | tf_op jit(solution)/shard_map/ppermute | solution.py:110
  12.2 16.1 %collective-permute-start.1 = (f32[128,512]{0,1:T(8,128)S(1)}, f32[128,512]{0,1:T(8,128)}, u32[]{:S(2)}, u32[]{:S(2)}) collective-permute-start(f32[128,512]{0,1:T(8,128)S(1)} %bitcast.51), channel_id=1, source_target_pairs={{0,2},{1,3},{2,0},{3,1},{4,6},{5,7},{6,4},{7,5},{8,10},{9,11},{10,... | collective-permute-start | bytes 786440 | tf_op jit(solution)/shard_map/ppermute | solution.py:110
  13.0 15.3 %collective-permute-start = (f32[128,512]{0,1:T(8,128)S(1)}, f32[128,512]{0,1:T(8,128)S(1)}, u32[]{:S(2)}, u32[]{:S(2)}) collective-permute-start(f32[128,512]{0,1:T(8,128)S(1)} %bitcast.52), channel_id=1, source_target_pairs={{0,1},{1,0},{2,3},{3,2},{4,5},{5,4},{6,7},{7,6},{8,9},{9,8},{10,11... | collective-permute-start | bytes 786440 | tf_op jit(solution)/shard_map/ppermute | solution.py:110
  13.2 5.0 %collective-permute-start.6 = (f32[4,16,128]{2,1,0:T(8,128)S(1)}, f32[4,16,128]{2,1,0:T(8,128)S(1)}, u32[]{:S(2)}, u32[]{:S(2)}) collective-permute-start(f32[4,16,128]{2,1,0:T(8,128)S(1)} %pad_maximum_fusion.1), channel_id=1, source_target_pairs={{0,16},{1,17},{2,18},{3,19},{4,20},{5,21},{6,22},{7,23},{8,24},{9,... | collective-permute-start | bytes 98312 | tf_op jit(solution)/shard_map/ppermute | solution.py:13
  18.2 5.0 %collective-permute-start.7 = (f32[8,16,128]{2,1,0:T(8,128)S(1)}, f32[8,16,128]{2,1,0:T(8,128)S(1)}, u32[]{:S(2)}, u32[]{:S(2)}) collective-permute-start(f32[8,16,128]{2,1,0:T(8,128)S(1)} %get-tuple-element.26), channel_id=1, source_target_pairs={{0,8},{1,9},{2,10},{3,11},{4,12},{5,13},{6,14},{7,15},{8,0},{9,1},... | collective-permute-start | bytes 196616 | tf_op jit(solution)/shard_map/ppermute | solution.py:13
  21.6 5.0 %collective-permute-start.8 = (f32[8,16,128]{2,1,0:T(8,128)S(1)}, f32[8,16,128]{2,1,0:T(8,128)S(1)}, u32[]{:S(2)}, u32[]{:S(2)}) collective-permute-start(f32[8,16,128]{2,1,0:T(8,128)S(1)} %get-tuple-element.26), channel_id=1, source_target_pairs={{0,4},{1,5},{2,6},{3,7},{4,0},{5,1},{6,2},{7,3},{8,12},{9,13},{10,... | collective-permute-start | bytes 196616 | tf_op jit(solution)/shard_map/ppermute | solution.py:13
  23.2 5.2 %collective-permute-start.9 = (f32[8,16,128]{2,1,0:T(8,128)S(1)}, f32[8,16,128]{2,1,0:T(8,128)S(1)}, u32[]{:S(2)}, u32[]{:S(2)}) collective-permute-start(f32[8,16,128]{2,1,0:T(8,128)S(1)} %get-tuple-element.26), channel_id=1, source_target_pairs={{0,12},{1,13},{2,14},{3,15},{4,8},{5,9},{6,10},{7,11},{8,4},{9,5},... | collective-permute-start | bytes 196616 | tf_op jit(solution)/shard_map/ppermute | solution.py:13
  30.8 25.9 %copy-start.5 = (f32[1,128,128]{2,1,0:T(8,128)}, f32[1,128,128]{2,1,0:T(8,128)S(1)}, u32[]{:S(2)}) copy-start(f32[1,128,128]{2,1,0:T(8,128)S(1)} %get-tuple-element.36) | copy-start | bytes 196612
  30.8 25.2 %copy-start.1 = (s32[8]{0:T(128)S(1)}, s32[8]{0:T(128)}, u32[]{:S(2)}) copy-start(s32[8]{0:T(128)} %param.19) | copy-start | bytes 100
  30.8 6.0 %collective-permute-start.10 = (f32[1,128,128]{2,1,0:T(8,128)S(1)}, f32[1,128,128]{2,1,0:T(8,128)S(1)}, u32[]{:S(2)}, u32[]{:S(2)}) collective-permute-start(f32[1,128,128]{2,1,0:T(8,128)S(1)} %get-tuple-element.36), channel_id=1, source_target_pairs={{0,16},{1,17},{2,18},{3,19},{4,20},{5,21},{6,22},{7,23},{8,24},{9,... | collective-permute-start | bytes 196616 | tf_op jit(solution)/shard_map/ppermute | solution.py:13
  36.8 5.0 %collective-permute-start.11 = (f32[2,128,128]{2,1,0:T(8,128)S(1)}, f32[2,128,128]{2,1,0:T(8,128)S(1)}, u32[]{:S(2)}, u32[]{:S(2)}) collective-permute-start(f32[2,128,128]{2,1,0:T(8,128)S(1)} %pad_maximum_fusion), channel_id=1, source_target_pairs={{0,8},{1,9},{2,10},{3,11},{4,12},{5,13},{6,14},{7,15},{8,0},{9,1},... | collective-permute-start | bytes 393224 | tf_op jit(solution)/shard_map/ppermute | solution.py:13
  37.3 5.2 %collective-permute-start.12 = (f32[2,128,128]{2,1,0:T(8,128)S(1)}, f32[2,128,128]{2,1,0:T(8,128)S(1)}, u32[]{:S(2)}, u32[]{:S(2)}) collective-permute-start(f32[2,128,128]{2,1,0:T(8,128)S(1)} %pad_maximum_fusion), channel_id=1, source_target_pairs={{0,4},{1,5},{2,6},{3,7},{4,0},{5,1},{6,2},{7,3},{8,12},{9,13},{10,... | collective-permute-start | bytes 393224 | tf_op jit(solution)/shard_map/ppermute | solution.py:13
  38.7 5.9 %collective-permute-start.13 = (f32[2,128,128]{2,1,0:T(8,128)S(1)}, f32[2,128,128]{2,1,0:T(8,128)S(1)}, u32[]{:S(2)}, u32[]{:S(2)}) collective-permute-start(f32[2,128,128]{2,1,0:T(8,128)S(1)} %pad_maximum_fusion), channel_id=1, source_target_pairs={{0,12},{1,13},{2,14},{3,15},{4,8},{5,9},{6,10},{7,11},{8,4},{9,5},... | collective-permute-start | bytes 393224 | tf_op jit(solution)/shard_map/ppermute | solution.py:13
  45.3 9.6 %collective-permute-start.14 = (f32[8,128,128]{2,1,0:T(8,128)S(1)}, f32[8,128,128]{2,1,0:T(8,128)S(1)}, u32[]{:S(2)}, u32[]{:S(2)}) collective-permute-start(f32[8,128,128]{2,1,0:T(8,128)S(1)} %get-tuple-element.13), channel_id=1, source_target_pairs={{0,2},{1,3},{2,0},{3,1},{4,6},{5,7},{6,4},{7,5},{8,10},{9,11},{10,... | collective-permute-start | bytes 1572872 | tf_op jit(solution)/shard_map/ppermute | solution.py:13
  56.0 2.9 %collective-permute-start.15 = (f32[16,128,128]{2,1,0:T(8,128)}, f32[16,128,128]{2,1,0:T(8,128)S(1)}, u32[]{:S(2)}, u32[]{:S(2)}) collective-permute-start(f32[16,128,128]{2,1,0:T(8,128)} %get-tuple-element.9), channel_id=1, source_target_pairs={{0,1},{1,0},{2,3},{3,2},{4,5},{5,4},{6,7},{7,6},{8,9},{9,8},{10,11... | collective-permute-start | bytes 3145736 | tf_op jit(solution)/shard_map/ppermute | solution.py:13
  59.9 3.6 %copy-start.7 = (s32[8,256]{1,0:T(8,128)S(1)}, s32[8,256]{1,0:T(8,128)}, u32[]{:S(2)}) copy-start(s32[8,256]{1,0:T(8,128)} %param.21) | copy-start | bytes 24580
  63.5 3.8 %copy-start.4 = (f32[8,256,128]{2,1,0:T(8,128)S(1)}, f32[8,256,128]{2,1,0:T(8,128)}, u32[]{:S(2)}) copy-start(f32[8,256,128]{2,1,0:T(8,128)} %param.23) | copy-start | bytes 3145732
  67.4 3.5 %copy-start.3 = (f32[8,256,256]{2,1,0:T(8,128)S(1)}, f32[8,256,256]{2,1,0:T(8,128)}, u32[]{:S(2)}) copy-start(f32[8,256,256]{2,1,0:T(8,128)} %param.24) | copy-start | bytes 6291460
  (4 other events, 6.4 us)

commit v7 on v6

--- a/solution.py
+++ b/solution.py
@@ -101,24 +101,40 @@
     pick_top = (top_index[0][:, None] == natural[None, :]).astype(jnp.float32)
     folded = jnp.einsum("kv,vw->kw", upper_panel[0], upper_inverse[0], precision=highest)
     weights = jnp.einsum("kj,kw->wj", pick_top, folded, precision=highest)
-    total = lax.dynamic_slice_in_dim(weights, begin, share, 0)
-    for v in range(1, panels):
-        outgoing = lax.dynamic_slice_in_dim(weights, (panel_index ^ v) * share, share, 0)
+
+    def to_partner(block, v):
         order = [static_position(static_offset(h, top_groups) ^ v, top_groups) for h in range(count)]
-        outgoing = outgoing.reshape(share, count, top_rows)[:, jnp.array(order), :]
-        outgoing = outgoing.reshape(share, count * top_rows)
-        total = total + lax.ppermute(outgoing, "panel", [(i, i ^ v) for i in range(panels)])
-    own_inverse = lax.dynamic_slice_in_dim(upper_inverse[0], begin, share, 1)
+        shape = block.shape
+        block = block.reshape(shape[:-1] + (count, top_rows))[..., jnp.array(order), :]
+        return block.reshape(shape)
+
+    core = panel_index & 1
+    halves = panels // 2
+    split = weights.reshape(halves, 2, share, count * top_rows)
+    mine = lax.dynamic_index_in_dim(split, core, 1, keepdims=False)
+    other = lax.dynamic_index_in_dim(split, 1 - core, 1, keepdims=False)
+    total = mine + lax.ppermute(to_partner(other, 1), "panel", [(i, i ^ 1) for i in range(panels)])
+    for b in panel_bits[1:]:
+        v = 1 << b
+        total = total + lax.ppermute(to_partner(total, v), "panel", [(i, i ^ v) for i in range(panels)])
+    total = total.reshape(halves * share, count * top_rows)
+    inverse_split = upper_inverse[0].reshape(width_upper, halves, 2, share)
+    own_inverse = lax.dynamic_index_in_dim(inverse_split, core, 2, keepdims=False)
+    own_inverse = own_inverse.reshape(width_upper, halves * share)
     own_base = jnp.einsum("kw,kr->wr", own_inverse, upper_rhs[0], precision=highest)
 
     top_held = xor_gather(top_solution, both, count, top_groups).reshape(count * top_rows, rhs)
-    own_rows = own_base - jnp.einsum("wj,jr->wr", total, top_held, precision=highest)
+    own_half = own_base - jnp.einsum("wj,jr->wr", total, top_held, precision=highest)
+    own_rows = lax.dynamic_slice_in_dim(own_half, (panel_index >> 1) * share, share, 0)
 
-    held = xor_gather(own_rows, both, count, spread_groups)
+    half_groups = leaf_groups + [[0]]
+    held = xor_gather(own_half, both, count, half_groups)
+    held = held.reshape(-1, share, own_half.shape[1])
     position = owner_map[parent_list]
-    sources = position[:, None] * panels + jnp.arange(panels, dtype=jnp.int32)[None, :]
-    places = xor_position(sources ^ me, spread_groups)
-    slabs = held[places].reshape(position.shape[0], width_upper, own_rows.shape[1])
+    quarters = jnp.arange(panels, dtype=jnp.int32)[None, :]
+    sources = position[:, None] * panels + ((panel_index & ~1) | (quarters & 1))
+    places = xor_position(sources ^ me, half_groups) * halves + (quarters >> 1)
+    slabs = held[places].reshape(position.shape[0], width_upper, own_half.shape[1])
 
     columns = lax.broadcasted_iota(jnp.int32, lower_index.shape + (width_upper,), 2)
     pick = (lower_index[:, :, None] == columns).astype(jnp.float32)

time: 74.5 us -> 81.1 us (1.089)
  local copies, waits for them, and re-layouts: 13.8 us -> 27.7 us
  starting transfers between devices: 21.7 us -> 18.1 us
  waiting for transfers between devices: 20.4 us -> 17.9 us
  matrix products: 16.5 us -> 14.3 us
    dynamic_slice x1 -> x3, local copies, waits for them, and re-layouts: 0.11 us -> 4.67 us  [the longest x1 2.55 us: local(): lax.dynamic_index_in_dim(inverse_split, core, 2, keepdims=False)]
    ppermute x13 -> x12, waiting for transfers between devices: 20.3 us -> 15.8 us  [xor_gather(): parts.append(lax.ppermute(held, axes, [(i, i ^ v) for i in range(count)]))]
    unnamed x35 -> x30, local copies, waits for them, and re-layouts: 5.09 us -> 9.27 us
    ppermute x13 -> x12, starting transfers between devices: 19.6 us -> 16.4 us  [xor_gather(): parts.append(lax.ppermute(held, axes, [(i, i ^ v) for i in range(count)]))]
    concatenate x4, local copies, waits for them, and re-layouts: 2.17 us -> 4.34 us  [xor_gather(): held = jnp.concatenate(parts, 0)]
    dot_general x1, matrix products: 3.52 us -> 1.41 us  [local(): jnp.einsum('skw,skr->swr', lower_panel, parent_rows, precision=highest)]
    ppermute x3 -> x2, waiting for transfers between devices: 0.01 us -> 2.04 us  [the longest x1 2.04 us: local(): lax.ppermute(to_partner(total, v), 'panel', [(i, i ^ v) for i in range(pa...]
    another operation x0 -> x1, local copies, waits for them, and re-layouts: none -> 1.88 us  [local(): inverse_split = upper_inverse[0].reshape(width_upper, halves, 2, share)]
  transfers between devices with their start and end apart: 16 -> 14, of which waited for: 8 -> 7; matrix products, arithmetic and copies ran while one was open for 15% -> 32% of each run, Pallas kernels for 0% -> 0%
where the time goes in v7:
time: 81.1 us; the launch traced here: 80.5 us
  local copies, waits for them, and re-layouts  27.7 us (34%)
  starting transfers between devices  18.1 us (22%)
  waiting for transfers between devices  17.9 us (22%)
  matrix products  14.3 us (18%)
  other arithmetic  1.52 us (2%)
  between operations  0.99 us (1%)
    ppermute x12, starting transfers between devices, xor_gather(): parts.append(lax.ppermute(held, axes, [(i, i ^ v) for i in range(count)]))  16.4 us
    ppermute x12, waiting for transfers between devices, xor_gather(): parts.append(lax.ppermute(held, axes, [(i, i ^ v) for i in range(count)]))  15.8 us
    unnamed x30, local copies, waits for them, and re-layouts  9.27 us
    concatenate x4, local copies, waits for them, and re-layouts, xor_gather(): held = jnp.concatenate(parts, 0)  4.34 us
    dot_general x1, matrix products, local(): parent_rows = jnp.einsum('skj,sjr->skr', pick, slabs, precision=highest)  4.07 us
    gather x1, local copies, waits for them, and re-layouts, local(): held[places].reshape(position.shape[0], width_upper, own_half.shape[1])  3.61 us
    dynamic_slice x1, local copies, waits for them, and re-layouts, local(): lax.dynamic_index_in_dim(inverse_split, core, 2, keepdims=False)  2.55 us
    dot_general x1, matrix products, local(): jnp.einsum('kv,vw->kw', upper_panel[0], upper_inverse[0], precision=highest)  2.45 us
  transfers between devices with their start and end apart: 14, of which 7 were waited for; matrix products, arithmetic and copies ran while one was open for 32% of the time, Pallas kernels for 0%

profile of v7, /device:TPU:0, one launch (start us, length us, event | category | flops | bytes accessed | tf_op | source)
XLA Modules:
  0.0 80.5 jit_solution(11364980257713633078)
XLA Ops:
  1.2 2.6 %collective-permute-start.3 = (f32[1,16,128]{2,1,0:T(8,128)}, f32[1,16,128]{2,1,0:T(8,128)S(1)}, u32[]{:S(2)}, u32[]{:S(2)}) collective-permute-start(f32[1,16,128]{2,1,0:T(8,128)} %bitcast.64), channel_id=1, source_target_pairs={{0,2},{1,3},{2,0},{3,1},{4,6},{5,7},{6,4},{7,5},{8,10},{9,11},{10,... | collective-permute-start | bytes 24584 | tf_op jit(solution)/shard_map/ppermute | solution.py:13
  4.4 2.4 %fusion.3 = f32[256,512]{1,0:T(8,128)S(1)} fusion(f32[1,512,512]{2,1,0:T(8,128)} %param.15, f32[1,256,512]{2,1,0:T(8,128)} %param.14), kind=kOutput, calls=%fused_computation.11 | convolution fusion | flops 805306368 | bytes 2097152 | tf_op jit(solution)/shard_map/kv,vw->kw/dot_general | solution.py:102
  10.9 1.9 %reshape_squeeze.3 = f32[512,2,2,128]{3,2,1,0:T(2,128)S(1)} reshape(f32[1,512,512]{2,1,0:T(8,128)} %param.15) | data formatting | bytes 2097152 | tf_op jit(solution)/shard_map/reshape;squeeze | solution.py:121
  12.8 2.6 %dynamic-slice_reduce_fusion = f32[512,2,128]{2,1,0:T(2,128)} fusion(f32[512,2,2,128]{3,2,1,0:T(2,128)S(1)} %reshape_squeeze.3, s32[]{:T(128)S(6)} %select_n.82), kind=kLoop, calls=%fused_computation.18 | loop fusion | bytes 1048580 | tf_op jit(solution)/shard_map/jit(dynamic_index_in_dim)/dynamic_slice | solution.py:122
  16.7 3.1 %collective-permute-start.5 = (f32[4,16,128]{2,1,0:T(8,128)S(1)}, f32[4,16,128]{2,1,0:T(8,128)S(1)}, u32[]{:S(2)}, u32[]{:S(2)}) collective-permute-start(f32[4,16,128]{2,1,0:T(8,128)S(1)} %pad_maximum_fusion.1), channel_id=1, source_target_pairs={{0,16},{1,17},{2,18},{3,19},{4,20},{5,21},{6,22},{7,23},{8,24},{9,... | collective-permute-start | bytes 98312 | tf_op jit(solution)/shard_map/ppermute | solution.py:13
  22.2 1.9 %collective-permute-start.6 = (f32[8,16,128]{2,1,0:T(8,128)S(1)}, f32[8,16,128]{2,1,0:T(8,128)S(1)}, u32[]{:S(2)}, u32[]{:S(2)}) collective-permute-start(f32[8,16,128]{2,1,0:T(8,128)S(1)} %get-tuple-element.20), channel_id=1, source_target_pairs={{0,8},{1,9},{2,10},{3,11},{4,12},{5,13},{6,14},{7,15},{8,0},{9,1},... | collective-permute-start | bytes 196616 | tf_op jit(solution)/shard_map/ppermute | solution.py:13
  25.9 1.6 %collective-permute-start.1 = (f32[2,128,512]{1,2,0:T(8,128)S(1)}, f32[2,128,512]{1,2,0:T(8,128)S(1)}, u32[]{:S(2)}, u32[]{:S(2)}) collective-permute-start(f32[2,128,512]{1,2,0:T(8,128)S(1)} %bitcast.61), channel_id=1, source_target_pairs={{0,2},{1,3},{2,0},{3,1},{4,6},{5,7},{6,4},{7,5},{8,10},{9,11},{10,... | collective-permute-start | bytes 1572872 | tf_op jit(solution)/shard_map/ppermute | solution.py:119
  27.5 2.1 %fusion.5 = f32[256,128]{1,0:T(8,128)S(1)} fusion(f32[64,8,2,128]{3,2,1,0:T(2,128)} %bitcast.57, f32[1,512,128]{2,1,0:T(8,128)} %param.13), kind=kOutput, calls=%fused_computation.13 | convolution fusion | flops 201326592 | bytes 917504 | tf_op jit(solution)/shard_map/kw,kr->wr/dot_general | solution.py:124
  29.6 1.6 %collective-permute-start.7 = (f32[8,16,128]{2,1,0:T(8,128)S(1)}, f32[8,16,128]{2,1,0:T(8,128)S(1)}, u32[]{:S(2)}, u32[]{:S(2)}) collective-permute-start(f32[8,16,128]{2,1,0:T(8,128)S(1)} %get-tuple-element.20), channel_id=1, source_target_pairs={{0,4},{1,5},{2,6},{3,7},{4,0},{5,1},{6,2},{7,3},{8,12},{9,13},{10,... | collective-permute-start | bytes 196616 | tf_op jit(solution)/shard_map/ppermute | solution.py:13
  32.5 2.1 %collective-permute-done.7 = f32[8,16,128]{2,1,0:T(8,128)S(1)} collective-permute-done((f32[8,16,128]{2,1,0:T(8,128)S(1)}, f32[8,16,128]{2,1,0:T(8,128)S(1)}, u32[]{:S(2)}, u32[]{:S(2)}) %collective-permute-start.7) | collective-permute-done | bytes 65568 | tf_op jit(solution)/shard_map/ppermute | solution.py:13
  36.9 2.0 %collective-permute-done.1 = f32[2,128,512]{1,2,0:T(8,128)S(1)} collective-permute-done((f32[2,128,512]{1,2,0:T(8,128)S(1)}, f32[2,128,512]{1,2,0:T(8,128)S(1)}, u32[]{:S(2)}, u32[]{:S(2)}) %collective-permute-start.1) | collective-permute-done | bytes 524320 | tf_op jit(solution)/shard_map/ppermute | solution.py:119
  39.2 2.2 %constant_dynamic-update-slice_fusion.17 = (f32[8,256,128]{2,1,0:T(8,128)}, f32[16,256,128]{2,1,0:T(8,128)}, f32[256,128]{1,0:T(8,128)S(1)}) fusion(f32[256,128]{1,0:T(8,128)S(1)} %fusion.5, f32[256,512]{1,0:T(8,128)S(1)} %bitcast.58, f32[512,128]{1,0:T(8,128)} %bitcast.62), kind=kOutput, calls=%fused_computation.43 | convolution fusion | flops 201359360 | bytes 1310720 | tf_op jit(solution)/shard_map/wj,jr->wr/dot_general | solution.py:127
  41.5 2.4 %collective-permute-start.9 = (f32[1,256,128]{2,1,0:T(8,128)S(1)}, f32[1,256,128]{2,1,0:T(8,128)S(1)}, u32[]{:S(2)}, u32[]{:S(2)}) collective-permute-start(f32[1,256,128]{2,1,0:T(8,128)S(1)} %bitcast.59), channel_id=1, source_target_pairs={{0,16},{1,17},{2,18},{3,19},{4,20},{5,21},{6,22},{7,23},{8,24},{9,... | collective-permute-start | bytes 393224 | tf_op jit(solution)/shard_map/ppermute | solution.py:13
  43.9 5.0 %collective-permute-done.9 = f32[1,256,128]{2,1,0:T(8,128)S(1)} collective-permute-done((f32[1,256,128]{2,1,0:T(8,128)S(1)}, f32[1,256,128]{2,1,0:T(8,128)S(1)}, u32[]{:S(2)}, u32[]{:S(2)}) %collective-permute-start.9) | collective-permute-done | bytes 131104 | tf_op jit(solution)/shard_map/ppermute | solution.py:13
  48.9 1.4 %collective-permute-start.11 = (f32[2,256,128]{2,1,0:T(8,128)S(1)}, f32[2,256,128]{2,1,0:T(8,128)S(1)}, u32[]{:S(2)}, u32[]{:S(2)}) collective-permute-start(f32[2,256,128]{2,1,0:T(8,128)S(1)} %pad_maximum_fusion), channel_id=1, source_target_pairs={{0,4},{1,5},{2,6},{3,7},{4,0},{5,1},{6,2},{7,3},{8,12},{9,13},{10,... | collective-permute-start | bytes 786440 | tf_op jit(solution)/shard_map/ppermute | solution.py:13
  50.4 2.1 %collective-permute-start.12 = (f32[2,256,128]{2,1,0:T(8,128)S(1)}, f32[2,256,128]{2,1,0:T(8,128)S(1)}, u32[]{:S(2)}, u32[]{:S(2)}) collective-permute-start(f32[2,256,128]{2,1,0:T(8,128)S(1)} %pad_maximum_fusion), channel_id=1, source_target_pairs={{0,12},{1,13},{2,14},{3,15},{4,8},{5,9},{6,10},{7,11},{8,4},{9,5},... | collective-permute-start | bytes 786440 | tf_op jit(solution)/shard_map/ppermute | solution.py:13
  53.1 5.0 %collective-permute-done.10 = f32[2,256,128]{2,1,0:T(8,128)S(1)} collective-permute-done((f32[2,256,128]{2,1,0:T(8,128)S(1)}, f32[2,256,128]{2,1,0:T(8,128)S(1)}, u32[]{:S(2)}, u32[]{:S(2)}) %collective-permute-start.10) | collective-permute-done | bytes 262176 | tf_op jit(solution)/shard_map/ppermute | solution.py:13
  59.0 2.6 %collective-permute-done.11 = f32[2,256,128]{2,1,0:T(8,128)S(1)} collective-permute-done((f32[2,256,128]{2,1,0:T(8,128)S(1)}, f32[2,256,128]{2,1,0:T(8,128)S(1)}, u32[]{:S(2)}, u32[]{:S(2)}) %collective-permute-start.11) | collective-permute-done | bytes 262176 | tf_op jit(solution)/shard_map/ppermute | solution.py:13
  64.1 1.6 %copy.29 = f32[8,256,128]{1,2,0:T(8,128)S(1)} copy(f32[8,256,128]{2,1,0:T(8,128)} %param.22) | data formatting | bytes 2097152 | tf_op args[9]
  66.3 2.3 %constant_dynamic-update-slice_fusion.18 = f32[16,256,128]{2,1,0:T(8,128)} fusion(f32[16,256,128]{2,1,0:T(8,128)} %get-tuple-element.11, f32[8,256,128]{2,1,0:T(8,128)} %collective-permute-done.13), kind=kLoop, calls=%fused_computation.44 | loop fusion | bytes 2097152 | tf_op jit(solution)/shard_map/concatenate | solution.py:14
  68.6 3.6 %gather_fusion.3 = f32[32,128,128]{2,1,0:T(8,128)} fusion(f32[32,128,128]{2,1,0:T(8,128)} %bitcast.17, s32[1024]{0:T(1024)S(1)} %pad_clamp_fusion), kind=kCustom, calls=%fused_computation.3 | custom fusion | bytes 4194432 | tf_op jit(solution)/shard_map/gather | solution.py:137
  72.2 4.1 %fusion = f32[8,256,128]{1,2,0:T(8,128)S(1)} fusion(f32[8,512,128]{2,1,0:T(8,128)} %bitcast.55, s32[8,256]{1,0:T(8,128)S(1)} %copy-done.4), kind=kOutput, calls=%fused_computation.5 | convolution fusion | flops 1611661312 | bytes 3153920 | tf_op jit(solution)/shard_map/skj,sjr->skr/dot_general | solution.py:141
  76.3 1.4 %fusion.2 = f32[8,256,128]{1,2,0:T(8,128)S(1)} fusion(f32[8,256,128]{1,2,0:T(8,128)S(1)} %copy.29, f32[8,256,128]{1,2,0:T(8,128)S(1)} %fusion, f32[8,256,256]{2,1,0:T(8,128)S(1)} %copy-done), kind=kOutput, calls=%fused_computation.9 | convolution fusion | flops 805568512 | bytes 5242880 | tf_op jit(solution)/shard_map/skw,skr->swr/dot_general | solution.py:143
  77.8 1.4 %convolution_bitcast_fusion = f32[8,256,128]{1,2,0:T(8,128)S(1)} fusion(f32[8,256,128]{1,2,0:T(8,128)S(1)} %fusion.2, f32[8,256,256]{2,1,0:T(8,128)S(1)} %copy-done.2), kind=kOutput, calls=%fused_computation.7 | convolution fusion | flops 805306368 | bytes 4194304 | tf_op jit(solution)/shard_map/skw,skr->swr/dot_general | solution.py:144
  (81 shorter events, 20.8 us)
Async XLA Ops:
  0.6 75.6 %copy-start = (f32[8,256,256]{2,1,0:T(8,128)S(1)}, f32[8,256,256]{2,1,0:T(8,128)}, u32[]{:S(2)}) copy-start(f32[8,256,256]{2,1,0:T(8,128)} %param.21) | copy-start | bytes 6291460
  0.6 6.2 %copy-start.5 = (s32[1,256]{1,0:T(1,128)S(1)}, s32[1,256]{1,0:T(1,128)}, u32[]{:S(2)}) copy-start(s32[1,256]{1,0:T(1,128)} %param.16) | copy-start | bytes 3076
  0.7 16.0 %collective-permute-start.2 = (f32[1,16,128]{2,1,0:T(8,128)}, f32[1,16,128]{2,1,0:T(8,128)S(1)}, u32[]{:S(2)}, u32[]{:S(2)}) collective-permute-start(f32[1,16,128]{2,1,0:T(8,128)} %bitcast.63), channel_id=1, source_target_pairs={{0,1},{1,0},{2,3},{3,2},{4,5},{5,4},{6,7},{7,6},{8,9},{9,8},{10,11... | collective-permute-start | bytes 24584 | tf_op jit(solution)/shard_map/ppermute | solution.py:13
  1.2 15.4 %collective-permute-start.3 = (f32[1,16,128]{2,1,0:T(8,128)}, f32[1,16,128]{2,1,0:T(8,128)S(1)}, u32[]{:S(2)}, u32[]{:S(2)}) collective-permute-start(f32[1,16,128]{2,1,0:T(8,128)} %bitcast.64), channel_id=1, source_target_pairs={{0,2},{1,3},{2,0},{3,1},{4,6},{5,7},{6,4},{7,5},{8,10},{9,11},{10,... | collective-permute-start | bytes 24584 | tf_op jit(solution)/shard_map/ppermute | solution.py:13
  3.8 12.9 %collective-permute-start.4 = (f32[1,16,128]{2,1,0:T(8,128)}, f32[1,16,128]{2,1,0:T(8,128)S(1)}, u32[]{:S(2)}, u32[]{:S(2)}) collective-permute-start(f32[1,16,128]{2,1,0:T(8,128)} %bitcast.65), channel_id=1, source_target_pairs={{0,3},{1,2},{2,1},{3,0},{4,7},{5,6},{6,5},{7,4},{8,11},{9,10},{10,... | collective-permute-start | bytes 24584 | tf_op jit(solution)/shard_map/ppermute | solution.py:13
  6.9 1.8 %copy-start.8 = (s32[8]{0:T(128)S(1)}, s32[8]{0:T(128)}, u32[]{:S(2)}) copy-start(s32[8]{0:T(128)} %param.19) | copy-start | bytes 100
  6.9 1.8 %copy-start.7 = (s32[32]{0:T(128)S(1)}, s32[32]{0:T(128)}, u32[]{:S(2)}) copy-start(s32[32]{0:T(128)} %constant.138) | copy-start | bytes 388
  8.7 1.6 %copy-start.3 = (f32[16,128]{1,0:T(8,128)S(1)}, f32[16,128]{1,0:T(8,128)}, u32[]{:S(2)}) copy-start(f32[16,128]{1,0:T(8,128)} %param.17) | copy-start | bytes 24580
  9.3 3.5 %copy-start.6 = (s32[32]{0:T(128)S(1)}, s32[32]{0:T(128)}, u32[]{:S(2)}) copy-start(s32[32]{0:T(128)} %constant.139) | copy-start | bytes 388
  10.2 14.0 %collective-permute-start = (f32[2,128,512]{1,2,0:T(8,128)}, f32[2,128,512]{1,2,0:T(8,128)}, u32[]{:S(2)}, u32[]{:S(2)}) collective-permute-start(f32[2,128,512]{1,2,0:T(8,128)} %bitcast.8), channel_id=1, source_target_pairs={{0,1},{1,0},{2,3},{3,2},{4,5},{5,4},{6,7},{7,6},{8,9},{9,8},{10,11... | collective-permute-start | bytes 1572872 | tf_op jit(solution)/shard_map/ppermute | solution.py:116
  16.7 5.0 %collective-permute-start.5 = (f32[4,16,128]{2,1,0:T(8,128)S(1)}, f32[4,16,128]{2,1,0:T(8,128)S(1)}, u32[]{:S(2)}, u32[]{:S(2)}) collective-permute-start(f32[4,16,128]{2,1,0:T(8,128)S(1)} %pad_maximum_fusion.1), channel_id=1, source_target_pairs={{0,16},{1,17},{2,18},{3,19},{4,20},{5,21},{6,22},{7,23},{8,24},{9,... | collective-permute-start | bytes 98312 | tf_op jit(solution)/shard_map/ppermute | solution.py:13
  22.2 9.7 %collective-permute-start.6 = (f32[8,16,128]{2,1,0:T(8,128)S(1)}, f32[8,16,128]{2,1,0:T(8,128)S(1)}, u32[]{:S(2)}, u32[]{:S(2)}) collective-permute-start(f32[8,16,128]{2,1,0:T(8,128)S(1)} %get-tuple-element.20), channel_id=1, source_target_pairs={{0,8},{1,9},{2,10},{3,11},{4,12},{5,13},{6,14},{7,15},{8,0},{9,1},... | collective-permute-start | bytes 196616 | tf_op jit(solution)/shard_map/ppermute | solution.py:13
  25.9 13.1 %collective-permute-start.1 = (f32[2,128,512]{1,2,0:T(8,128)S(1)}, f32[2,128,512]{1,2,0:T(8,128)S(1)}, u32[]{:S(2)}, u32[]{:S(2)}) collective-permute-start(f32[2,128,512]{1,2,0:T(8,128)S(1)} %bitcast.61), channel_id=1, source_target_pairs={{0,2},{1,3},{2,0},{3,1},{4,6},{5,7},{6,4},{7,5},{8,10},{9,11},{10,... | collective-permute-start | bytes 1572872 | tf_op jit(solution)/shard_map/ppermute | solution.py:119
  29.6 5.0 %collective-permute-start.7 = (f32[8,16,128]{2,1,0:T(8,128)S(1)}, f32[8,16,128]{2,1,0:T(8,128)S(1)}, u32[]{:S(2)}, u32[]{:S(2)}) collective-permute-start(f32[8,16,128]{2,1,0:T(8,128)S(1)} %get-tuple-element.20), channel_id=1, source_target_pairs={{0,4},{1,5},{2,6},{3,7},{4,0},{5,1},{6,2},{7,3},{8,12},{9,13},{10,... | collective-permute-start | bytes 196616 | tf_op jit(solution)/shard_map/ppermute | solution.py:13
  31.1 5.2 %collective-permute-start.8 = (f32[8,16,128]{2,1,0:T(8,128)S(1)}, f32[8,16,128]{2,1,0:T(8,128)S(1)}, u32[]{:S(2)}, u32[]{:S(2)}) collective-permute-start(f32[8,16,128]{2,1,0:T(8,128)S(1)} %get-tuple-element.20), channel_id=1, source_target_pairs={{0,12},{1,13},{2,14},{3,15},{4,8},{5,9},{6,10},{7,11},{8,4},{9,5},... | collective-permute-start | bytes 196616 | tf_op jit(solution)/shard_map/ppermute | solution.py:13
  39.2 24.0 %copy-start.1 = (s32[8]{0:T(128)S(1)}, s32[8]{0:T(128)}, u32[]{:S(2)}) copy-start(s32[8]{0:T(128)} %param.18) | copy-start | bytes 100
  41.5 7.4 %collective-permute-start.9 = (f32[1,256,128]{2,1,0:T(8,128)S(1)}, f32[1,256,128]{2,1,0:T(8,128)S(1)}, u32[]{:S(2)}, u32[]{:S(2)}) collective-permute-start(f32[1,256,128]{2,1,0:T(8,128)S(1)} %bitcast.59), channel_id=1, source_target_pairs={{0,16},{1,17},{2,18},{3,19},{4,20},{5,21},{6,22},{7,23},{8,24},{9,... | collective-permute-start | bytes 393224 | tf_op jit(solution)/shard_map/ppermute | solution.py:13
  48.9 9.3 %collective-permute-start.10 = (f32[2,256,128]{2,1,0:T(8,128)S(1)}, f32[2,256,128]{2,1,0:T(8,128)S(1)}, u32[]{:S(2)}, u32[]{:S(2)}) collective-permute-start(f32[2,256,128]{2,1,0:T(8,128)S(1)} %pad_maximum_fusion), channel_id=1, source_target_pairs={{0,8},{1,9},{2,10},{3,11},{4,12},{5,13},{6,14},{7,15},{8,0},{9,1},... | collective-permute-start | bytes 786440 | tf_op jit(solution)/shard_map/ppermute | solution.py:13
  48.9 12.6 %collective-permute-start.11 = (f32[2,256,128]{2,1,0:T(8,128)S(1)}, f32[2,256,128]{2,1,0:T(8,128)S(1)}, u32[]{:S(2)}, u32[]{:S(2)}) collective-permute-start(f32[2,256,128]{2,1,0:T(8,128)S(1)} %pad_maximum_fusion), channel_id=1, source_target_pairs={{0,4},{1,5},{2,6},{3,7},{4,0},{5,1},{6,2},{7,3},{8,12},{9,13},{10,... | collective-permute-start | bytes 786440 | tf_op jit(solution)/shard_map/ppermute | solution.py:13
  50.4 12.0 %collective-permute-start.12 = (f32[2,256,128]{2,1,0:T(8,128)S(1)}, f32[2,256,128]{2,1,0:T(8,128)S(1)}, u32[]{:S(2)}, u32[]{:S(2)}) collective-permute-start(f32[2,256,128]{2,1,0:T(8,128)S(1)} %pad_maximum_fusion), channel_id=1, source_target_pairs={{0,12},{1,13},{2,14},{3,15},{4,8},{5,9},{6,10},{7,11},{8,4},{9,5},... | collective-permute-start | bytes 786440 | tf_op jit(solution)/shard_map/ppermute | solution.py:13
  63.2 3.1 %collective-permute-start.13 = (f32[8,256,128]{2,1,0:T(8,128)}, f32[8,256,128]{2,1,0:T(8,128)}, u32[]{:S(2)}, u32[]{:S(2)}) collective-permute-start(f32[8,256,128]{2,1,0:T(8,128)} %get-tuple-element.10), channel_id=1, source_target_pairs={{0,1},{1,0},{2,3},{3,2},{4,5},{5,4},{6,7},{7,6},{8,9},{9,8},{10,11... | collective-permute-start | bytes 3145736 | tf_op jit(solution)/shard_map/ppermute | solution.py:13
  68.6 3.6 %copy-start.4 = (s32[8,256]{1,0:T(8,128)S(1)}, s32[8,256]{1,0:T(8,128)}, u32[]{:S(2)}) copy-start(s32[8,256]{1,0:T(8,128)} %param.20) | copy-start | bytes 24580
  76.2 1.6 %copy-start.2 = (f32[8,256,256]{2,1,0:T(8,128)S(1)}, f32[8,256,256]{2,1,0:T(8,128)}, u32[]{:S(2)}) copy-start(f32[8,256,256]{2,1,0:T(8,128)} %param.23) | copy-start | bytes 6291460

commit v8 on v6

--- a/solution.py
+++ b/solution.py
@@ -120,14 +120,15 @@
     places = xor_position(sources ^ me, spread_groups)
     slabs = held[places].reshape(position.shape[0], width_upper, own_rows.shape[1])
 
+    three = lax.Precision.HIGH
     columns = lax.broadcasted_iota(jnp.int32, lower_index.shape + (width_upper,), 2)
     pick = (lower_index[:, :, None] == columns).astype(jnp.float32)
-    parent_rows = jnp.einsum("skj,sjr->skr", pick, slabs, precision=highest)
+    parent_rows = jnp.einsum("skj,sjr->skr", pick, slabs, precision=three)
 
-    lower_update = jnp.einsum("skw,skr->swr", lower_panel, parent_rows, precision=highest)
-    lower_solution = jnp.einsum(
-        "skw,skr->swr", lower_inverse, lower_rhs - lower_update, precision=highest
-    )
+    panel_t = jnp.swapaxes(lower_panel, 1, 2)
+    inverse_t = jnp.swapaxes(lower_inverse, 1, 2)
+    lower_update = jnp.einsum("swk,skr->swr", panel_t, parent_rows, precision=three)
+    lower_solution = jnp.einsum("swk,skr->swr", inverse_t, lower_rhs - lower_update, precision=three)
     return (own_rows[None], lower_solution)
 
 

time: 74.5 us -> 71.2 us (0.956)
  matrix products: 16.5 us -> 13.3 us
    dot_general x3, matrix products: 9.31 us -> 6.1 us  [the longest x1 3.08 us: local(): parent_rows = jnp.einsum('skj,sjr->skr', pick, slabs, precision=three)]
where the time goes in v8:
time: 71.2 us; the launch traced here: 71 us
  starting transfers between devices  21.7 us (30%)
  waiting for transfers between devices  20.4 us (29%)
  local copies, waits for them, and re-layouts  13.8 us (19%)
  matrix products  13.3 us (19%)
  other arithmetic  0.98 us (1%)
  between operations  0.94 us (1%)
    ppermute x13, waiting for transfers between devices, xor_gather(): parts.append(lax.ppermute(held, axes, [(i, i ^ v) for i in range(count)]))  20.3 us
    ppermute x13, starting transfers between devices, xor_gather(): parts.append(lax.ppermute(held, axes, [(i, i ^ v) for i in range(count)]))  19.6 us
    unnamed x35, local copies, waits for them, and re-layouts  5.09 us
    gather x1, local copies, waits for them, and re-layouts, local(): held[places].reshape(position.shape[0], width_upper, own_rows.shape[1])  3.6 us
    dot_general x1, matrix products, local(): parent_rows = jnp.einsum('skj,sjr->skr', pick, slabs, precision=three)  3.08 us
    dot_general x1, matrix products, local(): jnp.einsum('kv,vw->kw', upper_panel[0], upper_inverse[0], precision=highest)  2.44 us
    dot_general x1, matrix products, local(): jnp.einsum('wj,jr->wr', total, top_held, precision=highest)  2.4 us
    concatenate x4, local copies, waits for them, and re-layouts, xor_gather(): held = jnp.concatenate(parts, 0)  2.17 us
  transfers between devices with their start and end apart: 16, of which 8 were waited for; matrix products, arithmetic and copies ran while one was open for 15% of the time, Pallas kernels for 0%

profile of v8, /device:TPU:0, one launch (start us, length us, event | category | flops | bytes accessed | tf_op | source)
XLA Modules:
  0.0 71.0 jit_solution(17447035505198600630)
XLA Ops:
  1.2 2.6 %collective-permute-start.4 = (f32[1,16,128]{2,1,0:T(8,128)}, f32[1,16,128]{2,1,0:T(8,128)S(1)}, u32[]{:S(2)}, u32[]{:S(2)}) collective-permute-start(f32[1,16,128]{2,1,0:T(8,128)} %bitcast.56), channel_id=1, source_target_pairs={{0,2},{1,3},{2,0},{3,1},{4,6},{5,7},{6,4},{7,5},{8,10},{9,11},{10,... | collective-permute-start | bytes 24584 | tf_op jit(solution)/shard_map/ppermute | solution.py:13
  5.1 2.4 %fusion.4 = f32[256,512]{1,0:T(8,128)S(1)} fusion(f32[1,512,512]{2,1,0:T(8,128)} %param.16, f32[1,256,512]{2,1,0:T(8,128)} %param.15), kind=kOutput, calls=%fused_computation.13 | convolution fusion | flops 805306368 | bytes 2097152 | tf_op jit(solution)/shard_map/kv,vw->kw/dot_general | solution.py:102
  9.9 1.7 %collective-permute-start.2 = (f32[128,512]{0,1:T(8,128)S(1)}, f32[128,512]{0,1:T(8,128)}, u32[]{:S(2)}, u32[]{:S(2)}) collective-permute-start(f32[128,512]{0,1:T(8,128)S(1)} %bitcast.50), channel_id=1, source_target_pairs={{0,3},{1,2},{2,1},{3,0},{4,7},{5,6},{6,5},{7,4},{8,11},{9,10},{10,... | collective-permute-start | bytes 786440 | tf_op jit(solution)/shard_map/ppermute | solution.py:110
  13.2 3.0 %collective-permute-start.6 = (f32[4,16,128]{2,1,0:T(8,128)S(1)}, f32[4,16,128]{2,1,0:T(8,128)S(1)}, u32[]{:S(2)}, u32[]{:S(2)}) collective-permute-start(f32[4,16,128]{2,1,0:T(8,128)S(1)} %pad_maximum_fusion.1), channel_id=1, source_target_pairs={{0,16},{1,17},{2,18},{3,19},{4,20},{5,21},{6,22},{7,23},{8,24},{9,... | collective-permute-start | bytes 98312 | tf_op jit(solution)/shard_map/ppermute | solution.py:13
  16.2 2.0 %collective-permute-done.6 = f32[4,16,128]{2,1,0:T(8,128)S(1)} collective-permute-done((f32[4,16,128]{2,1,0:T(8,128)S(1)}, f32[4,16,128]{2,1,0:T(8,128)S(1)}, u32[]{:S(2)}, u32[]{:S(2)}) %collective-permute-start.6) | collective-permute-done | bytes 32800 | tf_op jit(solution)/shard_map/ppermute | solution.py:13
  18.2 1.8 %collective-permute-start.7 = (f32[8,16,128]{2,1,0:T(8,128)S(1)}, f32[8,16,128]{2,1,0:T(8,128)S(1)}, u32[]{:S(2)}, u32[]{:S(2)}) collective-permute-start(f32[8,16,128]{2,1,0:T(8,128)S(1)} %get-tuple-element.26), channel_id=1, source_target_pairs={{0,8},{1,9},{2,10},{3,11},{4,12},{5,13},{6,14},{7,15},{8,0},{9,1},... | collective-permute-start | bytes 196616 | tf_op jit(solution)/shard_map/ppermute | solution.py:13
  20.0 1.6 %fusion.9 = f32[128,128]{1,0:T(8,128)S(1)} fusion(f32[1,512,128]{2,1,0:T(8,128)} %param.14, f32[1,512,512]{2,1,0:T(8,128)} %param.16, s32[]{:T(128)S(6)} %select_n.86), kind=kOutput, calls=%fused_computation.18 | convolution fusion | flops 100663296 | bytes 589828 | tf_op jit(solution)/shard_map/kw,kr->wr/dot_general | solution.py:112
  21.6 1.6 %collective-permute-start.8 = (f32[8,16,128]{2,1,0:T(8,128)S(1)}, f32[8,16,128]{2,1,0:T(8,128)S(1)}, u32[]{:S(2)}, u32[]{:S(2)}) collective-permute-start(f32[8,16,128]{2,1,0:T(8,128)S(1)} %get-tuple-element.26), channel_id=1, source_target_pairs={{0,4},{1,5},{2,6},{3,7},{4,0},{5,1},{6,2},{7,3},{8,12},{9,13},{10,... | collective-permute-start | bytes 196616 | tf_op jit(solution)/shard_map/ppermute | solution.py:13
  23.2 2.0 %collective-permute-start.9 = (f32[8,16,128]{2,1,0:T(8,128)S(1)}, f32[8,16,128]{2,1,0:T(8,128)S(1)}, u32[]{:S(2)}, u32[]{:S(2)}) collective-permute-start(f32[8,16,128]{2,1,0:T(8,128)S(1)} %get-tuple-element.26), channel_id=1, source_target_pairs={{0,12},{1,13},{2,14},{3,15},{4,8},{5,9},{6,10},{7,11},{8,4},{9,5},... | collective-permute-start | bytes 196616 | tf_op jit(solution)/shard_map/ppermute | solution.py:13
  25.2 1.5 %collective-permute-done.8 = f32[8,16,128]{2,1,0:T(8,128)S(1)} collective-permute-done((f32[8,16,128]{2,1,0:T(8,128)S(1)}, f32[8,16,128]{2,1,0:T(8,128)S(1)}, u32[]{:S(2)}, u32[]{:S(2)}) %collective-permute-start.8) | collective-permute-done | bytes 65568 | tf_op jit(solution)/shard_map/ppermute | solution.py:13
  26.6 1.7 %collective-permute-done.9 = f32[8,16,128]{2,1,0:T(8,128)S(1)} collective-permute-done((f32[8,16,128]{2,1,0:T(8,128)S(1)}, f32[8,16,128]{2,1,0:T(8,128)S(1)}, u32[]{:S(2)}, u32[]{:S(2)}) %collective-permute-start.9) | collective-permute-done | bytes 65568 | tf_op jit(solution)/shard_map/ppermute | solution.py:13
  28.4 2.4 %constant_dynamic-update-slice_fusion.23 = (f32[16,128,128]{2,1,0:T(8,128)}, f32[32,128,128]{2,1,0:T(8,128)}, f32[8,128,128]{2,1,0:T(8,128)S(1)}, f32[1,128,128]{2,1,0:T(8,128)S(1)}) fusion(f32[128,128]{1,0:T(8,128)S(1)} %fusion.9, f32[512,128]{1,0:T(8,128)S(1)} %bitcast.54, f32[128,512]{0,1:T(8,128)} %collective-permute-done.2, ...), kind=kOutput, calls=%fused_computation.52 | convolution fusion | flops 100876288 | bytes 1638404 | tf_op jit(solution)/shard_map/wj,jr->wr/dot_general | solution.py:115
  30.8 3.0 %collective-permute-start.10 = (f32[1,128,128]{2,1,0:T(8,128)S(1)}, f32[1,128,128]{2,1,0:T(8,128)S(1)}, u32[]{:S(2)}, u32[]{:S(2)}) collective-permute-start(f32[1,128,128]{2,1,0:T(8,128)S(1)} %get-tuple-element.36), channel_id=1, source_target_pairs={{0,16},{1,17},{2,18},{3,19},{4,20},{5,21},{6,22},{7,23},{8,24},{9,... | collective-permute-start | bytes 196616 | tf_op jit(solution)/shard_map/ppermute | solution.py:13
  33.8 2.9 %collective-permute-done.10 = f32[1,128,128]{2,1,0:T(8,128)S(1)} collective-permute-done((f32[1,128,128]{2,1,0:T(8,128)S(1)}, f32[1,128,128]{2,1,0:T(8,128)S(1)}, u32[]{:S(2)}, u32[]{:S(2)}) %collective-permute-start.10) | collective-permute-done | bytes 65568 | tf_op jit(solution)/shard_map/ppermute | solution.py:13
  37.3 1.4 %collective-permute-start.12 = (f32[2,128,128]{2,1,0:T(8,128)S(1)}, f32[2,128,128]{2,1,0:T(8,128)S(1)}, u32[]{:S(2)}, u32[]{:S(2)}) collective-permute-start(f32[2,128,128]{2,1,0:T(8,128)S(1)} %pad_maximum_fusion), channel_id=1, source_target_pairs={{0,4},{1,5},{2,6},{3,7},{4,0},{5,1},{6,2},{7,3},{8,12},{9,13},{10,... | collective-permute-start | bytes 393224 | tf_op jit(solution)/shard_map/ppermute | solution.py:13
  38.7 1.6 %collective-permute-start.13 = (f32[2,128,128]{2,1,0:T(8,128)S(1)}, f32[2,128,128]{2,1,0:T(8,128)S(1)}, u32[]{:S(2)}, u32[]{:S(2)}) collective-permute-start(f32[2,128,128]{2,1,0:T(8,128)S(1)} %pad_maximum_fusion), channel_id=1, source_target_pairs={{0,12},{1,13},{2,14},{3,15},{4,8},{5,9},{6,10},{7,11},{8,4},{9,5},... | collective-permute-start | bytes 393224 | tf_op jit(solution)/shard_map/ppermute | solution.py:13
  43.3 1.3 %collective-permute-done.13 = f32[2,128,128]{2,1,0:T(8,128)S(1)} collective-permute-done((f32[2,128,128]{2,1,0:T(8,128)S(1)}, f32[2,128,128]{2,1,0:T(8,128)S(1)}, u32[]{:S(2)}, u32[]{:S(2)}) %collective-permute-start.13) | collective-permute-done | bytes 131104 | tf_op jit(solution)/shard_map/ppermute | solution.py:13
  45.3 1.5 %collective-permute-start.14 = (f32[8,128,128]{2,1,0:T(8,128)S(1)}, f32[8,128,128]{2,1,0:T(8,128)S(1)}, u32[]{:S(2)}, u32[]{:S(2)}) collective-permute-start(f32[8,128,128]{2,1,0:T(8,128)S(1)} %get-tuple-element.13), channel_id=1, source_target_pairs={{0,2},{1,3},{2,0},{3,1},{4,6},{5,7},{6,4},{7,5},{8,10},{9,11},{10,... | collective-permute-start | bytes 1572872 | tf_op jit(solution)/shard_map/ppermute | solution.py:13
  46.8 8.1 %collective-permute-done.14 = f32[8,128,128]{2,1,0:T(8,128)S(1)} collective-permute-done((f32[8,128,128]{2,1,0:T(8,128)S(1)}, f32[8,128,128]{2,1,0:T(8,128)S(1)}, u32[]{:S(2)}, u32[]{:S(2)}) %collective-permute-start.14) | collective-permute-done | bytes 524320 | tf_op jit(solution)/shard_map/ppermute | solution.py:13
  56.8 2.0 %collective-permute-done.15 = f32[16,128,128]{2,1,0:T(8,128)S(1)} collective-permute-done((f32[16,128,128]{2,1,0:T(8,128)}, f32[16,128,128]{2,1,0:T(8,128)S(1)}, u32[]{:S(2)}, u32[]{:S(2)}) %collective-permute-start.15) | collective-permute-done | bytes 1048608 | tf_op jit(solution)/shard_map/ppermute | solution.py:13
  59.9 3.6 %gather_fusion.4 = f32[32,128,128]{2,1,0:T(8,128)} fusion(f32[32,128,128]{2,1,0:T(8,128)} %constant_dynamic-update-slice_fusion.24, s32[1024]{0:T(1024)S(1)} %pad_clamp_fusion), kind=kCustom, calls=%fused_computation.4 | custom fusion | bytes 4194432 | tf_op jit(solution)/shard_map/gather | solution.py:121
  63.5 3.1 %fusion = f32[8,256,128]{2,1,0:T(8,128)S(1)} fusion(f32[8,512,128]{2,1,0:T(8,128)} %bitcast.53, s32[8,256]{1,0:T(8,128)S(1)} %copy-done.7), kind=kOutput, calls=%fused_computation.6 | convolution fusion | flops 806354944 | bytes 3153920 | tf_op jit(solution)/shard_map/skj,sjr->skr/dot_general | solution.py:126
  66.7 1.9 %fusion.2 = f32[8,256,128]{2,1,0:T(8,128)S(1)} fusion(f32[8,256,128]{2,1,0:T(8,128)S(1)} %copy-done.4, f32[8,256,128]{2,1,0:T(8,128)S(1)} %fusion, f32[8,256,256]{2,1,0:T(8,128)S(1)} %copy-done), kind=kOutput, calls=%fused_computation.10 | convolution fusion | flops 402915328 | bytes 5242880 | tf_op jit(solution)/shard_map/swk,skr->swr/dot_general | solution.py:130
  69.7 1.3 %copy.19 = f32[8,256,128]{2,1,0:T(8,128)} copy(f32[8,256,128]{1,2,0:T(8,128)S(1)} %convolution_bitcast_fusion) | data formatting | bytes 2097152
  (81 shorter events, 14.0 us)
Async XLA Ops:
  0.6 66.0 %copy-start = (f32[8,256,256]{2,1,0:T(8,128)S(1)}, f32[8,256,256]{2,1,0:T(8,128)}, u32[]{:S(2)}) copy-start(f32[8,256,256]{2,1,0:T(8,128)} %param.22) | copy-start | bytes 6291460
  0.6 6.9 %copy-start.11 = (s32[32]{0:T(128)S(1)}, s32[32]{0:T(128)}, u32[]{:S(2)}) copy-start(s32[32]{0:T(128)} %constant.136) | copy-start | bytes 388
  0.7 6.9 %copy-start.8 = (s32[1,256]{1,0:T(1,128)S(1)}, s32[1,256]{1,0:T(1,128)}, u32[]{:S(2)}) copy-start(s32[1,256]{1,0:T(1,128)} %param.17) | copy-start | bytes 3076
  0.7 12.3 %collective-permute-start.3 = (f32[1,16,128]{2,1,0:T(8,128)}, f32[1,16,128]{2,1,0:T(8,128)S(1)}, u32[]{:S(2)}, u32[]{:S(2)}) collective-permute-start(f32[1,16,128]{2,1,0:T(8,128)} %bitcast.55), channel_id=1, source_target_pairs={{0,1},{1,0},{2,3},{3,2},{4,5},{5,4},{6,7},{7,6},{8,9},{9,8},{10,11... | collective-permute-start | bytes 24584 | tf_op jit(solution)/shard_map/ppermute | solution.py:13
  1.2 12.0 %collective-permute-start.4 = (f32[1,16,128]{2,1,0:T(8,128)}, f32[1,16,128]{2,1,0:T(8,128)S(1)}, u32[]{:S(2)}, u32[]{:S(2)}) collective-permute-start(f32[1,16,128]{2,1,0:T(8,128)} %bitcast.56), channel_id=1, source_target_pairs={{0,2},{1,3},{2,0},{3,1},{4,6},{5,7},{6,4},{7,5},{8,10},{9,11},{10,... | collective-permute-start | bytes 24584 | tf_op jit(solution)/shard_map/ppermute | solution.py:13
  3.8 9.4 %collective-permute-start.5 = (f32[1,16,128]{2,1,0:T(8,128)}, f32[1,16,128]{2,1,0:T(8,128)S(1)}, u32[]{:S(2)}, u32[]{:S(2)}) collective-permute-start(f32[1,16,128]{2,1,0:T(8,128)} %bitcast.57), channel_id=1, source_target_pairs={{0,3},{1,2},{2,1},{3,0},{4,7},{5,6},{6,5},{7,4},{8,11},{9,10},{10,... | collective-permute-start | bytes 24584 | tf_op jit(solution)/shard_map/ppermute | solution.py:13
  9.3 2.3 %copy-start.10 = (s32[32]{0:T(128)S(1)}, s32[32]{0:T(128)}, u32[]{:S(2)}) copy-start(s32[32]{0:T(128)} %constant.134) | copy-start | bytes 388
  9.9 18.5 %collective-permute-start.2 = (f32[128,512]{0,1:T(8,128)S(1)}, f32[128,512]{0,1:T(8,128)}, u32[]{:S(2)}, u32[]{:S(2)}) collective-permute-start(f32[128,512]{0,1:T(8,128)S(1)} %bitcast.50), channel_id=1, source_target_pairs={{0,3},{1,2},{2,1},{3,0},{4,7},{5,6},{6,5},{7,4},{8,11},{9,10},{10,... | collective-permute-start | bytes 786440 | tf_op jit(solution)/shard_map/ppermute | solution.py:110
  12.2 16.1 %collective-permute-start.1 = (f32[128,512]{0,1:T(8,128)S(1)}, f32[128,512]{0,1:T(8,128)}, u32[]{:S(2)}, u32[]{:S(2)}) collective-permute-start(f32[128,512]{0,1:T(8,128)S(1)} %bitcast.51), channel_id=1, source_target_pairs={{0,2},{1,3},{2,0},{3,1},{4,6},{5,7},{6,4},{7,5},{8,10},{9,11},{10,... | collective-permute-start | bytes 786440 | tf_op jit(solution)/shard_map/ppermute | solution.py:110
  13.0 15.3 %collective-permute-start = (f32[128,512]{0,1:T(8,128)S(1)}, f32[128,512]{0,1:T(8,128)S(1)}, u32[]{:S(2)}, u32[]{:S(2)}) collective-permute-start(f32[128,512]{0,1:T(8,128)S(1)} %bitcast.52), channel_id=1, source_target_pairs={{0,1},{1,0},{2,3},{3,2},{4,5},{5,4},{6,7},{7,6},{8,9},{9,8},{10,11... | collective-permute-start | bytes 786440 | tf_op jit(solution)/shard_map/ppermute | solution.py:110
  13.2 5.0 %collective-permute-start.6 = (f32[4,16,128]{2,1,0:T(8,128)S(1)}, f32[4,16,128]{2,1,0:T(8,128)S(1)}, u32[]{:S(2)}, u32[]{:S(2)}) collective-permute-start(f32[4,16,128]{2,1,0:T(8,128)S(1)} %pad_maximum_fusion.1), channel_id=1, source_target_pairs={{0,16},{1,17},{2,18},{3,19},{4,20},{5,21},{6,22},{7,23},{8,24},{9,... | collective-permute-start | bytes 98312 | tf_op jit(solution)/shard_map/ppermute | solution.py:13
  18.2 5.0 %collective-permute-start.7 = (f32[8,16,128]{2,1,0:T(8,128)S(1)}, f32[8,16,128]{2,1,0:T(8,128)S(1)}, u32[]{:S(2)}, u32[]{:S(2)}) collective-permute-start(f32[8,16,128]{2,1,0:T(8,128)S(1)} %get-tuple-element.26), channel_id=1, source_target_pairs={{0,8},{1,9},{2,10},{3,11},{4,12},{5,13},{6,14},{7,15},{8,0},{9,1},... | collective-permute-start | bytes 196616 | tf_op jit(solution)/shard_map/ppermute | solution.py:13
  21.6 5.0 %collective-permute-start.8 = (f32[8,16,128]{2,1,0:T(8,128)S(1)}, f32[8,16,128]{2,1,0:T(8,128)S(1)}, u32[]{:S(2)}, u32[]{:S(2)}) collective-permute-start(f32[8,16,128]{2,1,0:T(8,128)S(1)} %get-tuple-element.26), channel_id=1, source_target_pairs={{0,4},{1,5},{2,6},{3,7},{4,0},{5,1},{6,2},{7,3},{8,12},{9,13},{10,... | collective-permute-start | bytes 196616 | tf_op jit(solution)/shard_map/ppermute | solution.py:13
  23.2 5.2 %collective-permute-start.9 = (f32[8,16,128]{2,1,0:T(8,128)S(1)}, f32[8,16,128]{2,1,0:T(8,128)S(1)}, u32[]{:S(2)}, u32[]{:S(2)}) collective-permute-start(f32[8,16,128]{2,1,0:T(8,128)S(1)} %get-tuple-element.26), channel_id=1, source_target_pairs={{0,12},{1,13},{2,14},{3,15},{4,8},{5,9},{6,10},{7,11},{8,4},{9,5},... | collective-permute-start | bytes 196616 | tf_op jit(solution)/shard_map/ppermute | solution.py:13
  30.8 25.9 %copy-start.5 = (f32[1,128,128]{2,1,0:T(8,128)}, f32[1,128,128]{2,1,0:T(8,128)S(1)}, u32[]{:S(2)}) copy-start(f32[1,128,128]{2,1,0:T(8,128)S(1)} %get-tuple-element.36) | copy-start | bytes 196612
  30.8 25.2 %copy-start.1 = (s32[8]{0:T(128)S(1)}, s32[8]{0:T(128)}, u32[]{:S(2)}) copy-start(s32[8]{0:T(128)} %param.19) | copy-start | bytes 100
  30.8 6.0 %collective-permute-start.10 = (f32[1,128,128]{2,1,0:T(8,128)S(1)}, f32[1,128,128]{2,1,0:T(8,128)S(1)}, u32[]{:S(2)}, u32[]{:S(2)}) collective-permute-start(f32[1,128,128]{2,1,0:T(8,128)S(1)} %get-tuple-element.36), channel_id=1, source_target_pairs={{0,16},{1,17},{2,18},{3,19},{4,20},{5,21},{6,22},{7,23},{8,24},{9,... | collective-permute-start | bytes 196616 | tf_op jit(solution)/shard_map/ppermute | solution.py:13
  36.8 5.0 %collective-permute-start.11 = (f32[2,128,128]{2,1,0:T(8,128)S(1)}, f32[2,128,128]{2,1,0:T(8,128)S(1)}, u32[]{:S(2)}, u32[]{:S(2)}) collective-permute-start(f32[2,128,128]{2,1,0:T(8,128)S(1)} %pad_maximum_fusion), channel_id=1, source_target_pairs={{0,8},{1,9},{2,10},{3,11},{4,12},{5,13},{6,14},{7,15},{8,0},{9,1},... | collective-permute-start | bytes 393224 | tf_op jit(solution)/shard_map/ppermute | solution.py:13
  37.3 5.2 %collective-permute-start.12 = (f32[2,128,128]{2,1,0:T(8,128)S(1)}, f32[2,128,128]{2,1,0:T(8,128)S(1)}, u32[]{:S(2)}, u32[]{:S(2)}) collective-permute-start(f32[2,128,128]{2,1,0:T(8,128)S(1)} %pad_maximum_fusion), channel_id=1, source_target_pairs={{0,4},{1,5},{2,6},{3,7},{4,0},{5,1},{6,2},{7,3},{8,12},{9,13},{10,... | collective-permute-start | bytes 393224 | tf_op jit(solution)/shard_map/ppermute | solution.py:13
  38.7 5.9 %collective-permute-start.13 = (f32[2,128,128]{2,1,0:T(8,128)S(1)}, f32[2,128,128]{2,1,0:T(8,128)S(1)}, u32[]{:S(2)}, u32[]{:S(2)}) collective-permute-start(f32[2,128,128]{2,1,0:T(8,128)S(1)} %pad_maximum_fusion), channel_id=1, source_target_pairs={{0,12},{1,13},{2,14},{3,15},{4,8},{5,9},{6,10},{7,11},{8,4},{9,5},... | collective-permute-start | bytes 393224 | tf_op jit(solution)/shard_map/ppermute | solution.py:13
  45.3 9.6 %collective-permute-start.14 = (f32[8,128,128]{2,1,0:T(8,128)S(1)}, f32[8,128,128]{2,1,0:T(8,128)S(1)}, u32[]{:S(2)}, u32[]{:S(2)}) collective-permute-start(f32[8,128,128]{2,1,0:T(8,128)S(1)} %get-tuple-element.13), channel_id=1, source_target_pairs={{0,2},{1,3},{2,0},{3,1},{4,6},{5,7},{6,4},{7,5},{8,10},{9,11},{10,... | collective-permute-start | bytes 1572872 | tf_op jit(solution)/shard_map/ppermute | solution.py:13
  56.0 2.9 %collective-permute-start.15 = (f32[16,128,128]{2,1,0:T(8,128)}, f32[16,128,128]{2,1,0:T(8,128)S(1)}, u32[]{:S(2)}, u32[]{:S(2)}) collective-permute-start(f32[16,128,128]{2,1,0:T(8,128)} %get-tuple-element.9), channel_id=1, source_target_pairs={{0,1},{1,0},{2,3},{3,2},{4,5},{5,4},{6,7},{7,6},{8,9},{9,8},{10,11... | collective-permute-start | bytes 3145736 | tf_op jit(solution)/shard_map/ppermute | solution.py:13
  59.9 3.6 %copy-start.7 = (s32[8,256]{1,0:T(8,128)S(1)}, s32[8,256]{1,0:T(8,128)}, u32[]{:S(2)}) copy-start(s32[8,256]{1,0:T(8,128)} %param.21) | copy-start | bytes 24580
  63.5 3.1 %copy-start.4 = (f32[8,256,128]{2,1,0:T(8,128)S(1)}, f32[8,256,128]{2,1,0:T(8,128)}, u32[]{:S(2)}) copy-start(f32[8,256,128]{2,1,0:T(8,128)} %param.23) | copy-start | bytes 3145732
  (4 other events, 6.0 us)

commit v9 on v6

--- a/solution.py
+++ b/solution.py
@@ -114,19 +114,28 @@
     top_held = xor_gather(top_solution, both, count, top_groups).reshape(count * top_rows, rhs)
     own_rows = own_base - jnp.einsum("wj,jr->wr", total, top_held, precision=highest)
 
-    held = xor_gather(own_rows, both, count, spread_groups)
+    held = xor_gather(own_rows, both, count, spread_groups[:-1])
+    last = spread_groups[-1][0]
+    partner = lax.ppermute(held, both, [(i, i ^ (1 << last)) for i in range(count)])
     position = owner_map[parent_list]
-    sources = position[:, None] * panels + jnp.arange(panels, dtype=jnp.int32)[None, :]
-    places = xor_position(sources ^ me, spread_groups)
-    slabs = held[places].reshape(position.shape[0], width_upper, own_rows.shape[1])
+    parent_rows = None
+    for side, source in ((0, held), (1, partner)):
+        offsets = jnp.array([o for o in range(panels) if ((o >> last) & 1) == side], jnp.int32)
+        quarters = panel_index ^ offsets
+        sources = position[:, None] * panels + quarters[None, :]
+        places = xor_position(sources ^ me, spread_groups) - side * held.shape[0]
+        slabs = source[places].reshape(position.shape[0], -1, own_rows.shape[1])
+        within = lax.broadcasted_iota(jnp.int32, (offsets.shape[0], share), 1)
+        columns = (quarters[:, None] * share + within).reshape(-1)
+        pick = (lower_index[:, :, None] == columns[None, None, :]).astype(jnp.float32)
+        term = jnp.einsum("skj,sjr->skr", pick, slabs, precision=highest)
+        parent_rows = term if parent_rows is None else parent_rows + term
 
-    columns = lax.broadcasted_iota(jnp.int32, lower_index.shape + (width_upper,), 2)
-    pick = (lower_index[:, :, None] == columns).astype(jnp.float32)
-    parent_rows = jnp.einsum("skj,sjr->skr", pick, slabs, precision=highest)
-
-    lower_update = jnp.einsum("skw,skr->swr", lower_panel, parent_rows, precision=highest)
+    panel_t = jnp.swapaxes(lower_panel, 1, 2)
+    inverse_t = jnp.swapaxes(lower_inverse, 1, 2)
+    lower_update = jnp.einsum("swk,skr->swr", panel_t, parent_rows, precision=highest)
     lower_solution = jnp.einsum(
-        "skw,skr->swr", lower_inverse, lower_rhs - lower_update, precision=highest
+        "swk,skr->swr", inverse_t, lower_rhs - lower_update, precision=highest
     )
     return (own_rows[None], lower_solution)
 

time: 74.5 us -> 72 us (0.966)
  waiting for transfers between devices: 20.4 us -> 18.3 us
    ppermute x13 -> x12, waiting for transfers between devices: 20.3 us -> 17.6 us  [xor_gather(): parts.append(lax.ppermute(held, axes, [(i, i ^ v) for i in range(count)]))]
    gather x1 -> x2, local copies, waits for them, and re-layouts: 3.6 us -> 4.66 us  [local(): slabs = source[places].reshape(position.shape[0], -1, own_rows.shape[1])]
    unnamed x35 -> x36, local copies, waits for them, and re-layouts: 5.09 us -> 4.21 us
    ppermute x13 -> x12, starting transfers between devices: 19.6 us -> 19.3 us  [xor_gather(): parts.append(lax.ppermute(held, axes, [(i, i ^ v) for i in range(count)]))]
    dot_general x3 -> x4, matrix products: 9.31 us -> 9.12 us  [the longest x2 3.6 us: local(): term = jnp.einsum('skj,sjr->skr', pick, slabs, precision=highest)]
  transfers between devices with their start and end apart: 16 -> 16, of which waited for: 8 -> 8; matrix products, arithmetic and copies ran while one was open for 15% -> 18% of each run, Pallas kernels for 0% -> 0%
where the time goes in v9:
time: 72 us; the launch traced here: 71.7 us
  starting transfers between devices  21.7 us (30%)
  waiting for transfers between devices  18.3 us (25%)
  matrix products  16.2 us (22%)
  local copies, waits for them, and re-layouts  13.4 us (19%)
  other arithmetic  1.13 us (2%)
  between operations  0.98 us (1%)
    ppermute x12, starting transfers between devices, xor_gather(): parts.append(lax.ppermute(held, axes, [(i, i ^ v) for i in range(count)]))  19.3 us
    ppermute x12, waiting for transfers between devices, xor_gather(): parts.append(lax.ppermute(held, axes, [(i, i ^ v) for i in range(count)]))  17.6 us
    gather x2, local copies, waits for them, and re-layouts, local(): slabs = source[places].reshape(position.shape[0], -1, own_rows.shape[1])  4.66 us
    unnamed x36, local copies, waits for them, and re-layouts  4.21 us
    dot_general x2, matrix products, local(): term = jnp.einsum('skj,sjr->skr', pick, slabs, precision=highest)  3.6 us
    dot_general x1, matrix products, local(): jnp.einsum('swk,skr->swr', panel_t, parent_rows, precision=highest)  3.52 us
    dot_general x1, matrix products, local(): jnp.einsum('kv,vw->kw', upper_panel[0], upper_inverse[0], precision=highest)  2.44 us
    dot_general x1, matrix products, local(): jnp.einsum('wj,jr->wr', total, top_held, precision=highest)  2.36 us
  transfers between devices with their start and end apart: 16, of which 8 were waited for; matrix products, arithmetic and copies ran while one was open for 18% of the time, Pallas kernels for 0%

profile of v9, /device:TPU:0, one launch (start us, length us, event | category | flops | bytes accessed | tf_op | source)
XLA Modules:
  0.0 71.7 jit_solution(13408432459859098150)
XLA Ops:
  1.2 2.6 %collective-permute-start.4 = (f32[1,16,128]{2,1,0:T(8,128)}, f32[1,16,128]{2,1,0:T(8,128)S(1)}, u32[]{:S(2)}, u32[]{:S(2)}) collective-permute-start(f32[1,16,128]{2,1,0:T(8,128)} %bitcast.65), channel_id=1, source_target_pairs={{0,2},{1,3},{2,0},{3,1},{4,6},{5,7},{6,4},{7,5},{8,10},{9,11},{10,... | collective-permute-start | bytes 24584 | tf_op jit(solution)/shard_map/ppermute | solution.py:13
  5.1 2.4 %fusion.9 = f32[256,512]{1,0:T(8,128)S(1)} fusion(f32[1,512,512]{2,1,0:T(8,128)} %param.18, f32[1,256,512]{2,1,0:T(8,128)} %param.17), kind=kOutput, calls=%fused_computation.16 | convolution fusion | flops 805306368 | bytes 2097152 | tf_op jit(solution)/shard_map/kv,vw->kw/dot_general | solution.py:102
  9.8 1.7 %collective-permute-start.2 = (f32[128,512]{0,1:T(8,128)S(1)}, f32[128,512]{0,1:T(8,128)}, u32[]{:S(2)}, u32[]{:S(2)}) collective-permute-start(f32[128,512]{0,1:T(8,128)S(1)} %bitcast.58), channel_id=1, source_target_pairs={{0,3},{1,2},{2,1},{3,0},{4,7},{5,6},{6,5},{7,4},{8,11},{9,10},{10,... | collective-permute-start | bytes 786440 | tf_op jit(solution)/shard_map/ppermute | solution.py:110
  13.4 2.9 %collective-permute-start.6 = (f32[4,16,128]{2,1,0:T(8,128)S(1)}, f32[4,16,128]{2,1,0:T(8,128)S(1)}, u32[]{:S(2)}, u32[]{:S(2)}) collective-permute-start(f32[4,16,128]{2,1,0:T(8,128)S(1)} %pad_maximum_fusion.1), channel_id=1, source_target_pairs={{0,16},{1,17},{2,18},{3,19},{4,20},{5,21},{6,22},{7,23},{8,24},{9,... | collective-permute-start | bytes 98312 | tf_op jit(solution)/shard_map/ppermute | solution.py:13
  16.3 2.0 %collective-permute-done.6 = f32[4,16,128]{2,1,0:T(8,128)S(1)} collective-permute-done((f32[4,16,128]{2,1,0:T(8,128)S(1)}, f32[4,16,128]{2,1,0:T(8,128)S(1)}, u32[]{:S(2)}, u32[]{:S(2)}) %collective-permute-start.6) | collective-permute-done | bytes 32800 | tf_op jit(solution)/shard_map/ppermute | solution.py:13
  18.3 1.8 %collective-permute-start.7 = (f32[8,16,128]{2,1,0:T(8,128)S(1)}, f32[8,16,128]{2,1,0:T(8,128)S(1)}, u32[]{:S(2)}, u32[]{:S(2)}) collective-permute-start(f32[8,16,128]{2,1,0:T(8,128)S(1)} %get-tuple-element.19), channel_id=1, source_target_pairs={{0,8},{1,9},{2,10},{3,11},{4,12},{5,13},{6,14},{7,15},{8,0},{9,1},... | collective-permute-start | bytes 196616 | tf_op jit(solution)/shard_map/ppermute | solution.py:13
  20.2 1.6 %fusion.18 = f32[128,128]{1,0:T(8,128)S(1)} fusion(f32[1,512,128]{2,1,0:T(8,128)} %param.16, f32[1,512,512]{2,1,0:T(8,128)} %param.18, s32[]{:T(128)S(6)} %select_n.96), kind=kOutput, calls=%fused_computation.25 | convolution fusion | flops 100663296 | bytes 589828 | tf_op jit(solution)/shard_map/kw,kr->wr/dot_general | solution.py:112
  21.8 1.6 %collective-permute-start.8 = (f32[8,16,128]{2,1,0:T(8,128)S(1)}, f32[8,16,128]{2,1,0:T(8,128)S(1)}, u32[]{:S(2)}, u32[]{:S(2)}) collective-permute-start(f32[8,16,128]{2,1,0:T(8,128)S(1)} %get-tuple-element.19), channel_id=1, source_target_pairs={{0,4},{1,5},{2,6},{3,7},{4,0},{5,1},{6,2},{7,3},{8,12},{9,13},{10,... | collective-permute-start | bytes 196616 | tf_op jit(solution)/shard_map/ppermute | solution.py:13
  23.4 2.0 %collective-permute-start.9 = (f32[8,16,128]{2,1,0:T(8,128)S(1)}, f32[8,16,128]{2,1,0:T(8,128)S(1)}, u32[]{:S(2)}, u32[]{:S(2)}) collective-permute-start(f32[8,16,128]{2,1,0:T(8,128)S(1)} %get-tuple-element.19), channel_id=1, source_target_pairs={{0,12},{1,13},{2,14},{3,15},{4,8},{5,9},{6,10},{7,11},{8,4},{9,5},... | collective-permute-start | bytes 196616 | tf_op jit(solution)/shard_map/ppermute | solution.py:13
  25.4 1.4 %collective-permute-done.8 = f32[8,16,128]{2,1,0:T(8,128)S(1)} collective-permute-done((f32[8,16,128]{2,1,0:T(8,128)S(1)}, f32[8,16,128]{2,1,0:T(8,128)S(1)}, u32[]{:S(2)}, u32[]{:S(2)}) %collective-permute-start.8) | collective-permute-done | bytes 65568 | tf_op jit(solution)/shard_map/ppermute | solution.py:13
  26.7 1.8 %collective-permute-done.9 = f32[8,16,128]{2,1,0:T(8,128)S(1)} collective-permute-done((f32[8,16,128]{2,1,0:T(8,128)S(1)}, f32[8,16,128]{2,1,0:T(8,128)S(1)}, u32[]{:S(2)}, u32[]{:S(2)}) %collective-permute-start.9) | collective-permute-done | bytes 65568 | tf_op jit(solution)/shard_map/ppermute | solution.py:13
  28.6 2.4 %constant_dynamic-update-slice_fusion.17 = (f32[8,128,128]{2,1,0:T(8,128)S(1)}, f32[16,128,128]{2,1,0:T(8,128)}, f32[1,128,128]{2,1,0:T(8,128)S(1)}) fusion(f32[128,128]{1,0:T(8,128)S(1)} %fusion.18, f32[512,128]{1,0:T(8,128)S(1)} %bitcast.63, f32[128,512]{0,1:T(8,128)} %collective-permute-done.2, f32[128,512]{0,1:T(8,128)S(1)} %collective-permute-done.1, ...), kind=kOutput, calls=%fused_computation.53 | convolution fusion | flops 100876288 | bytes 1572868 | tf_op jit(solution)/shard_map/wj,jr->wr/dot_general | solution.py:115
  30.9 2.8 %collective-permute-start.10 = (f32[1,128,128]{2,1,0:T(8,128)S(1)}, f32[1,128,128]{2,1,0:T(8,128)S(1)}, u32[]{:S(2)}, u32[]{:S(2)}) collective-permute-start(f32[1,128,128]{2,1,0:T(8,128)S(1)} %get-tuple-element.33), channel_id=1, source_target_pairs={{0,16},{1,17},{2,18},{3,19},{4,20},{5,21},{6,22},{7,23},{8,24},{9,... | collective-permute-start | bytes 196616 | tf_op jit(solution)/shard_map/ppermute | solution.py:13
  33.7 3.1 %collective-permute-done.10 = f32[1,128,128]{2,1,0:T(8,128)S(1)} collective-permute-done((f32[1,128,128]{2,1,0:T(8,128)S(1)}, f32[1,128,128]{2,1,0:T(8,128)S(1)}, u32[]{:S(2)}, u32[]{:S(2)}) %collective-permute-start.10) | collective-permute-done | bytes 65568 | tf_op jit(solution)/shard_map/ppermute | solution.py:13
  37.3 1.5 %collective-permute-start.12 = (f32[2,128,128]{2,1,0:T(8,128)S(1)}, f32[2,128,128]{2,1,0:T(8,128)S(1)}, u32[]{:S(2)}, u32[]{:S(2)}) collective-permute-start(f32[2,128,128]{2,1,0:T(8,128)S(1)} %pad_maximum_fusion), channel_id=1, source_target_pairs={{0,4},{1,5},{2,6},{3,7},{4,0},{5,1},{6,2},{7,3},{8,12},{9,13},{10,... | collective-permute-start | bytes 393224 | tf_op jit(solution)/shard_map/ppermute | solution.py:13
  38.8 1.6 %collective-permute-start.13 = (f32[2,128,128]{2,1,0:T(8,128)S(1)}, f32[2,128,128]{2,1,0:T(8,128)S(1)}, u32[]{:S(2)}, u32[]{:S(2)}) collective-permute-start(f32[2,128,128]{2,1,0:T(8,128)S(1)} %pad_maximum_fusion), channel_id=1, source_target_pairs={{0,12},{1,13},{2,14},{3,15},{4,8},{5,9},{6,10},{7,11},{8,4},{9,5},... | collective-permute-start | bytes 393224 | tf_op jit(solution)/shard_map/ppermute | solution.py:13
  43.3 1.4 %collective-permute-done.13 = f32[2,128,128]{2,1,0:T(8,128)S(1)} collective-permute-done((f32[2,128,128]{2,1,0:T(8,128)S(1)}, f32[2,128,128]{2,1,0:T(8,128)S(1)}, u32[]{:S(2)}, u32[]{:S(2)}) %collective-permute-start.13) | collective-permute-done | bytes 131104 | tf_op jit(solution)/shard_map/ppermute | solution.py:13
  45.3 1.5 %collective-permute-start.14 = (f32[8,128,128]{2,1,0:T(8,128)S(1)}, f32[8,128,128]{2,1,0:T(8,128)S(1)}, u32[]{:S(2)}, u32[]{:S(2)}) collective-permute-start(f32[8,128,128]{2,1,0:T(8,128)S(1)} %get-tuple-element.9), channel_id=1, source_target_pairs={{0,2},{1,3},{2,0},{3,1},{4,6},{5,7},{6,4},{7,5},{8,10},{9,11},{10,... | collective-permute-start | bytes 1572872 | tf_op jit(solution)/shard_map/ppermute | solution.py:13
  47.5 7.0 %collective-permute-done.14 = f32[8,128,128]{2,1,0:T(8,128)S(1)} collective-permute-done((f32[8,128,128]{2,1,0:T(8,128)S(1)}, f32[8,128,128]{2,1,0:T(8,128)S(1)}, u32[]{:S(2)}, u32[]{:S(2)}) %collective-permute-start.14) | collective-permute-done | bytes 524320 | tf_op jit(solution)/shard_map/ppermute | solution.py:13
  55.8 1.9 %gather_fusion.4 = f32[16,128,128]{2,1,0:T(8,128)S(1)} fusion(f32[16,128,128]{2,1,0:T(8,128)} %constant_dynamic-update-slice_fusion.18, s32[1024]{0:T(1024)S(1)} %pad_clamp_fusion.1), kind=kCustom, calls=%fused_computation.4 | custom fusion | bytes 2097216 | tf_op jit(solution)/shard_map/gather | solution.py:127
  58.4 2.8 %gather_fusion.5 = f32[16,128,128]{2,1,0:T(8,128)} fusion(f32[16,128,128]{2,1,0:T(8,128)} %collective-permute-done.15, s32[1024]{0:T(1024)S(1)} %pad_clamp_fusion), kind=kCustom, calls=%fused_computation.5 | custom fusion | bytes 2097216 | tf_op jit(solution)/shard_map/gather | solution.py:127
  61.2 2.4 %fusion = f32[8,256,128]{2,1,0:T(8,128)S(1)} fusion(f32[8,256,128]{2,1,0:T(8,128)} %bitcast.62, s32[256]{0:T(256)S(1)} %add_bitcast_fusion, s32[8,256]{1,0:T(8,128)S(1)} %copy-done.6), kind=kOutput, calls=%fused_computation.6 | convolution fusion | flops 805830656 | bytes 2106368 | tf_op jit(solution)/shard_map/skj,sjr->skr/dot_general | solution.py:131
  64.9 3.5 %fusion.7 = f32[8,256,128]{2,1,0:T(8,128)S(1)} fusion(f32[8,256,128]{2,1,0:T(8,128)S(1)} %copy-done.4, f32[8,256,128]{2,1,0:T(8,128)S(1)} %fusion.4, f32[8,256,256]{2,1,0:T(8,128)S(1)} %copy-done), kind=kOutput, calls=%fused_computation.13 | convolution fusion | flops 805568512 | bytes 5242880 | tf_op jit(solution)/shard_map/swk,skr->swr/dot_general | solution.py:136
  68.4 2.0 %convolution_bitcast_fusion = f32[8,256,128]{1,2,0:T(8,128)S(1)} fusion(f32[8,256,128]{2,1,0:T(8,128)S(1)} %fusion.7, f32[8,256,256]{2,1,0:T(8,128)S(1)} %copy-done.3), kind=kOutput, calls=%fused_computation.11 | convolution fusion | flops 805306368 | bytes 4194304 | tf_op jit(solution)/shard_map/swk,skr->swr/dot_general | solution.py:137
  (90 shorter events, 15.0 us)
Async XLA Ops:
  0.6 64.2 %copy-start = (f32[8,256,256]{2,1,0:T(8,128)S(1)}, f32[8,256,256]{2,1,0:T(8,128)}, u32[]{:S(2)}) copy-start(f32[8,256,256]{2,1,0:T(8,128)} %param.24) | copy-start | bytes 6291460
  0.6 6.9 %copy-start.12 = (s32[32]{0:T(128)S(1)}, s32[32]{0:T(128)}, u32[]{:S(2)}) copy-start(s32[32]{0:T(128)} %constant.146) | copy-start | bytes 388
  0.7 6.9 %copy-start.8 = (s32[1,256]{1,0:T(1,128)S(1)}, s32[1,256]{1,0:T(1,128)}, u32[]{:S(2)}) copy-start(s32[1,256]{1,0:T(1,128)} %param.19) | copy-start | bytes 3076
  0.7 12.4 %collective-permute-start.3 = (f32[1,16,128]{2,1,0:T(8,128)}, f32[1,16,128]{2,1,0:T(8,128)S(1)}, u32[]{:S(2)}, u32[]{:S(2)}) collective-permute-start(f32[1,16,128]{2,1,0:T(8,128)} %bitcast.64), channel_id=1, source_target_pairs={{0,1},{1,0},{2,3},{3,2},{4,5},{5,4},{6,7},{7,6},{8,9},{9,8},{10,11... | collective-permute-start | bytes 24584 | tf_op jit(solution)/shard_map/ppermute | solution.py:13
  1.2 12.2 %collective-permute-start.4 = (f32[1,16,128]{2,1,0:T(8,128)}, f32[1,16,128]{2,1,0:T(8,128)S(1)}, u32[]{:S(2)}, u32[]{:S(2)}) collective-permute-start(f32[1,16,128]{2,1,0:T(8,128)} %bitcast.65), channel_id=1, source_target_pairs={{0,2},{1,3},{2,0},{3,1},{4,6},{5,7},{6,4},{7,5},{8,10},{9,11},{10,... | collective-permute-start | bytes 24584 | tf_op jit(solution)/shard_map/ppermute | solution.py:13
  3.8 9.6 %collective-permute-start.5 = (f32[1,16,128]{2,1,0:T(8,128)}, f32[1,16,128]{2,1,0:T(8,128)S(1)}, u32[]{:S(2)}, u32[]{:S(2)}) collective-permute-start(f32[1,16,128]{2,1,0:T(8,128)} %bitcast.66), channel_id=1, source_target_pairs={{0,3},{1,2},{2,1},{3,0},{4,7},{5,6},{6,5},{7,4},{8,11},{9,10},{10,... | collective-permute-start | bytes 24584 | tf_op jit(solution)/shard_map/ppermute | solution.py:13
  9.8 18.7 %collective-permute-start.2 = (f32[128,512]{0,1:T(8,128)S(1)}, f32[128,512]{0,1:T(8,128)}, u32[]{:S(2)}, u32[]{:S(2)}) collective-permute-start(f32[128,512]{0,1:T(8,128)S(1)} %bitcast.58), channel_id=1, source_target_pairs={{0,3},{1,2},{2,1},{3,0},{4,7},{5,6},{6,5},{7,4},{8,11},{9,10},{10,... | collective-permute-start | bytes 786440 | tf_op jit(solution)/shard_map/ppermute | solution.py:110
  12.2 16.3 %collective-permute-start = (f32[128,512]{0,1:T(8,128)S(1)}, f32[128,512]{0,1:T(8,128)}, u32[]{:S(2)}, u32[]{:S(2)}) collective-permute-start(f32[128,512]{0,1:T(8,128)S(1)} %bitcast.59), channel_id=1, source_target_pairs={{0,1},{1,0},{2,3},{3,2},{4,5},{5,4},{6,7},{7,6},{8,9},{9,8},{10,11... | collective-permute-start | bytes 786440 | tf_op jit(solution)/shard_map/ppermute | solution.py:110
  13.0 15.5 %collective-permute-start.1 = (f32[128,512]{0,1:T(8,128)S(1)}, f32[128,512]{0,1:T(8,128)S(1)}, u32[]{:S(2)}, u32[]{:S(2)}) collective-permute-start(f32[128,512]{0,1:T(8,128)S(1)} %bitcast.60), channel_id=1, source_target_pairs={{0,2},{1,3},{2,0},{3,1},{4,6},{5,7},{6,4},{7,5},{8,10},{9,11},{10,... | collective-permute-start | bytes 786440 | tf_op jit(solution)/shard_map/ppermute | solution.py:110
  13.4 4.9 %collective-permute-start.6 = (f32[4,16,128]{2,1,0:T(8,128)S(1)}, f32[4,16,128]{2,1,0:T(8,128)S(1)}, u32[]{:S(2)}, u32[]{:S(2)}) collective-permute-start(f32[4,16,128]{2,1,0:T(8,128)S(1)} %pad_maximum_fusion.1), channel_id=1, source_target_pairs={{0,16},{1,17},{2,18},{3,19},{4,20},{5,21},{6,22},{7,23},{8,24},{9,... | collective-permute-start | bytes 98312 | tf_op jit(solution)/shard_map/ppermute | solution.py:13
  18.3 28.6 %copy-start.1 = (s32[8]{0:T(128)S(1)}, s32[8]{0:T(128)}, u32[]{:S(2)}) copy-start(s32[8]{0:T(128)} %param.21) | copy-start | bytes 100
  18.3 5.0 %collective-permute-start.7 = (f32[8,16,128]{2,1,0:T(8,128)S(1)}, f32[8,16,128]{2,1,0:T(8,128)S(1)}, u32[]{:S(2)}, u32[]{:S(2)}) collective-permute-start(f32[8,16,128]{2,1,0:T(8,128)S(1)} %get-tuple-element.19), channel_id=1, source_target_pairs={{0,8},{1,9},{2,10},{3,11},{4,12},{5,13},{6,14},{7,15},{8,0},{9,1},... | collective-permute-start | bytes 196616 | tf_op jit(solution)/shard_map/ppermute | solution.py:13
  21.8 25.7 %copy-start.9 = (s32[2]{0:T(128)S(1)}, s32[2]{0:T(128)}, u32[]{:S(2)}) copy-start(s32[2]{0:T(128)} %constant.121.clone) | copy-start | bytes 28
  21.8 4.9 %collective-permute-start.8 = (f32[8,16,128]{2,1,0:T(8,128)S(1)}, f32[8,16,128]{2,1,0:T(8,128)S(1)}, u32[]{:S(2)}, u32[]{:S(2)}) collective-permute-start(f32[8,16,128]{2,1,0:T(8,128)S(1)} %get-tuple-element.19), channel_id=1, source_target_pairs={{0,4},{1,5},{2,6},{3,7},{4,0},{5,1},{6,2},{7,3},{8,12},{9,13},{10,... | collective-permute-start | bytes 196616 | tf_op jit(solution)/shard_map/ppermute | solution.py:13
  23.4 5.2 %collective-permute-start.9 = (f32[8,16,128]{2,1,0:T(8,128)S(1)}, f32[8,16,128]{2,1,0:T(8,128)S(1)}, u32[]{:S(2)}, u32[]{:S(2)}) collective-permute-start(f32[8,16,128]{2,1,0:T(8,128)S(1)} %get-tuple-element.19), channel_id=1, source_target_pairs={{0,12},{1,13},{2,14},{3,15},{4,8},{5,9},{6,10},{7,11},{8,4},{9,5},... | collective-permute-start | bytes 196616 | tf_op jit(solution)/shard_map/ppermute | solution.py:13
  30.9 26.8 %copy-start.5 = (f32[1,128,128]{2,1,0:T(8,128)}, f32[1,128,128]{2,1,0:T(8,128)S(1)}, u32[]{:S(2)}) copy-start(f32[1,128,128]{2,1,0:T(8,128)S(1)} %get-tuple-element.33) | copy-start | bytes 196612
  30.9 6.0 %collective-permute-start.10 = (f32[1,128,128]{2,1,0:T(8,128)S(1)}, f32[1,128,128]{2,1,0:T(8,128)S(1)}, u32[]{:S(2)}, u32[]{:S(2)}) collective-permute-start(f32[1,128,128]{2,1,0:T(8,128)S(1)} %get-tuple-element.33), channel_id=1, source_target_pairs={{0,16},{1,17},{2,18},{3,19},{4,20},{5,21},{6,22},{7,23},{8,24},{9,... | collective-permute-start | bytes 196616 | tf_op jit(solution)/shard_map/ppermute | solution.py:13
  36.9 5.0 %collective-permute-start.11 = (f32[2,128,128]{2,1,0:T(8,128)S(1)}, f32[2,128,128]{2,1,0:T(8,128)S(1)}, u32[]{:S(2)}, u32[]{:S(2)}) collective-permute-start(f32[2,128,128]{2,1,0:T(8,128)S(1)} %pad_maximum_fusion), channel_id=1, source_target_pairs={{0,8},{1,9},{2,10},{3,11},{4,12},{5,13},{6,14},{7,15},{8,0},{9,1},... | collective-permute-start | bytes 393224 | tf_op jit(solution)/shard_map/ppermute | solution.py:13
  37.3 5.3 %collective-permute-start.12 = (f32[2,128,128]{2,1,0:T(8,128)S(1)}, f32[2,128,128]{2,1,0:T(8,128)S(1)}, u32[]{:S(2)}, u32[]{:S(2)}) collective-permute-start(f32[2,128,128]{2,1,0:T(8,128)S(1)} %pad_maximum_fusion), channel_id=1, source_target_pairs={{0,4},{1,5},{2,6},{3,7},{4,0},{5,1},{6,2},{7,3},{8,12},{9,13},{10,... | collective-permute-start | bytes 393224 | tf_op jit(solution)/shard_map/ppermute | solution.py:13
  38.8 5.9 %collective-permute-start.13 = (f32[2,128,128]{2,1,0:T(8,128)S(1)}, f32[2,128,128]{2,1,0:T(8,128)S(1)}, u32[]{:S(2)}, u32[]{:S(2)}) collective-permute-start(f32[2,128,128]{2,1,0:T(8,128)S(1)} %pad_maximum_fusion), channel_id=1, source_target_pairs={{0,12},{1,13},{2,14},{3,15},{4,8},{5,9},{6,10},{7,11},{8,4},{9,5},... | collective-permute-start | bytes 393224 | tf_op jit(solution)/shard_map/ppermute | solution.py:13
  45.3 9.2 %collective-permute-start.14 = (f32[8,128,128]{2,1,0:T(8,128)S(1)}, f32[8,128,128]{2,1,0:T(8,128)S(1)}, u32[]{:S(2)}, u32[]{:S(2)}) collective-permute-start(f32[8,128,128]{2,1,0:T(8,128)S(1)} %get-tuple-element.9), channel_id=1, source_target_pairs={{0,2},{1,3},{2,0},{3,1},{4,6},{5,7},{6,4},{7,5},{8,10},{9,11},{10,... | collective-permute-start | bytes 1572872 | tf_op jit(solution)/shard_map/ppermute | solution.py:13
  55.4 3.0 %collective-permute-start.15 = (f32[16,128,128]{2,1,0:T(8,128)}, f32[16,128,128]{2,1,0:T(8,128)}, u32[]{:S(2)}, u32[]{:S(2)}) collective-permute-start(f32[16,128,128]{2,1,0:T(8,128)} %constant_dynamic-update-slice_fusion.18), channel_id=1, source_target_pairs={{0,1},{1,0},{2,3},{3,2},{4,5},{5,4},{6,7},{7,6},{8,9},{9,8},{10,11... | collective-permute-start | bytes 3145736 | tf_op jit(solution)/shard_map/ppermute | solution.py:119
  55.8 5.4 %copy-start.6 = (s32[8,256]{1,0:T(8,128)S(1)}, s32[8,256]{1,0:T(8,128)}, u32[]{:S(2)}) copy-start(s32[8,256]{1,0:T(8,128)} %param.23) | copy-start | bytes 24580
  64.9 3.5 %copy-start.3 = (f32[8,256,256]{2,1,0:T(8,128)S(1)}, f32[8,256,256]{2,1,0:T(8,128)}, u32[]{:S(2)}) copy-start(f32[8,256,256]{2,1,0:T(8,128)} %param.26) | copy-start | bytes 6291460
  (5 other events, 7.7 us)

commit v10 on v9

--- a/solution.py
+++ b/solution.py
@@ -92,7 +92,7 @@
         high_first = high_first[1:]
     leaf_groups += [high_first[i : i + 2] for i in range(0, len(high_first), 2)]
     top_groups = [panel_bits] + leaf_groups
-    spread_groups = leaf_groups + [[b] for b in panel_bits[::-1]]
+    spread_groups = [[b] for b in panel_bits[1:]] + leaf_groups + [[0]]
 
     top_rows, rhs = top_solution.shape
     places = lax.broadcasted_iota(jnp.int32, (count, top_rows), 0)

time: 72 us -> 70.7 us (0.982)
  waiting for transfers between devices: 18.3 us -> 16.6 us
    ppermute x12, waiting for transfers between devices: 17.6 us -> 15.9 us  [xor_gather(): parts.append(lax.ppermute(held, axes, [(i, i ^ v) for i in range(count)]))]
    concatenate x4 -> x3, local copies, waits for them, and re-layouts: 1.55 us -> 0.74 us  [xor_gather(): held = jnp.concatenate(parts, 0)]
    unnamed x36 -> x37, local copies, waits for them, and re-layouts: 4.21 us -> 4.95 us
  transfers between devices with their start and end apart: 16 -> 16, of which waited for: 8 -> 9; matrix products, arithmetic and copies ran while one was open for 18% -> 19% of each run, Pallas kernels for 0% -> 0%
where the time goes in v10:
time: 70.7 us; the launch traced here: 70.1 us
  starting transfers between devices  21.7 us (31%)
  waiting for transfers between devices  16.6 us (23%)
  matrix products  16.3 us (23%)
  local copies, waits for them, and re-layouts  13.3 us (19%)
  other arithmetic  1.15 us (2%)
  between operations  1.01 us (1%)
    ppermute x12, starting transfers between devices, xor_gather(): parts.append(lax.ppermute(held, axes, [(i, i ^ v) for i in range(count)]))  19.4 us
    ppermute x12, waiting for transfers between devices, xor_gather(): parts.append(lax.ppermute(held, axes, [(i, i ^ v) for i in range(count)]))  15.9 us
    unnamed x37, local copies, waits for them, and re-layouts  4.95 us
    gather x2, local copies, waits for them, and re-layouts, local(): slabs = source[places].reshape(position.shape[0], -1, own_rows.shape[1])  4.66 us
    dot_general x2, matrix products, local(): term = jnp.einsum('skj,sjr->skr', pick, slabs, precision=highest)  3.6 us
    dot_general x1, matrix products, local(): jnp.einsum('swk,skr->swr', panel_t, parent_rows, precision=highest)  3.52 us
    dot_general x1, matrix products, local(): jnp.einsum('kv,vw->kw', upper_panel[0], upper_inverse[0], precision=highest)  2.44 us
    dot_general x1, matrix products, local(): jnp.einsum('wj,jr->wr', total, top_held, precision=highest)  2.37 us
  transfers between devices with their start and end apart: 16, of which 9 were waited for; matrix products, arithmetic and copies ran while one was open for 19% of the time, Pallas kernels for 0%

profile of v10, /device:TPU:0, one launch (start us, length us, event | category | flops | bytes accessed | tf_op | source)
XLA Modules:
  0.0 70.1 jit_solution(15312302403414776622)
XLA Ops:
  1.2 2.6 %collective-permute-start.4 = (f32[1,16,128]{2,1,0:T(8,128)}, f32[1,16,128]{2,1,0:T(8,128)S(1)}, u32[]{:S(2)}, u32[]{:S(2)}) collective-permute-start(f32[1,16,128]{2,1,0:T(8,128)} %bitcast.65), channel_id=1, source_target_pairs={{0,2},{1,3},{2,0},{3,1},{4,6},{5,7},{6,4},{7,5},{8,10},{9,11},{10,... | collective-permute-start | bytes 24584 | tf_op jit(solution)/shard_map/ppermute | solution.py:13
  5.1 2.4 %fusion.9 = f32[256,512]{1,0:T(8,128)S(1)} fusion(f32[1,512,512]{2,1,0:T(8,128)} %param.18, f32[1,256,512]{2,1,0:T(8,128)} %param.17), kind=kOutput, calls=%fused_computation.16 | convolution fusion | flops 805306368 | bytes 2097152 | tf_op jit(solution)/shard_map/kv,vw->kw/dot_general | solution.py:102
  9.8 1.7 %collective-permute-start.2 = (f32[128,512]{0,1:T(8,128)S(1)}, f32[128,512]{0,1:T(8,128)}, u32[]{:S(2)}, u32[]{:S(2)}) collective-permute-start(f32[128,512]{0,1:T(8,128)S(1)} %bitcast.58), channel_id=1, source_target_pairs={{0,3},{1,2},{2,1},{3,0},{4,7},{5,6},{6,5},{7,4},{8,11},{9,10},{10,... | collective-permute-start | bytes 786440 | tf_op jit(solution)/shard_map/ppermute | solution.py:110
  13.4 2.9 %collective-permute-start.6 = (f32[4,16,128]{2,1,0:T(8,128)S(1)}, f32[4,16,128]{2,1,0:T(8,128)S(1)}, u32[]{:S(2)}, u32[]{:S(2)}) collective-permute-start(f32[4,16,128]{2,1,0:T(8,128)S(1)} %pad_maximum_fusion.2), channel_id=1, source_target_pairs={{0,16},{1,17},{2,18},{3,19},{4,20},{5,21},{6,22},{7,23},{8,24},{9,... | collective-permute-start | bytes 98312 | tf_op jit(solution)/shard_map/ppermute | solution.py:13
  16.3 2.0 %collective-permute-done.6 = f32[4,16,128]{2,1,0:T(8,128)S(1)} collective-permute-done((f32[4,16,128]{2,1,0:T(8,128)S(1)}, f32[4,16,128]{2,1,0:T(8,128)S(1)}, u32[]{:S(2)}, u32[]{:S(2)}) %collective-permute-start.6) | collective-permute-done | bytes 32800 | tf_op jit(solution)/shard_map/ppermute | solution.py:13
  18.3 1.8 %collective-permute-start.7 = (f32[8,16,128]{2,1,0:T(8,128)S(1)}, f32[8,16,128]{2,1,0:T(8,128)S(1)}, u32[]{:S(2)}, u32[]{:S(2)}) collective-permute-start(f32[8,16,128]{2,1,0:T(8,128)S(1)} %get-tuple-element.9), channel_id=1, source_target_pairs={{0,8},{1,9},{2,10},{3,11},{4,12},{5,13},{6,14},{7,15},{8,0},{9,1},... | collective-permute-start | bytes 196616 | tf_op jit(solution)/shard_map/ppermute | solution.py:13
  20.1 1.6 %fusion.18 = f32[128,128]{1,0:T(8,128)S(1)} fusion(f32[1,512,128]{2,1,0:T(8,128)} %param.16, f32[1,512,512]{2,1,0:T(8,128)} %param.18, s32[]{:T(128)S(6)} %select_n.96), kind=kOutput, calls=%fused_computation.26 | convolution fusion | flops 100663296 | bytes 589828 | tf_op jit(solution)/shard_map/kw,kr->wr/dot_general | solution.py:112
  21.7 1.6 %collective-permute-start.8 = (f32[8,16,128]{2,1,0:T(8,128)S(1)}, f32[8,16,128]{2,1,0:T(8,128)S(1)}, u32[]{:S(2)}, u32[]{:S(2)}) collective-permute-start(f32[8,16,128]{2,1,0:T(8,128)S(1)} %get-tuple-element.9), channel_id=1, source_target_pairs={{0,4},{1,5},{2,6},{3,7},{4,0},{5,1},{6,2},{7,3},{8,12},{9,13},{10,... | collective-permute-start | bytes 196616 | tf_op jit(solution)/shard_map/ppermute | solution.py:13
  23.3 2.0 %collective-permute-start.9 = (f32[8,16,128]{2,1,0:T(8,128)S(1)}, f32[8,16,128]{2,1,0:T(8,128)S(1)}, u32[]{:S(2)}, u32[]{:S(2)}) collective-permute-start(f32[8,16,128]{2,1,0:T(8,128)S(1)} %get-tuple-element.9), channel_id=1, source_target_pairs={{0,12},{1,13},{2,14},{3,15},{4,8},{5,9},{6,10},{7,11},{8,4},{9,5},... | collective-permute-start | bytes 196616 | tf_op jit(solution)/shard_map/ppermute | solution.py:13
  26.7 1.8 %collective-permute-done.9 = f32[8,16,128]{2,1,0:T(8,128)S(1)} collective-permute-done((f32[8,16,128]{2,1,0:T(8,128)S(1)}, f32[8,16,128]{2,1,0:T(8,128)S(1)}, u32[]{:S(2)}, u32[]{:S(2)}) %collective-permute-start.9) | collective-permute-done | bytes 65568 | tf_op jit(solution)/shard_map/ppermute | solution.py:13
  28.5 2.4 %constant_dynamic-update-slice_fusion.18 = (f32[16,128,128]{2,1,0:T(8,128)}, f32[1,128,128]{2,1,0:T(8,128)S(1)}) fusion(f32[128,128]{1,0:T(8,128)S(1)} %fusion.18, f32[512,128]{1,0:T(8,128)S(1)} %bitcast.63, f32[128,512]{0,1:T(8,128)} %collective-permute-done.2, f32[128,512]{0,1:T(8,128)S(1)} %collective-permute-done.1, ...), kind=kOutput, calls=%fused_computation.55 | convolution fusion | flops 100876288 | bytes 1507332 | tf_op jit(solution)/shard_map/wj,jr->wr/dot_general | solution.py:115
  30.9 1.5 %collective-permute-start.10 = (f32[1,128,128]{2,1,0:T(8,128)S(1)}, f32[1,128,128]{2,1,0:T(8,128)S(1)}, u32[]{:S(2)}, u32[]{:S(2)}) collective-permute-start(f32[1,128,128]{2,1,0:T(8,128)S(1)} %get-tuple-element.24), channel_id=1, source_target_pairs={{0,2},{1,3},{2,0},{3,1},{4,6},{5,7},{6,4},{7,5},{8,10},{9,11},{10,... | collective-permute-start | bytes 196616 | tf_op jit(solution)/shard_map/ppermute | solution.py:13
  32.4 2.7 %collective-permute-done.10 = f32[1,128,128]{2,1,0:T(8,128)S(1)} collective-permute-done((f32[1,128,128]{2,1,0:T(8,128)S(1)}, f32[1,128,128]{2,1,0:T(8,128)S(1)}, u32[]{:S(2)}, u32[]{:S(2)}) %collective-permute-start.10) | collective-permute-done | bytes 65568 | tf_op jit(solution)/shard_map/ppermute | solution.py:13
  35.1 2.9 %collective-permute-start.11 = (f32[2,128,128]{2,1,0:T(8,128)S(1)}, f32[2,128,128]{2,1,0:T(8,128)S(1)}, u32[]{:S(2)}, u32[]{:S(2)}) collective-permute-start(f32[2,128,128]{2,1,0:T(8,128)S(1)} %pad_maximum_fusion.1), channel_id=1, source_target_pairs={{0,16},{1,17},{2,18},{3,19},{4,20},{5,21},{6,22},{7,23},{8,24},{9,... | collective-permute-start | bytes 393224 | tf_op jit(solution)/shard_map/ppermute | solution.py:13
  38.0 4.5 %collective-permute-done.11 = f32[2,128,128]{2,1,0:T(8,128)S(1)} collective-permute-done((f32[2,128,128]{2,1,0:T(8,128)S(1)}, f32[2,128,128]{2,1,0:T(8,128)S(1)}, u32[]{:S(2)}, u32[]{:S(2)}) %collective-permute-start.11) | collective-permute-done | bytes 131104 | tf_op jit(solution)/shard_map/ppermute | solution.py:13
  43.4 1.8 %collective-permute-start.13 = (f32[4,128,128]{2,1,0:T(8,128)S(1)}, f32[4,128,128]{2,1,0:T(8,128)S(1)}, u32[]{:S(2)}, u32[]{:S(2)}) collective-permute-start(f32[4,128,128]{2,1,0:T(8,128)S(1)} %pad_maximum_fusion), channel_id=1, source_target_pairs={{0,4},{1,5},{2,6},{3,7},{4,0},{5,1},{6,2},{7,3},{8,12},{9,13},{10,... | collective-permute-start | bytes 786440 | tf_op jit(solution)/shard_map/ppermute | solution.py:13
  45.8 1.7 %collective-permute-start.14 = (f32[4,128,128]{2,1,0:T(8,128)S(1)}, f32[4,128,128]{2,1,0:T(8,128)S(1)}, u32[]{:S(2)}, u32[]{:S(2)}) collective-permute-start(f32[4,128,128]{2,1,0:T(8,128)S(1)} %pad_maximum_fusion), channel_id=1, source_target_pairs={{0,12},{1,13},{2,14},{3,15},{4,8},{5,9},{6,10},{7,11},{8,4},{9,5},... | collective-permute-start | bytes 786440 | tf_op jit(solution)/shard_map/ppermute | solution.py:13
  48.2 1.4 %collective-permute-done.12 = f32[4,128,128]{2,1,0:T(8,128)S(1)} collective-permute-done((f32[4,128,128]{2,1,0:T(8,128)S(1)}, f32[4,128,128]{2,1,0:T(8,128)S(1)}, u32[]{:S(2)}, u32[]{:S(2)}) %collective-permute-start.12) | collective-permute-done | bytes 262176 | tf_op jit(solution)/shard_map/ppermute | solution.py:13
  50.2 1.6 %collective-permute-done.13 = f32[4,128,128]{2,1,0:T(8,128)S(1)} collective-permute-done((f32[4,128,128]{2,1,0:T(8,128)S(1)}, f32[4,128,128]{2,1,0:T(8,128)S(1)}, u32[]{:S(2)}, u32[]{:S(2)}) %collective-permute-start.13) | collective-permute-done | bytes 262176 | tf_op jit(solution)/shard_map/ppermute | solution.py:13
  54.2 1.9 %gather_fusion.4 = f32[16,128,128]{2,1,0:T(8,128)S(1)} fusion(f32[16,128,128]{2,1,0:T(8,128)} %constant_dynamic-update-slice_fusion.13, s32[1024]{0:T(1024)S(1)} %pad_clamp_fusion.1), kind=kCustom, calls=%fused_computation.4 | custom fusion | bytes 2097216 | tf_op jit(solution)/shard_map/gather | solution.py:127
  56.8 2.8 %gather_fusion.5 = f32[16,128,128]{2,1,0:T(8,128)} fusion(f32[16,128,128]{2,1,0:T(8,128)} %collective-permute-done.15, s32[1024]{0:T(1024)S(1)} %pad_clamp_fusion), kind=kCustom, calls=%fused_computation.5 | custom fusion | bytes 2097216 | tf_op jit(solution)/shard_map/gather | solution.py:127
  59.6 2.4 %fusion = f32[8,256,128]{2,1,0:T(8,128)S(1)} fusion(f32[8,256,128]{2,1,0:T(8,128)} %bitcast.62, s32[256]{0:T(256)S(1)} %add_bitcast_fusion, s32[8,256]{1,0:T(8,128)S(1)} %copy-done.6), kind=kOutput, calls=%fused_computation.6 | convolution fusion | flops 805830656 | bytes 2106368 | tf_op jit(solution)/shard_map/skj,sjr->skr/dot_general | solution.py:131
  63.2 3.5 %fusion.7 = f32[8,256,128]{2,1,0:T(8,128)S(1)} fusion(f32[8,256,128]{2,1,0:T(8,128)S(1)} %copy-done.4, f32[8,256,128]{2,1,0:T(8,128)S(1)} %fusion.4, f32[8,256,256]{2,1,0:T(8,128)S(1)} %copy-done), kind=kOutput, calls=%fused_computation.13 | convolution fusion | flops 805568512 | bytes 5242880 | tf_op jit(solution)/shard_map/swk,skr->swr/dot_general | solution.py:136
  66.8 2.0 %convolution_bitcast_fusion = f32[8,256,128]{1,2,0:T(8,128)S(1)} fusion(f32[8,256,128]{2,1,0:T(8,128)S(1)} %fusion.7, f32[8,256,256]{2,1,0:T(8,128)S(1)} %copy-done.3), kind=kOutput, calls=%fused_computation.11 | convolution fusion | flops 805306368 | bytes 4194304 | tf_op jit(solution)/shard_map/swk,skr->swr/dot_general | solution.py:137
  (91 shorter events, 15.5 us)
Async XLA Ops:
  0.6 62.6 %copy-start = (f32[8,256,256]{2,1,0:T(8,128)S(1)}, f32[8,256,256]{2,1,0:T(8,128)}, u32[]{:S(2)}) copy-start(f32[8,256,256]{2,1,0:T(8,128)} %param.24) | copy-start | bytes 6291460
  0.6 6.9 %copy-start.12 = (s32[32]{0:T(128)S(1)}, s32[32]{0:T(128)}, u32[]{:S(2)}) copy-start(s32[32]{0:T(128)} %constant.145) | copy-start | bytes 388
  0.7 6.9 %copy-start.8 = (s32[1,256]{1,0:T(1,128)S(1)}, s32[1,256]{1,0:T(1,128)}, u32[]{:S(2)}) copy-start(s32[1,256]{1,0:T(1,128)} %param.19) | copy-start | bytes 3076
  0.7 12.4 %collective-permute-start.3 = (f32[1,16,128]{2,1,0:T(8,128)}, f32[1,16,128]{2,1,0:T(8,128)S(1)}, u32[]{:S(2)}, u32[]{:S(2)}) collective-permute-start(f32[1,16,128]{2,1,0:T(8,128)} %bitcast.64), channel_id=1, source_target_pairs={{0,1},{1,0},{2,3},{3,2},{4,5},{5,4},{6,7},{7,6},{8,9},{9,8},{10,11... | collective-permute-start | bytes 24584 | tf_op jit(solution)/shard_map/ppermute | solution.py:13
  1.2 12.2 %collective-permute-start.4 = (f32[1,16,128]{2,1,0:T(8,128)}, f32[1,16,128]{2,1,0:T(8,128)S(1)}, u32[]{:S(2)}, u32[]{:S(2)}) collective-permute-start(f32[1,16,128]{2,1,0:T(8,128)} %bitcast.65), channel_id=1, source_target_pairs={{0,2},{1,3},{2,0},{3,1},{4,6},{5,7},{6,4},{7,5},{8,10},{9,11},{10,... | collective-permute-start | bytes 24584 | tf_op jit(solution)/shard_map/ppermute | solution.py:13
  3.8 9.7 %collective-permute-start.5 = (f32[1,16,128]{2,1,0:T(8,128)}, f32[1,16,128]{2,1,0:T(8,128)S(1)}, u32[]{:S(2)}, u32[]{:S(2)}) collective-permute-start(f32[1,16,128]{2,1,0:T(8,128)} %bitcast.66), channel_id=1, source_target_pairs={{0,3},{1,2},{2,1},{3,0},{4,7},{5,6},{6,5},{7,4},{8,11},{9,10},{10,... | collective-permute-start | bytes 24584 | tf_op jit(solution)/shard_map/ppermute | solution.py:13
  9.8 18.6 %collective-permute-start.2 = (f32[128,512]{0,1:T(8,128)S(1)}, f32[128,512]{0,1:T(8,128)}, u32[]{:S(2)}, u32[]{:S(2)}) collective-permute-start(f32[128,512]{0,1:T(8,128)S(1)} %bitcast.58), channel_id=1, source_target_pairs={{0,3},{1,2},{2,1},{3,0},{4,7},{5,6},{6,5},{7,4},{8,11},{9,10},{10,... | collective-permute-start | bytes 786440 | tf_op jit(solution)/shard_map/ppermute | solution.py:110
  12.2 16.3 %collective-permute-start = (f32[128,512]{0,1:T(8,128)S(1)}, f32[128,512]{0,1:T(8,128)}, u32[]{:S(2)}, u32[]{:S(2)}) collective-permute-start(f32[128,512]{0,1:T(8,128)S(1)} %bitcast.59), channel_id=1, source_target_pairs={{0,1},{1,0},{2,3},{3,2},{4,5},{5,4},{6,7},{7,6},{8,9},{9,8},{10,11... | collective-permute-start | bytes 786440 | tf_op jit(solution)/shard_map/ppermute | solution.py:110
  13.0 29.7 %copy-start.9 = (s32[2]{0:T(128)S(1)}, s32[2]{0:T(128)}, u32[]{:S(2)}) copy-start(s32[2]{0:T(128)} %constant.120.clone) | copy-start | bytes 28
  13.0 29.7 %copy-start.1 = (s32[8]{0:T(128)S(1)}, s32[8]{0:T(128)}, u32[]{:S(2)}) copy-start(s32[8]{0:T(128)} %param.21) | copy-start | bytes 100
  13.1 15.4 %collective-permute-start.1 = (f32[128,512]{0,1:T(8,128)S(1)}, f32[128,512]{0,1:T(8,128)S(1)}, u32[]{:S(2)}, u32[]{:S(2)}) collective-permute-start(f32[128,512]{0,1:T(8,128)S(1)} %bitcast.60), channel_id=1, source_target_pairs={{0,2},{1,3},{2,0},{3,1},{4,6},{5,7},{6,4},{7,5},{8,10},{9,11},{10,... | collective-permute-start | bytes 786440 | tf_op jit(solution)/shard_map/ppermute | solution.py:110
  13.4 4.9 %collective-permute-start.6 = (f32[4,16,128]{2,1,0:T(8,128)S(1)}, f32[4,16,128]{2,1,0:T(8,128)S(1)}, u32[]{:S(2)}, u32[]{:S(2)}) collective-permute-start(f32[4,16,128]{2,1,0:T(8,128)S(1)} %pad_maximum_fusion.2), channel_id=1, source_target_pairs={{0,16},{1,17},{2,18},{3,19},{4,20},{5,21},{6,22},{7,23},{8,24},{9,... | collective-permute-start | bytes 98312 | tf_op jit(solution)/shard_map/ppermute | solution.py:13
  18.3 5.0 %collective-permute-start.7 = (f32[8,16,128]{2,1,0:T(8,128)S(1)}, f32[8,16,128]{2,1,0:T(8,128)S(1)}, u32[]{:S(2)}, u32[]{:S(2)}) collective-permute-start(f32[8,16,128]{2,1,0:T(8,128)S(1)} %get-tuple-element.9), channel_id=1, source_target_pairs={{0,8},{1,9},{2,10},{3,11},{4,12},{5,13},{6,14},{7,15},{8,0},{9,1},... | collective-permute-start | bytes 196616 | tf_op jit(solution)/shard_map/ppermute | solution.py:13
  21.7 4.9 %collective-permute-start.8 = (f32[8,16,128]{2,1,0:T(8,128)S(1)}, f32[8,16,128]{2,1,0:T(8,128)S(1)}, u32[]{:S(2)}, u32[]{:S(2)}) collective-permute-start(f32[8,16,128]{2,1,0:T(8,128)S(1)} %get-tuple-element.9), channel_id=1, source_target_pairs={{0,4},{1,5},{2,6},{3,7},{4,0},{5,1},{6,2},{7,3},{8,12},{9,13},{10,... | collective-permute-start | bytes 196616 | tf_op jit(solution)/shard_map/ppermute | solution.py:13
  23.3 5.2 %collective-permute-start.9 = (f32[8,16,128]{2,1,0:T(8,128)S(1)}, f32[8,16,128]{2,1,0:T(8,128)S(1)}, u32[]{:S(2)}, u32[]{:S(2)}) collective-permute-start(f32[8,16,128]{2,1,0:T(8,128)S(1)} %get-tuple-element.9), channel_id=1, source_target_pairs={{0,12},{1,13},{2,14},{3,15},{4,8},{5,9},{6,10},{7,11},{8,4},{9,5},... | collective-permute-start | bytes 196616 | tf_op jit(solution)/shard_map/ppermute | solution.py:13
  30.9 25.2 %copy-start.5 = (f32[1,128,128]{2,1,0:T(8,128)}, f32[1,128,128]{2,1,0:T(8,128)S(1)}, u32[]{:S(2)}) copy-start(f32[1,128,128]{2,1,0:T(8,128)S(1)} %get-tuple-element.24) | copy-start | bytes 196612
  30.9 4.3 %collective-permute-start.10 = (f32[1,128,128]{2,1,0:T(8,128)S(1)}, f32[1,128,128]{2,1,0:T(8,128)S(1)}, u32[]{:S(2)}, u32[]{:S(2)}) collective-permute-start(f32[1,128,128]{2,1,0:T(8,128)S(1)} %get-tuple-element.24), channel_id=1, source_target_pairs={{0,2},{1,3},{2,0},{3,1},{4,6},{5,7},{6,4},{7,5},{8,10},{9,11},{10,... | collective-permute-start | bytes 196616 | tf_op jit(solution)/shard_map/ppermute | solution.py:13
  35.1 7.4 %collective-permute-start.11 = (f32[2,128,128]{2,1,0:T(8,128)S(1)}, f32[2,128,128]{2,1,0:T(8,128)S(1)}, u32[]{:S(2)}, u32[]{:S(2)}) collective-permute-start(f32[2,128,128]{2,1,0:T(8,128)S(1)} %pad_maximum_fusion.1), channel_id=1, source_target_pairs={{0,16},{1,17},{2,18},{3,19},{4,20},{5,21},{6,22},{7,23},{8,24},{9,... | collective-permute-start | bytes 393224 | tf_op jit(solution)/shard_map/ppermute | solution.py:13
  42.6 6.9 %collective-permute-start.12 = (f32[4,128,128]{2,1,0:T(8,128)S(1)}, f32[4,128,128]{2,1,0:T(8,128)S(1)}, u32[]{:S(2)}, u32[]{:S(2)}) collective-permute-start(f32[4,128,128]{2,1,0:T(8,128)S(1)} %pad_maximum_fusion), channel_id=1, source_target_pairs={{0,8},{1,9},{2,10},{3,11},{4,12},{5,13},{6,14},{7,15},{8,0},{9,1},... | collective-permute-start | bytes 786440 | tf_op jit(solution)/shard_map/ppermute | solution.py:13
  43.4 8.5 %collective-permute-start.13 = (f32[4,128,128]{2,1,0:T(8,128)S(1)}, f32[4,128,128]{2,1,0:T(8,128)S(1)}, u32[]{:S(2)}, u32[]{:S(2)}) collective-permute-start(f32[4,128,128]{2,1,0:T(8,128)S(1)} %pad_maximum_fusion), channel_id=1, source_target_pairs={{0,4},{1,5},{2,6},{3,7},{4,0},{5,1},{6,2},{7,3},{8,12},{9,13},{10,... | collective-permute-start | bytes 786440 | tf_op jit(solution)/shard_map/ppermute | solution.py:13
  45.8 7.3 %collective-permute-start.14 = (f32[4,128,128]{2,1,0:T(8,128)S(1)}, f32[4,128,128]{2,1,0:T(8,128)S(1)}, u32[]{:S(2)}, u32[]{:S(2)}) collective-permute-start(f32[4,128,128]{2,1,0:T(8,128)S(1)} %pad_maximum_fusion), channel_id=1, source_target_pairs={{0,12},{1,13},{2,14},{3,15},{4,8},{5,9},{6,10},{7,11},{8,4},{9,5},... | collective-permute-start | bytes 786440 | tf_op jit(solution)/shard_map/ppermute | solution.py:13
  53.8 3.0 %collective-permute-start.15 = (f32[16,128,128]{2,1,0:T(8,128)}, f32[16,128,128]{2,1,0:T(8,128)}, u32[]{:S(2)}, u32[]{:S(2)}) collective-permute-start(f32[16,128,128]{2,1,0:T(8,128)} %constant_dynamic-update-slice_fusion.13), channel_id=1, source_target_pairs={{0,1},{1,0},{2,3},{3,2},{4,5},{5,4},{6,7},{7,6},{8,9},{9,8},{10,11... | collective-permute-start | bytes 3145736 | tf_op jit(solution)/shard_map/ppermute | solution.py:119
  54.2 5.4 %copy-start.6 = (s32[8,256]{1,0:T(8,128)S(1)}, s32[8,256]{1,0:T(8,128)}, u32[]{:S(2)}) copy-start(s32[8,256]{1,0:T(8,128)} %param.23) | copy-start | bytes 24580
  63.2 3.5 %copy-start.3 = (f32[8,256,256]{2,1,0:T(8,128)S(1)}, f32[8,256,256]{2,1,0:T(8,128)}, u32[]{:S(2)}) copy-start(f32[8,256,256]{2,1,0:T(8,128)} %param.26) | copy-start | bytes 6291460
  (5 other events, 7.7 us)

commit v11 on v10

--- a/solution.py
+++ b/solution.py
@@ -111,6 +111,7 @@
     own_inverse = lax.dynamic_slice_in_dim(upper_inverse[0], begin, share, 1)
     own_base = jnp.einsum("kw,kr->wr", own_inverse, upper_rhs[0], precision=highest)
 
+    total = lax.optimization_barrier(total)
     top_held = xor_gather(top_solution, both, count, top_groups).reshape(count * top_rows, rhs)
     own_rows = own_base - jnp.einsum("wj,jr->wr", total, top_held, precision=highest)
 

time: 70.7 us -> 70.7 us (level)
  matrix products: 16.3 us -> 15.1 us
  other arithmetic: 1.15 us -> 2.34 us
    add x0 -> x1, other arithmetic: none -> 1.2 us  [local(): total + lax.ppermute(outgoing, 'panel', [(i, i ^ v) for i in range(panels)])]
    dot_general x1, matrix products: 2.37 us -> 1.23 us  [local(): jnp.einsum('wj,jr->wr', total, top_held, precision=highest)]
where the time goes in v11:
time: 70.7 us; the launch traced here: 70.2 us
  starting transfers between devices  21.7 us (31%)
  waiting for transfers between devices  16.6 us (23%)
  matrix products  15.1 us (21%)
  local copies, waits for them, and re-layouts  13.4 us (19%)
  other arithmetic  2.34 us (3%)
  between operations  1.01 us (1%)
    ppermute x12, starting transfers between devices, xor_gather(): parts.append(lax.ppermute(held, axes, [(i, i ^ v) for i in range(count)]))  19.4 us
    ppermute x12, waiting for transfers between devices, xor_gather(): parts.append(lax.ppermute(held, axes, [(i, i ^ v) for i in range(count)]))  15.9 us
    unnamed x37, local copies, waits for them, and re-layouts  4.97 us
    gather x2, local copies, waits for them, and re-layouts, local(): slabs = source[places].reshape(position.shape[0], -1, own_rows.shape[1])  4.66 us
    dot_general x2, matrix products, local(): term = jnp.einsum('skj,sjr->skr', pick, slabs, precision=highest)  3.6 us
    dot_general x1, matrix products, local(): jnp.einsum('swk,skr->swr', panel_t, parent_rows, precision=highest)  3.52 us
    dot_general x1, matrix products, local(): jnp.einsum('kv,vw->kw', upper_panel[0], upper_inverse[0], precision=highest)  2.44 us
    ppermute x3, starting transfers between devices, local(): lax.ppermute(outgoing, 'panel', [(i, i ^ v) for i in range(panels)])  2.34 us
  transfers between devices with their start and end apart: 16, of which 9 were waited for; matrix products, arithmetic and copies ran while one was open for 19% of the time, Pallas kernels for 0%

profile of v11, /device:TPU:0, one launch (start us, length us, event | category | flops | bytes accessed | tf_op | source)
XLA Modules:
  0.0 70.2 jit_solution(1721896617293710514)
XLA Ops:
  1.2 2.6 %collective-permute-start.4 = (f32[1,16,128]{2,1,0:T(8,128)}, f32[1,16,128]{2,1,0:T(8,128)S(1)}, u32[]{:S(2)}, u32[]{:S(2)}) collective-permute-start(f32[1,16,128]{2,1,0:T(8,128)} %bitcast.66), channel_id=1, source_target_pairs={{0,2},{1,3},{2,0},{3,1},{4,6},{5,7},{6,4},{7,5},{8,10},{9,11},{10,... | collective-permute-start | bytes 24584 | tf_op jit(solution)/shard_map/ppermute | solution.py:13
  5.1 2.4 %fusion.9 = f32[256,512]{1,0:T(8,128)S(1)} fusion(f32[1,512,512]{2,1,0:T(8,128)} %param.18, f32[1,256,512]{2,1,0:T(8,128)} %param.17), kind=kOutput, calls=%fused_computation.16 | convolution fusion | flops 805306368 | bytes 2097152 | tf_op jit(solution)/shard_map/kv,vw->kw/dot_general | solution.py:102
  9.8 1.7 %collective-permute-start.2 = (f32[128,512]{0,1:T(8,128)S(1)}, f32[128,512]{0,1:T(8,128)}, u32[]{:S(2)}, u32[]{:S(2)}) collective-permute-start(f32[128,512]{0,1:T(8,128)S(1)} %bitcast.59), channel_id=1, source_target_pairs={{0,3},{1,2},{2,1},{3,0},{4,7},{5,6},{6,5},{7,4},{8,11},{9,10},{10,... | collective-permute-start | bytes 786440 | tf_op jit(solution)/shard_map/ppermute | solution.py:110
  13.4 2.9 %collective-permute-start.6 = (f32[4,16,128]{2,1,0:T(8,128)S(1)}, f32[4,16,128]{2,1,0:T(8,128)S(1)}, u32[]{:S(2)}, u32[]{:S(2)}) collective-permute-start(f32[4,16,128]{2,1,0:T(8,128)S(1)} %pad_maximum_fusion.2), channel_id=1, source_target_pairs={{0,16},{1,17},{2,18},{3,19},{4,20},{5,21},{6,22},{7,23},{8,24},{9,... | collective-permute-start | bytes 98312 | tf_op jit(solution)/shard_map/ppermute | solution.py:13
  16.3 2.0 %collective-permute-done.6 = f32[4,16,128]{2,1,0:T(8,128)S(1)} collective-permute-done((f32[4,16,128]{2,1,0:T(8,128)S(1)}, f32[4,16,128]{2,1,0:T(8,128)S(1)}, u32[]{:S(2)}, u32[]{:S(2)}) %collective-permute-start.6) | collective-permute-done | bytes 32800 | tf_op jit(solution)/shard_map/ppermute | solution.py:13
  18.3 1.8 %collective-permute-start.7 = (f32[8,16,128]{2,1,0:T(8,128)S(1)}, f32[8,16,128]{2,1,0:T(8,128)S(1)}, u32[]{:S(2)}, u32[]{:S(2)}) collective-permute-start(f32[8,16,128]{2,1,0:T(8,128)S(1)} %get-tuple-element.9), channel_id=1, source_target_pairs={{0,8},{1,9},{2,10},{3,11},{4,12},{5,13},{6,14},{7,15},{8,0},{9,1},... | collective-permute-start | bytes 196616 | tf_op jit(solution)/shard_map/ppermute | solution.py:13
  20.1 1.6 %fusion.18 = f32[128,128]{1,0:T(8,128)S(1)} fusion(f32[1,512,128]{2,1,0:T(8,128)} %param.16, f32[1,512,512]{2,1,0:T(8,128)} %param.18, s32[]{:T(128)S(6)} %select_n.96), kind=kOutput, calls=%fused_computation.26 | convolution fusion | flops 100663296 | bytes 589828 | tf_op jit(solution)/shard_map/kw,kr->wr/dot_general | solution.py:112
  21.7 1.6 %collective-permute-start.8 = (f32[8,16,128]{2,1,0:T(8,128)S(1)}, f32[8,16,128]{2,1,0:T(8,128)S(1)}, u32[]{:S(2)}, u32[]{:S(2)}) collective-permute-start(f32[8,16,128]{2,1,0:T(8,128)S(1)} %get-tuple-element.9), channel_id=1, source_target_pairs={{0,4},{1,5},{2,6},{3,7},{4,0},{5,1},{6,2},{7,3},{8,12},{9,13},{10,... | collective-permute-start | bytes 196616 | tf_op jit(solution)/shard_map/ppermute | solution.py:13
  23.3 2.0 %collective-permute-start.9 = (f32[8,16,128]{2,1,0:T(8,128)S(1)}, f32[8,16,128]{2,1,0:T(8,128)S(1)}, u32[]{:S(2)}, u32[]{:S(2)}) collective-permute-start(f32[8,16,128]{2,1,0:T(8,128)S(1)} %get-tuple-element.9), channel_id=1, source_target_pairs={{0,12},{1,13},{2,14},{3,15},{4,8},{5,9},{6,10},{7,11},{8,4},{9,5},... | collective-permute-start | bytes 196616 | tf_op jit(solution)/shard_map/ppermute | solution.py:13
  25.3 1.3 %collective-permute-done.8 = f32[8,16,128]{2,1,0:T(8,128)S(1)} collective-permute-done((f32[8,16,128]{2,1,0:T(8,128)S(1)}, f32[8,16,128]{2,1,0:T(8,128)S(1)}, u32[]{:S(2)}, u32[]{:S(2)}) %collective-permute-start.8) | collective-permute-done | bytes 65568 | tf_op jit(solution)/shard_map/ppermute | solution.py:13
  26.7 1.8 %collective-permute-done.9 = f32[8,16,128]{2,1,0:T(8,128)S(1)} collective-permute-done((f32[8,16,128]{2,1,0:T(8,128)S(1)}, f32[8,16,128]{2,1,0:T(8,128)S(1)}, u32[]{:S(2)}, u32[]{:S(2)}) %collective-permute-start.9) | collective-permute-done | bytes 65568 | tf_op jit(solution)/shard_map/ppermute | solution.py:13
  30.9 1.5 %collective-permute-start.10 = (f32[1,128,128]{2,1,0:T(8,128)S(1)}, f32[1,128,128]{2,1,0:T(8,128)S(1)}, u32[]{:S(2)}, u32[]{:S(2)}) collective-permute-start(f32[1,128,128]{2,1,0:T(8,128)S(1)} %get-tuple-element.24), channel_id=1, source_target_pairs={{0,2},{1,3},{2,0},{3,1},{4,6},{5,7},{6,4},{7,5},{8,10},{9,11},{10,... | collective-permute-start | bytes 196616 | tf_op jit(solution)/shard_map/ppermute | solution.py:13
  32.4 2.7 %collective-permute-done.10 = f32[1,128,128]{2,1,0:T(8,128)S(1)} collective-permute-done((f32[1,128,128]{2,1,0:T(8,128)S(1)}, f32[1,128,128]{2,1,0:T(8,128)S(1)}, u32[]{:S(2)}, u32[]{:S(2)}) %collective-permute-start.10) | collective-permute-done | bytes 65568 | tf_op jit(solution)/shard_map/ppermute | solution.py:13
  35.2 2.9 %collective-permute-start.11 = (f32[2,128,128]{2,1,0:T(8,128)S(1)}, f32[2,128,128]{2,1,0:T(8,128)S(1)}, u32[]{:S(2)}, u32[]{:S(2)}) collective-permute-start(f32[2,128,128]{2,1,0:T(8,128)S(1)} %pad_maximum_fusion.1), channel_id=1, source_target_pairs={{0,16},{1,17},{2,18},{3,19},{4,20},{5,21},{6,22},{7,23},{8,24},{9,... | collective-permute-start | bytes 393224 | tf_op jit(solution)/shard_map/ppermute | solution.py:13
  38.1 4.5 %collective-permute-done.11 = f32[2,128,128]{2,1,0:T(8,128)S(1)} collective-permute-done((f32[2,128,128]{2,1,0:T(8,128)S(1)}, f32[2,128,128]{2,1,0:T(8,128)S(1)}, u32[]{:S(2)}, u32[]{:S(2)}) %collective-permute-start.11) | collective-permute-done | bytes 131104 | tf_op jit(solution)/shard_map/ppermute | solution.py:13
  43.4 1.8 %collective-permute-start.13 = (f32[4,128,128]{2,1,0:T(8,128)S(1)}, f32[4,128,128]{2,1,0:T(8,128)S(1)}, u32[]{:S(2)}, u32[]{:S(2)}) collective-permute-start(f32[4,128,128]{2,1,0:T(8,128)S(1)} %pad_maximum_fusion), channel_id=1, source_target_pairs={{0,4},{1,5},{2,6},{3,7},{4,0},{5,1},{6,2},{7,3},{8,12},{9,13},{10,... | collective-permute-start | bytes 786440 | tf_op jit(solution)/shard_map/ppermute | solution.py:13
  45.8 1.7 %collective-permute-start.14 = (f32[4,128,128]{2,1,0:T(8,128)S(1)}, f32[4,128,128]{2,1,0:T(8,128)S(1)}, u32[]{:S(2)}, u32[]{:S(2)}) collective-permute-start(f32[4,128,128]{2,1,0:T(8,128)S(1)} %pad_maximum_fusion), channel_id=1, source_target_pairs={{0,12},{1,13},{2,14},{3,15},{4,8},{5,9},{6,10},{7,11},{8,4},{9,5},... | collective-permute-start | bytes 786440 | tf_op jit(solution)/shard_map/ppermute | solution.py:13
  48.2 1.3 %collective-permute-done.12 = f32[4,128,128]{2,1,0:T(8,128)S(1)} collective-permute-done((f32[4,128,128]{2,1,0:T(8,128)S(1)}, f32[4,128,128]{2,1,0:T(8,128)S(1)}, u32[]{:S(2)}, u32[]{:S(2)}) %collective-permute-start.12) | collective-permute-done | bytes 262176 | tf_op jit(solution)/shard_map/ppermute | solution.py:13
  50.3 1.6 %collective-permute-done.13 = f32[4,128,128]{2,1,0:T(8,128)S(1)} collective-permute-done((f32[4,128,128]{2,1,0:T(8,128)S(1)}, f32[4,128,128]{2,1,0:T(8,128)S(1)}, u32[]{:S(2)}, u32[]{:S(2)}) %collective-permute-start.13) | collective-permute-done | bytes 262176 | tf_op jit(solution)/shard_map/ppermute | solution.py:13
  54.3 1.9 %gather_fusion.4 = f32[16,128,128]{2,1,0:T(8,128)S(1)} fusion(f32[16,128,128]{2,1,0:T(8,128)} %constant_dynamic-update-slice_fusion.13, s32[1024]{0:T(1024)S(1)} %pad_clamp_fusion.1), kind=kCustom, calls=%fused_computation.4 | custom fusion | bytes 2097216 | tf_op jit(solution)/shard_map/gather | solution.py:128
  56.8 2.8 %gather_fusion.5 = f32[16,128,128]{2,1,0:T(8,128)} fusion(f32[16,128,128]{2,1,0:T(8,128)} %collective-permute-done.15, s32[1024]{0:T(1024)S(1)} %pad_clamp_fusion), kind=kCustom, calls=%fused_computation.5 | custom fusion | bytes 2097216 | tf_op jit(solution)/shard_map/gather | solution.py:128
  59.6 2.4 %fusion = f32[8,256,128]{2,1,0:T(8,128)S(1)} fusion(f32[8,256,128]{2,1,0:T(8,128)} %bitcast.63, s32[256]{0:T(256)S(1)} %add_bitcast_fusion, s32[8,256]{1,0:T(8,128)S(1)} %copy-done.6), kind=kOutput, calls=%fused_computation.6 | convolution fusion | flops 805830656 | bytes 2106368 | tf_op jit(solution)/shard_map/skj,sjr->skr/dot_general | solution.py:132
  63.3 3.5 %fusion.7 = f32[8,256,128]{2,1,0:T(8,128)S(1)} fusion(f32[8,256,128]{2,1,0:T(8,128)S(1)} %copy-done.4, f32[8,256,128]{2,1,0:T(8,128)S(1)} %fusion.4, f32[8,256,256]{2,1,0:T(8,128)S(1)} %copy-done), kind=kOutput, calls=%fused_computation.13 | convolution fusion | flops 805568512 | bytes 5242880 | tf_op jit(solution)/shard_map/swk,skr->swr/dot_general | solution.py:137
  66.8 2.0 %convolution_bitcast_fusion = f32[8,256,128]{1,2,0:T(8,128)S(1)} fusion(f32[8,256,128]{2,1,0:T(8,128)S(1)} %fusion.7, f32[8,256,256]{2,1,0:T(8,128)S(1)} %copy-done.3), kind=kOutput, calls=%fused_computation.11 | convolution fusion | flops 805306368 | bytes 4194304 | tf_op jit(solution)/shard_map/swk,skr->swr/dot_general | solution.py:138
  (92 shorter events, 16.6 us)
Async XLA Ops:
  0.6 62.6 %copy-start = (f32[8,256,256]{2,1,0:T(8,128)S(1)}, f32[8,256,256]{2,1,0:T(8,128)}, u32[]{:S(2)}) copy-start(f32[8,256,256]{2,1,0:T(8,128)} %param.24) | copy-start | bytes 6291460
  0.6 6.9 %copy-start.12 = (s32[32]{0:T(128)S(1)}, s32[32]{0:T(128)}, u32[]{:S(2)}) copy-start(s32[32]{0:T(128)} %constant.145) | copy-start | bytes 388
  0.7 6.9 %copy-start.8 = (s32[1,256]{1,0:T(1,128)S(1)}, s32[1,256]{1,0:T(1,128)}, u32[]{:S(2)}) copy-start(s32[1,256]{1,0:T(1,128)} %param.19) | copy-start | bytes 3076
  0.7 12.4 %collective-permute-start.3 = (f32[1,16,128]{2,1,0:T(8,128)}, f32[1,16,128]{2,1,0:T(8,128)S(1)}, u32[]{:S(2)}, u32[]{:S(2)}) collective-permute-start(f32[1,16,128]{2,1,0:T(8,128)} %bitcast.65), channel_id=1, source_target_pairs={{0,1},{1,0},{2,3},{3,2},{4,5},{5,4},{6,7},{7,6},{8,9},{9,8},{10,11... | collective-permute-start | bytes 24584 | tf_op jit(solution)/shard_map/ppermute | solution.py:13
  1.2 12.2 %collective-permute-start.4 = (f32[1,16,128]{2,1,0:T(8,128)}, f32[1,16,128]{2,1,0:T(8,128)S(1)}, u32[]{:S(2)}, u32[]{:S(2)}) collective-permute-start(f32[1,16,128]{2,1,0:T(8,128)} %bitcast.66), channel_id=1, source_target_pairs={{0,2},{1,3},{2,0},{3,1},{4,6},{5,7},{6,4},{7,5},{8,10},{9,11},{10,... | collective-permute-start | bytes 24584 | tf_op jit(solution)/shard_map/ppermute | solution.py:13
  3.8 9.7 %collective-permute-start.5 = (f32[1,16,128]{2,1,0:T(8,128)}, f32[1,16,128]{2,1,0:T(8,128)S(1)}, u32[]{:S(2)}, u32[]{:S(2)}) collective-permute-start(f32[1,16,128]{2,1,0:T(8,128)} %bitcast.67), channel_id=1, source_target_pairs={{0,3},{1,2},{2,1},{3,0},{4,7},{5,6},{6,5},{7,4},{8,11},{9,10},{10,... | collective-permute-start | bytes 24584 | tf_op jit(solution)/shard_map/ppermute | solution.py:13
  9.8 18.6 %collective-permute-start.2 = (f32[128,512]{0,1:T(8,128)S(1)}, f32[128,512]{0,1:T(8,128)}, u32[]{:S(2)}, u32[]{:S(2)}) collective-permute-start(f32[128,512]{0,1:T(8,128)S(1)} %bitcast.59), channel_id=1, source_target_pairs={{0,3},{1,2},{2,1},{3,0},{4,7},{5,6},{6,5},{7,4},{8,11},{9,10},{10,... | collective-permute-start | bytes 786440 | tf_op jit(solution)/shard_map/ppermute | solution.py:110
  12.2 16.3 %collective-permute-start = (f32[128,512]{0,1:T(8,128)S(1)}, f32[128,512]{0,1:T(8,128)}, u32[]{:S(2)}, u32[]{:S(2)}) collective-permute-start(f32[128,512]{0,1:T(8,128)S(1)} %bitcast.60), channel_id=1, source_target_pairs={{0,1},{1,0},{2,3},{3,2},{4,5},{5,4},{6,7},{7,6},{8,9},{9,8},{10,11... | collective-permute-start | bytes 786440 | tf_op jit(solution)/shard_map/ppermute | solution.py:110
  13.0 29.7 %copy-start.9 = (s32[2]{0:T(128)S(1)}, s32[2]{0:T(128)}, u32[]{:S(2)}) copy-start(s32[2]{0:T(128)} %constant.120.clone) | copy-start | bytes 28
  13.0 29.7 %copy-start.1 = (s32[8]{0:T(128)S(1)}, s32[8]{0:T(128)}, u32[]{:S(2)}) copy-start(s32[8]{0:T(128)} %param.21) | copy-start | bytes 100
  13.1 15.4 %collective-permute-start.1 = (f32[128,512]{0,1:T(8,128)S(1)}, f32[128,512]{0,1:T(8,128)S(1)}, u32[]{:S(2)}, u32[]{:S(2)}) collective-permute-start(f32[128,512]{0,1:T(8,128)S(1)} %bitcast.61), channel_id=1, source_target_pairs={{0,2},{1,3},{2,0},{3,1},{4,6},{5,7},{6,4},{7,5},{8,10},{9,11},{10,... | collective-permute-start | bytes 786440 | tf_op jit(solution)/shard_map/ppermute | solution.py:110
  13.4 4.9 %collective-permute-start.6 = (f32[4,16,128]{2,1,0:T(8,128)S(1)}, f32[4,16,128]{2,1,0:T(8,128)S(1)}, u32[]{:S(2)}, u32[]{:S(2)}) collective-permute-start(f32[4,16,128]{2,1,0:T(8,128)S(1)} %pad_maximum_fusion.2), channel_id=1, source_target_pairs={{0,16},{1,17},{2,18},{3,19},{4,20},{5,21},{6,22},{7,23},{8,24},{9,... | collective-permute-start | bytes 98312 | tf_op jit(solution)/shard_map/ppermute | solution.py:13
  18.3 5.0 %collective-permute-start.7 = (f32[8,16,128]{2,1,0:T(8,128)S(1)}, f32[8,16,128]{2,1,0:T(8,128)S(1)}, u32[]{:S(2)}, u32[]{:S(2)}) collective-permute-start(f32[8,16,128]{2,1,0:T(8,128)S(1)} %get-tuple-element.9), channel_id=1, source_target_pairs={{0,8},{1,9},{2,10},{3,11},{4,12},{5,13},{6,14},{7,15},{8,0},{9,1},... | collective-permute-start | bytes 196616 | tf_op jit(solution)/shard_map/ppermute | solution.py:13
  21.7 4.9 %collective-permute-start.8 = (f32[8,16,128]{2,1,0:T(8,128)S(1)}, f32[8,16,128]{2,1,0:T(8,128)S(1)}, u32[]{:S(2)}, u32[]{:S(2)}) collective-permute-start(f32[8,16,128]{2,1,0:T(8,128)S(1)} %get-tuple-element.9), channel_id=1, source_target_pairs={{0,4},{1,5},{2,6},{3,7},{4,0},{5,1},{6,2},{7,3},{8,12},{9,13},{10,... | collective-permute-start | bytes 196616 | tf_op jit(solution)/shard_map/ppermute | solution.py:13
  23.3 5.2 %collective-permute-start.9 = (f32[8,16,128]{2,1,0:T(8,128)S(1)}, f32[8,16,128]{2,1,0:T(8,128)S(1)}, u32[]{:S(2)}, u32[]{:S(2)}) collective-permute-start(f32[8,16,128]{2,1,0:T(8,128)S(1)} %get-tuple-element.9), channel_id=1, source_target_pairs={{0,12},{1,13},{2,14},{3,15},{4,8},{5,9},{6,10},{7,11},{8,4},{9,5},... | collective-permute-start | bytes 196616 | tf_op jit(solution)/shard_map/ppermute | solution.py:13
  30.9 25.2 %copy-start.5 = (f32[1,128,128]{2,1,0:T(8,128)}, f32[1,128,128]{2,1,0:T(8,128)S(1)}, u32[]{:S(2)}) copy-start(f32[1,128,128]{2,1,0:T(8,128)S(1)} %get-tuple-element.24) | copy-start | bytes 196612
  30.9 4.3 %collective-permute-start.10 = (f32[1,128,128]{2,1,0:T(8,128)S(1)}, f32[1,128,128]{2,1,0:T(8,128)S(1)}, u32[]{:S(2)}, u32[]{:S(2)}) collective-permute-start(f32[1,128,128]{2,1,0:T(8,128)S(1)} %get-tuple-element.24), channel_id=1, source_target_pairs={{0,2},{1,3},{2,0},{3,1},{4,6},{5,7},{6,4},{7,5},{8,10},{9,11},{10,... | collective-permute-start | bytes 196616 | tf_op jit(solution)/shard_map/ppermute | solution.py:13
  35.2 7.4 %collective-permute-start.11 = (f32[2,128,128]{2,1,0:T(8,128)S(1)}, f32[2,128,128]{2,1,0:T(8,128)S(1)}, u32[]{:S(2)}, u32[]{:S(2)}) collective-permute-start(f32[2,128,128]{2,1,0:T(8,128)S(1)} %pad_maximum_fusion.1), channel_id=1, source_target_pairs={{0,16},{1,17},{2,18},{3,19},{4,20},{5,21},{6,22},{7,23},{8,24},{9,... | collective-permute-start | bytes 393224 | tf_op jit(solution)/shard_map/ppermute | solution.py:13
  42.7 6.9 %collective-permute-start.12 = (f32[4,128,128]{2,1,0:T(8,128)S(1)}, f32[4,128,128]{2,1,0:T(8,128)S(1)}, u32[]{:S(2)}, u32[]{:S(2)}) collective-permute-start(f32[4,128,128]{2,1,0:T(8,128)S(1)} %pad_maximum_fusion), channel_id=1, source_target_pairs={{0,8},{1,9},{2,10},{3,11},{4,12},{5,13},{6,14},{7,15},{8,0},{9,1},... | collective-permute-start | bytes 786440 | tf_op jit(solution)/shard_map/ppermute | solution.py:13
  43.4 8.5 %collective-permute-start.13 = (f32[4,128,128]{2,1,0:T(8,128)S(1)}, f32[4,128,128]{2,1,0:T(8,128)S(1)}, u32[]{:S(2)}, u32[]{:S(2)}) collective-permute-start(f32[4,128,128]{2,1,0:T(8,128)S(1)} %pad_maximum_fusion), channel_id=1, source_target_pairs={{0,4},{1,5},{2,6},{3,7},{4,0},{5,1},{6,2},{7,3},{8,12},{9,13},{10,... | collective-permute-start | bytes 786440 | tf_op jit(solution)/shard_map/ppermute | solution.py:13
  45.8 7.3 %collective-permute-start.14 = (f32[4,128,128]{2,1,0:T(8,128)S(1)}, f32[4,128,128]{2,1,0:T(8,128)S(1)}, u32[]{:S(2)}, u32[]{:S(2)}) collective-permute-start(f32[4,128,128]{2,1,0:T(8,128)S(1)} %pad_maximum_fusion), channel_id=1, source_target_pairs={{0,12},{1,13},{2,14},{3,15},{4,8},{5,9},{6,10},{7,11},{8,4},{9,5},... | collective-permute-start | bytes 786440 | tf_op jit(solution)/shard_map/ppermute | solution.py:13
  53.8 3.0 %collective-permute-start.15 = (f32[16,128,128]{2,1,0:T(8,128)}, f32[16,128,128]{2,1,0:T(8,128)}, u32[]{:S(2)}, u32[]{:S(2)}) collective-permute-start(f32[16,128,128]{2,1,0:T(8,128)} %constant_dynamic-update-slice_fusion.13), channel_id=1, source_target_pairs={{0,1},{1,0},{2,3},{3,2},{4,5},{5,4},{6,7},{7,6},{8,9},{9,8},{10,11... | collective-permute-start | bytes 3145736 | tf_op jit(solution)/shard_map/ppermute | solution.py:120
  54.3 5.4 %copy-start.6 = (s32[8,256]{1,0:T(8,128)S(1)}, s32[8,256]{1,0:T(8,128)}, u32[]{:S(2)}) copy-start(s32[8,256]{1,0:T(8,128)} %param.23) | copy-start | bytes 24580
  63.3 3.5 %copy-start.3 = (f32[8,256,256]{2,1,0:T(8,128)S(1)}, f32[8,256,256]{2,1,0:T(8,128)}, u32[]{:S(2)}) copy-start(f32[8,256,256]{2,1,0:T(8,128)} %param.26) | copy-start | bytes 6291460
  (5 other events, 7.7 us)

commit v12 on v10

--- a/solution.py
+++ b/solution.py
@@ -7,12 +7,16 @@
 def xor_gather(block, axes, count, groups):
     held = block[None]
     for bits in groups:
-        parts = [held]
-        for k in range(1, 1 << len(bits)):
-            v = sum(((k >> t) & 1) << b for t, b in enumerate(bits))
-            parts.append(lax.ppermute(held, axes, [(i, i ^ v) for i in range(count)]))
-        held = jnp.concatenate(parts, 0)
+        held = xor_gather_step(held, axes, count, bits)
     return held
+
+
+def xor_gather_step(held, axes, count, bits):
+    parts = [held]
+    for k in range(1, 1 << len(bits)):
+        v = sum(((k >> t) & 1) << b for t, b in enumerate(bits))
+        parts.append(lax.ppermute(held, axes, [(i, i ^ v) for i in range(count)]))
+    return jnp.concatenate(parts, 0)
 
 
 def xor_position(offset, groups):
@@ -99,7 +103,9 @@
     within = lax.broadcasted_iota(jnp.int32, (count, top_rows), 1)
     natural = ((me ^ xor_offset(places, top_groups)) * top_rows + within).reshape(-1)
     pick_top = (top_index[0][:, None] == natural[None, :]).astype(jnp.float32)
-    folded = jnp.einsum("kv,vw->kw", upper_panel[0], upper_inverse[0], precision=highest)
+    top_first = xor_gather_step(top_solution[None], both, count, top_groups[0])
+    top_first, panel_rows = lax.optimization_barrier((top_first, upper_panel[0]))
+    folded = jnp.einsum("kv,vw->kw", panel_rows, upper_inverse[0], precision=highest)
     weights = jnp.einsum("kj,kw->wj", pick_top, folded, precision=highest)
     total = lax.dynamic_slice_in_dim(weights, begin, share, 0)
     for v in range(1, panels):
@@ -111,7 +117,10 @@
     own_inverse = lax.dynamic_slice_in_dim(upper_inverse[0], begin, share, 1)
     own_base = jnp.einsum("kw,kr->wr", own_inverse, upper_rhs[0], precision=highest)
 
-    top_held = xor_gather(top_solution, both, count, top_groups).reshape(count * top_rows, rhs)
+    top_held = top_first
+    for bits in top_groups[1:]:
+        top_held = xor_gather_step(top_held, both, count, bits)
+    top_held = top_held.reshape(count * top_rows, rhs)
     own_rows = own_base - jnp.einsum("wj,jr->wr", total, top_held, precision=highest)
 
     held = xor_gather(own_rows, both, count, spread_groups[:-1])

time: 70.7 us -> 78.8 us (1.11)
  waiting for transfers between devices: 16.6 us -> 25.2 us
  starting transfers between devices: 21.7 us -> 18.2 us
  other arithmetic: 1.15 us -> 3.19 us
  local copies, waits for them, and re-layouts: 13.3 us -> 14.6 us
    ppermute x12, waiting for transfers between devices: 15.9 us -> 20.7 us  [xor_gather_step(): parts.append(lax.ppermute(held, axes, [(i, i ^ v) for i in range(count)]))]
    ppermute x3, waiting for transfers between devices: 0.01 us -> 3.85 us  [local(): lax.ppermute(outgoing, 'panel', [(i, i ^ v) for i in range(panels)])]
    ppermute x12, starting transfers between devices: 19.4 us -> 15.8 us  [xor_gather_step(): parts.append(lax.ppermute(held, axes, [(i, i ^ v) for i in range(count)]))]
    unnamed x37 -> x26, local copies, waits for them, and re-layouts: 4.95 us -> 5.58 us
  transfers between devices with their start and end apart: 16 -> 16, of which waited for: 9 -> 9; matrix products, arithmetic and copies ran while one was open for 19% -> 21% of each run, Pallas kernels for 0% -> 0%
where the time goes in v12:
time: 78.8 us; the launch traced here: 78.4 us
  waiting for transfers between devices  25.2 us (32%)
  starting transfers between devices  18.2 us (23%)
  matrix products  16.2 us (21%)
  local copies, waits for them, and re-layouts  14.6 us (19%)
  other arithmetic  3.19 us (4%)
  between operations  0.96 us (1%)
    ppermute x12, waiting for transfers between devices, xor_gather_step(): parts.append(lax.ppermute(held, axes, [(i, i ^ v) for i in range(count)]))  20.7 us
    ppermute x12, starting transfers between devices, xor_gather_step(): parts.append(lax.ppermute(held, axes, [(i, i ^ v) for i in range(count)]))  15.8 us
    unnamed x26, local copies, waits for them, and re-layouts  5.58 us
    gather x2, local copies, waits for them, and re-layouts, local(): slabs = source[places].reshape(position.shape[0], -1, own_rows.shape[1])  4.66 us
    ppermute x3, waiting for transfers between devices, local(): lax.ppermute(outgoing, 'panel', [(i, i ^ v) for i in range(panels)])  3.85 us
    dot_general x2, matrix products, local(): term = jnp.einsum('skj,sjr->skr', pick, slabs, precision=highest)  3.6 us
    dot_general x1, matrix products, local(): jnp.einsum('swk,skr->swr', panel_t, parent_rows, precision=highest)  3.52 us
    dot_general x1, matrix products, local(): jnp.einsum('kv,vw->kw', panel_rows, upper_inverse[0], precision=highest)  2.44 us
  transfers between devices with their start and end apart: 16, of which 9 were waited for; matrix products, arithmetic and copies ran while one was open for 21% of the time, Pallas kernels for 0%

profile of v12, /device:TPU:0, one launch (start us, length us, event | category | flops | bytes accessed | tf_op | source)
XLA Modules:
  0.0 78.4 jit_solution(7679827048152979731)
XLA Ops:
  1.2 2.6 %collective-permute-start.1 = (f32[1,16,128]{2,1,0:T(8,128)}, f32[1,16,128]{2,1,0:T(8,128)S(1)}, u32[]{:S(2)}, u32[]{:S(2)}) collective-permute-start(f32[1,16,128]{2,1,0:T(8,128)} %bitcast.63), channel_id=1, source_target_pairs={{0,2},{1,3},{2,0},{3,1},{4,6},{5,7},{6,4},{7,5},{8,10},{9,11},{10,... | collective-permute-start | bytes 24584 | tf_op jit(solution)/shard_map/ppermute | solution.py:18
  5.7 1.6 %fusion.17 = f32[128,128]{1,0:T(8,128)S(1)} fusion(f32[1,512,128]{2,1,0:T(8,128)} %param.16, f32[1,512,512]{2,1,0:T(8,128)} %param.18, s32[]{:T(128)S(6)} %select_n.96), kind=kOutput, calls=%fused_computation.25 | convolution fusion | flops 100663296 | bytes 589828 | tf_op jit(solution)/shard_map/kw,kr->wr/dot_general | solution.py:118
  8.8 2.8 %collective-permute-start.6 = (f32[4,16,128]{2,1,0:T(8,128)S(1)}, f32[4,16,128]{2,1,0:T(8,128)S(1)}, u32[]{:S(2)}, u32[]{:S(2)}) collective-permute-start(f32[4,16,128]{2,1,0:T(8,128)S(1)} %pad_maximum_fusion.2), channel_id=1, source_target_pairs={{0,16},{1,17},{2,18},{3,19},{4,20},{5,21},{6,22},{7,23},{8,24},{9,... | collective-permute-start | bytes 98312 | tf_op jit(solution)/shard_map/ppermute | solution.py:18
  11.6 2.4 %fusion.9 = f32[256,512]{1,0:T(8,128)S(1)} fusion(f32[256,512]{1,0:T(8,128)} %bitcast.60, f32[1,512,512]{2,1,0:T(8,128)} %param.18), kind=kOutput, calls=%fused_computation.16 | convolution fusion | flops 805306368 | bytes 2097152 | tf_op jit(solution)/shard_map/kv,vw->kw/dot_general | solution.py:108
  16.0 1.6 %collective-permute-start.7 = (f32[8,16,128]{2,1,0:T(8,128)}, f32[8,16,128]{2,1,0:T(8,128)}, u32[]{:S(2)}, u32[]{:S(2)}) collective-permute-start(f32[8,16,128]{2,1,0:T(8,128)} %get-tuple-element.13), channel_id=1, source_target_pairs={{0,8},{1,9},{2,10},{3,11},{4,12},{5,13},{6,14},{7,15},{8,0},{9,1},... | collective-permute-start | bytes 196616 | tf_op jit(solution)/shard_map/ppermute | solution.py:18
  21.8 1.5 %collective-permute-start.8 = (f32[8,16,128]{2,1,0:T(8,128)}, f32[8,16,128]{2,1,0:T(8,128)S(1)}, u32[]{:S(2)}, u32[]{:S(2)}) collective-permute-start(f32[8,16,128]{2,1,0:T(8,128)} %get-tuple-element.13), channel_id=1, source_target_pairs={{0,4},{1,5},{2,6},{3,7},{4,0},{5,1},{6,2},{7,3},{8,12},{9,13},{10,... | collective-permute-start | bytes 196616 | tf_op jit(solution)/shard_map/ppermute | solution.py:18
  24.6 1.7 %collective-permute-done.8 = f32[8,16,128]{2,1,0:T(8,128)S(1)} collective-permute-done((f32[8,16,128]{2,1,0:T(8,128)}, f32[8,16,128]{2,1,0:T(8,128)S(1)}, u32[]{:S(2)}, u32[]{:S(2)}) %collective-permute-start.8) | collective-permute-done | bytes 65568 | tf_op jit(solution)/shard_map/ppermute | solution.py:18
  26.3 2.4 %collective-permute-done.9 = f32[8,16,128]{2,1,0:T(8,128)S(1)} collective-permute-done((f32[8,16,128]{2,1,0:T(8,128)}, f32[8,16,128]{2,1,0:T(8,128)S(1)}, u32[]{:S(2)}, u32[]{:S(2)}) %collective-permute-start.9) | collective-permute-done | bytes 65568 | tf_op jit(solution)/shard_map/ppermute | solution.py:18
  28.7 3.8 %collective-permute-done.4 = f32[128,512]{0,1:T(8,128)S(1)} collective-permute-done((f32[128,512]{0,1:T(8,128)S(1)}, f32[128,512]{0,1:T(8,128)S(1)}, u32[]{:S(2)}, u32[]{:S(2)}) %collective-permute-start.4) | collective-permute-done | bytes 262176 | tf_op jit(solution)/shard_map/ppermute | solution.py:116
  32.6 2.4 %constant_dynamic-update-slice_fusion.12 = (f32[16,128,128]{2,1,0:T(8,128)}, f32[1,128,128]{2,1,0:T(8,128)S(1)}) fusion(f32[128,128]{1,0:T(8,128)S(1)} %fusion.17, f32[512,128]{1,0:T(8,128)S(1)} %bitcast.61, f32[128,512]{0,1:T(8,128)} %collective-permute-done.5, f32[128,512]{0,1:T(8,128)S(1)} %collective-permute-done.4, ...), kind=kOutput, calls=%fused_computation.49 | convolution fusion | flops 100876288 | bytes 1507332 | tf_op jit(solution)/shard_map/wj,jr->wr/dot_general | solution.py:124
  34.9 1.4 %collective-permute-start.10 = (f32[1,128,128]{2,1,0:T(8,128)S(1)}, f32[1,128,128]{2,1,0:T(8,128)S(1)}, u32[]{:S(2)}, u32[]{:S(2)}) collective-permute-start(f32[1,128,128]{2,1,0:T(8,128)S(1)} %get-tuple-element.22), channel_id=1, source_target_pairs={{0,2},{1,3},{2,0},{3,1},{4,6},{5,7},{6,4},{7,5},{8,10},{9,11},{10,... | collective-permute-start | bytes 196616 | tf_op jit(solution)/shard_map/ppermute | solution.py:18
  36.4 2.8 %collective-permute-done.10 = f32[1,128,128]{2,1,0:T(8,128)S(1)} collective-permute-done((f32[1,128,128]{2,1,0:T(8,128)S(1)}, f32[1,128,128]{2,1,0:T(8,128)S(1)}, u32[]{:S(2)}, u32[]{:S(2)}) %collective-permute-start.10) | collective-permute-done | bytes 65568 | tf_op jit(solution)/shard_map/ppermute | solution.py:18
  39.2 1.3 %collective-permute-start.11 = (f32[2,128,128]{2,1,0:T(8,128)S(1)}, f32[2,128,128]{2,1,0:T(8,128)S(1)}, u32[]{:S(2)}, u32[]{:S(2)}) collective-permute-start(f32[2,128,128]{2,1,0:T(8,128)S(1)} %pad_maximum_fusion.1), channel_id=1, source_target_pairs={{0,16},{1,17},{2,18},{3,19},{4,20},{5,21},{6,22},{7,23},{8,24},{9,... | collective-permute-start | bytes 393224 | tf_op jit(solution)/shard_map/ppermute | solution.py:18
  40.6 6.6 %collective-permute-done.11 = f32[2,128,128]{2,1,0:T(8,128)S(1)} collective-permute-done((f32[2,128,128]{2,1,0:T(8,128)S(1)}, f32[2,128,128]{2,1,0:T(8,128)S(1)}, u32[]{:S(2)}, u32[]{:S(2)}) %collective-permute-start.11) | collective-permute-done | bytes 131104 | tf_op jit(solution)/shard_map/ppermute | solution.py:18
  48.0 1.6 %collective-permute-start.13 = (f32[4,128,128]{2,1,0:T(8,128)S(1)}, f32[4,128,128]{2,1,0:T(8,128)S(1)}, u32[]{:S(2)}, u32[]{:S(2)}) collective-permute-start(f32[4,128,128]{2,1,0:T(8,128)S(1)} %pad_maximum_fusion), channel_id=1, source_target_pairs={{0,4},{1,5},{2,6},{3,7},{4,0},{5,1},{6,2},{7,3},{8,12},{9,13},{10,... | collective-permute-start | bytes 786440 | tf_op jit(solution)/shard_map/ppermute | solution.py:18
  50.1 2.0 %collective-permute-start.14 = (f32[4,128,128]{2,1,0:T(8,128)S(1)}, f32[4,128,128]{2,1,0:T(8,128)S(1)}, u32[]{:S(2)}, u32[]{:S(2)}) collective-permute-start(f32[4,128,128]{2,1,0:T(8,128)S(1)} %pad_maximum_fusion), channel_id=1, source_target_pairs={{0,12},{1,13},{2,14},{3,15},{4,8},{5,9},{6,10},{7,11},{8,4},{9,5},... | collective-permute-start | bytes 786440 | tf_op jit(solution)/shard_map/ppermute | solution.py:18
  52.7 3.8 %collective-permute-done.12 = f32[4,128,128]{2,1,0:T(8,128)S(1)} collective-permute-done((f32[4,128,128]{2,1,0:T(8,128)S(1)}, f32[4,128,128]{2,1,0:T(8,128)S(1)}, u32[]{:S(2)}, u32[]{:S(2)}) %collective-permute-start.12) | collective-permute-done | bytes 262176 | tf_op jit(solution)/shard_map/ppermute | solution.py:18
  57.2 2.9 %collective-permute-done.13 = f32[4,128,128]{2,1,0:T(8,128)S(1)} collective-permute-done((f32[4,128,128]{2,1,0:T(8,128)S(1)}, f32[4,128,128]{2,1,0:T(8,128)S(1)}, u32[]{:S(2)}, u32[]{:S(2)}) %collective-permute-start.13) | collective-permute-done | bytes 262176 | tf_op jit(solution)/shard_map/ppermute | solution.py:18
  62.5 1.9 %gather_fusion.4 = f32[16,128,128]{2,1,0:T(8,128)S(1)} fusion(f32[16,128,128]{2,1,0:T(8,128)} %constant_dynamic-update-slice_fusion.7, s32[1024]{0:T(1024)S(1)} %pad_clamp_fusion.1), kind=kCustom, calls=%fused_computation.4 | custom fusion | bytes 2097216 | tf_op jit(solution)/shard_map/gather | solution.py:136
  65.0 2.8 %gather_fusion.5 = f32[16,128,128]{2,1,0:T(8,128)} fusion(f32[16,128,128]{2,1,0:T(8,128)} %collective-permute-done.15, s32[1024]{0:T(1024)S(1)} %pad_clamp_fusion), kind=kCustom, calls=%fused_computation.5 | custom fusion | bytes 2097216 | tf_op jit(solution)/shard_map/gather | solution.py:136
  67.8 2.4 %fusion = f32[8,256,128]{2,1,0:T(8,128)S(1)} fusion(f32[8,256,128]{2,1,0:T(8,128)} %bitcast.59, s32[256]{0:T(256)S(1)} %add_bitcast_fusion, s32[8,256]{1,0:T(8,128)S(1)} %copy-done.6), kind=kOutput, calls=%fused_computation.6 | convolution fusion | flops 805830656 | bytes 2106368 | tf_op jit(solution)/shard_map/skj,sjr->skr/dot_general | solution.py:140
  71.5 3.5 %fusion.7 = f32[8,256,128]{2,1,0:T(8,128)S(1)} fusion(f32[8,256,128]{2,1,0:T(8,128)S(1)} %copy-done.4, f32[8,256,128]{2,1,0:T(8,128)S(1)} %fusion.4, f32[8,256,256]{2,1,0:T(8,128)S(1)} %copy-done), kind=kOutput, calls=%fused_computation.13 | convolution fusion | flops 805568512 | bytes 5242880 | tf_op jit(solution)/shard_map/swk,skr->swr/dot_general | solution.py:145
  75.0 2.0 %convolution_bitcast_fusion = f32[8,256,128]{1,2,0:T(8,128)S(1)} fusion(f32[8,256,128]{2,1,0:T(8,128)S(1)} %fusion.7, f32[8,256,256]{2,1,0:T(8,128)S(1)} %copy-done.3), kind=kOutput, calls=%fused_computation.11 | convolution fusion | flops 805306368 | bytes 4194304 | tf_op jit(solution)/shard_map/swk,skr->swr/dot_general | solution.py:146
  77.1 1.3 %copy.21 = f32[8,256,128]{2,1,0:T(8,128)} copy(f32[8,256,128]{1,2,0:T(8,128)S(1)} %convolution_bitcast_fusion) | data formatting | bytes 2097152
  (80 shorter events, 18.3 us)
Async XLA Ops:
  0.6 70.8 %copy-start = (f32[8,256,256]{2,1,0:T(8,128)S(1)}, f32[8,256,256]{2,1,0:T(8,128)}, u32[]{:S(2)}) copy-start(f32[8,256,256]{2,1,0:T(8,128)} %param.24) | copy-start | bytes 6291460
  0.6 13.4 %copy-start.7 = (s32[1,256]{1,0:T(1,128)S(1)}, s32[1,256]{1,0:T(1,128)}, u32[]{:S(2)}) copy-start(s32[1,256]{1,0:T(1,128)} %param.19) | copy-start | bytes 3076
  0.7 7.4 %collective-permute-start = (f32[1,16,128]{2,1,0:T(8,128)}, f32[1,16,128]{2,1,0:T(8,128)S(1)}, u32[]{:S(2)}, u32[]{:S(2)}) collective-permute-start(f32[1,16,128]{2,1,0:T(8,128)} %bitcast.62), channel_id=1, source_target_pairs={{0,1},{1,0},{2,3},{3,2},{4,5},{5,4},{6,7},{7,6},{8,9},{9,8},{10,11... | collective-permute-start | bytes 24584 | tf_op jit(solution)/shard_map/ppermute | solution.py:18
  1.2 6.9 %collective-permute-start.1 = (f32[1,16,128]{2,1,0:T(8,128)}, f32[1,16,128]{2,1,0:T(8,128)S(1)}, u32[]{:S(2)}, u32[]{:S(2)}) collective-permute-start(f32[1,16,128]{2,1,0:T(8,128)} %bitcast.63), channel_id=1, source_target_pairs={{0,2},{1,3},{2,0},{3,1},{4,6},{5,7},{6,4},{7,5},{8,10},{9,11},{10,... | collective-permute-start | bytes 24584 | tf_op jit(solution)/shard_map/ppermute | solution.py:18
  3.8 4.3 %collective-permute-start.2 = (f32[1,16,128]{2,1,0:T(8,128)}, f32[1,16,128]{2,1,0:T(8,128)S(1)}, u32[]{:S(2)}, u32[]{:S(2)}) collective-permute-start(f32[1,16,128]{2,1,0:T(8,128)} %bitcast.64), channel_id=1, source_target_pairs={{0,3},{1,2},{2,1},{3,0},{4,7},{5,6},{6,5},{7,4},{8,11},{9,10},{10,... | collective-permute-start | bytes 24584 | tf_op jit(solution)/shard_map/ppermute | solution.py:18
  8.8 6.6 %collective-permute-start.6 = (f32[4,16,128]{2,1,0:T(8,128)S(1)}, f32[4,16,128]{2,1,0:T(8,128)S(1)}, u32[]{:S(2)}, u32[]{:S(2)}) collective-permute-start(f32[4,16,128]{2,1,0:T(8,128)S(1)} %pad_maximum_fusion.2), channel_id=1, source_target_pairs={{0,16},{1,17},{2,18},{3,19},{4,20},{5,21},{6,22},{7,23},{8,24},{9,... | collective-permute-start | bytes 98312 | tf_op jit(solution)/shard_map/ppermute | solution.py:18
  14.7 3.0 %copy-start.2 = (f32[512,512]{0,1:T(8,128)}, f32[512,512]{0,1:T(8,128)S(1)}, u32[]{:S(2)}) copy-start(f32[512,512]{0,1:T(8,128)S(1)} %fusion.15) | copy-start | bytes 3145732
  16.0 7.3 %collective-permute-start.7 = (f32[8,16,128]{2,1,0:T(8,128)}, f32[8,16,128]{2,1,0:T(8,128)}, u32[]{:S(2)}, u32[]{:S(2)}) collective-permute-start(f32[8,16,128]{2,1,0:T(8,128)} %get-tuple-element.13), channel_id=1, source_target_pairs={{0,8},{1,9},{2,10},{3,11},{4,12},{5,13},{6,14},{7,15},{8,0},{9,1},... | collective-permute-start | bytes 196616 | tf_op jit(solution)/shard_map/ppermute | solution.py:18
  18.3 10.4 %collective-permute-start.5 = (f32[128,512]{0,1:T(8,128)S(1)}, f32[128,512]{0,1:T(8,128)}, u32[]{:S(2)}, u32[]{:S(2)}) collective-permute-start(f32[128,512]{0,1:T(8,128)S(1)} %bitcast.55), channel_id=1, source_target_pairs={{0,3},{1,2},{2,1},{3,0},{4,7},{5,6},{6,5},{7,4},{8,11},{9,10},{10,... | collective-permute-start | bytes 786440 | tf_op jit(solution)/shard_map/ppermute | solution.py:116
  19.9 8.9 %collective-permute-start.3 = (f32[128,512]{0,1:T(8,128)S(1)}, f32[128,512]{0,1:T(8,128)}, u32[]{:S(2)}, u32[]{:S(2)}) collective-permute-start(f32[128,512]{0,1:T(8,128)S(1)} %bitcast.56), channel_id=1, source_target_pairs={{0,1},{1,0},{2,3},{3,2},{4,5},{5,4},{6,7},{7,6},{8,9},{9,8},{10,11... | collective-permute-start | bytes 786440 | tf_op jit(solution)/shard_map/ppermute | solution.py:116
  21.3 26.0 %copy-start.8 = (s32[2]{0:T(128)S(1)}, s32[2]{0:T(128)}, u32[]{:S(2)}) copy-start(s32[2]{0:T(128)} %constant.120.clone) | copy-start | bytes 28
  21.3 26.0 %copy-start.1 = (s32[8]{0:T(128)S(1)}, s32[8]{0:T(128)}, u32[]{:S(2)}) copy-start(s32[8]{0:T(128)} %param.21) | copy-start | bytes 100
  21.3 11.3 %collective-permute-start.4 = (f32[128,512]{0,1:T(8,128)S(1)}, f32[128,512]{0,1:T(8,128)S(1)}, u32[]{:S(2)}, u32[]{:S(2)}) collective-permute-start(f32[128,512]{0,1:T(8,128)S(1)} %bitcast.57), channel_id=1, source_target_pairs={{0,2},{1,3},{2,0},{3,1},{4,6},{5,7},{6,4},{7,5},{8,10},{9,11},{10,... | collective-permute-start | bytes 786440 | tf_op jit(solution)/shard_map/ppermute | solution.py:116
  21.8 4.5 %collective-permute-start.8 = (f32[8,16,128]{2,1,0:T(8,128)}, f32[8,16,128]{2,1,0:T(8,128)S(1)}, u32[]{:S(2)}, u32[]{:S(2)}) collective-permute-start(f32[8,16,128]{2,1,0:T(8,128)} %get-tuple-element.13), channel_id=1, source_target_pairs={{0,4},{1,5},{2,6},{3,7},{4,0},{5,1},{6,2},{7,3},{8,12},{9,13},{10,... | collective-permute-start | bytes 196616 | tf_op jit(solution)/shard_map/ppermute | solution.py:18
  23.3 5.4 %collective-permute-start.9 = (f32[8,16,128]{2,1,0:T(8,128)}, f32[8,16,128]{2,1,0:T(8,128)S(1)}, u32[]{:S(2)}, u32[]{:S(2)}) collective-permute-start(f32[8,16,128]{2,1,0:T(8,128)} %get-tuple-element.13), channel_id=1, source_target_pairs={{0,12},{1,13},{2,14},{3,15},{4,8},{5,9},{6,10},{7,11},{8,4},{9,5},... | collective-permute-start | bytes 196616 | tf_op jit(solution)/shard_map/ppermute | solution.py:18
  34.9 29.4 %copy-start.5 = (f32[1,128,128]{2,1,0:T(8,128)}, f32[1,128,128]{2,1,0:T(8,128)S(1)}, u32[]{:S(2)}) copy-start(f32[1,128,128]{2,1,0:T(8,128)S(1)} %get-tuple-element.22) | copy-start | bytes 196612
  34.9 4.3 %collective-permute-start.10 = (f32[1,128,128]{2,1,0:T(8,128)S(1)}, f32[1,128,128]{2,1,0:T(8,128)S(1)}, u32[]{:S(2)}, u32[]{:S(2)}) collective-permute-start(f32[1,128,128]{2,1,0:T(8,128)S(1)} %get-tuple-element.22), channel_id=1, source_target_pairs={{0,2},{1,3},{2,0},{3,1},{4,6},{5,7},{6,4},{7,5},{8,10},{9,11},{10,... | collective-permute-start | bytes 196616 | tf_op jit(solution)/shard_map/ppermute | solution.py:18
  39.2 7.9 %collective-permute-start.11 = (f32[2,128,128]{2,1,0:T(8,128)S(1)}, f32[2,128,128]{2,1,0:T(8,128)S(1)}, u32[]{:S(2)}, u32[]{:S(2)}) collective-permute-start(f32[2,128,128]{2,1,0:T(8,128)S(1)} %pad_maximum_fusion.1), channel_id=1, source_target_pairs={{0,16},{1,17},{2,18},{3,19},{4,20},{5,21},{6,22},{7,23},{8,24},{9,... | collective-permute-start | bytes 393224 | tf_op jit(solution)/shard_map/ppermute | solution.py:18
  47.2 9.3 %collective-permute-start.12 = (f32[4,128,128]{2,1,0:T(8,128)S(1)}, f32[4,128,128]{2,1,0:T(8,128)S(1)}, u32[]{:S(2)}, u32[]{:S(2)}) collective-permute-start(f32[4,128,128]{2,1,0:T(8,128)S(1)} %pad_maximum_fusion), channel_id=1, source_target_pairs={{0,8},{1,9},{2,10},{3,11},{4,12},{5,13},{6,14},{7,15},{8,0},{9,1},... | collective-permute-start | bytes 786440 | tf_op jit(solution)/shard_map/ppermute | solution.py:18
  48.0 12.2 %collective-permute-start.13 = (f32[4,128,128]{2,1,0:T(8,128)S(1)}, f32[4,128,128]{2,1,0:T(8,128)S(1)}, u32[]{:S(2)}, u32[]{:S(2)}) collective-permute-start(f32[4,128,128]{2,1,0:T(8,128)S(1)} %pad_maximum_fusion), channel_id=1, source_target_pairs={{0,4},{1,5},{2,6},{3,7},{4,0},{5,1},{6,2},{7,3},{8,12},{9,13},{10,... | collective-permute-start | bytes 786440 | tf_op jit(solution)/shard_map/ppermute | solution.py:18
  50.1 11.2 %collective-permute-start.14 = (f32[4,128,128]{2,1,0:T(8,128)S(1)}, f32[4,128,128]{2,1,0:T(8,128)S(1)}, u32[]{:S(2)}, u32[]{:S(2)}) collective-permute-start(f32[4,128,128]{2,1,0:T(8,128)S(1)} %pad_maximum_fusion), channel_id=1, source_target_pairs={{0,12},{1,13},{2,14},{3,15},{4,8},{5,9},{6,10},{7,11},{8,4},{9,5},... | collective-permute-start | bytes 786440 | tf_op jit(solution)/shard_map/ppermute | solution.py:18
  62.0 3.0 %collective-permute-start.15 = (f32[16,128,128]{2,1,0:T(8,128)}, f32[16,128,128]{2,1,0:T(8,128)}, u32[]{:S(2)}, u32[]{:S(2)}) collective-permute-start(f32[16,128,128]{2,1,0:T(8,128)} %constant_dynamic-update-slice_fusion.7), channel_id=1, source_target_pairs={{0,1},{1,0},{2,3},{3,2},{4,5},{5,4},{6,7},{7,6},{8,9},{9,8},{10,11... | collective-permute-start | bytes 3145736 | tf_op jit(solution)/shard_map/ppermute | solution.py:128
  62.5 5.4 %copy-start.6 = (s32[8,256]{1,0:T(8,128)S(1)}, s32[8,256]{1,0:T(8,128)}, u32[]{:S(2)}) copy-start(s32[8,256]{1,0:T(8,128)} %param.23) | copy-start | bytes 24580
  71.5 3.5 %copy-start.3 = (f32[8,256,256]{2,1,0:T(8,128)S(1)}, f32[8,256,256]{2,1,0:T(8,128)}, u32[]{:S(2)}) copy-start(f32[8,256,256]{2,1,0:T(8,128)} %param.26) | copy-start | bytes 6291460
  (1 other events, 1.2 us)

commit v13 on v10

--- a/solution.py
+++ b/solution.py
@@ -101,6 +101,7 @@
     pick_top = (top_index[0][:, None] == natural[None, :]).astype(jnp.float32)
     folded = jnp.einsum("kv,vw->kw", upper_panel[0], upper_inverse[0], precision=highest)
     weights = jnp.einsum("kj,kw->wj", pick_top, folded, precision=highest)
+    top_block, weights = lax.optimization_barrier((top_solution, weights))
     total = lax.dynamic_slice_in_dim(weights, begin, share, 0)
     for v in range(1, panels):
         outgoing = lax.dynamic_slice_in_dim(weights, (panel_index ^ v) * share, share, 0)
@@ -111,7 +112,7 @@
     own_inverse = lax.dynamic_slice_in_dim(upper_inverse[0], begin, share, 1)
     own_base = jnp.einsum("kw,kr->wr", own_inverse, upper_rhs[0], precision=highest)
 
-    top_held = xor_gather(top_solution, both, count, top_groups).reshape(count * top_rows, rhs)
+    top_held = xor_gather(top_block, both, count, top_groups).reshape(count * top_rows, rhs)
     own_rows = own_base - jnp.einsum("wj,jr->wr", total, top_held, precision=highest)
 
     held = xor_gather(own_rows, both, count, spread_groups[:-1])

time: 70.7 us -> 72.2 us (1.021)
  local copies, waits for them, and re-layouts: 13.3 us -> 15.7 us
    dynamic_slice x1 -> x4, local copies, waits for them, and re-layouts: 0.11 us -> 2.17 us  [local(): lax.dynamic_slice_in_dim(weights, (panel_index ^ v) * share, share, 0)]
    reshape x0 -> x3, local copies, waits for them, and re-layouts: none -> 1.08 us  [local(): outgoing = outgoing.reshape(share, count * top_rows)]
    unnamed x37 -> x41, local copies, waits for them, and re-layouts: 4.95 us -> 4.17 us
  transfers between devices with their start and end apart: 16 -> 16, of which waited for: 9 -> 9; matrix products, arithmetic and copies ran while one was open for 19% -> 17% of each run, Pallas kernels for 0% -> 0%
where the time goes in v13:
time: 72.2 us; the launch traced here: 71.7 us
  starting transfers between devices  21.6 us (30%)
  waiting for transfers between devices  16.6 us (23%)
  matrix products  16.1 us (22%)
  local copies, waits for them, and re-layouts  15.7 us (22%)
  between operations  1.12 us (2%)
    ppermute x12, starting transfers between devices, xor_gather(): parts.append(lax.ppermute(held, axes, [(i, i ^ v) for i in range(count)]))  19.3 us
    ppermute x12, waiting for transfers between devices, xor_gather(): parts.append(lax.ppermute(held, axes, [(i, i ^ v) for i in range(count)]))  15.9 us
    gather x2, local copies, waits for them, and re-layouts, local(): slabs = source[places].reshape(position.shape[0], -1, own_rows.shape[1])  4.66 us
    unnamed x41, local copies, waits for them, and re-layouts  4.17 us
    dot_general x2, matrix products, local(): term = jnp.einsum('skj,sjr->skr', pick, slabs, precision=highest)  3.6 us
    dot_general x1, matrix products, local(): jnp.einsum('swk,skr->swr', panel_t, parent_rows, precision=highest)  3.52 us
    dot_general x1, matrix products, local(): jnp.einsum('kv,vw->kw', upper_panel[0], upper_inverse[0], precision=highest)  2.49 us
    ppermute x3, starting transfers between devices, local(): lax.ppermute(outgoing, 'panel', [(i, i ^ v) for i in range(panels)])  2.32 us
  transfers between devices with their start and end apart: 16, of which 9 were waited for; matrix products, arithmetic and copies ran while one was open for 17% of the time, Pallas kernels for 0%

profile of v13, /device:TPU:0, one launch (start us, length us, event | category | flops | bytes accessed | tf_op | source)
XLA Modules:
  0.0 71.7 jit_solution(6952923142154058248)
XLA Ops:
  1.2 2.5 %fusion.9 = f32[256,512]{1,0:T(8,128)S(1)} fusion(f32[1,512,512]{2,1,0:T(8,128)} %param.18, f32[1,256,512]{2,1,0:T(8,128)} %param.17), kind=kOutput, calls=%fused_computation.16 | convolution fusion | flops 805306368 | bytes 2097152 | tf_op jit(solution)/shard_map/kv,vw->kw/dot_general | solution.py:102
  5.0 2.6 %collective-permute-start.4 = (f32[1,16,128]{2,1,0:T(8,128)S(1)}, f32[1,16,128]{2,1,0:T(8,128)S(1)}, u32[]{:S(2)}, u32[]{:S(2)}) collective-permute-start(f32[1,16,128]{2,1,0:T(8,128)S(1)} %bitcast.65), channel_id=1, source_target_pairs={{0,2},{1,3},{2,0},{3,1},{4,6},{5,7},{6,4},{7,5},{8,10},{9,11},{10,... | collective-permute-start | bytes 24584 | tf_op jit(solution)/shard_map/ppermute | solution.py:13
  10.4 1.7 %collective-permute-start.2 = (f32[128,512]{1,0:T(8,128)S(1)}, f32[128,512]{1,0:T(8,128)}, u32[]{:S(2)}, u32[]{:S(2)}) collective-permute-start(f32[128,512]{1,0:T(8,128)S(1)} %copy.25), channel_id=1, source_target_pairs={{0,3},{1,2},{2,1},{3,0},{4,7},{5,6},{6,5},{7,4},{8,11},{9,10},{10,... | collective-permute-start | bytes 786440 | tf_op jit(solution)/shard_map/ppermute | solution.py:111
  15.3 2.8 %collective-permute-start.6 = (f32[4,16,128]{2,1,0:T(8,128)S(1)}, f32[4,16,128]{2,1,0:T(8,128)S(1)}, u32[]{:S(2)}, u32[]{:S(2)}) collective-permute-start(f32[4,16,128]{2,1,0:T(8,128)S(1)} %pad_maximum_fusion.2), channel_id=1, source_target_pairs={{0,16},{1,17},{2,18},{3,19},{4,20},{5,21},{6,22},{7,23},{8,24},{9,... | collective-permute-start | bytes 98312 | tf_op jit(solution)/shard_map/ppermute | solution.py:13
  18.1 2.1 %collective-permute-done.6 = f32[4,16,128]{2,1,0:T(8,128)S(1)} collective-permute-done((f32[4,16,128]{2,1,0:T(8,128)S(1)}, f32[4,16,128]{2,1,0:T(8,128)S(1)}, u32[]{:S(2)}, u32[]{:S(2)}) %collective-permute-start.6) | collective-permute-done | bytes 32800 | tf_op jit(solution)/shard_map/ppermute | solution.py:13
  20.2 1.7 %collective-permute-start.7 = (f32[8,16,128]{2,1,0:T(8,128)S(1)}, f32[8,16,128]{2,1,0:T(8,128)S(1)}, u32[]{:S(2)}, u32[]{:S(2)}) collective-permute-start(f32[8,16,128]{2,1,0:T(8,128)S(1)} %get-tuple-element.13), channel_id=1, source_target_pairs={{0,8},{1,9},{2,10},{3,11},{4,12},{5,13},{6,14},{7,15},{8,0},{9,1},... | collective-permute-start | bytes 196616 | tf_op jit(solution)/shard_map/ppermute | solution.py:13
  21.9 1.6 %fusion.18 = f32[128,128]{1,0:T(8,128)S(1)} fusion(f32[1,512,128]{2,1,0:T(8,128)} %param.16, f32[1,512,512]{2,1,0:T(8,128)} %param.18, s32[]{:T(128)S(6)} %select_n.96), kind=kOutput, calls=%fused_computation.26 | convolution fusion | flops 100663296 | bytes 589828 | tf_op jit(solution)/shard_map/kw,kr->wr/dot_general | solution.py:113
  23.5 1.6 %collective-permute-start.8 = (f32[8,16,128]{2,1,0:T(8,128)S(1)}, f32[8,16,128]{2,1,0:T(8,128)S(1)}, u32[]{:S(2)}, u32[]{:S(2)}) collective-permute-start(f32[8,16,128]{2,1,0:T(8,128)S(1)} %get-tuple-element.13), channel_id=1, source_target_pairs={{0,4},{1,5},{2,6},{3,7},{4,0},{5,1},{6,2},{7,3},{8,12},{9,13},{10,... | collective-permute-start | bytes 196616 | tf_op jit(solution)/shard_map/ppermute | solution.py:13
  25.1 2.0 %collective-permute-start.9 = (f32[8,16,128]{2,1,0:T(8,128)S(1)}, f32[8,16,128]{2,1,0:T(8,128)S(1)}, u32[]{:S(2)}, u32[]{:S(2)}) collective-permute-start(f32[8,16,128]{2,1,0:T(8,128)S(1)} %get-tuple-element.13), channel_id=1, source_target_pairs={{0,12},{1,13},{2,14},{3,15},{4,8},{5,9},{6,10},{7,11},{8,4},{9,5},... | collective-permute-start | bytes 196616 | tf_op jit(solution)/shard_map/ppermute | solution.py:13
  28.4 1.8 %collective-permute-done.9 = f32[8,16,128]{2,1,0:T(8,128)S(1)} collective-permute-done((f32[8,16,128]{2,1,0:T(8,128)S(1)}, f32[8,16,128]{2,1,0:T(8,128)S(1)}, u32[]{:S(2)}, u32[]{:S(2)}) %collective-permute-start.9) | collective-permute-done | bytes 65568 | tf_op jit(solution)/shard_map/ppermute | solution.py:13
  30.3 2.2 %constant_dynamic-update-slice_fusion.18 = (f32[16,128,128]{2,1,0:T(8,128)}, f32[1,128,128]{2,1,0:T(8,128)S(1)}) fusion(f32[128,128]{1,0:T(8,128)S(1)} %fusion.18, f32[512,128]{1,0:T(8,128)S(1)} %bitcast.63, f32[128,512]{1,0:T(8,128)} %collective-permute-done.2, f32[128,512]{1,0:T(8,128)S(1)} %collective-permute-done.1, ...), kind=kOutput, calls=%fused_computation.55 | convolution fusion | flops 100876288 | bytes 1507332 | tf_op jit(solution)/shard_map/wj,jr->wr/dot_general | solution.py:116
  32.4 1.5 %collective-permute-start.10 = (f32[1,128,128]{2,1,0:T(8,128)S(1)}, f32[1,128,128]{2,1,0:T(8,128)S(1)}, u32[]{:S(2)}, u32[]{:S(2)}) collective-permute-start(f32[1,128,128]{2,1,0:T(8,128)S(1)} %get-tuple-element.28), channel_id=1, source_target_pairs={{0,2},{1,3},{2,0},{3,1},{4,6},{5,7},{6,4},{7,5},{8,10},{9,11},{10,... | collective-permute-start | bytes 196616 | tf_op jit(solution)/shard_map/ppermute | solution.py:13
  34.0 2.7 %collective-permute-done.10 = f32[1,128,128]{2,1,0:T(8,128)S(1)} collective-permute-done((f32[1,128,128]{2,1,0:T(8,128)S(1)}, f32[1,128,128]{2,1,0:T(8,128)S(1)}, u32[]{:S(2)}, u32[]{:S(2)}) %collective-permute-start.10) | collective-permute-done | bytes 65568 | tf_op jit(solution)/shard_map/ppermute | solution.py:13
  36.7 2.9 %collective-permute-start.11 = (f32[2,128,128]{2,1,0:T(8,128)S(1)}, f32[2,128,128]{2,1,0:T(8,128)S(1)}, u32[]{:S(2)}, u32[]{:S(2)}) collective-permute-start(f32[2,128,128]{2,1,0:T(8,128)S(1)} %pad_maximum_fusion.1), channel_id=1, source_target_pairs={{0,16},{1,17},{2,18},{3,19},{4,20},{5,21},{6,22},{7,23},{8,24},{9,... | collective-permute-start | bytes 393224 | tf_op jit(solution)/shard_map/ppermute | solution.py:13
  39.6 4.6 %collective-permute-done.11 = f32[2,128,128]{2,1,0:T(8,128)S(1)} collective-permute-done((f32[2,128,128]{2,1,0:T(8,128)S(1)}, f32[2,128,128]{2,1,0:T(8,128)S(1)}, u32[]{:S(2)}, u32[]{:S(2)}) %collective-permute-start.11) | collective-permute-done | bytes 131104 | tf_op jit(solution)/shard_map/ppermute | solution.py:13
  44.9 1.8 %collective-permute-start.13 = (f32[4,128,128]{2,1,0:T(8,128)S(1)}, f32[4,128,128]{2,1,0:T(8,128)S(1)}, u32[]{:S(2)}, u32[]{:S(2)}) collective-permute-start(f32[4,128,128]{2,1,0:T(8,128)S(1)} %pad_maximum_fusion), channel_id=1, source_target_pairs={{0,4},{1,5},{2,6},{3,7},{4,0},{5,1},{6,2},{7,3},{8,12},{9,13},{10,... | collective-permute-start | bytes 786440 | tf_op jit(solution)/shard_map/ppermute | solution.py:13
  47.3 1.7 %collective-permute-start.14 = (f32[4,128,128]{2,1,0:T(8,128)S(1)}, f32[4,128,128]{2,1,0:T(8,128)S(1)}, u32[]{:S(2)}, u32[]{:S(2)}) collective-permute-start(f32[4,128,128]{2,1,0:T(8,128)S(1)} %pad_maximum_fusion), channel_id=1, source_target_pairs={{0,12},{1,13},{2,14},{3,15},{4,8},{5,9},{6,10},{7,11},{8,4},{9,5},... | collective-permute-start | bytes 786440 | tf_op jit(solution)/shard_map/ppermute | solution.py:13
  49.7 1.3 %collective-permute-done.12 = f32[4,128,128]{2,1,0:T(8,128)S(1)} collective-permute-done((f32[4,128,128]{2,1,0:T(8,128)S(1)}, f32[4,128,128]{2,1,0:T(8,128)S(1)}, u32[]{:S(2)}, u32[]{:S(2)}) %collective-permute-start.12) | collective-permute-done | bytes 262176 | tf_op jit(solution)/shard_map/ppermute | solution.py:13
  51.8 1.6 %collective-permute-done.13 = f32[4,128,128]{2,1,0:T(8,128)S(1)} collective-permute-done((f32[4,128,128]{2,1,0:T(8,128)S(1)}, f32[4,128,128]{2,1,0:T(8,128)S(1)}, u32[]{:S(2)}, u32[]{:S(2)}) %collective-permute-start.13) | collective-permute-done | bytes 262176 | tf_op jit(solution)/shard_map/ppermute | solution.py:13
  55.8 1.9 %gather_fusion.4 = f32[16,128,128]{2,1,0:T(8,128)S(1)} fusion(f32[16,128,128]{2,1,0:T(8,128)} %constant_dynamic-update-slice_fusion.13, s32[1024]{0:T(1024)S(1)} %pad_clamp_fusion.1), kind=kCustom, calls=%fused_computation.4 | custom fusion | bytes 2097216 | tf_op jit(solution)/shard_map/gather | solution.py:128
  58.3 2.8 %gather_fusion.5 = f32[16,128,128]{2,1,0:T(8,128)} fusion(f32[16,128,128]{2,1,0:T(8,128)} %collective-permute-done.15, s32[1024]{0:T(1024)S(1)} %pad_clamp_fusion), kind=kCustom, calls=%fused_computation.5 | custom fusion | bytes 2097216 | tf_op jit(solution)/shard_map/gather | solution.py:128
  61.2 2.4 %fusion = f32[8,256,128]{2,1,0:T(8,128)S(1)} fusion(f32[8,256,128]{2,1,0:T(8,128)} %bitcast.62, s32[256]{0:T(256)S(1)} %add_bitcast_fusion, s32[8,256]{1,0:T(8,128)S(1)} %copy-done.7), kind=kOutput, calls=%fused_computation.6 | convolution fusion | flops 805830656 | bytes 2106368 | tf_op jit(solution)/shard_map/skj,sjr->skr/dot_general | solution.py:132
  64.8 3.5 %fusion.7 = f32[8,256,128]{2,1,0:T(8,128)S(1)} fusion(f32[8,256,128]{2,1,0:T(8,128)S(1)} %copy-done.4, f32[8,256,128]{2,1,0:T(8,128)S(1)} %fusion.4, f32[8,256,256]{2,1,0:T(8,128)S(1)} %copy-done), kind=kOutput, calls=%fused_computation.13 | convolution fusion | flops 805568512 | bytes 5242880 | tf_op jit(solution)/shard_map/swk,skr->swr/dot_general | solution.py:137
  68.3 2.0 %convolution_bitcast_fusion = f32[8,256,128]{1,2,0:T(8,128)S(1)} fusion(f32[8,256,128]{2,1,0:T(8,128)S(1)} %fusion.7, f32[8,256,256]{2,1,0:T(8,128)S(1)} %copy-done.3), kind=kOutput, calls=%fused_computation.11 | convolution fusion | flops 805306368 | bytes 4194304 | tf_op jit(solution)/shard_map/swk,skr->swr/dot_general | solution.py:138
  (101 shorter events, 17.2 us)
Async XLA Ops:
  0.6 64.1 %copy-start = (f32[8,256,256]{2,1,0:T(8,128)S(1)}, f32[8,256,256]{2,1,0:T(8,128)}, u32[]{:S(2)}) copy-start(f32[8,256,256]{2,1,0:T(8,128)} %param.24) | copy-start | bytes 6291460
  3.7 5.9 %copy-start.14 = (s32[8]{0:T(128)S(1)}, s32[8]{0:T(128)}, u32[]{:S(2)}) copy-start(s32[8]{0:T(128)} %param.22) | copy-start | bytes 100
  3.7 5.9 %copy-start.13 = (s32[32]{0:T(128)S(1)}, s32[32]{0:T(128)}, u32[]{:S(2)}) copy-start(s32[32]{0:T(128)} %constant.145) | copy-start | bytes 388
  4.5 4.1 %copy-start.2 = (f32[512,512]{1,0:T(8,128)}, f32[512,512]{1,0:T(8,128)S(1)}, u32[]{:S(2)}) copy-start(f32[512,512]{1,0:T(8,128)S(1)} %fusion.16) | copy-start | bytes 3145732
  4.5 10.3 %collective-permute-start.3 = (f32[1,16,128]{2,1,0:T(8,128)S(1)}, f32[1,16,128]{2,1,0:T(8,128)S(1)}, u32[]{:S(2)}, u32[]{:S(2)}) collective-permute-start(f32[1,16,128]{2,1,0:T(8,128)S(1)} %bitcast.64), channel_id=1, source_target_pairs={{0,1},{1,0},{2,3},{3,2},{4,5},{5,4},{6,7},{7,6},{8,9},{9,8},{10,11... | collective-permute-start | bytes 24584 | tf_op jit(solution)/shard_map/ppermute | solution.py:13
  5.0 10.2 %collective-permute-start.4 = (f32[1,16,128]{2,1,0:T(8,128)S(1)}, f32[1,16,128]{2,1,0:T(8,128)S(1)}, u32[]{:S(2)}, u32[]{:S(2)}) collective-permute-start(f32[1,16,128]{2,1,0:T(8,128)S(1)} %bitcast.65), channel_id=1, source_target_pairs={{0,2},{1,3},{2,0},{3,1},{4,6},{5,7},{6,4},{7,5},{8,10},{9,11},{10,... | collective-permute-start | bytes 24584 | tf_op jit(solution)/shard_map/ppermute | solution.py:13
  7.6 7.6 %collective-permute-start.5 = (f32[1,16,128]{2,1,0:T(8,128)S(1)}, f32[1,16,128]{2,1,0:T(8,128)S(1)}, u32[]{:S(2)}, u32[]{:S(2)}) collective-permute-start(f32[1,16,128]{2,1,0:T(8,128)S(1)} %bitcast.66), channel_id=1, source_target_pairs={{0,3},{1,2},{2,1},{3,0},{4,7},{5,6},{6,5},{7,4},{8,11},{9,10},{10,... | collective-permute-start | bytes 24584 | tf_op jit(solution)/shard_map/ppermute | solution.py:13
  10.4 19.8 %collective-permute-start.2 = (f32[128,512]{1,0:T(8,128)S(1)}, f32[128,512]{1,0:T(8,128)}, u32[]{:S(2)}, u32[]{:S(2)}) collective-permute-start(f32[128,512]{1,0:T(8,128)S(1)} %copy.25), channel_id=1, source_target_pairs={{0,3},{1,2},{2,1},{3,0},{4,7},{5,6},{6,5},{7,4},{8,11},{9,10},{10,... | collective-permute-start | bytes 786440 | tf_op jit(solution)/shard_map/ppermute | solution.py:111
  13.8 16.5 %collective-permute-start = (f32[128,512]{1,0:T(8,128)}, f32[128,512]{1,0:T(8,128)}, u32[]{:S(2)}, u32[]{:S(2)}) collective-permute-start(f32[128,512]{1,0:T(8,128)} %copy.21), channel_id=1, source_target_pairs={{0,1},{1,0},{2,3},{3,2},{4,5},{5,4},{6,7},{7,6},{8,9},{9,8},{10,11... | collective-permute-start | bytes 786440 | tf_op jit(solution)/shard_map/ppermute | solution.py:111
  14.7 29.6 %copy-start.10 = (s32[2]{0:T(128)S(1)}, s32[2]{0:T(128)}, u32[]{:S(2)}) copy-start(s32[2]{0:T(128)} %constant.120.clone) | copy-start | bytes 28
  14.7 29.6 %copy-start.1 = (s32[8]{0:T(128)S(1)}, s32[8]{0:T(128)}, u32[]{:S(2)}) copy-start(s32[8]{0:T(128)} %param.21) | copy-start | bytes 100
  14.8 15.4 %collective-permute-start.1 = (f32[128,512]{1,0:T(8,128)S(1)}, f32[128,512]{1,0:T(8,128)S(1)}, u32[]{:S(2)}, u32[]{:S(2)}) collective-permute-start(f32[128,512]{1,0:T(8,128)S(1)} %copy.23), channel_id=1, source_target_pairs={{0,2},{1,3},{2,0},{3,1},{4,6},{5,7},{6,4},{7,5},{8,10},{9,11},{10,... | collective-permute-start | bytes 786440 | tf_op jit(solution)/shard_map/ppermute | solution.py:111
  15.3 4.9 %collective-permute-start.6 = (f32[4,16,128]{2,1,0:T(8,128)S(1)}, f32[4,16,128]{2,1,0:T(8,128)S(1)}, u32[]{:S(2)}, u32[]{:S(2)}) collective-permute-start(f32[4,16,128]{2,1,0:T(8,128)S(1)} %pad_maximum_fusion.2), channel_id=1, source_target_pairs={{0,16},{1,17},{2,18},{3,19},{4,20},{5,21},{6,22},{7,23},{8,24},{9,... | collective-permute-start | bytes 98312 | tf_op jit(solution)/shard_map/ppermute | solution.py:13
  20.2 4.9 %collective-permute-start.7 = (f32[8,16,128]{2,1,0:T(8,128)S(1)}, f32[8,16,128]{2,1,0:T(8,128)S(1)}, u32[]{:S(2)}, u32[]{:S(2)}) collective-permute-start(f32[8,16,128]{2,1,0:T(8,128)S(1)} %get-tuple-element.13), channel_id=1, source_target_pairs={{0,8},{1,9},{2,10},{3,11},{4,12},{5,13},{6,14},{7,15},{8,0},{9,1},... | collective-permute-start | bytes 196616 | tf_op jit(solution)/shard_map/ppermute | solution.py:13
  23.5 4.9 %collective-permute-start.8 = (f32[8,16,128]{2,1,0:T(8,128)S(1)}, f32[8,16,128]{2,1,0:T(8,128)S(1)}, u32[]{:S(2)}, u32[]{:S(2)}) collective-permute-start(f32[8,16,128]{2,1,0:T(8,128)S(1)} %get-tuple-element.13), channel_id=1, source_target_pairs={{0,4},{1,5},{2,6},{3,7},{4,0},{5,1},{6,2},{7,3},{8,12},{9,13},{10,... | collective-permute-start | bytes 196616 | tf_op jit(solution)/shard_map/ppermute | solution.py:13
  25.1 5.2 %collective-permute-start.9 = (f32[8,16,128]{2,1,0:T(8,128)S(1)}, f32[8,16,128]{2,1,0:T(8,128)S(1)}, u32[]{:S(2)}, u32[]{:S(2)}) collective-permute-start(f32[8,16,128]{2,1,0:T(8,128)S(1)} %get-tuple-element.13), channel_id=1, source_target_pairs={{0,12},{1,13},{2,14},{3,15},{4,8},{5,9},{6,10},{7,11},{8,4},{9,5},... | collective-permute-start | bytes 196616 | tf_op jit(solution)/shard_map/ppermute | solution.py:13
  32.4 25.2 %copy-start.6 = (f32[1,128,128]{2,1,0:T(8,128)}, f32[1,128,128]{2,1,0:T(8,128)S(1)}, u32[]{:S(2)}) copy-start(f32[1,128,128]{2,1,0:T(8,128)S(1)} %get-tuple-element.28) | copy-start | bytes 196612
  32.4 4.3 %collective-permute-start.10 = (f32[1,128,128]{2,1,0:T(8,128)S(1)}, f32[1,128,128]{2,1,0:T(8,128)S(1)}, u32[]{:S(2)}, u32[]{:S(2)}) collective-permute-start(f32[1,128,128]{2,1,0:T(8,128)S(1)} %get-tuple-element.28), channel_id=1, source_target_pairs={{0,2},{1,3},{2,0},{3,1},{4,6},{5,7},{6,4},{7,5},{8,10},{9,11},{10,... | collective-permute-start | bytes 196616 | tf_op jit(solution)/shard_map/ppermute | solution.py:13
  36.7 7.4 %collective-permute-start.11 = (f32[2,128,128]{2,1,0:T(8,128)S(1)}, f32[2,128,128]{2,1,0:T(8,128)S(1)}, u32[]{:S(2)}, u32[]{:S(2)}) collective-permute-start(f32[2,128,128]{2,1,0:T(8,128)S(1)} %pad_maximum_fusion.1), channel_id=1, source_target_pairs={{0,16},{1,17},{2,18},{3,19},{4,20},{5,21},{6,22},{7,23},{8,24},{9,... | collective-permute-start | bytes 393224 | tf_op jit(solution)/shard_map/ppermute | solution.py:13
  44.2 6.9 %collective-permute-start.12 = (f32[4,128,128]{2,1,0:T(8,128)S(1)}, f32[4,128,128]{2,1,0:T(8,128)S(1)}, u32[]{:S(2)}, u32[]{:S(2)}) collective-permute-start(f32[4,128,128]{2,1,0:T(8,128)S(1)} %pad_maximum_fusion), channel_id=1, source_target_pairs={{0,8},{1,9},{2,10},{3,11},{4,12},{5,13},{6,14},{7,15},{8,0},{9,1},... | collective-permute-start | bytes 786440 | tf_op jit(solution)/shard_map/ppermute | solution.py:13
  44.9 8.5 %collective-permute-start.13 = (f32[4,128,128]{2,1,0:T(8,128)S(1)}, f32[4,128,128]{2,1,0:T(8,128)S(1)}, u32[]{:S(2)}, u32[]{:S(2)}) collective-permute-start(f32[4,128,128]{2,1,0:T(8,128)S(1)} %pad_maximum_fusion), channel_id=1, source_target_pairs={{0,4},{1,5},{2,6},{3,7},{4,0},{5,1},{6,2},{7,3},{8,12},{9,13},{10,... | collective-permute-start | bytes 786440 | tf_op jit(solution)/shard_map/ppermute | solution.py:13
  47.3 7.3 %collective-permute-start.14 = (f32[4,128,128]{2,1,0:T(8,128)S(1)}, f32[4,128,128]{2,1,0:T(8,128)S(1)}, u32[]{:S(2)}, u32[]{:S(2)}) collective-permute-start(f32[4,128,128]{2,1,0:T(8,128)S(1)} %pad_maximum_fusion), channel_id=1, source_target_pairs={{0,12},{1,13},{2,14},{3,15},{4,8},{5,9},{6,10},{7,11},{8,4},{9,5},... | collective-permute-start | bytes 786440 | tf_op jit(solution)/shard_map/ppermute | solution.py:13
  55.3 3.0 %collective-permute-start.15 = (f32[16,128,128]{2,1,0:T(8,128)}, f32[16,128,128]{2,1,0:T(8,128)}, u32[]{:S(2)}, u32[]{:S(2)}) collective-permute-start(f32[16,128,128]{2,1,0:T(8,128)} %constant_dynamic-update-slice_fusion.13), channel_id=1, source_target_pairs={{0,1},{1,0},{2,3},{3,2},{4,5},{5,4},{6,7},{7,6},{8,9},{9,8},{10,11... | collective-permute-start | bytes 3145736 | tf_op jit(solution)/shard_map/ppermute | solution.py:120
  55.8 5.4 %copy-start.7 = (s32[8,256]{1,0:T(8,128)S(1)}, s32[8,256]{1,0:T(8,128)}, u32[]{:S(2)}) copy-start(s32[8,256]{1,0:T(8,128)} %param.23) | copy-start | bytes 24580
  (7 other events, 19.5 us)

commit v14 on v10

--- a/solution.py
+++ b/solution.py
@@ -101,13 +101,19 @@
     pick_top = (top_index[0][:, None] == natural[None, :]).astype(jnp.float32)
     folded = jnp.einsum("kv,vw->kw", upper_panel[0], upper_inverse[0], precision=highest)
     weights = jnp.einsum("kj,kw->wj", pick_top, folded, precision=highest)
-    total = lax.dynamic_slice_in_dim(weights, begin, share, 0)
-    for v in range(1, panels):
-        outgoing = lax.dynamic_slice_in_dim(weights, (panel_index ^ v) * share, share, 0)
+    keep = list(range(panels))
+    rows = jnp.stack([lax.dynamic_slice_in_dim(weights, (panel_index ^ o) * share, share, 0) for o in keep])
+    for b in panel_bits:
+        v = 1 << b
+        send = [i for i, o in enumerate(keep) if (o >> b) & 1]
+        stay = [i for i, o in enumerate(keep) if not (o >> b) & 1]
         order = [static_position(static_offset(h, top_groups) ^ v, top_groups) for h in range(count)]
-        outgoing = outgoing.reshape(share, count, top_rows)[:, jnp.array(order), :]
-        outgoing = outgoing.reshape(share, count * top_rows)
-        total = total + lax.ppermute(outgoing, "panel", [(i, i ^ v) for i in range(panels)])
+        outgoing = rows[jnp.array(send)].reshape(len(send), share, count, top_rows)[:, :, jnp.array(order), :]
+        outgoing = outgoing.reshape(len(send), share, count * top_rows)
+        received = lax.ppermute(outgoing, "panel", [(i, i ^ v) for i in range(panels)])
+        rows = rows[jnp.array(stay)] + received
+        keep = [keep[i] for i in stay]
+    total = rows[0]
     own_inverse = lax.dynamic_slice_in_dim(upper_inverse[0], begin, share, 1)
     own_base = jnp.einsum("kw,kr->wr", own_inverse, upper_rhs[0], precision=highest)
 

time: 70.7 us -> 80.7 us (1.14)
  the two profiles are of different devices: /device:TPU:0 before, /device:TPU:21 now
where the time goes in v14:
time: 80.7 us; the launch traced here: 80.1 us
  local copies, waits for them, and re-layouts  27.2 us (34%)
  waiting for transfers between devices  19.1 us (24%)
  starting transfers between devices  16.9 us (21%)
  matrix products  12.9 us (16%)
  other arithmetic  2.89 us (4%)
  between operations  1.06 us (1%)
    ppermute x12, waiting for transfers between devices, xor_gather(): parts.append(lax.ppermute(held, axes, [(i, i ^ v) for i in range(count)]))  14.8 us
    unnamed x40, local copies, waits for them, and re-layouts  11.4 us
    ppermute x12, starting transfers between devices, xor_gather(): parts.append(lax.ppermute(held, axes, [(i, i ^ v) for i in range(count)]))  10.5 us
    ppermute x1, starting transfers between devices, local(): lax.ppermute(held, both, [(i, i ^ 1 << last) for i in range(count)])  6.01 us
    gather x2, local copies, waits for them, and re-layouts, local(): slabs = source[places].reshape(position.shape[0], -1, own_rows.shape[1])  5.63 us
    ppermute x2, waiting for transfers between devices, local(): lax.ppermute(outgoing, 'panel', [(i, i ^ v) for i in range(panels)])  4.24 us
    gather x7, local copies, waits for them, and re-layouts, local(): rows[jnp.array(send)].reshape(len(send), share, count, top_rows)  3.94 us
    dot_general x2, matrix products, local(): term = jnp.einsum('skj,sjr->skr', pick, slabs, precision=highest)  3.68 us
  transfers between devices with their start and end apart: 15, of which 8 were waited for; matrix products, arithmetic and copies ran while one was open for 35% of the time, Pallas kernels for 0%

profile of v14, /device:TPU:21, one launch (start us, length us, event | category | flops | bytes accessed | tf_op | source)
XLA Modules:
  0.0 80.1 jit_solution(11114510842466795352)
XLA Ops:
  1.7 1.5 %collective-permute-start.4 = (f32[1,16,128]{2,1,0:T(8,128)}, f32[1,16,128]{2,1,0:T(8,128)S(1)}, u32[]{:S(2)}, u32[]{:S(2)}) collective-permute-start(f32[1,16,128]{2,1,0:T(8,128)} %bitcast.73), channel_id=1, source_target_pairs={{0,3},{1,2},{2,1},{3,0},{4,7},{5,6},{6,5},{7,4},{8,11},{9,10},{10,... | collective-permute-start | bytes 24584 | tf_op jit(solution)/shard_map/ppermute | solution.py:13
  3.7 2.4 %fusion.9 = f32[256,512]{1,0:T(8,128)S(1)} fusion(f32[1,512,512]{2,1,0:T(8,128)} %param.21, f32[1,256,512]{2,1,0:T(8,128)} %param.20), kind=kOutput, calls=%fused_computation.18 | convolution fusion | flops 805306368 | bytes 2097152 | tf_op jit(solution)/shard_map/kv,vw->kw/dot_general | solution.py:102
  8.0 1.4 %gather_fusion.1 = f32[2,128,512]{2,1,0:T(8,128)} fusion(f32[4,128,512]{2,1,0:T(8,128)S(1)} %pad_maximum_fusion, s32[1024]{0:T(1024)S(1)} %get-tuple-element.60), kind=kCustom, calls=%fused_computation.1 | custom fusion | bytes 1048584 | tf_op jit(solution)/shard_map/gather | solution.py:111
  9.4 1.2 %copy.26 = f32[2,128,512]{1,2,0:T(8,128)S(1)} copy(f32[2,128,512]{2,1,0:T(8,128)} %gather_fusion.1) | data formatting | bytes 1048576 | tf_op jit(solution)/shard_map/gather | solution.py:111
  13.1 1.6 %fusion.20 = f32[128,128]{1,0:T(8,128)S(1)} fusion(f32[1,512,128]{2,1,0:T(8,128)} %param.19, f32[1,512,512]{2,1,0:T(8,128)} %param.21, s32[]{:T(128)S(6)} %select_n.105), kind=kOutput, calls=%fused_computation.30 | convolution fusion | flops 100663296 | bytes 589828 | tf_op jit(solution)/shard_map/kw,kr->wr/dot_general | solution.py:118
  14.7 1.8 %gather_fusion = f32[2,128,512]{2,1,0:T(8,128)S(1)} fusion(f32[4,128,512]{2,1,0:T(8,128)} %copy-done.3, s32[1024]{0:T(1024)S(1)} %pad_clamp_fusion.6), kind=kCustom, calls=%fused_computation | custom fusion | bytes 1048584 | tf_op jit(solution)/shard_map/gather | solution.py:114
  17.2 1.3 %constant_dynamic-update-slice_fusion.3 = (f32[8,16,128]{2,1,0:T(8,128)}, f32[32,16,128]{2,1,0:T(8,128)S(1)}) fusion(f32[8,16,128]{2,1,0:T(8,128)} %get-tuple-element.42, f32[1,16,128]{2,1,0:T(8,128)} %copy-done.8, f32[32,16,128]{2,1,0:T(8,128)S(1)} %get-tuple-element.43), kind=kLoop, calls=%fused_computation.44 | loop fusion | bytes 24576
  21.5 2.2 %collective-permute-start.6 = (f32[8,16,128]{2,1,0:T(8,128)}, f32[8,16,128]{2,1,0:T(8,128)S(1)}, u32[]{:S(2)}, u32[]{:S(2)}) collective-permute-start(f32[8,16,128]{2,1,0:T(8,128)} %get-tuple-element.34), channel_id=1, source_target_pairs={{0,8},{1,9},{2,10},{3,11},{4,12},{5,13},{6,14},{7,15},{8,0},{9,1},... | collective-permute-start | bytes 196616 | tf_op jit(solution)/shard_map/ppermute | solution.py:13
  24.4 1.2 %collective-permute-start.7 = (f32[8,16,128]{2,1,0:T(8,128)}, f32[8,16,128]{2,1,0:T(8,128)}, u32[]{:S(2)}, u32[]{:S(2)}) collective-permute-start(f32[8,16,128]{2,1,0:T(8,128)} %get-tuple-element.34), channel_id=1, source_target_pairs={{0,4},{1,5},{2,6},{3,7},{4,0},{5,1},{6,2},{7,3},{8,12},{9,13},{10,... | collective-permute-start | bytes 196616 | tf_op jit(solution)/shard_map/ppermute | solution.py:13
  30.7 4.2 %collective-permute-done.1 = f32[1,128,512]{2,1,0:T(8,128)S(1)} collective-permute-done((f32[1,128,512]{2,1,0:T(8,128)}, f32[1,128,512]{2,1,0:T(8,128)S(1)}, u32[]{:S(2)}, u32[]{:S(2)}) %collective-permute-start.1) | collective-permute-done | bytes 262176 | tf_op jit(solution)/shard_map/ppermute | solution.py:113
  36.2 2.9 %collective-permute-done.9 = f32[1,128,128]{2,1,0:T(8,128)S(1)} collective-permute-done((f32[1,128,128]{2,1,0:T(8,128)S(1)}, f32[1,128,128]{2,1,0:T(8,128)S(1)}, u32[]{:S(2)}, u32[]{:S(2)}) %collective-permute-start.9) | collective-permute-done | bytes 65568 | tf_op jit(solution)/shard_map/ppermute | solution.py:13
  39.6 4.4 %collective-permute-done.10 = f32[2,128,128]{2,1,0:T(8,128)S(1)} collective-permute-done((f32[2,128,128]{2,1,0:T(8,128)S(1)}, f32[2,128,128]{2,1,0:T(8,128)S(1)}, u32[]{:S(2)}, u32[]{:S(2)}) %collective-permute-start.10) | collective-permute-done | bytes 131104 | tf_op jit(solution)/shard_map/ppermute | solution.py:13
  44.1 2.6 %collective-permute-start.11 = (f32[4,128,128]{2,1,0:T(8,128)S(1)}, f32[4,128,128]{2,1,0:T(8,128)S(1)}, u32[]{:S(2)}, u32[]{:S(2)}) collective-permute-start(f32[4,128,128]{2,1,0:T(8,128)S(1)} %pad_maximum_fusion.1), channel_id=1, source_target_pairs={{0,8},{1,9},{2,10},{3,11},{4,12},{5,13},{6,14},{7,15},{8,0},{9,1},... | collective-permute-start | bytes 786440 | tf_op jit(solution)/shard_map/ppermute | solution.py:13
  47.3 1.2 %collective-permute-start.12 = (f32[4,128,128]{2,1,0:T(8,128)S(1)}, f32[4,128,128]{2,1,0:T(8,128)S(1)}, u32[]{:S(2)}, u32[]{:S(2)}) collective-permute-start(f32[4,128,128]{2,1,0:T(8,128)S(1)} %pad_maximum_fusion.1), channel_id=1, source_target_pairs={{0,4},{1,5},{2,6},{3,7},{4,0},{5,1},{6,2},{7,3},{8,12},{9,13},{10,... | collective-permute-start | bytes 786440 | tf_op jit(solution)/shard_map/ppermute | solution.py:13
  51.7 2.1 %collective-permute-done.12 = f32[4,128,128]{2,1,0:T(8,128)S(1)} collective-permute-done((f32[4,128,128]{2,1,0:T(8,128)S(1)}, f32[4,128,128]{2,1,0:T(8,128)S(1)}, u32[]{:S(2)}, u32[]{:S(2)}) %collective-permute-start.12) | collective-permute-done | bytes 262176 | tf_op jit(solution)/shard_map/ppermute | solution.py:13
  54.5 2.7 %collective-permute-done.13 = f32[4,128,128]{2,1,0:T(8,128)S(1)} collective-permute-done((f32[4,128,128]{2,1,0:T(8,128)S(1)}, f32[4,128,128]{2,1,0:T(8,128)S(1)}, u32[]{:S(2)}, u32[]{:S(2)}) %collective-permute-start.13) | collective-permute-done | bytes 262176 | tf_op jit(solution)/shard_map/ppermute | solution.py:13
  57.9 6.0 %collective-permute-start.14 = (f32[16,128,128]{2,1,0:T(8,128)}, f32[16,128,128]{2,1,0:T(8,128)}, u32[]{:S(2)}, u32[]{:S(2)}) collective-permute-start(f32[16,128,128]{2,1,0:T(8,128)} %constant_dynamic-update-slice_fusion.13), channel_id=1, source_target_pairs={{0,1},{1,0},{2,3},{3,2},{4,5},{5,4},{6,7},{7,6},{8,9},{9,8},{10,11... | collective-permute-start | bytes 3145736 | tf_op jit(solution)/shard_map/ppermute | solution.py:125
  64.2 1.6 %copy.32 = f32[8,256,128]{1,2,0:T(8,128)S(1)} copy(f32[8,256,128]{2,1,0:T(8,128)} %param.28) | data formatting | bytes 2097152 | tf_op args[9]
  65.9 2.8 %gather_fusion.5 = f32[16,128,128]{2,1,0:T(8,128)} fusion(f32[16,128,128]{2,1,0:T(8,128)} %constant_dynamic-update-slice_fusion.13, s32[1024]{0:T(1024)S(1)} %pad_clamp_fusion.1), kind=kCustom, calls=%fused_computation.5 | custom fusion | bytes 2097216 | tf_op jit(solution)/shard_map/gather | solution.py:133
  68.8 2.8 %gather_fusion.6 = f32[16,128,128]{2,1,0:T(8,128)} fusion(f32[16,128,128]{2,1,0:T(8,128)} %collective-permute-done.14, s32[1024]{0:T(1024)S(1)} %pad_clamp_fusion), kind=kCustom, calls=%fused_computation.6 | custom fusion | bytes 2097216 | tf_op jit(solution)/shard_map/gather | solution.py:133
  71.6 2.5 %fusion = f32[8,256,128]{2,1,0:T(8,128)S(1)} fusion(f32[8,256,128]{2,1,0:T(8,128)} %bitcast.68, s32[256]{0:T(256)S(1)} %add_bitcast_fusion, s32[8,256]{1,0:T(8,128)S(1)} %copy-done.6), kind=kOutput, calls=%fused_computation.7 | convolution fusion | flops 805830656 | bytes 2106368 | tf_op jit(solution)/shard_map/skj,sjr->skr/dot_general | solution.py:137
  75.3 2.1 %fusion.7 = f32[8,256,128]{1,2,0:T(8,128)S(1)} fusion(f32[8,256,128]{1,2,0:T(8,128)S(1)} %copy.32, f32[8,256,128]{2,1,0:T(8,128)S(1)} %fusion.4, f32[8,256,256]{2,1,0:T(8,128)S(1)} %copy-done), kind=kOutput, calls=%fused_computation.14 | convolution fusion | flops 805568512 | bytes 5242880 | tf_op jit(solution)/shard_map/swk,skr->swr/dot_general | solution.py:142
  77.4 1.4 %convolution_bitcast_fusion = f32[8,256,128]{1,2,0:T(8,128)S(1)} fusion(f32[8,256,128]{1,2,0:T(8,128)S(1)} %fusion.7, f32[8,256,256]{2,1,0:T(8,128)S(1)} %copy-done.4), kind=kOutput, calls=%fused_computation.12 | convolution fusion | flops 805306368 | bytes 4194304 | tf_op jit(solution)/shard_map/swk,skr->swr/dot_general | solution.py:143
  78.8 1.3 %copy.33 = f32[8,256,128]{2,1,0:T(8,128)} copy(f32[8,256,128]{1,2,0:T(8,128)S(1)} %convolution_bitcast_fusion) | data formatting | bytes 2097152
  (103 shorter events, 23.8 us)
Async XLA Ops:
  0.6 74.7 %copy-start = (f32[8,256,256]{2,1,0:T(8,128)S(1)}, f32[8,256,256]{2,1,0:T(8,128)}, u32[]{:S(2)}) copy-start(f32[8,256,256]{2,1,0:T(8,128)} %param.27) | copy-start | bytes 6291460
  0.6 5.5 %copy-start.9 = (s32[2]{0:T(128)S(1)}, s32[2]{0:T(128)}, u32[]{:S(2)}) copy-start(s32[2]{0:T(128)} %constant.124.clone) | copy-start | bytes 28
  0.7 5.5 %copy-start.12 = (s32[32]{0:T(128)S(1)}, s32[32]{0:T(128)}, u32[]{:S(2)}) copy-start(s32[32]{0:T(128)} %constant.197) | copy-start | bytes 388
  0.7 5.5 %copy-start.11 = (s32[1,256]{1,0:T(1,128)S(1)}, s32[1,256]{1,0:T(1,128)}, u32[]{:S(2)}) copy-start(s32[1,256]{1,0:T(1,128)} %param.22) | copy-start | bytes 3076
  0.7 15.9 %collective-permute-start.2 = (f32[1,16,128]{2,1,0:T(8,128)}, f32[1,16,128]{2,1,0:T(8,128)S(1)}, u32[]{:S(2)}, u32[]{:S(2)}) collective-permute-start(f32[1,16,128]{2,1,0:T(8,128)} %bitcast.71), channel_id=1, source_target_pairs={{0,1},{1,0},{2,3},{3,2},{4,5},{5,4},{6,7},{7,6},{8,9},{9,8},{10,11... | collective-permute-start | bytes 24584 | tf_op jit(solution)/shard_map/ppermute | solution.py:13
  1.4 15.1 %collective-permute-start.3 = (f32[1,16,128]{2,1,0:T(8,128)}, f32[1,16,128]{2,1,0:T(8,128)S(1)}, u32[]{:S(2)}, u32[]{:S(2)}) collective-permute-start(f32[1,16,128]{2,1,0:T(8,128)} %bitcast.72), channel_id=1, source_target_pairs={{0,2},{1,3},{2,0},{3,1},{4,6},{5,7},{6,4},{7,5},{8,10},{9,11},{10,... | collective-permute-start | bytes 24584 | tf_op jit(solution)/shard_map/ppermute | solution.py:13
  1.7 14.9 %collective-permute-start.4 = (f32[1,16,128]{2,1,0:T(8,128)}, f32[1,16,128]{2,1,0:T(8,128)S(1)}, u32[]{:S(2)}, u32[]{:S(2)}) collective-permute-start(f32[1,16,128]{2,1,0:T(8,128)} %bitcast.73), channel_id=1, source_target_pairs={{0,3},{1,2},{2,1},{3,0},{4,7},{5,6},{6,5},{7,4},{8,11},{9,10},{10,... | collective-permute-start | bytes 24584 | tf_op jit(solution)/shard_map/ppermute | solution.py:13
  11.5 14.1 %collective-permute-start = (f32[2,128,512]{2,1,0:T(8,128)S(1)}, f32[2,128,512]{2,1,0:T(8,128)}, u32[]{:S(2)}, u32[]{:S(2)}) collective-permute-start(f32[2,128,512]{2,1,0:T(8,128)S(1)} %copy.28), channel_id=1, source_target_pairs={{0,1},{1,0},{2,3},{3,2},{4,5},{5,4},{6,7},{7,6},{8,9},{9,8},{10,11... | collective-permute-start | bytes 1572872 | tf_op jit(solution)/shard_map/ppermute | solution.py:113
  17.1 3.7 %collective-permute-start.5 = (f32[4,16,128]{2,1,0:T(8,128)S(1)}, f32[4,16,128]{2,1,0:T(8,128)S(1)}, u32[]{:S(2)}, u32[]{:S(2)}) collective-permute-start(f32[4,16,128]{2,1,0:T(8,128)S(1)} %pad_maximum_fusion.3), channel_id=1, source_target_pairs={{0,16},{1,17},{2,18},{3,19},{4,20},{5,21},{6,22},{7,23},{8,24},{9,... | collective-permute-start | bytes 98312 | tf_op jit(solution)/shard_map/ppermute | solution.py:13
  21.5 7.1 %collective-permute-start.6 = (f32[8,16,128]{2,1,0:T(8,128)}, f32[8,16,128]{2,1,0:T(8,128)S(1)}, u32[]{:S(2)}, u32[]{:S(2)}) collective-permute-start(f32[8,16,128]{2,1,0:T(8,128)} %get-tuple-element.34), channel_id=1, source_target_pairs={{0,8},{1,9},{2,10},{3,11},{4,12},{5,13},{6,14},{7,15},{8,0},{9,1},... | collective-permute-start | bytes 196616 | tf_op jit(solution)/shard_map/ppermute | solution.py:13
  24.4 4.2 %collective-permute-start.7 = (f32[8,16,128]{2,1,0:T(8,128)}, f32[8,16,128]{2,1,0:T(8,128)}, u32[]{:S(2)}, u32[]{:S(2)}) collective-permute-start(f32[8,16,128]{2,1,0:T(8,128)} %get-tuple-element.34), channel_id=1, source_target_pairs={{0,4},{1,5},{2,6},{3,7},{4,0},{5,1},{6,2},{7,3},{8,12},{9,13},{10,... | collective-permute-start | bytes 196616 | tf_op jit(solution)/shard_map/ppermute | solution.py:13
  25.6 4.3 %collective-permute-start.8 = (f32[8,16,128]{2,1,0:T(8,128)}, f32[8,16,128]{2,1,0:T(8,128)}, u32[]{:S(2)}, u32[]{:S(2)}) collective-permute-start(f32[8,16,128]{2,1,0:T(8,128)} %get-tuple-element.34), channel_id=1, source_target_pairs={{0,12},{1,13},{2,14},{3,15},{4,8},{5,9},{6,10},{7,11},{8,4},{9,5},... | collective-permute-start | bytes 196616 | tf_op jit(solution)/shard_map/ppermute | solution.py:13
  27.4 19.2 %copy-start.10 = (s32[2]{0:T(128)S(1)}, s32[2]{0:T(128)}, u32[]{:S(2)}) copy-start(s32[2]{0:T(128)} %constant.124.clone) | copy-start | bytes 28
  27.5 19.2 %copy-start.1 = (s32[8]{0:T(128)S(1)}, s32[8]{0:T(128)}, u32[]{:S(2)}) copy-start(s32[8]{0:T(128)} %param.24) | copy-start | bytes 100
  28.3 6.7 %collective-permute-start.1 = (f32[1,128,512]{2,1,0:T(8,128)}, f32[1,128,512]{2,1,0:T(8,128)S(1)}, u32[]{:S(2)}, u32[]{:S(2)}) collective-permute-start(f32[1,128,512]{2,1,0:T(8,128)} %copy.30), channel_id=1, source_target_pairs={{0,2},{1,3},{2,0},{3,1},{4,6},{5,7},{6,4},{7,5},{8,10},{9,11},{10,... | collective-permute-start | bytes 786440 | tf_op jit(solution)/shard_map/ppermute | solution.py:113
  36.0 29.7 %copy-start.5 = (f32[1,128,128]{2,1,0:T(8,128)}, f32[1,128,128]{2,1,0:T(8,128)S(1)}, u32[]{:S(2)}) copy-start(f32[1,128,128]{2,1,0:T(8,128)S(1)} %get-tuple-element.49) | copy-start | bytes 196612
  36.0 3.1 %collective-permute-start.9 = (f32[1,128,128]{2,1,0:T(8,128)S(1)}, f32[1,128,128]{2,1,0:T(8,128)S(1)}, u32[]{:S(2)}, u32[]{:S(2)}) collective-permute-start(f32[1,128,128]{2,1,0:T(8,128)S(1)} %get-tuple-element.49), channel_id=1, source_target_pairs={{0,2},{1,3},{2,0},{3,1},{4,6},{5,7},{6,4},{7,5},{8,10},{9,11},{10,... | collective-permute-start | bytes 196616 | tf_op jit(solution)/shard_map/ppermute | solution.py:13
  39.1 4.9 %collective-permute-start.10 = (f32[2,128,128]{2,1,0:T(8,128)S(1)}, f32[2,128,128]{2,1,0:T(8,128)S(1)}, u32[]{:S(2)}, u32[]{:S(2)}) collective-permute-start(f32[2,128,128]{2,1,0:T(8,128)S(1)} %pad_maximum_fusion.2), channel_id=1, source_target_pairs={{0,16},{1,17},{2,18},{3,19},{4,20},{5,21},{6,22},{7,23},{8,24},{9,... | collective-permute-start | bytes 393224 | tf_op jit(solution)/shard_map/ppermute | solution.py:13
  44.1 6.9 %collective-permute-start.11 = (f32[4,128,128]{2,1,0:T(8,128)S(1)}, f32[4,128,128]{2,1,0:T(8,128)S(1)}, u32[]{:S(2)}, u32[]{:S(2)}) collective-permute-start(f32[4,128,128]{2,1,0:T(8,128)S(1)} %pad_maximum_fusion.1), channel_id=1, source_target_pairs={{0,8},{1,9},{2,10},{3,11},{4,12},{5,13},{6,14},{7,15},{8,0},{9,1},... | collective-permute-start | bytes 786440 | tf_op jit(solution)/shard_map/ppermute | solution.py:13
  47.3 6.5 %collective-permute-start.12 = (f32[4,128,128]{2,1,0:T(8,128)S(1)}, f32[4,128,128]{2,1,0:T(8,128)S(1)}, u32[]{:S(2)}, u32[]{:S(2)}) collective-permute-start(f32[4,128,128]{2,1,0:T(8,128)S(1)} %pad_maximum_fusion.1), channel_id=1, source_target_pairs={{0,4},{1,5},{2,6},{3,7},{4,0},{5,1},{6,2},{7,3},{8,12},{9,13},{10,... | collective-permute-start | bytes 786440 | tf_op jit(solution)/shard_map/ppermute | solution.py:13
  49.1 8.1 %collective-permute-start.13 = (f32[4,128,128]{2,1,0:T(8,128)S(1)}, f32[4,128,128]{2,1,0:T(8,128)S(1)}, u32[]{:S(2)}, u32[]{:S(2)}) collective-permute-start(f32[4,128,128]{2,1,0:T(8,128)S(1)} %pad_maximum_fusion.1), channel_id=1, source_target_pairs={{0,12},{1,13},{2,14},{3,15},{4,8},{5,9},{6,10},{7,11},{8,4},{9,5},... | collective-permute-start | bytes 786440 | tf_op jit(solution)/shard_map/ppermute | solution.py:13
  57.9 10.8 %collective-permute-start.14 = (f32[16,128,128]{2,1,0:T(8,128)}, f32[16,128,128]{2,1,0:T(8,128)}, u32[]{:S(2)}, u32[]{:S(2)}) collective-permute-start(f32[16,128,128]{2,1,0:T(8,128)} %constant_dynamic-update-slice_fusion.13), channel_id=1, source_target_pairs={{0,1},{1,0},{2,3},{3,2},{4,5},{5,4},{6,7},{7,6},{8,9},{9,8},{10,11... | collective-permute-start | bytes 3145736 | tf_op jit(solution)/shard_map/ppermute | solution.py:125
  65.9 5.6 %copy-start.6 = (s32[8,256]{1,0:T(8,128)S(1)}, s32[8,256]{1,0:T(8,128)}, u32[]{:S(2)}) copy-start(s32[8,256]{1,0:T(8,128)} %param.26) | copy-start | bytes 24580
  71.6 2.5 %copy-start.2 = (f32[16,128,128]{2,1,0:T(8,128)S(1)}, f32[16,128,128]{2,1,0:T(8,128)}, u32[]{:S(2)}) copy-start(f32[16,128,128]{2,1,0:T(8,128)} %gather_fusion.5) | copy-start | bytes 3145732
  (5 other events, 5.6 us)

commit v15 on v10

--- a/solution.py
+++ b/solution.py
@@ -91,7 +91,7 @@
         leaf_groups.append([high_first[0]])
         high_first = high_first[1:]
     leaf_groups += [high_first[i : i + 2] for i in range(0, len(high_first), 2)]
-    top_groups = [panel_bits] + leaf_groups
+    top_groups = leaf_groups + [panel_bits]
     spread_groups = [[b] for b in panel_bits[1:]] + leaf_groups + [[0]]
 
     top_rows, rhs = top_solution.shape
@@ -101,17 +101,23 @@
     pick_top = (top_index[0][:, None] == natural[None, :]).astype(jnp.float32)
     folded = jnp.einsum("kv,vw->kw", upper_panel[0], upper_inverse[0], precision=highest)
     weights = jnp.einsum("kj,kw->wj", pick_top, folded, precision=highest)
+    own_inverse = lax.dynamic_slice_in_dim(upper_inverse[0], begin, share, 1)
+    own_base = jnp.einsum("kw,kr->wr", own_inverse, upper_rhs[0], precision=highest)
+
+    top_held = xor_gather(top_solution, both, count, top_groups[:-1])
+    top_size = top_held.size
     total = lax.dynamic_slice_in_dim(weights, begin, share, 0)
-    for v in range(1, panels):
+    parts = [top_held]
+    for k in range(1, panels):
+        v = sum(((k >> t) & 1) << b for t, b in enumerate(panel_bits))
         outgoing = lax.dynamic_slice_in_dim(weights, (panel_index ^ v) * share, share, 0)
         order = [static_position(static_offset(h, top_groups) ^ v, top_groups) for h in range(count)]
         outgoing = outgoing.reshape(share, count, top_rows)[:, jnp.array(order), :]
-        outgoing = outgoing.reshape(share, count * top_rows)
-        total = total + lax.ppermute(outgoing, "panel", [(i, i ^ v) for i in range(panels)])
-    own_inverse = lax.dynamic_slice_in_dim(upper_inverse[0], begin, share, 1)
-    own_base = jnp.einsum("kw,kr->wr", own_inverse, upper_rhs[0], precision=highest)
-
-    top_held = xor_gather(top_solution, both, count, top_groups).reshape(count * top_rows, rhs)
+        message = jnp.concatenate([top_held.reshape(-1), outgoing.reshape(-1)])
+        arrived = lax.ppermute(message, both, [(i, i ^ v) for i in range(count)])
+        parts.append(arrived[:top_size].reshape(top_held.shape))
+        total = total + arrived[top_size:].reshape(share, count * top_rows)
+    top_held = jnp.concatenate(parts, 0).reshape(count * top_rows, rhs)
     own_rows = own_base - jnp.einsum("wj,jr->wr", total, top_held, precision=highest)
 
     held = xor_gather(own_rows, both, count, spread_groups[:-1])

time: 70.7 us -> 107 us (1.51)
  local copies, waits for them, and re-layouts: 13.3 us -> 41.4 us
  waiting for transfers between devices: 16.6 us -> 31.7 us
  starting transfers between devices: 21.7 us -> 15.1 us
  matrix products: 16.3 us -> 14.9 us
    ppermute x3, waiting for transfers between devices: 0.01 us -> 11 us  [local(): arrived = lax.ppermute(message, both, [(i, i ^ v) for i in range(count)])]
    gather x3 -> x6, local copies, waits for them, and re-layouts: 1.75 us -> 10.3 us  [local(): outgoing = outgoing.reshape(share, count, top_rows)[:, jnp.array(order), :]]
    unnamed x37 -> x42, local copies, waits for them, and re-layouts: 4.95 us -> 11.6 us
    reshape x0 -> x3, local copies, waits for them, and re-layouts: none -> 6.54 us  [local(): message = jnp.concatenate([top_held.reshape(-1), outgoing.reshape(-1)])]
    ppermute x12 -> x9, starting transfers between devices: 19.4 us -> 13.2 us  [xor_gather(): parts.append(lax.ppermute(held, axes, [(i, i ^ v) for i in range(count)]))]
    ppermute x12 -> x9, waiting for transfers between devices: 15.9 us -> 20.7 us  [xor_gather(): parts.append(lax.ppermute(held, axes, [(i, i ^ v) for i in range(count)]))]
    slice x0 -> x13, local copies, waits for them, and re-layouts: none -> 4.13 us  [the longest x9 2.44 us: local(): total = total + arrived[top_size:].reshape(share, count * top_rows)]
    dot_general x1, matrix products: 3.52 us -> 2.06 us  [local(): jnp.einsum('swk,skr->swr', panel_t, parent_rows, precision=highest)]
  transfers between devices with their start and end apart: 16 -> 13, of which waited for: 9 -> 8; matrix products, arithmetic and copies ran while one was open for 19% -> 34% of each run, Pallas kernels for 0% -> 0%
where the time goes in v15:
time: 107 us; the launch traced here: 106 us
  local copies, waits for them, and re-layouts  41.4 us (39%)
  waiting for transfers between devices  31.7 us (30%)
  starting transfers between devices  15.1 us (14%)
  matrix products  14.9 us (14%)
  other arithmetic  2.07 us (2%)
  between operations  1.12 us (1%)
    ppermute x9, waiting for transfers between devices, xor_gather(): parts.append(lax.ppermute(held, axes, [(i, i ^ v) for i in range(count)]))  20.7 us
    ppermute x9, starting transfers between devices, xor_gather(): parts.append(lax.ppermute(held, axes, [(i, i ^ v) for i in range(count)]))  13.2 us
    unnamed x42, local copies, waits for them, and re-layouts  11.6 us
    ppermute x3, waiting for transfers between devices, local(): arrived = lax.ppermute(message, both, [(i, i ^ v) for i in range(count)])  11 us
    gather x6, local copies, waits for them, and re-layouts, local(): outgoing = outgoing.reshape(share, count, top_rows)[:, jnp.array(order), :]  10.3 us
    reshape x3, local copies, waits for them, and re-layouts, local(): message = jnp.concatenate([top_held.reshape(-1), outgoing.reshape(-1)])  6.54 us
    gather x2, local copies, waits for them, and re-layouts, local(): slabs = source[places].reshape(position.shape[0], -1, own_rows.shape[1])  5.64 us
    dot_general x2, matrix products, local(): term = jnp.einsum('skj,sjr->skr', pick, slabs, precision=highest)  3.87 us
  transfers between devices with their start and end apart: 13, of which 8 were waited for; matrix products, arithmetic and copies ran while one was open for 34% of the time, Pallas kernels for 0%

profile of v15, /device:TPU:0, one launch (start us, length us, event | category | flops | bytes accessed | tf_op | source)
XLA Modules:
  0.0 106.2 jit_solution(10116467615587309523)
XLA Ops:
  0.7 4.1 %collective-permute-start = (f32[1,16,128]{2,1,0:T(8,128)}, f32[1,16,128]{2,1,0:T(8,128)S(1)}, u32[]{:S(2)}, u32[]{:S(2)}) collective-permute-start(f32[1,16,128]{2,1,0:T(8,128)} %bitcast.66), channel_id=1, source_target_pairs={{0,16},{1,17},{2,18},{3,19},{4,20},{5,21},{6,22},{7,23},{8,24},{9,... | collective-permute-start | bytes 24584 | tf_op jit(solution)/shard_map/ppermute | solution.py:13
  7.3 2.4 %fusion.9 = f32[256,512]{1,0:T(8,128)S(1)} fusion(f32[1,512,512]{2,1,0:T(8,128)} %param.18, f32[1,256,512]{2,1,0:T(8,128)} %param.17), kind=kOutput, calls=%fused_computation.16 | convolution fusion | flops 805306368 | bytes 2097152 | tf_op jit(solution)/shard_map/kv,vw->kw/dot_general | solution.py:102
  12.1 2.8 %copy.29 = f32[128,32,16]{2,1,0:T(8,128)} copy(f32[128,32,16]{0,2,1:T(8,128)S(1)} %bitcast.56) | data formatting | bytes 524288 | tf_op jit(solution)/shard_map/gather | solution.py:115
  14.9 2.2 %reshape.512 = f32[65536]{0:T(1024)S(1)} reshape(f32[128,32,16]{2,1,0:T(8,128)} %copy.29) | data formatting | bytes 524288 | tf_op jit(solution)/shard_map/reshape | solution.py:116
  17.7 2.8 %copy.25 = f32[128,32,16]{2,1,0:T(8,128)} copy(f32[128,32,16]{0,2,1:T(8,128)S(1)} %bitcast.57) | data formatting | bytes 524288 | tf_op jit(solution)/shard_map/gather | solution.py:115
  20.5 2.2 %reshape.508 = f32[65536]{0:T(1024)S(1)} reshape(f32[128,32,16]{2,1,0:T(8,128)} %copy.25) | data formatting | bytes 524288 | tf_op jit(solution)/shard_map/reshape | solution.py:116
  23.3 2.8 %copy.27 = f32[128,32,16]{2,1,0:T(8,128)} copy(f32[128,32,16]{0,2,1:T(8,128)S(1)} %bitcast.58) | data formatting | bytes 524288 | tf_op jit(solution)/shard_map/gather | solution.py:115
  26.2 2.2 %reshape.510 = f32[65536]{0:T(1024)S(1)} reshape(f32[128,32,16]{2,1,0:T(8,128)} %copy.27) | data formatting | bytes 524288 | tf_op jit(solution)/shard_map/reshape | solution.py:116
  28.4 1.6 %collective-permute-start.1 = (f32[2,16,128]{2,1,0:T(8,128)S(1)}, f32[2,16,128]{2,1,0:T(8,128)S(1)}, u32[]{:S(2)}, u32[]{:S(2)}) collective-permute-start(f32[2,16,128]{2,1,0:T(8,128)S(1)} %pad_maximum_fusion.5), channel_id=1, source_target_pairs={{0,8},{1,9},{2,10},{3,11},{4,12},{5,13},{6,14},{7,15},{8,0},{9,1},... | collective-permute-start | bytes 49160 | tf_op jit(solution)/shard_map/ppermute | solution.py:13
  34.4 1.8 %collective-permute-done.3 = f32[2,16,128]{2,1,0:T(8,128)S(1)} collective-permute-done((f32[2,16,128]{2,1,0:T(8,128)S(1)}, f32[2,16,128]{2,1,0:T(8,128)S(1)}, u32[]{:S(2)}, u32[]{:S(2)}) %collective-permute-start.3) | collective-permute-done | bytes 16416 | tf_op jit(solution)/shard_map/ppermute | solution.py:13
  39.6 2.2 %fusion.18 = f32[128,128]{1,0:T(8,128)} fusion(f32[1,512,128]{2,1,0:T(8,128)S(1)} %copy-done.7, f32[1,512,512]{2,1,0:T(8,128)} %param.18, s32[]{:T(128)S(6)} %select_n.96), kind=kOutput, calls=%fused_computation.29 | convolution fusion | flops 100663296 | bytes 589828 | tf_op jit(solution)/shard_map/kw,kr->wr/dot_general | solution.py:105
  42.7 5.9 %collective-permute-done.5 = f32[81920]{0:T(1024)} collective-permute-done((f32[81920]{0:T(1024)}, f32[81920]{0:T(1024)}, u32[]{:S(2)}, u32[]{:S(2)}) %collective-permute-start.5) | collective-permute-done | bytes 327712 | tf_op jit(solution)/shard_map/ppermute | solution.py:117
  49.7 5.1 %collective-permute-done.6 = f32[81920]{0:T(1024)} collective-permute-done((f32[81920]{0:T(1024)S(1)}, f32[81920]{0:T(1024)}, u32[]{:S(2)}, u32[]{:S(2)}) %collective-permute-start.6) | collective-permute-done | bytes 327712 | tf_op jit(solution)/shard_map/ppermute | solution.py:117
  59.5 2.3 %constant_dynamic-update-slice_fusion.18 = (f32[16,128,128]{2,1,0:T(8,128)}, f32[1,128,128]{2,1,0:T(8,128)S(1)}) fusion(f32[128,128]{1,0:T(8,128)} %fusion.18, f32[512,128]{1,0:T(8,128)} %bitcast.62, f32[128,512]{0,1:T(8,128)S(1)} %copy.30, f32[128,512]{0,1:T(8,128)S(1)} %copy.28, f32[128,512]{0,1:T(8,128)S(1)} %copy.26, f32[512,512]{0,1:T(8,128)} %copy-done.2, ...), kind=kOutput, calls=%fused_computation.58 | convolution fusion | flops 100876288 | bytes 1507332 | tf_op jit(solution)/shard_map/wj,jr->wr/dot_general | solution.py:121
  63.3 2.7 %collective-permute-done.7 = f32[1,128,128]{2,1,0:T(8,128)S(1)} collective-permute-done((f32[1,128,128]{2,1,0:T(8,128)S(1)}, f32[1,128,128]{2,1,0:T(8,128)S(1)}, u32[]{:S(2)}, u32[]{:S(2)}) %collective-permute-start.7) | collective-permute-done | bytes 65568 | tf_op jit(solution)/shard_map/ppermute | solution.py:13
  66.5 7.7 %collective-permute-done.8 = f32[2,128,128]{2,1,0:T(8,128)S(1)} collective-permute-done((f32[2,128,128]{2,1,0:T(8,128)S(1)}, f32[2,128,128]{2,1,0:T(8,128)S(1)}, u32[]{:S(2)}, u32[]{:S(2)}) %collective-permute-start.8) | collective-permute-done | bytes 131104 | tf_op jit(solution)/shard_map/ppermute | solution.py:13
  76.2 2.9 %collective-permute-start.11 = (f32[4,128,128]{2,1,0:T(8,128)S(1)}, f32[4,128,128]{2,1,0:T(8,128)S(1)}, u32[]{:S(2)}, u32[]{:S(2)}) collective-permute-start(f32[4,128,128]{2,1,0:T(8,128)S(1)} %pad_maximum_fusion.3), channel_id=1, source_target_pairs={{0,12},{1,13},{2,14},{3,15},{4,8},{5,9},{6,10},{7,11},{8,4},{9,5},... | collective-permute-start | bytes 786440 | tf_op jit(solution)/shard_map/ppermute | solution.py:13
  79.8 3.7 %collective-permute-done.9 = f32[4,128,128]{2,1,0:T(8,128)S(1)} collective-permute-done((f32[4,128,128]{2,1,0:T(8,128)S(1)}, f32[4,128,128]{2,1,0:T(8,128)S(1)}, u32[]{:S(2)}, u32[]{:S(2)}) %collective-permute-start.9) | collective-permute-done | bytes 262176 | tf_op jit(solution)/shard_map/ppermute | solution.py:13
  84.3 4.2 %collective-permute-done.10 = f32[4,128,128]{2,1,0:T(8,128)S(1)} collective-permute-done((f32[4,128,128]{2,1,0:T(8,128)S(1)}, f32[4,128,128]{2,1,0:T(8,128)S(1)}, u32[]{:S(2)}, u32[]{:S(2)}) %collective-permute-start.10) | collective-permute-done | bytes 262176 | tf_op jit(solution)/shard_map/ppermute | solution.py:13
  90.1 1.6 %copy.32 = f32[8,256,128]{1,2,0:T(8,128)S(1)} copy(f32[8,256,128]{2,1,0:T(8,128)} %param.25) | data formatting | bytes 2097152 | tf_op args[9]
  91.9 2.8 %gather_fusion.4 = f32[16,128,128]{2,1,0:T(8,128)} fusion(f32[16,128,128]{2,1,0:T(8,128)} %constant_dynamic-update-slice_fusion.13, s32[1024]{0:T(1024)S(1)} %pad_clamp_fusion.1), kind=kCustom, calls=%fused_computation.4 | custom fusion | bytes 2097216 | tf_op jit(solution)/shard_map/gather | solution.py:133
  94.7 2.8 %gather_fusion.5 = f32[16,128,128]{2,1,0:T(8,128)} fusion(f32[16,128,128]{2,1,0:T(8,128)} %collective-permute-done.12, s32[1024]{0:T(1024)S(1)} %pad_clamp_fusion), kind=kCustom, calls=%fused_computation.5 | custom fusion | bytes 2097216 | tf_op jit(solution)/shard_map/gather | solution.py:133
  97.6 2.7 %fusion = f32[8,256,128]{2,1,0:T(8,128)S(1)} fusion(f32[8,256,128]{2,1,0:T(8,128)} %bitcast.60, s32[256]{0:T(256)S(1)} %add_bitcast_fusion, s32[8,256]{1,0:T(8,128)S(1)} %copy-done.8), kind=kOutput, calls=%fused_computation.6 | convolution fusion | flops 805830656 | bytes 2106368 | tf_op jit(solution)/shard_map/skj,sjr->skr/dot_general | solution.py:137
  101.5 2.1 %fusion.7 = f32[8,256,128]{1,2,0:T(8,128)S(1)} fusion(f32[8,256,128]{1,2,0:T(8,128)S(1)} %copy.32, f32[8,256,128]{2,1,0:T(8,128)S(1)} %fusion.4, f32[8,256,256]{2,1,0:T(8,128)S(1)} %copy-done), kind=kOutput, calls=%fused_computation.13 | convolution fusion | flops 805568512 | bytes 5242880 | tf_op jit(solution)/shard_map/swk,skr->swr/dot_general | solution.py:142
  (110 shorter events, 31.5 us)
Async XLA Ops:
  0.6 100.8 %copy-start = (f32[8,256,256]{2,1,0:T(8,128)S(1)}, f32[8,256,256]{2,1,0:T(8,128)}, u32[]{:S(2)}) copy-start(f32[8,256,256]{2,1,0:T(8,128)} %param.24) | copy-start | bytes 6291460
  0.6 9.1 %copy-start.14 = (s32[32]{0:T(128)S(1)}, s32[32]{0:T(128)}, u32[]{:S(2)}) copy-start(s32[32]{0:T(128)} %constant.145) | copy-start | bytes 388
  0.7 9.1 %copy-start.10 = (s32[1,256]{1,0:T(1,128)S(1)}, s32[1,256]{1,0:T(1,128)}, u32[]{:S(2)}) copy-start(s32[1,256]{1,0:T(1,128)} %param.19) | copy-start | bytes 3076
  0.7 27.7 %collective-permute-start = (f32[1,16,128]{2,1,0:T(8,128)}, f32[1,16,128]{2,1,0:T(8,128)S(1)}, u32[]{:S(2)}, u32[]{:S(2)}) collective-permute-start(f32[1,16,128]{2,1,0:T(8,128)} %bitcast.66), channel_id=1, source_target_pairs={{0,16},{1,17},{2,18},{3,19},{4,20},{5,21},{6,22},{7,23},{8,24},{9,... | collective-permute-start | bytes 24584 | tf_op jit(solution)/shard_map/ppermute | solution.py:13
  23.3 5.1 %copy-start.9 = (f32[16,128]{1,0:T(8,128)S(1)}, f32[16,128]{1,0:T(8,128)}, u32[]{:S(2)}) copy-start(f32[16,128]{1,0:T(8,128)} %param.20) | copy-start | bytes 24580
  26.2 13.4 %copy-start.7 = (f32[1,512,128]{2,1,0:T(8,128)S(1)}, f32[1,512,128]{2,1,0:T(8,128)}, u32[]{:S(2)}) copy-start(f32[1,512,128]{2,1,0:T(8,128)} %param.16) | copy-start | bytes 786436
  28.4 4.2 %collective-permute-start.1 = (f32[2,16,128]{2,1,0:T(8,128)S(1)}, f32[2,16,128]{2,1,0:T(8,128)S(1)}, u32[]{:S(2)}, u32[]{:S(2)}) collective-permute-start(f32[2,16,128]{2,1,0:T(8,128)S(1)} %pad_maximum_fusion.5), channel_id=1, source_target_pairs={{0,8},{1,9},{2,10},{3,11},{4,12},{5,13},{6,14},{7,15},{8,0},{9,1},... | collective-permute-start | bytes 49160 | tf_op jit(solution)/shard_map/ppermute | solution.py:13
  30.0 3.7 %collective-permute-start.2 = (f32[2,16,128]{2,1,0:T(8,128)S(1)}, f32[2,16,128]{2,1,0:T(8,128)S(1)}, u32[]{:S(2)}, u32[]{:S(2)}) collective-permute-start(f32[2,16,128]{2,1,0:T(8,128)S(1)} %pad_maximum_fusion.5), channel_id=1, source_target_pairs={{0,4},{1,5},{2,6},{3,7},{4,0},{5,1},{6,2},{7,3},{8,12},{9,13},{10,... | collective-permute-start | bytes 49160 | tf_op jit(solution)/shard_map/ppermute | solution.py:13
  31.5 4.6 %collective-permute-start.3 = (f32[2,16,128]{2,1,0:T(8,128)S(1)}, f32[2,16,128]{2,1,0:T(8,128)S(1)}, u32[]{:S(2)}, u32[]{:S(2)}) collective-permute-start(f32[2,16,128]{2,1,0:T(8,128)S(1)} %pad_maximum_fusion.5), channel_id=1, source_target_pairs={{0,12},{1,13},{2,14},{3,15},{4,8},{5,9},{6,10},{7,11},{8,4},{9,5},... | collective-permute-start | bytes 49160 | tf_op jit(solution)/shard_map/ppermute | solution.py:13
  37.7 4.0 %collective-permute-start.4 = (f32[81920]{0:T(1024)}, f32[81920]{0:T(1024)S(1)}, u32[]{:S(2)}, u32[]{:S(2)}) collective-permute-start(f32[81920]{0:T(1024)} %get-tuple-element.13), channel_id=1, source_target_pairs={{0,1},{1,0},{2,3},{3,2},{4,5},{5,4},{6,7},{7,6},{8,9},{9,8},{10,11... | collective-permute-start | bytes 983048 | tf_op jit(solution)/shard_map/ppermute | solution.py:117
  37.7 10.8 %collective-permute-start.5 = (f32[81920]{0:T(1024)}, f32[81920]{0:T(1024)}, u32[]{:S(2)}, u32[]{:S(2)}) collective-permute-start(f32[81920]{0:T(1024)} %get-tuple-element.12), channel_id=1, source_target_pairs={{0,2},{1,3},{2,0},{3,1},{4,6},{5,7},{6,4},{7,5},{8,10},{9,11},{10,... | collective-permute-start | bytes 983048 | tf_op jit(solution)/shard_map/ppermute | solution.py:117
  39.2 15.5 %collective-permute-start.6 = (f32[81920]{0:T(1024)S(1)}, f32[81920]{0:T(1024)}, u32[]{:S(2)}, u32[]{:S(2)}) collective-permute-start(f32[81920]{0:T(1024)S(1)} %get-tuple-element.11), channel_id=1, source_target_pairs={{0,3},{1,2},{2,1},{3,0},{4,7},{5,6},{6,5},{7,4},{8,11},{9,10},{10,... | collective-permute-start | bytes 983048 | tf_op jit(solution)/shard_map/ppermute | solution.py:117
  42.5 13.4 %slice-start = ((f32[81920]{0:T(1024)}), f32[16384]{0:T(1024)S(1)}, s32[]{:S(2)}) async-start(f32[81920]{0:T(1024)} %copy-done.6), calls=%async_computation | async-start | bytes 131072 | tf_op jit(solution)/shard_map/slice | solution.py:118
  55.7 18.6 %copy-start.11 = (s32[2]{0:T(128)S(1)}, s32[2]{0:T(128)}, u32[]{:S(2)}) copy-start(s32[2]{0:T(128)} %constant.120.clone) | copy-start | bytes 28
  55.8 18.6 %copy-start.1 = (s32[8]{0:T(128)S(1)}, s32[8]{0:T(128)}, u32[]{:S(2)}) copy-start(s32[8]{0:T(128)} %param.21) | copy-start | bytes 100
  61.8 29.9 %copy-start.5 = (f32[1,128,128]{2,1,0:T(8,128)}, f32[1,128,128]{2,1,0:T(8,128)S(1)}, u32[]{:S(2)}) copy-start(f32[1,128,128]{2,1,0:T(8,128)S(1)} %get-tuple-element.29) | copy-start | bytes 196612
  61.8 4.3 %collective-permute-start.7 = (f32[1,128,128]{2,1,0:T(8,128)S(1)}, f32[1,128,128]{2,1,0:T(8,128)S(1)}, u32[]{:S(2)}, u32[]{:S(2)}) collective-permute-start(f32[1,128,128]{2,1,0:T(8,128)S(1)} %get-tuple-element.29), channel_id=1, source_target_pairs={{0,2},{1,3},{2,0},{3,1},{4,6},{5,7},{6,4},{7,5},{8,10},{9,11},{10,... | collective-permute-start | bytes 196616 | tf_op jit(solution)/shard_map/ppermute | solution.py:13
  66.1 8.1 %collective-permute-start.8 = (f32[2,128,128]{2,1,0:T(8,128)S(1)}, f32[2,128,128]{2,1,0:T(8,128)S(1)}, u32[]{:S(2)}, u32[]{:S(2)}) collective-permute-start(f32[2,128,128]{2,1,0:T(8,128)S(1)} %pad_maximum_fusion.4), channel_id=1, source_target_pairs={{0,16},{1,17},{2,18},{3,19},{4,20},{5,21},{6,22},{7,23},{8,24},{9,... | collective-permute-start | bytes 393224 | tf_op jit(solution)/shard_map/ppermute | solution.py:13
  74.2 9.3 %collective-permute-start.9 = (f32[4,128,128]{2,1,0:T(8,128)S(1)}, f32[4,128,128]{2,1,0:T(8,128)S(1)}, u32[]{:S(2)}, u32[]{:S(2)}) collective-permute-start(f32[4,128,128]{2,1,0:T(8,128)S(1)} %pad_maximum_fusion.3), channel_id=1, source_target_pairs={{0,8},{1,9},{2,10},{3,11},{4,12},{5,13},{6,14},{7,15},{8,0},{9,1},... | collective-permute-start | bytes 786440 | tf_op jit(solution)/shard_map/ppermute | solution.py:13
  75.0 13.4 %collective-permute-start.10 = (f32[4,128,128]{2,1,0:T(8,128)S(1)}, f32[4,128,128]{2,1,0:T(8,128)S(1)}, u32[]{:S(2)}, u32[]{:S(2)}) collective-permute-start(f32[4,128,128]{2,1,0:T(8,128)S(1)} %pad_maximum_fusion.3), channel_id=1, source_target_pairs={{0,4},{1,5},{2,6},{3,7},{4,0},{5,1},{6,2},{7,3},{8,12},{9,13},{10,... | collective-permute-start | bytes 786440 | tf_op jit(solution)/shard_map/ppermute | solution.py:13
  76.2 12.9 %collective-permute-start.11 = (f32[4,128,128]{2,1,0:T(8,128)S(1)}, f32[4,128,128]{2,1,0:T(8,128)S(1)}, u32[]{:S(2)}, u32[]{:S(2)}) collective-permute-start(f32[4,128,128]{2,1,0:T(8,128)S(1)} %pad_maximum_fusion.3), channel_id=1, source_target_pairs={{0,12},{1,13},{2,14},{3,15},{4,8},{5,9},{6,10},{7,11},{8,4},{9,5},... | collective-permute-start | bytes 786440 | tf_op jit(solution)/shard_map/ppermute | solution.py:13
  89.9 4.9 %collective-permute-start.12 = (f32[16,128,128]{2,1,0:T(8,128)}, f32[16,128,128]{2,1,0:T(8,128)}, u32[]{:S(2)}, u32[]{:S(2)}) collective-permute-start(f32[16,128,128]{2,1,0:T(8,128)} %constant_dynamic-update-slice_fusion.13), channel_id=1, source_target_pairs={{0,1},{1,0},{2,3},{3,2},{4,5},{5,4},{6,7},{7,6},{8,9},{9,8},{10,11... | collective-permute-start | bytes 3145736 | tf_op jit(solution)/shard_map/ppermute | solution.py:125
  91.9 5.6 %copy-start.8 = (s32[8,256]{1,0:T(8,128)S(1)}, s32[8,256]{1,0:T(8,128)}, u32[]{:S(2)}) copy-start(s32[8,256]{1,0:T(8,128)} %param.23) | copy-start | bytes 24580
  97.6 2.7 %copy-start.3 = (f32[16,128,128]{2,1,0:T(8,128)S(1)}, f32[16,128,128]{2,1,0:T(8,128)}, u32[]{:S(2)}) copy-start(f32[16,128,128]{2,1,0:T(8,128)} %gather_fusion.4) | copy-start | bytes 3145732
  (5 other events, 5.6 us)

commit v16 on v10

--- a/solution.py
+++ b/solution.py
@@ -133,10 +133,9 @@
 
     panel_t = jnp.swapaxes(lower_panel, 1, 2)
     inverse_t = jnp.swapaxes(lower_inverse, 1, 2)
-    lower_update = jnp.einsum("swk,skr->swr", panel_t, parent_rows, precision=highest)
-    lower_solution = jnp.einsum(
-        "swk,skr->swr", inverse_t, lower_rhs - lower_update, precision=highest
-    )
+    lower_base = jnp.einsum("swk,skr->swr", inverse_t, lower_rhs, precision=highest)
+    chained_t = jnp.einsum("swv,svk->swk", inverse_t, panel_t, precision=highest)
+    lower_solution = lower_base - jnp.einsum("swk,skr->swr", chained_t, parent_rows, precision=highest)
     return (own_rows[None], lower_solution)
 
 

time: 70.7 us -> 82.3 us (1.16)
  matrix products: 16.3 us -> 23.4 us
  local copies, waits for them, and re-layouts: 13.3 us -> 18.2 us
  waiting for transfers between devices: 16.6 us -> 14.1 us
  other arithmetic: 1.15 us -> 3.63 us
    dot_general x2 -> x3, matrix products: 5.53 us -> 12.7 us  [the longest x1 4.86 us: local(): jnp.einsum('swv,svk->swk', inverse_t, panel_t, precision=highest)]
    unnamed x37 -> x40, local copies, waits for them, and re-layouts: 4.95 us -> 7.48 us
    ppermute x12, waiting for transfers between devices: 15.9 us -> 14.1 us  [xor_gather(): parts.append(lax.ppermute(held, axes, [(i, i ^ v) for i in range(count)]))]
    gather x2, local copies, waits for them, and re-layouts: 4.66 us -> 5.84 us  [local(): slabs = source[places].reshape(position.shape[0], -1, own_rows.shape[1])]
  transfers between devices with their start and end apart: 16 -> 16, of which waited for: 9 -> 7; matrix products, arithmetic and copies ran while one was open for 19% -> 38% of each run, Pallas kernels for 0% -> 0%
where the time goes in v16:
time: 82.3 us; the launch traced here: 81.5 us
  matrix products  23.4 us (28%)
  starting transfers between devices  21.2 us (26%)
  local copies, waits for them, and re-layouts  18.2 us (22%)
  waiting for transfers between devices  14.1 us (17%)
  other arithmetic  3.63 us (4%)
  between operations  0.94 us (1%)
    ppermute x12, starting transfers between devices, xor_gather(): parts.append(lax.ppermute(held, axes, [(i, i ^ v) for i in range(count)]))  18.9 us
    ppermute x12, waiting for transfers between devices, xor_gather(): parts.append(lax.ppermute(held, axes, [(i, i ^ v) for i in range(count)]))  14.1 us
    unnamed x40, local copies, waits for them, and re-layouts  7.48 us
    gather x2, local copies, waits for them, and re-layouts, local(): slabs = source[places].reshape(position.shape[0], -1, own_rows.shape[1])  5.84 us
    dot_general x1, matrix products, local(): jnp.einsum('swv,svk->swk', inverse_t, panel_t, precision=highest)  4.86 us
    dot_general x1, matrix products, local(): jnp.einsum('swk,skr->swr', inverse_t, lower_rhs, precision=highest)  4.84 us
    dot_general x2, matrix products, local(): term = jnp.einsum('skj,sjr->skr', pick, slabs, precision=highest)  3.69 us
    dot_general x1, matrix products, local(): jnp.einsum('swk,skr->swr', chained_t, parent_rows, precision=highest)  2.95 us
  transfers between devices with their start and end apart: 16, of which 7 were waited for; matrix products, arithmetic and copies ran while one was open for 38% of the time, Pallas kernels for 0%

profile of v16, /device:TPU:0, one launch (start us, length us, event | category | flops | bytes accessed | tf_op | source)
XLA Modules:
  0.0 81.5 jit_solution(15726753093309590592)
XLA Ops:
  1.2 2.6 %collective-permute-start.4 = (f32[1,16,128]{2,1,0:T(8,128)}, f32[1,16,128]{2,1,0:T(8,128)S(1)}, u32[]{:S(2)}, u32[]{:S(2)}) collective-permute-start(f32[1,16,128]{2,1,0:T(8,128)} %bitcast.61), channel_id=1, source_target_pairs={{0,2},{1,3},{2,0},{3,1},{4,6},{5,7},{6,4},{7,5},{8,10},{9,11},{10,... | collective-permute-start | bytes 24584 | tf_op jit(solution)/shard_map/ppermute | solution.py:13
  5.1 2.4 %fusion.8 = f32[256,512]{1,0:T(8,128)S(1)} fusion(f32[1,512,512]{2,1,0:T(8,128)} %param.18, f32[1,256,512]{2,1,0:T(8,128)} %param.17), kind=kOutput, calls=%fused_computation.14 | convolution fusion | flops 805306368 | bytes 2097152 | tf_op jit(solution)/shard_map/kv,vw->kw/dot_general | solution.py:102
  9.8 1.7 %collective-permute-start.2 = (f32[128,512]{0,1:T(8,128)S(1)}, f32[128,512]{0,1:T(8,128)}, u32[]{:S(2)}, u32[]{:S(2)}) collective-permute-start(f32[128,512]{0,1:T(8,128)S(1)} %bitcast.54), channel_id=1, source_target_pairs={{0,3},{1,2},{2,1},{3,0},{4,7},{5,6},{6,5},{7,4},{8,11},{9,10},{10,... | collective-permute-start | bytes 786440 | tf_op jit(solution)/shard_map/ppermute | solution.py:110
  13.0 1.6 %fusion.17 = f32[128,128]{1,0:T(8,128)S(1)} fusion(f32[1,512,128]{2,1,0:T(8,128)} %param.16, f32[1,512,512]{2,1,0:T(8,128)} %param.18, s32[]{:T(128)S(6)} %select_n.96), kind=kOutput, calls=%fused_computation.24 | convolution fusion | flops 100663296 | bytes 589828 | tf_op jit(solution)/shard_map/kw,kr->wr/dot_general | solution.py:112
  17.7 2.6 %collective-permute-start.6 = (f32[4,16,128]{2,1,0:T(8,128)S(1)}, f32[4,16,128]{2,1,0:T(8,128)S(1)}, u32[]{:S(2)}, u32[]{:S(2)}) collective-permute-start(f32[4,16,128]{2,1,0:T(8,128)S(1)} %pad_maximum_fusion.2), channel_id=1, source_target_pairs={{0,16},{1,17},{2,18},{3,19},{4,20},{5,21},{6,22},{7,23},{8,24},{9,... | collective-permute-start | bytes 98312 | tf_op jit(solution)/shard_map/ppermute | solution.py:13
  23.4 1.6 %collective-permute-start.7 = (f32[8,16,128]{2,1,0:T(8,128)}, f32[8,16,128]{2,1,0:T(8,128)S(1)}, u32[]{:S(2)}, u32[]{:S(2)}) collective-permute-start(f32[8,16,128]{2,1,0:T(8,128)} %get-tuple-element.5), channel_id=1, source_target_pairs={{0,8},{1,9},{2,10},{3,11},{4,12},{5,13},{6,14},{7,15},{8,0},{9,1},... | collective-permute-start | bytes 196616 | tf_op jit(solution)/shard_map/ppermute | solution.py:13
  25.6 1.5 %collective-permute-start.8 = (f32[8,16,128]{2,1,0:T(8,128)}, f32[8,16,128]{2,1,0:T(8,128)S(1)}, u32[]{:S(2)}, u32[]{:S(2)}) collective-permute-start(f32[8,16,128]{2,1,0:T(8,128)} %get-tuple-element.5), channel_id=1, source_target_pairs={{0,4},{1,5},{2,6},{3,7},{4,0},{5,1},{6,2},{7,3},{8,12},{9,13},{10,... | collective-permute-start | bytes 196616 | tf_op jit(solution)/shard_map/ppermute | solution.py:13
  27.9 2.5 %collective-permute-start.9 = (f32[8,16,128]{2,1,0:T(8,128)}, f32[8,16,128]{2,1,0:T(8,128)S(1)}, u32[]{:S(2)}, u32[]{:S(2)}) collective-permute-start(f32[8,16,128]{2,1,0:T(8,128)} %get-tuple-element.5), channel_id=1, source_target_pairs={{0,12},{1,13},{2,14},{3,15},{4,8},{5,9},{6,10},{7,11},{8,4},{9,5},... | collective-permute-start | bytes 196616 | tf_op jit(solution)/shard_map/ppermute | solution.py:13
  30.4 2.8 %collective-permute-done.9 = f32[8,16,128]{2,1,0:T(8,128)S(1)} collective-permute-done((f32[8,16,128]{2,1,0:T(8,128)}, f32[8,16,128]{2,1,0:T(8,128)S(1)}, u32[]{:S(2)}, u32[]{:S(2)}) %collective-permute-start.9) | collective-permute-done | bytes 65568 | tf_op jit(solution)/shard_map/ppermute | solution.py:13
  33.3 2.3 %constant_dynamic-update-slice_fusion.18 = (f32[16,128,128]{2,1,0:T(8,128)}, f32[1,128,128]{2,1,0:T(8,128)S(1)}) fusion(f32[128,128]{1,0:T(8,128)S(1)} %fusion.17, f32[512,128]{1,0:T(8,128)S(1)} %bitcast.59, f32[128,512]{0,1:T(8,128)} %collective-permute-done.2, f32[128,512]{0,1:T(8,128)S(1)} %collective-permute-done.1, ...), kind=kOutput, calls=%fused_computation.53 | convolution fusion | flops 100876288 | bytes 1507332 | tf_op jit(solution)/shard_map/wj,jr->wr/dot_general | solution.py:115
  35.6 1.6 %collective-permute-start.10 = (f32[1,128,128]{2,1,0:T(8,128)S(1)}, f32[1,128,128]{2,1,0:T(8,128)S(1)}, u32[]{:S(2)}, u32[]{:S(2)}) collective-permute-start(f32[1,128,128]{2,1,0:T(8,128)S(1)} %get-tuple-element.20), channel_id=1, source_target_pairs={{0,2},{1,3},{2,0},{3,1},{4,6},{5,7},{6,4},{7,5},{8,10},{9,11},{10,... | collective-permute-start | bytes 196616 | tf_op jit(solution)/shard_map/ppermute | solution.py:13
  38.0 1.9 %collective-permute-done.10 = f32[1,128,128]{2,1,0:T(8,128)S(1)} collective-permute-done((f32[1,128,128]{2,1,0:T(8,128)S(1)}, f32[1,128,128]{2,1,0:T(8,128)S(1)}, u32[]{:S(2)}, u32[]{:S(2)}) %collective-permute-start.10) | collective-permute-done | bytes 65568 | tf_op jit(solution)/shard_map/ppermute | solution.py:13
  39.9 2.4 %collective-permute-start.11 = (f32[2,128,128]{2,1,0:T(8,128)S(1)}, f32[2,128,128]{2,1,0:T(8,128)S(1)}, u32[]{:S(2)}, u32[]{:S(2)}) collective-permute-start(f32[2,128,128]{2,1,0:T(8,128)S(1)} %pad_maximum_fusion.1), channel_id=1, source_target_pairs={{0,16},{1,17},{2,18},{3,19},{4,20},{5,21},{6,22},{7,23},{8,24},{9,... | collective-permute-start | bytes 393224 | tf_op jit(solution)/shard_map/ppermute | solution.py:13
  43.1 4.2 %collective-permute-done.11 = f32[2,128,128]{2,1,0:T(8,128)S(1)} collective-permute-done((f32[2,128,128]{2,1,0:T(8,128)S(1)}, f32[2,128,128]{2,1,0:T(8,128)S(1)}, u32[]{:S(2)}, u32[]{:S(2)}) %collective-permute-start.11) | collective-permute-done | bytes 131104 | tf_op jit(solution)/shard_map/ppermute | solution.py:13
  47.9 1.5 %collective-permute-start.13 = (f32[4,128,128]{2,1,0:T(8,128)S(1)}, f32[4,128,128]{2,1,0:T(8,128)S(1)}, u32[]{:S(2)}, u32[]{:S(2)}) collective-permute-start(f32[4,128,128]{2,1,0:T(8,128)S(1)} %pad_maximum_fusion), channel_id=1, source_target_pairs={{0,4},{1,5},{2,6},{3,7},{4,0},{5,1},{6,2},{7,3},{8,12},{9,13},{10,... | collective-permute-start | bytes 786440 | tf_op jit(solution)/shard_map/ppermute | solution.py:13
  50.0 1.5 %collective-permute-start.14 = (f32[4,128,128]{2,1,0:T(8,128)S(1)}, f32[4,128,128]{2,1,0:T(8,128)S(1)}, u32[]{:S(2)}, u32[]{:S(2)}) collective-permute-start(f32[4,128,128]{2,1,0:T(8,128)S(1)} %pad_maximum_fusion), channel_id=1, source_target_pairs={{0,12},{1,13},{2,14},{3,15},{4,8},{5,9},{6,10},{7,11},{8,4},{9,5},... | collective-permute-start | bytes 786440 | tf_op jit(solution)/shard_map/ppermute | solution.py:13
  52.2 2.1 %collective-permute-done.12 = f32[4,128,128]{2,1,0:T(8,128)S(1)} collective-permute-done((f32[4,128,128]{2,1,0:T(8,128)S(1)}, f32[4,128,128]{2,1,0:T(8,128)S(1)}, u32[]{:S(2)}, u32[]{:S(2)}) %collective-permute-start.12) | collective-permute-done | bytes 262176 | tf_op jit(solution)/shard_map/ppermute | solution.py:13
  55.9 2.1 %collective-permute-done.14 = f32[4,128,128]{2,1,0:T(8,128)S(1)} collective-permute-done((f32[4,128,128]{2,1,0:T(8,128)S(1)}, f32[4,128,128]{2,1,0:T(8,128)S(1)}, u32[]{:S(2)}, u32[]{:S(2)}) %collective-permute-start.14) | collective-permute-done | bytes 262176 | tf_op jit(solution)/shard_map/ppermute | solution.py:13
  58.8 4.8 %fusion.39 = f32[8,256,128]{2,1,0:T(8,128)S(1)} fusion(f32[8,256,256]{2,1,0:T(8,128)S(1)} %copy-done, f32[8,256,128]{2,1,0:T(8,128)} %param.25), kind=kOutput, calls=%fused_computation.107 | convolution fusion | flops 805306368 | bytes 4194304 | tf_op jit(solution)/shard_map/swk,skr->swr/dot_general | solution.py:136
  63.7 4.9 %fusion.40 = f32[8,256,256]{2,1,0:T(8,128)} fusion(f32[8,256,256]{2,1,0:T(8,128)S(1)} %copy-done, f32[8,256,256]{2,1,0:T(8,128)S(1)} %copy-done.5), kind=kOutput, calls=%fused_computation.108 | convolution fusion | flops 1610612736 | bytes 6291456 | tf_op jit(solution)/shard_map/swv,svk->swk/dot_general | solution.py:137
  68.6 2.8 %gather_fusion.4 = f32[16,128,128]{2,1,0:T(8,128)} fusion(f32[16,128,128]{2,1,0:T(8,128)} %constant_dynamic-update-slice_fusion.13, s32[1024]{0:T(1024)S(1)} %pad_clamp_fusion.1), kind=kCustom, calls=%fused_computation.4 | custom fusion | bytes 2097216 | tf_op jit(solution)/shard_map/gather | solution.py:127
  71.4 3.0 %gather_fusion.5 = f32[16,128,128]{2,1,0:T(8,128)} fusion(f32[16,128,128]{2,1,0:T(8,128)} %collective-permute-done.15, s32[1024]{0:T(1024)S(1)} %pad_clamp_fusion), kind=kCustom, calls=%fused_computation.5 | custom fusion | bytes 2097216 | tf_op jit(solution)/shard_map/gather | solution.py:127
  74.4 2.5 %fusion = f32[8,256,128]{2,1,0:T(8,128)S(1)} fusion(f32[8,256,128]{2,1,0:T(8,128)} %bitcast.58, s32[256]{0:T(256)S(1)} %add_bitcast_fusion, s32[8,256]{1,0:T(8,128)S(1)} %copy-done.7), kind=kOutput, calls=%fused_computation.6 | convolution fusion | flops 805830656 | bytes 2106368 | tf_op jit(solution)/shard_map/skj,sjr->skr/dot_general | solution.py:131
  78.5 3.0 %convolution_subtract_fusion = f32[8,256,128]{2,1,0:T(8,128)} fusion(f32[8,256,128]{2,1,0:T(8,128)S(1)} %fusion.39, f32[8,256,256]{2,1,0:T(8,128)S(1)} %copy-done.2, f32[8,256,128]{2,1,0:T(8,128)S(1)} %fusion.4), kind=kOutput, calls=%fused_computation.11 | convolution fusion | flops 805568512 | bytes 5242880 | tf_op jit(solution)/shard_map/swk,skr->swr/dot_general | solution.py:138
  (95 shorter events, 20.5 us)
Async XLA Ops:
  0.6 58.2 %copy-start = (f32[8,256,256]{2,1,0:T(8,128)S(1)}, f32[8,256,256]{2,1,0:T(8,128)}, u32[]{:S(2)}) copy-start(f32[8,256,256]{2,1,0:T(8,128)} %param.26) | copy-start | bytes 6291460
  0.6 6.9 %copy-start.14 = (s32[32]{0:T(128)S(1)}, s32[32]{0:T(128)}, u32[]{:S(2)}) copy-start(s32[32]{0:T(128)} %constant.145) | copy-start | bytes 388
  0.7 6.9 %copy-start.10 = (s32[1,256]{1,0:T(1,128)S(1)}, s32[1,256]{1,0:T(1,128)}, u32[]{:S(2)}) copy-start(s32[1,256]{1,0:T(1,128)} %param.19) | copy-start | bytes 3076
  0.7 16.4 %collective-permute-start.3 = (f32[1,16,128]{2,1,0:T(8,128)}, f32[1,16,128]{2,1,0:T(8,128)S(1)}, u32[]{:S(2)}, u32[]{:S(2)}) collective-permute-start(f32[1,16,128]{2,1,0:T(8,128)} %bitcast.60), channel_id=1, source_target_pairs={{0,1},{1,0},{2,3},{3,2},{4,5},{5,4},{6,7},{7,6},{8,9},{9,8},{10,11... | collective-permute-start | bytes 24584 | tf_op jit(solution)/shard_map/ppermute | solution.py:13
  1.2 16.2 %collective-permute-start.4 = (f32[1,16,128]{2,1,0:T(8,128)}, f32[1,16,128]{2,1,0:T(8,128)S(1)}, u32[]{:S(2)}, u32[]{:S(2)}) collective-permute-start(f32[1,16,128]{2,1,0:T(8,128)} %bitcast.61), channel_id=1, source_target_pairs={{0,2},{1,3},{2,0},{3,1},{4,6},{5,7},{6,4},{7,5},{8,10},{9,11},{10,... | collective-permute-start | bytes 24584 | tf_op jit(solution)/shard_map/ppermute | solution.py:13
  3.8 13.6 %collective-permute-start.5 = (f32[1,16,128]{2,1,0:T(8,128)}, f32[1,16,128]{2,1,0:T(8,128)S(1)}, u32[]{:S(2)}, u32[]{:S(2)}) collective-permute-start(f32[1,16,128]{2,1,0:T(8,128)} %bitcast.62), channel_id=1, source_target_pairs={{0,3},{1,2},{2,1},{3,0},{4,7},{5,6},{6,5},{7,4},{8,11},{9,10},{10,... | collective-permute-start | bytes 24584 | tf_op jit(solution)/shard_map/ppermute | solution.py:13
  9.8 23.4 %collective-permute-start.2 = (f32[128,512]{0,1:T(8,128)S(1)}, f32[128,512]{0,1:T(8,128)}, u32[]{:S(2)}, u32[]{:S(2)}) collective-permute-start(f32[128,512]{0,1:T(8,128)S(1)} %bitcast.54), channel_id=1, source_target_pairs={{0,3},{1,2},{2,1},{3,0},{4,7},{5,6},{6,5},{7,4},{8,11},{9,10},{10,... | collective-permute-start | bytes 786440 | tf_op jit(solution)/shard_map/ppermute | solution.py:110
  11.6 3.1 %copy-start.11 = (s32[2]{0:T(128)S(1)}, s32[2]{0:T(128)}, u32[]{:S(2)}) copy-start(s32[2]{0:T(128)} %constant.120.clone) | copy-start | bytes 28
  12.2 21.1 %collective-permute-start = (f32[128,512]{0,1:T(8,128)S(1)}, f32[128,512]{0,1:T(8,128)}, u32[]{:S(2)}, u32[]{:S(2)}) collective-permute-start(f32[128,512]{0,1:T(8,128)S(1)} %bitcast.55), channel_id=1, source_target_pairs={{0,1},{1,0},{2,3},{3,2},{4,5},{5,4},{6,7},{7,6},{8,9},{9,8},{10,11... | collective-permute-start | bytes 786440 | tf_op jit(solution)/shard_map/ppermute | solution.py:110
  17.1 16.2 %collective-permute-start.1 = (f32[128,512]{0,1:T(8,128)S(1)}, f32[128,512]{0,1:T(8,128)S(1)}, u32[]{:S(2)}, u32[]{:S(2)}) collective-permute-start(f32[128,512]{0,1:T(8,128)S(1)} %bitcast.56), channel_id=1, source_target_pairs={{0,2},{1,3},{2,0},{3,1},{4,6},{5,7},{6,4},{7,5},{8,10},{9,11},{10,... | collective-permute-start | bytes 786440 | tf_op jit(solution)/shard_map/ppermute | solution.py:110
  17.7 5.1 %collective-permute-start.6 = (f32[4,16,128]{2,1,0:T(8,128)S(1)}, f32[4,16,128]{2,1,0:T(8,128)S(1)}, u32[]{:S(2)}, u32[]{:S(2)}) collective-permute-start(f32[4,16,128]{2,1,0:T(8,128)S(1)} %pad_maximum_fusion.2), channel_id=1, source_target_pairs={{0,16},{1,17},{2,18},{3,19},{4,20},{5,21},{6,22},{7,23},{8,24},{9,... | collective-permute-start | bytes 98312 | tf_op jit(solution)/shard_map/ppermute | solution.py:13
  23.4 4.5 %collective-permute-start.7 = (f32[8,16,128]{2,1,0:T(8,128)}, f32[8,16,128]{2,1,0:T(8,128)S(1)}, u32[]{:S(2)}, u32[]{:S(2)}) collective-permute-start(f32[8,16,128]{2,1,0:T(8,128)} %get-tuple-element.5), channel_id=1, source_target_pairs={{0,8},{1,9},{2,10},{3,11},{4,12},{5,13},{6,14},{7,15},{8,0},{9,1},... | collective-permute-start | bytes 196616 | tf_op jit(solution)/shard_map/ppermute | solution.py:13
  25.6 4.8 %collective-permute-start.8 = (f32[8,16,128]{2,1,0:T(8,128)}, f32[8,16,128]{2,1,0:T(8,128)S(1)}, u32[]{:S(2)}, u32[]{:S(2)}) collective-permute-start(f32[8,16,128]{2,1,0:T(8,128)} %get-tuple-element.5), channel_id=1, source_target_pairs={{0,4},{1,5},{2,6},{3,7},{4,0},{5,1},{6,2},{7,3},{8,12},{9,13},{10,... | collective-permute-start | bytes 196616 | tf_op jit(solution)/shard_map/ppermute | solution.py:13
  27.9 5.4 %collective-permute-start.9 = (f32[8,16,128]{2,1,0:T(8,128)}, f32[8,16,128]{2,1,0:T(8,128)S(1)}, u32[]{:S(2)}, u32[]{:S(2)}) collective-permute-start(f32[8,16,128]{2,1,0:T(8,128)} %get-tuple-element.5), channel_id=1, source_target_pairs={{0,12},{1,13},{2,14},{3,15},{4,8},{5,9},{6,10},{7,11},{8,4},{9,5},... | collective-permute-start | bytes 196616 | tf_op jit(solution)/shard_map/ppermute | solution.py:13
  35.6 28.0 %copy-start.6 = (f32[1,128,128]{2,1,0:T(8,128)}, f32[1,128,128]{2,1,0:T(8,128)S(1)}, u32[]{:S(2)}) copy-start(f32[1,128,128]{2,1,0:T(8,128)S(1)} %get-tuple-element.20) | copy-start | bytes 196612
  35.6 4.3 %collective-permute-start.10 = (f32[1,128,128]{2,1,0:T(8,128)S(1)}, f32[1,128,128]{2,1,0:T(8,128)S(1)}, u32[]{:S(2)}, u32[]{:S(2)}) collective-permute-start(f32[1,128,128]{2,1,0:T(8,128)S(1)} %get-tuple-element.20), channel_id=1, source_target_pairs={{0,2},{1,3},{2,0},{3,1},{4,6},{5,7},{6,4},{7,5},{8,10},{9,11},{10,... | collective-permute-start | bytes 196616 | tf_op jit(solution)/shard_map/ppermute | solution.py:13
  39.9 7.4 %collective-permute-start.11 = (f32[2,128,128]{2,1,0:T(8,128)S(1)}, f32[2,128,128]{2,1,0:T(8,128)S(1)}, u32[]{:S(2)}, u32[]{:S(2)}) collective-permute-start(f32[2,128,128]{2,1,0:T(8,128)S(1)} %pad_maximum_fusion.1), channel_id=1, source_target_pairs={{0,16},{1,17},{2,18},{3,19},{4,20},{5,21},{6,22},{7,23},{8,24},{9,... | collective-permute-start | bytes 393224 | tf_op jit(solution)/shard_map/ppermute | solution.py:13
  47.4 6.9 %collective-permute-start.12 = (f32[4,128,128]{2,1,0:T(8,128)S(1)}, f32[4,128,128]{2,1,0:T(8,128)S(1)}, u32[]{:S(2)}, u32[]{:S(2)}) collective-permute-start(f32[4,128,128]{2,1,0:T(8,128)S(1)} %pad_maximum_fusion), channel_id=1, source_target_pairs={{0,8},{1,9},{2,10},{3,11},{4,12},{5,13},{6,14},{7,15},{8,0},{9,1},... | collective-permute-start | bytes 786440 | tf_op jit(solution)/shard_map/ppermute | solution.py:13
  47.9 7.3 %collective-permute-start.13 = (f32[4,128,128]{2,1,0:T(8,128)S(1)}, f32[4,128,128]{2,1,0:T(8,128)S(1)}, u32[]{:S(2)}, u32[]{:S(2)}) collective-permute-start(f32[4,128,128]{2,1,0:T(8,128)S(1)} %pad_maximum_fusion), channel_id=1, source_target_pairs={{0,4},{1,5},{2,6},{3,7},{4,0},{5,1},{6,2},{7,3},{8,12},{9,13},{10,... | collective-permute-start | bytes 786440 | tf_op jit(solution)/shard_map/ppermute | solution.py:13
  50.0 8.0 %collective-permute-start.14 = (f32[4,128,128]{2,1,0:T(8,128)S(1)}, f32[4,128,128]{2,1,0:T(8,128)S(1)}, u32[]{:S(2)}, u32[]{:S(2)}) collective-permute-start(f32[4,128,128]{2,1,0:T(8,128)S(1)} %pad_maximum_fusion), channel_id=1, source_target_pairs={{0,12},{1,13},{2,14},{3,15},{4,8},{5,9},{6,10},{7,11},{8,4},{9,5},... | collective-permute-start | bytes 786440 | tf_op jit(solution)/shard_map/ppermute | solution.py:13
  58.8 12.7 %collective-permute-start.15 = (f32[16,128,128]{2,1,0:T(8,128)}, f32[16,128,128]{2,1,0:T(8,128)}, u32[]{:S(2)}, u32[]{:S(2)}) collective-permute-start(f32[16,128,128]{2,1,0:T(8,128)} %constant_dynamic-update-slice_fusion.13), channel_id=1, source_target_pairs={{0,1},{1,0},{2,3},{3,2},{4,5},{5,4},{6,7},{7,6},{8,9},{9,8},{10,11... | collective-permute-start | bytes 3145736 | tf_op jit(solution)/shard_map/ppermute | solution.py:119
  58.8 4.9 %copy-start.5 = (f32[8,256,256]{2,1,0:T(8,128)S(1)}, f32[8,256,256]{2,1,0:T(8,128)}, u32[]{:S(2)}) copy-start(f32[8,256,256]{2,1,0:T(8,128)} %param.24) | copy-start | bytes 6291460
  68.6 5.8 %copy-start.7 = (s32[8,256]{1,0:T(8,128)S(1)}, s32[8,256]{1,0:T(8,128)}, u32[]{:S(2)}) copy-start(s32[8,256]{1,0:T(8,128)} %param.23) | copy-start | bytes 24580
  74.4 2.5 %copy-start.4 = (f32[16,128,128]{2,1,0:T(8,128)S(1)}, f32[16,128,128]{2,1,0:T(8,128)}, u32[]{:S(2)}) copy-start(f32[16,128,128]{2,1,0:T(8,128)} %gather_fusion.4) | copy-start | bytes 3145732
  (7 other events, 9.3 us)

commit v17 on v10

--- a/solution.py
+++ b/solution.py
@@ -129,6 +129,8 @@
         columns = (quarters[:, None] * share + within).reshape(-1)
         pick = (lower_index[:, :, None] == columns[None, None, :]).astype(jnp.float32)
         term = jnp.einsum("skj,sjr->skr", pick, slabs, precision=highest)
+        if side == 0:
+            partner, term = lax.optimization_barrier((partner, term))
         parent_rows = term if parent_rows is None else parent_rows + term
 
     panel_t = jnp.swapaxes(lower_panel, 1, 2)

time: 70.7 us -> 69.5 us (0.983)
  waiting for transfers between devices: 16.6 us -> 15.7 us
    gather x2, local copies, waits for them, and re-layouts: 4.66 us -> 3.67 us  [local(): slabs = source[places].reshape(position.shape[0], -1, own_rows.shape[1])]
    unnamed x37 -> x39, local copies, waits for them, and re-layouts: 4.95 us -> 5.27 us
  transfers between devices with their start and end apart: 16 -> 16, of which waited for: 9 -> 7; matrix products, arithmetic and copies ran while one was open for 19% -> 23% of each run, Pallas kernels for 0% -> 0%
where the time goes in v17:
time: 69.5 us; the launch traced here: 68.2 us
  starting transfers between devices  21.8 us (31%)
  matrix products  16 us (23%)
  waiting for transfers between devices  15.7 us (23%)
  local copies, waits for them, and re-layouts  12.7 us (18%)
  other arithmetic  1.14 us (2%)
  between operations  1.01 us (1%)
    ppermute x12, starting transfers between devices, xor_gather(): parts.append(lax.ppermute(held, axes, [(i, i ^ v) for i in range(count)]))  19.7 us
    ppermute x12, waiting for transfers between devices, xor_gather(): parts.append(lax.ppermute(held, axes, [(i, i ^ v) for i in range(count)]))  15.6 us
    unnamed x39, local copies, waits for them, and re-layouts  5.27 us
    gather x2, local copies, waits for them, and re-layouts, local(): slabs = source[places].reshape(position.shape[0], -1, own_rows.shape[1])  3.67 us
    dot_general x1, matrix products, local(): jnp.einsum('swk,skr->swr', panel_t, parent_rows, precision=highest)  3.54 us
    dot_general x2, matrix products, local(): term = jnp.einsum('skj,sjr->skr', pick, slabs, precision=highest)  3.32 us
    dot_general x1, matrix products, local(): jnp.einsum('kv,vw->kw', upper_panel[0], upper_inverse[0], precision=highest)  2.44 us
    dot_general x1, matrix products, local(): jnp.einsum('wj,jr->wr', total, top_held, precision=highest)  2.35 us
  transfers between devices with their start and end apart: 16, of which 7 were waited for; matrix products, arithmetic and copies ran while one was open for 23% of the time, Pallas kernels for 0%

profile of v17, /device:TPU:0, one launch (start us, length us, event | category | flops | bytes accessed | tf_op | source)
XLA Modules:
  0.0 68.2 jit_solution(2789266058048972682)
XLA Ops:
  1.2 2.6 %collective-permute-start.4 = (f32[1,16,128]{2,1,0:T(8,128)}, f32[1,16,128]{2,1,0:T(8,128)S(1)}, u32[]{:S(2)}, u32[]{:S(2)}) collective-permute-start(f32[1,16,128]{2,1,0:T(8,128)} %bitcast.64), channel_id=1, source_target_pairs={{0,2},{1,3},{2,0},{3,1},{4,6},{5,7},{6,4},{7,5},{8,10},{9,11},{10,... | collective-permute-start | bytes 24584 | tf_op jit(solution)/shard_map/ppermute | solution.py:13
  5.1 2.4 %fusion.6 = f32[256,512]{1,0:T(8,128)S(1)} fusion(f32[1,512,512]{2,1,0:T(8,128)} %param.18, f32[1,256,512]{2,1,0:T(8,128)} %param.17), kind=kOutput, calls=%fused_computation.15 | convolution fusion | flops 805306368 | bytes 2097152 | tf_op jit(solution)/shard_map/kv,vw->kw/dot_general | solution.py:102
  9.9 1.7 %collective-permute-start.2 = (f32[128,512]{0,1:T(8,128)S(1)}, f32[128,512]{0,1:T(8,128)}, u32[]{:S(2)}, u32[]{:S(2)}) collective-permute-start(f32[128,512]{0,1:T(8,128)S(1)} %bitcast.57), channel_id=1, source_target_pairs={{0,3},{1,2},{2,1},{3,0},{4,7},{5,6},{6,5},{7,4},{8,11},{9,10},{10,... | collective-permute-start | bytes 786440 | tf_op jit(solution)/shard_map/ppermute | solution.py:110
  13.2 3.0 %collective-permute-start.6 = (f32[4,16,128]{2,1,0:T(8,128)S(1)}, f32[4,16,128]{2,1,0:T(8,128)S(1)}, u32[]{:S(2)}, u32[]{:S(2)}) collective-permute-start(f32[4,16,128]{2,1,0:T(8,128)S(1)} %pad_maximum_fusion.2), channel_id=1, source_target_pairs={{0,16},{1,17},{2,18},{3,19},{4,20},{5,21},{6,22},{7,23},{8,24},{9,... | collective-permute-start | bytes 98312 | tf_op jit(solution)/shard_map/ppermute | solution.py:13
  16.2 2.0 %collective-permute-done.6 = f32[4,16,128]{2,1,0:T(8,128)S(1)} collective-permute-done((f32[4,16,128]{2,1,0:T(8,128)S(1)}, f32[4,16,128]{2,1,0:T(8,128)S(1)}, u32[]{:S(2)}, u32[]{:S(2)}) %collective-permute-start.6) | collective-permute-done | bytes 32800 | tf_op jit(solution)/shard_map/ppermute | solution.py:13
  18.2 1.8 %collective-permute-start.7 = (f32[8,16,128]{2,1,0:T(8,128)S(1)}, f32[8,16,128]{2,1,0:T(8,128)S(1)}, u32[]{:S(2)}, u32[]{:S(2)}) collective-permute-start(f32[8,16,128]{2,1,0:T(8,128)S(1)} %get-tuple-element.11), channel_id=1, source_target_pairs={{0,8},{1,9},{2,10},{3,11},{4,12},{5,13},{6,14},{7,15},{8,0},{9,1},... | collective-permute-start | bytes 196616 | tf_op jit(solution)/shard_map/ppermute | solution.py:13
  20.0 1.6 %fusion.16 = f32[128,128]{1,0:T(8,128)S(1)} fusion(f32[1,512,128]{2,1,0:T(8,128)} %param.16, f32[1,512,512]{2,1,0:T(8,128)} %param.18, s32[]{:T(128)S(6)} %select_n.96), kind=kOutput, calls=%fused_computation.26 | convolution fusion | flops 100663296 | bytes 589828 | tf_op jit(solution)/shard_map/kw,kr->wr/dot_general | solution.py:112
  21.6 1.6 %collective-permute-start.8 = (f32[8,16,128]{2,1,0:T(8,128)S(1)}, f32[8,16,128]{2,1,0:T(8,128)S(1)}, u32[]{:S(2)}, u32[]{:S(2)}) collective-permute-start(f32[8,16,128]{2,1,0:T(8,128)S(1)} %get-tuple-element.11), channel_id=1, source_target_pairs={{0,4},{1,5},{2,6},{3,7},{4,0},{5,1},{6,2},{7,3},{8,12},{9,13},{10,... | collective-permute-start | bytes 196616 | tf_op jit(solution)/shard_map/ppermute | solution.py:13
  23.2 2.0 %collective-permute-start.9 = (f32[8,16,128]{2,1,0:T(8,128)S(1)}, f32[8,16,128]{2,1,0:T(8,128)S(1)}, u32[]{:S(2)}, u32[]{:S(2)}) collective-permute-start(f32[8,16,128]{2,1,0:T(8,128)S(1)} %get-tuple-element.11), channel_id=1, source_target_pairs={{0,12},{1,13},{2,14},{3,15},{4,8},{5,9},{6,10},{7,11},{8,4},{9,5},... | collective-permute-start | bytes 196616 | tf_op jit(solution)/shard_map/ppermute | solution.py:13
  25.2 1.5 %collective-permute-done.8 = f32[8,16,128]{2,1,0:T(8,128)S(1)} collective-permute-done((f32[8,16,128]{2,1,0:T(8,128)S(1)}, f32[8,16,128]{2,1,0:T(8,128)S(1)}, u32[]{:S(2)}, u32[]{:S(2)}) %collective-permute-start.8) | collective-permute-done | bytes 65568 | tf_op jit(solution)/shard_map/ppermute | solution.py:13
  26.7 1.7 %collective-permute-done.9 = f32[8,16,128]{2,1,0:T(8,128)S(1)} collective-permute-done((f32[8,16,128]{2,1,0:T(8,128)S(1)}, f32[8,16,128]{2,1,0:T(8,128)S(1)}, u32[]{:S(2)}, u32[]{:S(2)}) %collective-permute-start.9) | collective-permute-done | bytes 65568 | tf_op jit(solution)/shard_map/ppermute | solution.py:13
  28.4 2.3 %constant_dynamic-update-slice_fusion.18 = (f32[16,128,128]{2,1,0:T(8,128)}, f32[1,128,128]{2,1,0:T(8,128)S(1)}) fusion(f32[128,128]{1,0:T(8,128)S(1)} %fusion.16, f32[512,128]{1,0:T(8,128)S(1)} %bitcast.62, f32[128,512]{0,1:T(8,128)} %collective-permute-done.2, f32[128,512]{0,1:T(8,128)} %collective-permute-done.1, ...), kind=kOutput, calls=%fused_computation.55 | convolution fusion | flops 100876288 | bytes 1507332 | tf_op jit(solution)/shard_map/wj,jr->wr/dot_general | solution.py:115
  30.7 1.5 %collective-permute-start.10 = (f32[1,128,128]{2,1,0:T(8,128)S(1)}, f32[1,128,128]{2,1,0:T(8,128)S(1)}, u32[]{:S(2)}, u32[]{:S(2)}) collective-permute-start(f32[1,128,128]{2,1,0:T(8,128)S(1)} %get-tuple-element.26), channel_id=1, source_target_pairs={{0,2},{1,3},{2,0},{3,1},{4,6},{5,7},{6,4},{7,5},{8,10},{9,11},{10,... | collective-permute-start | bytes 196616 | tf_op jit(solution)/shard_map/ppermute | solution.py:13
  32.9 2.1 %collective-permute-done.10 = f32[1,128,128]{2,1,0:T(8,128)S(1)} collective-permute-done((f32[1,128,128]{2,1,0:T(8,128)S(1)}, f32[1,128,128]{2,1,0:T(8,128)S(1)}, u32[]{:S(2)}, u32[]{:S(2)}) %collective-permute-start.10) | collective-permute-done | bytes 65568 | tf_op jit(solution)/shard_map/ppermute | solution.py:13
  35.0 3.1 %collective-permute-start.11 = (f32[2,128,128]{2,1,0:T(8,128)S(1)}, f32[2,128,128]{2,1,0:T(8,128)S(1)}, u32[]{:S(2)}, u32[]{:S(2)}) collective-permute-start(f32[2,128,128]{2,1,0:T(8,128)S(1)} %pad_maximum_fusion.1), channel_id=1, source_target_pairs={{0,16},{1,17},{2,18},{3,19},{4,20},{5,21},{6,22},{7,23},{8,24},{9,... | collective-permute-start | bytes 393224 | tf_op jit(solution)/shard_map/ppermute | solution.py:13
  38.1 4.5 %collective-permute-done.11 = f32[2,128,128]{2,1,0:T(8,128)S(1)} collective-permute-done((f32[2,128,128]{2,1,0:T(8,128)S(1)}, f32[2,128,128]{2,1,0:T(8,128)S(1)}, u32[]{:S(2)}, u32[]{:S(2)}) %collective-permute-start.11) | collective-permute-done | bytes 131104 | tf_op jit(solution)/shard_map/ppermute | solution.py:13
  43.1 1.3 %collective-permute-start.13 = (f32[4,128,128]{2,1,0:T(8,128)S(1)}, f32[4,128,128]{2,1,0:T(8,128)S(1)}, u32[]{:S(2)}, u32[]{:S(2)}) collective-permute-start(f32[4,128,128]{2,1,0:T(8,128)S(1)} %pad_maximum_fusion), channel_id=1, source_target_pairs={{0,4},{1,5},{2,6},{3,7},{4,0},{5,1},{6,2},{7,3},{8,12},{9,13},{10,... | collective-permute-start | bytes 786440 | tf_op jit(solution)/shard_map/ppermute | solution.py:13
  45.0 2.0 %collective-permute-start.14 = (f32[4,128,128]{2,1,0:T(8,128)S(1)}, f32[4,128,128]{2,1,0:T(8,128)S(1)}, u32[]{:S(2)}, u32[]{:S(2)}) collective-permute-start(f32[4,128,128]{2,1,0:T(8,128)S(1)} %pad_maximum_fusion), channel_id=1, source_target_pairs={{0,12},{1,13},{2,14},{3,15},{4,8},{5,9},{6,10},{7,11},{8,4},{9,5},... | collective-permute-start | bytes 786440 | tf_op jit(solution)/shard_map/ppermute | solution.py:13
  47.7 2.9 %collective-permute-done.12 = f32[4,128,128]{2,1,0:T(8,128)S(1)} collective-permute-done((f32[4,128,128]{2,1,0:T(8,128)S(1)}, f32[4,128,128]{2,1,0:T(8,128)S(1)}, u32[]{:S(2)}, u32[]{:S(2)}) %collective-permute-start.12) | collective-permute-done | bytes 262176 | tf_op jit(solution)/shard_map/ppermute | solution.py:13
  53.9 1.8 %gather_fusion.4 = f32[16,128,128]{2,1,0:T(8,128)S(1)} fusion(f32[16,128,128]{2,1,0:T(8,128)} %constant_dynamic-update-slice_fusion.13, s32[1024]{0:T(1024)S(1)} %pad_clamp_fusion.1), kind=kCustom, calls=%fused_computation.4 | custom fusion | bytes 2097216 | tf_op jit(solution)/shard_map/gather | solution.py:127
  55.8 2.1 %fusion.2 = f32[8,256,128]{2,1,0:T(8,128)} fusion(f32[8,256,128]{2,1,0:T(8,128)S(1)} %bitcast.61, s32[256]{0:T(256)S(1)} %add_bitcast_fusion.1, s32[8,256]{1,0:T(8,128)S(1)} %copy-done.7), kind=kOutput, calls=%fused_computation.8 | convolution fusion | flops 805830656 | bytes 2106368 | tf_op jit(solution)/shard_map/skj,sjr->skr/dot_general | solution.py:131
  57.9 1.8 %gather_fusion.5 = f32[16,128,128]{2,1,0:T(8,128)S(1)} fusion(f32[16,128,128]{2,1,0:T(8,128)} %collective-permute-done.15, s32[1024]{0:T(1024)S(1)} %pad_clamp_fusion), kind=kCustom, calls=%fused_computation.5 | custom fusion | bytes 2097216 | tf_op jit(solution)/shard_map/gather | solution.py:127
  61.3 3.5 %fusion.4 = f32[8,256,128]{2,1,0:T(8,128)S(1)} fusion(f32[8,256,128]{2,1,0:T(8,128)S(1)} %copy-done.5, f32[8,256,256]{2,1,0:T(8,128)S(1)} %copy-done, f32[8,256,128]{2,1,0:T(8,128)S(1)} %copy-done.3, f32[8,256,128]{2,1,0:T(8,128)S(1)} %fusion), kind=kOutput, calls=%fused_computation.12 | convolution fusion | flops 805830656 | bytes 6291456 | tf_op jit(solution)/shard_map/swk,skr->swr/dot_general | solution.py:138
  64.9 2.0 %convolution_bitcast_fusion = f32[8,256,128]{1,2,0:T(8,128)S(1)} fusion(f32[8,256,128]{2,1,0:T(8,128)S(1)} %fusion.4, f32[8,256,256]{2,1,0:T(8,128)S(1)} %copy-done.4), kind=kOutput, calls=%fused_computation.10 | convolution fusion | flops 805306368 | bytes 4194304 | tf_op jit(solution)/shard_map/swk,skr->swr/dot_general | solution.py:139
  (93 shorter events, 14.2 us)
Async XLA Ops:
  0.6 60.4 %copy-start = (f32[8,256,256]{2,1,0:T(8,128)S(1)}, f32[8,256,256]{2,1,0:T(8,128)}, u32[]{:S(2)}) copy-start(f32[8,256,256]{2,1,0:T(8,128)} %param.24) | copy-start | bytes 6291460
  0.6 6.9 %copy-start.13 = (s32[32]{0:T(128)S(1)}, s32[32]{0:T(128)}, u32[]{:S(2)}) copy-start(s32[32]{0:T(128)} %constant.145) | copy-start | bytes 388
  0.7 6.9 %copy-start.9 = (s32[1,256]{1,0:T(1,128)S(1)}, s32[1,256]{1,0:T(1,128)}, u32[]{:S(2)}) copy-start(s32[1,256]{1,0:T(1,128)} %param.19) | copy-start | bytes 3076
  0.7 12.4 %collective-permute-start.3 = (f32[1,16,128]{2,1,0:T(8,128)}, f32[1,16,128]{2,1,0:T(8,128)S(1)}, u32[]{:S(2)}, u32[]{:S(2)}) collective-permute-start(f32[1,16,128]{2,1,0:T(8,128)} %bitcast.63), channel_id=1, source_target_pairs={{0,1},{1,0},{2,3},{3,2},{4,5},{5,4},{6,7},{7,6},{8,9},{9,8},{10,11... | collective-permute-start | bytes 24584 | tf_op jit(solution)/shard_map/ppermute | solution.py:13
  1.2 12.0 %collective-permute-start.4 = (f32[1,16,128]{2,1,0:T(8,128)}, f32[1,16,128]{2,1,0:T(8,128)S(1)}, u32[]{:S(2)}, u32[]{:S(2)}) collective-permute-start(f32[1,16,128]{2,1,0:T(8,128)} %bitcast.64), channel_id=1, source_target_pairs={{0,2},{1,3},{2,0},{3,1},{4,6},{5,7},{6,4},{7,5},{8,10},{9,11},{10,... | collective-permute-start | bytes 24584 | tf_op jit(solution)/shard_map/ppermute | solution.py:13
  3.8 9.4 %collective-permute-start.5 = (f32[1,16,128]{2,1,0:T(8,128)}, f32[1,16,128]{2,1,0:T(8,128)S(1)}, u32[]{:S(2)}, u32[]{:S(2)}) collective-permute-start(f32[1,16,128]{2,1,0:T(8,128)} %bitcast.65), channel_id=1, source_target_pairs={{0,3},{1,2},{2,1},{3,0},{4,7},{5,6},{6,5},{7,4},{8,11},{9,10},{10,... | collective-permute-start | bytes 24584 | tf_op jit(solution)/shard_map/ppermute | solution.py:13
  9.9 18.5 %collective-permute-start.2 = (f32[128,512]{0,1:T(8,128)S(1)}, f32[128,512]{0,1:T(8,128)}, u32[]{:S(2)}, u32[]{:S(2)}) collective-permute-start(f32[128,512]{0,1:T(8,128)S(1)} %bitcast.57), channel_id=1, source_target_pairs={{0,3},{1,2},{2,1},{3,0},{4,7},{5,6},{6,5},{7,4},{8,11},{9,10},{10,... | collective-permute-start | bytes 786440 | tf_op jit(solution)/shard_map/ppermute | solution.py:110
  12.2 16.1 %collective-permute-start.1 = (f32[128,512]{0,1:T(8,128)S(1)}, f32[128,512]{0,1:T(8,128)}, u32[]{:S(2)}, u32[]{:S(2)}) collective-permute-start(f32[128,512]{0,1:T(8,128)S(1)} %bitcast.58), channel_id=1, source_target_pairs={{0,2},{1,3},{2,0},{3,1},{4,6},{5,7},{6,4},{7,5},{8,10},{9,11},{10,... | collective-permute-start | bytes 786440 | tf_op jit(solution)/shard_map/ppermute | solution.py:110
  13.0 19.3 %copy-start.10 = (s32[2]{0:T(128)S(1)}, s32[2]{0:T(128)}, u32[]{:S(2)}) copy-start(s32[2]{0:T(128)} %constant.120.clone) | copy-start | bytes 28
  13.0 19.3 %copy-start.1 = (s32[8]{0:T(128)S(1)}, s32[8]{0:T(128)}, u32[]{:S(2)}) copy-start(s32[8]{0:T(128)} %param.21) | copy-start | bytes 100
  13.0 15.3 %collective-permute-start = (f32[128,512]{0,1:T(8,128)S(1)}, f32[128,512]{0,1:T(8,128)S(1)}, u32[]{:S(2)}, u32[]{:S(2)}) collective-permute-start(f32[128,512]{0,1:T(8,128)S(1)} %bitcast.59), channel_id=1, source_target_pairs={{0,1},{1,0},{2,3},{3,2},{4,5},{5,4},{6,7},{7,6},{8,9},{9,8},{10,11... | collective-permute-start | bytes 786440 | tf_op jit(solution)/shard_map/ppermute | solution.py:110
  13.2 5.0 %collective-permute-start.6 = (f32[4,16,128]{2,1,0:T(8,128)S(1)}, f32[4,16,128]{2,1,0:T(8,128)S(1)}, u32[]{:S(2)}, u32[]{:S(2)}) collective-permute-start(f32[4,16,128]{2,1,0:T(8,128)S(1)} %pad_maximum_fusion.2), channel_id=1, source_target_pairs={{0,16},{1,17},{2,18},{3,19},{4,20},{5,21},{6,22},{7,23},{8,24},{9,... | collective-permute-start | bytes 98312 | tf_op jit(solution)/shard_map/ppermute | solution.py:13
  18.2 5.0 %collective-permute-start.7 = (f32[8,16,128]{2,1,0:T(8,128)S(1)}, f32[8,16,128]{2,1,0:T(8,128)S(1)}, u32[]{:S(2)}, u32[]{:S(2)}) collective-permute-start(f32[8,16,128]{2,1,0:T(8,128)S(1)} %get-tuple-element.11), channel_id=1, source_target_pairs={{0,8},{1,9},{2,10},{3,11},{4,12},{5,13},{6,14},{7,15},{8,0},{9,1},... | collective-permute-start | bytes 196616 | tf_op jit(solution)/shard_map/ppermute | solution.py:13
  21.6 5.0 %collective-permute-start.8 = (f32[8,16,128]{2,1,0:T(8,128)S(1)}, f32[8,16,128]{2,1,0:T(8,128)S(1)}, u32[]{:S(2)}, u32[]{:S(2)}) collective-permute-start(f32[8,16,128]{2,1,0:T(8,128)S(1)} %get-tuple-element.11), channel_id=1, source_target_pairs={{0,4},{1,5},{2,6},{3,7},{4,0},{5,1},{6,2},{7,3},{8,12},{9,13},{10,... | collective-permute-start | bytes 196616 | tf_op jit(solution)/shard_map/ppermute | solution.py:13
  23.2 5.2 %collective-permute-start.9 = (f32[8,16,128]{2,1,0:T(8,128)S(1)}, f32[8,16,128]{2,1,0:T(8,128)S(1)}, u32[]{:S(2)}, u32[]{:S(2)}) collective-permute-start(f32[8,16,128]{2,1,0:T(8,128)S(1)} %get-tuple-element.11), channel_id=1, source_target_pairs={{0,12},{1,13},{2,14},{3,15},{4,8},{5,9},{6,10},{7,11},{8,4},{9,5},... | collective-permute-start | bytes 196616 | tf_op jit(solution)/shard_map/ppermute | solution.py:13
  30.7 25.0 %copy-start.6 = (f32[1,128,128]{2,1,0:T(8,128)}, f32[1,128,128]{2,1,0:T(8,128)S(1)}, u32[]{:S(2)}) copy-start(f32[1,128,128]{2,1,0:T(8,128)S(1)} %get-tuple-element.26) | copy-start | bytes 196612
  30.7 4.3 %collective-permute-start.10 = (f32[1,128,128]{2,1,0:T(8,128)S(1)}, f32[1,128,128]{2,1,0:T(8,128)S(1)}, u32[]{:S(2)}, u32[]{:S(2)}) collective-permute-start(f32[1,128,128]{2,1,0:T(8,128)S(1)} %get-tuple-element.26), channel_id=1, source_target_pairs={{0,2},{1,3},{2,0},{3,1},{4,6},{5,7},{6,4},{7,5},{8,10},{9,11},{10,... | collective-permute-start | bytes 196616 | tf_op jit(solution)/shard_map/ppermute | solution.py:13
  35.0 7.6 %collective-permute-start.11 = (f32[2,128,128]{2,1,0:T(8,128)S(1)}, f32[2,128,128]{2,1,0:T(8,128)S(1)}, u32[]{:S(2)}, u32[]{:S(2)}) collective-permute-start(f32[2,128,128]{2,1,0:T(8,128)S(1)} %pad_maximum_fusion.1), channel_id=1, source_target_pairs={{0,16},{1,17},{2,18},{3,19},{4,20},{5,21},{6,22},{7,23},{8,24},{9,... | collective-permute-start | bytes 393224 | tf_op jit(solution)/shard_map/ppermute | solution.py:13
  42.6 13.2 %copy-start.7 = (s32[8,256]{1,0:T(8,128)S(1)}, s32[8,256]{1,0:T(8,128)}, u32[]{:S(2)}) copy-start(s32[8,256]{1,0:T(8,128)} %param.23) | copy-start | bytes 24580
  42.6 8.0 %collective-permute-start.12 = (f32[4,128,128]{2,1,0:T(8,128)S(1)}, f32[4,128,128]{2,1,0:T(8,128)S(1)}, u32[]{:S(2)}, u32[]{:S(2)}) collective-permute-start(f32[4,128,128]{2,1,0:T(8,128)S(1)} %pad_maximum_fusion), channel_id=1, source_target_pairs={{0,8},{1,9},{2,10},{3,11},{4,12},{5,13},{6,14},{7,15},{8,0},{9,1},... | collective-permute-start | bytes 786440 | tf_op jit(solution)/shard_map/ppermute | solution.py:13
  43.1 8.3 %collective-permute-start.13 = (f32[4,128,128]{2,1,0:T(8,128)S(1)}, f32[4,128,128]{2,1,0:T(8,128)S(1)}, u32[]{:S(2)}, u32[]{:S(2)}) collective-permute-start(f32[4,128,128]{2,1,0:T(8,128)S(1)} %pad_maximum_fusion), channel_id=1, source_target_pairs={{0,4},{1,5},{2,6},{3,7},{4,0},{5,1},{6,2},{7,3},{8,12},{9,13},{10,... | collective-permute-start | bytes 786440 | tf_op jit(solution)/shard_map/ppermute | solution.py:13
  45.0 8.1 %collective-permute-start.14 = (f32[4,128,128]{2,1,0:T(8,128)S(1)}, f32[4,128,128]{2,1,0:T(8,128)S(1)}, u32[]{:S(2)}, u32[]{:S(2)}) collective-permute-start(f32[4,128,128]{2,1,0:T(8,128)S(1)} %pad_maximum_fusion), channel_id=1, source_target_pairs={{0,12},{1,13},{2,14},{3,15},{4,8},{5,9},{6,10},{7,11},{8,4},{9,5},... | collective-permute-start | bytes 786440 | tf_op jit(solution)/shard_map/ppermute | solution.py:13
  53.8 4.2 %collective-permute-start.15 = (f32[16,128,128]{2,1,0:T(8,128)}, f32[16,128,128]{2,1,0:T(8,128)}, u32[]{:S(2)}, u32[]{:S(2)}) collective-permute-start(f32[16,128,128]{2,1,0:T(8,128)} %constant_dynamic-update-slice_fusion.13), channel_id=1, source_target_pairs={{0,1},{1,0},{2,3},{3,2},{4,5},{5,4},{6,7},{7,6},{8,9},{9,8},{10,11... | collective-permute-start | bytes 3145736 | tf_op jit(solution)/shard_map/ppermute | solution.py:119
  61.3 3.6 %copy-start.4 = (f32[8,256,256]{2,1,0:T(8,128)S(1)}, f32[8,256,256]{2,1,0:T(8,128)}, u32[]{:S(2)}) copy-start(f32[8,256,256]{2,1,0:T(8,128)} %param.26) | copy-start | bytes 6291460
  (6 other events, 9.2 us)

commit v18 on v17

--- a/solution.py
+++ b/solution.py
@@ -13,6 +13,14 @@
             parts.append(lax.ppermute(held, axes, [(i, i ^ v) for i in range(count)]))
         held = jnp.concatenate(parts, 0)
     return held
+
+
+def xor_gather_step(held, axes, count, bits):
+    parts = [held]
+    for k in range(1, 1 << len(bits)):
+        v = sum(((k >> t) & 1) << b for t, b in enumerate(bits))
+        parts.append(lax.ppermute(held, axes, [(i, i ^ v) for i in range(count)]))
+    return jnp.concatenate(parts, 0)
 
 
 def xor_position(offset, groups):
@@ -114,7 +122,13 @@
     top_held = xor_gather(top_solution, both, count, top_groups).reshape(count * top_rows, rhs)
     own_rows = own_base - jnp.einsum("wj,jr->wr", total, top_held, precision=highest)
 
-    held = xor_gather(own_rows, both, count, spread_groups[:-1])
+    inverse_t = jnp.swapaxes(lower_inverse, 1, 2)
+    held = xor_gather_step(own_rows[None], both, count, spread_groups[0])
+    _, inverse_late = lax.optimization_barrier((own_rows, lower_inverse))
+    lower_base = jnp.einsum("skw,skr->swr", inverse_late, lower_rhs, precision=highest)
+    held, lower_base = lax.optimization_barrier((held, lower_base))
+    for bits in spread_groups[1:-1]:
+        held = xor_gather_step(held, both, count, bits)
     last = spread_groups[-1][0]
     partner = lax.ppermute(held, both, [(i, i ^ (1 << last)) for i in range(count)])
     position = owner_map[parent_list]
@@ -134,11 +148,8 @@
         parent_rows = term if parent_rows is None else parent_rows + term
 
     panel_t = jnp.swapaxes(lower_panel, 1, 2)
-    inverse_t = jnp.swapaxes(lower_inverse, 1, 2)
     lower_update = jnp.einsum("swk,skr->swr", panel_t, parent_rows, precision=highest)
-    lower_solution = jnp.einsum(
-        "swk,skr->swr", inverse_t, lower_rhs - lower_update, precision=highest
-    )
+    lower_solution = lower_base - jnp.einsum("swk,skr->swr", inverse_t, lower_update, precision=highest)
     return (own_rows[None], lower_solution)
 
 

time: 69.5 us -> 74.8 us (1.076); the launches traced: 68.2 us -> 74.4 us
  matrix products: 16 us -> 21.3 us
  other arithmetic: 1.14 us -> 2.21 us
    ppermute x12 -> x7, waiting for transfers between devices: 15.6 us -> 5.18 us  [xor_gather(): parts.append(lax.ppermute(held, axes, [(i, i ^ v) for i in range(count)]))]
    ppermute x0 -> x5, waiting for transfers between devices: none -> 9.81 us  [xor_gather_step(): parts.append(lax.ppermute(held, axes, [(i, i ^ v) for i in range(count)]))]
    ppermute x12 -> x7, starting transfers between devices: 19.7 us -> 11.5 us  [xor_gather(): parts.append(lax.ppermute(held, axes, [(i, i ^ v) for i in range(count)]))]
    ppermute x0 -> x5, starting transfers between devices: none -> 8.17 us  [xor_gather_step(): parts.append(lax.ppermute(held, axes, [(i, i ^ v) for i in range(count)]))]
    dot_general x1 -> x2, matrix products: 1.99 us -> 7.95 us  [the longest x1 4.45 us: local(): jnp.einsum('skw,skr->swr', inverse_late, lower_rhs, precision=highest)]
    unnamed x39 -> x37, local copies, waits for them, and re-layouts: 5.27 us -> 3.06 us
    gather x2, local copies, waits for them, and re-layouts: 3.67 us -> 5.64 us  [local(): slabs = source[places].reshape(position.shape[0], -1, own_rows.shape[1])]
    dot_general x2, matrix products: 3.32 us -> 4.94 us  [local(): term = jnp.einsum('skj,sjr->skr', pick, slabs, precision=highest)]
  transfers between devices with their start and end apart: 16 -> 16, of which waited for: 7 -> 6; matrix products, arithmetic and copies ran while one was open for 23% -> 28% of each run, Pallas kernels for 0% -> 0%
where the time goes in v18:
time: 74.8 us; the launch traced here: 74.4 us
  starting transfers between devices  21.8 us (29%)
  matrix products  21.3 us (28%)
  waiting for transfers between devices  15 us (20%)
  local copies, waits for them, and re-layouts  13.1 us (18%)
  other arithmetic  2.21 us (3%)
  between operations  0.99 us (1%)
    ppermute x7, starting transfers between devices, xor_gather(): parts.append(lax.ppermute(held, axes, [(i, i ^ v) for i in range(count)]))  11.5 us
    ppermute x5, waiting for transfers between devices, xor_gather_step(): parts.append(lax.ppermute(held, axes, [(i, i ^ v) for i in range(count)]))  9.81 us
    ppermute x5, starting transfers between devices, xor_gather_step(): parts.append(lax.ppermute(held, axes, [(i, i ^ v) for i in range(count)]))  8.17 us
    gather x2, local copies, waits for them, and re-layouts, local(): slabs = source[places].reshape(position.shape[0], -1, own_rows.shape[1])  5.64 us
    ppermute x7, waiting for transfers between devices, xor_gather(): parts.append(lax.ppermute(held, axes, [(i, i ^ v) for i in range(count)]))  5.18 us
    dot_general x2, matrix products, local(): term = jnp.einsum('skj,sjr->skr', pick, slabs, precision=highest)  4.94 us
    dot_general x1, matrix products, local(): jnp.einsum('skw,skr->swr', inverse_late, lower_rhs, precision=highest)  4.45 us
    dot_general x1, matrix products, local(): jnp.einsum('swk,skr->swr', inverse_t, lower_update, precision=highest)  3.49 us
  transfers between devices with their start and end apart: 16, of which 6 were waited for; matrix products, arithmetic and copies ran while one was open for 28% of the time, Pallas kernels for 0%

profile of v18, /device:TPU:0, one launch (start us, length us, event | category | flops | bytes accessed | tf_op | source)
XLA Modules:
  0.0 74.4 jit_solution(16671887229810519224)
XLA Ops:
  1.2 2.6 %collective-permute-start.4 = (f32[1,16,128]{2,1,0:T(8,128)}, f32[1,16,128]{2,1,0:T(8,128)S(1)}, u32[]{:S(2)}, u32[]{:S(2)}) collective-permute-start(f32[1,16,128]{2,1,0:T(8,128)} %bitcast.64), channel_id=1, source_target_pairs={{0,2},{1,3},{2,0},{3,1},{4,6},{5,7},{6,4},{7,5},{8,10},{9,11},{10,... | collective-permute-start | bytes 24584 | tf_op jit(solution)/shard_map/ppermute | solution.py:13
  5.1 2.4 %fusion.4 = f32[256,512]{1,0:T(8,128)S(1)} fusion(f32[1,512,512]{2,1,0:T(8,128)} %param.18, f32[1,256,512]{2,1,0:T(8,128)} %param.17), kind=kOutput, calls=%fused_computation.12 | convolution fusion | flops 805306368 | bytes 2097152 | tf_op jit(solution)/shard_map/kv,vw->kw/dot_general | solution.py:110
  9.9 1.7 %collective-permute-start.2 = (f32[128,512]{0,1:T(8,128)S(1)}, f32[128,512]{0,1:T(8,128)}, u32[]{:S(2)}, u32[]{:S(2)}) collective-permute-start(f32[128,512]{0,1:T(8,128)S(1)} %bitcast.54), channel_id=1, source_target_pairs={{0,3},{1,2},{2,1},{3,0},{4,7},{5,6},{6,5},{7,4},{8,11},{9,10},{10,... | collective-permute-start | bytes 786440 | tf_op jit(solution)/shard_map/ppermute | solution.py:118
  13.2 3.0 %collective-permute-start.6 = (f32[4,16,128]{2,1,0:T(8,128)S(1)}, f32[4,16,128]{2,1,0:T(8,128)S(1)}, u32[]{:S(2)}, u32[]{:S(2)}) collective-permute-start(f32[4,16,128]{2,1,0:T(8,128)S(1)} %pad_maximum_fusion.1), channel_id=1, source_target_pairs={{0,16},{1,17},{2,18},{3,19},{4,20},{5,21},{6,22},{7,23},{8,24},{9,... | collective-permute-start | bytes 98312 | tf_op jit(solution)/shard_map/ppermute | solution.py:13
  16.2 2.0 %collective-permute-done.6 = f32[4,16,128]{2,1,0:T(8,128)S(1)} collective-permute-done((f32[4,16,128]{2,1,0:T(8,128)S(1)}, f32[4,16,128]{2,1,0:T(8,128)S(1)}, u32[]{:S(2)}, u32[]{:S(2)}) %collective-permute-start.6) | collective-permute-done | bytes 32800 | tf_op jit(solution)/shard_map/ppermute | solution.py:13
  18.2 1.8 %collective-permute-start.7 = (f32[8,16,128]{2,1,0:T(8,128)S(1)}, f32[8,16,128]{2,1,0:T(8,128)S(1)}, u32[]{:S(2)}, u32[]{:S(2)}) collective-permute-start(f32[8,16,128]{2,1,0:T(8,128)S(1)} %get-tuple-element.17), channel_id=1, source_target_pairs={{0,8},{1,9},{2,10},{3,11},{4,12},{5,13},{6,14},{7,15},{8,0},{9,1},... | collective-permute-start | bytes 196616 | tf_op jit(solution)/shard_map/ppermute | solution.py:13
  20.0 1.6 %fusion.15 = f32[128,128]{1,0:T(8,128)S(1)} fusion(f32[1,512,128]{2,1,0:T(8,128)} %param.16, f32[1,512,512]{2,1,0:T(8,128)} %param.18, s32[]{:T(128)S(6)} %select_n.96), kind=kOutput, calls=%fused_computation.23 | convolution fusion | flops 100663296 | bytes 589828 | tf_op jit(solution)/shard_map/kw,kr->wr/dot_general | solution.py:120
  21.6 1.6 %collective-permute-start.8 = (f32[8,16,128]{2,1,0:T(8,128)S(1)}, f32[8,16,128]{2,1,0:T(8,128)S(1)}, u32[]{:S(2)}, u32[]{:S(2)}) collective-permute-start(f32[8,16,128]{2,1,0:T(8,128)S(1)} %get-tuple-element.17), channel_id=1, source_target_pairs={{0,4},{1,5},{2,6},{3,7},{4,0},{5,1},{6,2},{7,3},{8,12},{9,13},{10,... | collective-permute-start | bytes 196616 | tf_op jit(solution)/shard_map/ppermute | solution.py:13
  23.2 2.0 %collective-permute-start.9 = (f32[8,16,128]{2,1,0:T(8,128)S(1)}, f32[8,16,128]{2,1,0:T(8,128)S(1)}, u32[]{:S(2)}, u32[]{:S(2)}) collective-permute-start(f32[8,16,128]{2,1,0:T(8,128)S(1)} %get-tuple-element.17), channel_id=1, source_target_pairs={{0,12},{1,13},{2,14},{3,15},{4,8},{5,9},{6,10},{7,11},{8,4},{9,5},... | collective-permute-start | bytes 196616 | tf_op jit(solution)/shard_map/ppermute | solution.py:13
  26.7 1.7 %collective-permute-done.9 = f32[8,16,128]{2,1,0:T(8,128)S(1)} collective-permute-done((f32[8,16,128]{2,1,0:T(8,128)S(1)}, f32[8,16,128]{2,1,0:T(8,128)S(1)}, u32[]{:S(2)}, u32[]{:S(2)}) %collective-permute-start.9) | collective-permute-done | bytes 65568 | tf_op jit(solution)/shard_map/ppermute | solution.py:13
  28.4 1.7 %convolution_subtract_fusion = f32[128,128]{1,0:T(8,128)S(1)} fusion(f32[128,128]{1,0:T(8,128)S(1)} %fusion.15, f32[512,128]{1,0:T(8,128)S(1)} %bitcast.59, f32[128,512]{0,1:T(8,128)} %collective-permute-done.2, f32[128,512]{0,1:T(8,128)} %collective-permute-done.1, f32[128,512]{0,1:T(8,128)S(1)} %collective-permute-done, f32[512,512]{0,1:T(8,128)} %copy-done.2, ...), kind=kOutput, calls=%fused_computation.11 | convolution fusion | flops 100876288 | bytes 1441796 | tf_op jit(solution)/shard_map/wj,jr->wr/dot_general | solution.py:123
  30.1 1.6 %collective-permute-start.10 = (f32[1,128,128]{2,1,0:T(8,128)S(1)}, f32[1,128,128]{2,1,0:T(8,128)S(1)}, u32[]{:S(2)}, u32[]{:S(2)}) collective-permute-start(f32[1,128,128]{2,1,0:T(8,128)S(1)} %bitcast.60), channel_id=1, source_target_pairs={{0,2},{1,3},{2,0},{3,1},{4,6},{5,7},{6,4},{7,5},{8,10},{9,11},{10,... | collective-permute-start | bytes 196616 | tf_op jit(solution)/shard_map/ppermute | solution.py:22
  31.7 4.5 %fusion.37 = f32[8,256,128]{2,1,0:T(8,128)} fusion(f32[8,256,256]{2,1,0:T(8,128)S(1)} %copy-done, f32[8,256,128]{2,1,0:T(8,128)S(1)} %copy-done.5), kind=kOutput, calls=%fused_computation.107 | convolution fusion | flops 805306368 | bytes 4194304 | tf_op jit(solution)/shard_map/skw,skr->swr/dot_general | solution.py:128
  36.2 3.1 %collective-permute-start.11 = (f32[2,128,128]{2,1,0:T(8,128)S(1)}, f32[2,128,128]{2,1,0:T(8,128)S(1)}, u32[]{:S(2)}, u32[]{:S(2)}) collective-permute-start(f32[2,128,128]{2,1,0:T(8,128)S(1)} %pad_maximum_fusion), channel_id=1, source_target_pairs={{0,16},{1,17},{2,18},{3,19},{4,20},{5,21},{6,22},{7,23},{8,24},{9,... | collective-permute-start | bytes 393224 | tf_op jit(solution)/shard_map/ppermute | solution.py:22
  40.6 3.1 %collective-permute-done.11 = f32[2,128,128]{2,1,0:T(8,128)S(1)} collective-permute-done((f32[2,128,128]{2,1,0:T(8,128)S(1)}, f32[2,128,128]{2,1,0:T(8,128)S(1)}, u32[]{:S(2)}, u32[]{:S(2)}) %collective-permute-start.11) | collective-permute-done | bytes 131104 | tf_op jit(solution)/shard_map/ppermute | solution.py:22
  45.9 2.0 %collective-permute-start.14 = (f32[4,128,128]{2,1,0:T(8,128)S(1)}, f32[4,128,128]{2,1,0:T(8,128)S(1)}, u32[]{:S(2)}, u32[]{:S(2)}) collective-permute-start(f32[4,128,128]{2,1,0:T(8,128)S(1)} %get-tuple-element.13), channel_id=1, source_target_pairs={{0,12},{1,13},{2,14},{3,15},{4,8},{5,9},{6,10},{7,11},{8,4},{9,5},... | collective-permute-start | bytes 786440 | tf_op jit(solution)/shard_map/ppermute | solution.py:22
  48.2 4.6 %collective-permute-done.12 = f32[4,128,128]{2,1,0:T(8,128)S(1)} collective-permute-done((f32[4,128,128]{2,1,0:T(8,128)S(1)}, f32[4,128,128]{2,1,0:T(8,128)S(1)}, u32[]{:S(2)}, u32[]{:S(2)}) %collective-permute-start.12) | collective-permute-done | bytes 262176 | tf_op jit(solution)/shard_map/ppermute | solution.py:22
  53.5 2.1 %collective-permute-done.13 = f32[4,128,128]{2,1,0:T(8,128)S(1)} collective-permute-done((f32[4,128,128]{2,1,0:T(8,128)S(1)}, f32[4,128,128]{2,1,0:T(8,128)S(1)}, u32[]{:S(2)}, u32[]{:S(2)}) %collective-permute-start.13) | collective-permute-done | bytes 262176 | tf_op jit(solution)/shard_map/ppermute | solution.py:22
  57.2 2.8 %gather_fusion.4 = f32[16,128,128]{2,1,0:T(8,128)} fusion(f32[16,128,128]{2,1,0:T(8,128)} %constant_dynamic-update-slice_fusion.15, s32[1024]{0:T(1024)S(1)} %pad_clamp_fusion.1), kind=kCustom, calls=%fused_computation.4 | custom fusion | bytes 2097216 | tf_op jit(solution)/shard_map/gather | solution.py:141
  60.0 2.4 %fusion.2 = f32[8,256,128]{2,1,0:T(8,128)S(1)} fusion(f32[8,256,128]{2,1,0:T(8,128)} %bitcast.58, s32[256]{0:T(256)S(1)} %add_bitcast_fusion.1, s32[8,256]{1,0:T(8,128)S(1)} %copy-done.7), kind=kOutput, calls=%fused_computation.8 | convolution fusion | flops 805830656 | bytes 2106368 | tf_op jit(solution)/shard_map/skj,sjr->skr/dot_general | solution.py:145
  62.4 2.8 %gather_fusion.5 = f32[16,128,128]{2,1,0:T(8,128)} fusion(f32[16,128,128]{2,1,0:T(8,128)} %collective-permute-done.15, s32[1024]{0:T(1024)S(1)} %pad_clamp_fusion), kind=kCustom, calls=%fused_computation.5 | custom fusion | bytes 2097216 | tf_op jit(solution)/shard_map/gather | solution.py:141
  65.3 2.5 %fusion = f32[8,256,128]{2,1,0:T(8,128)S(1)} fusion(f32[8,256,128]{2,1,0:T(8,128)} %bitcast.57, s32[256]{0:T(256)S(1)} %add_bitcast_fusion, s32[8,256]{1,0:T(8,128)S(1)} %copy-done.7), kind=kOutput, calls=%fused_computation.6 | convolution fusion | flops 805830656 | bytes 2106368 | tf_op jit(solution)/shard_map/skj,sjr->skr/dot_general | solution.py:145
  67.8 2.0 %fusion.6 = f32[8,128,256]{2,1,0:T(8,128)S(1)} fusion(f32[8,256,256]{2,1,0:T(8,128)S(1)} %copy-done.4, f32[8,256,128]{2,1,0:T(8,128)S(1)} %fusion.2, f32[8,256,128]{2,1,0:T(8,128)S(1)} %fusion), kind=kOutput, calls=%fused_computation.14 | convolution fusion | flops 805568512 | bytes 5242880 | tf_op jit(solution)/shard_map/swk,skr->swr/dot_general | solution.py:151
  69.8 3.5 %convolution_bitcast_fusion = f32[8,256,128]{2,1,0:T(8,128)S(1)} fusion(f32[8,128,256]{2,1,0:T(8,128)S(1)} %fusion.6, f32[8,256,256]{2,1,0:T(8,128)S(1)} %copy-done), kind=kOutput, calls=%fused_computation.10 | convolution fusion | flops 805306368 | bytes 4194304 | tf_op jit(solution)/shard_map/swk,skr->swr/dot_general | solution.py:152
  (93 shorter events, 14.2 us)
Async XLA Ops:
  0.6 31.1 %copy-start = (f32[8,256,256]{2,1,0:T(8,128)S(1)}, f32[8,256,256]{2,1,0:T(8,128)}, u32[]{:S(2)}) copy-start(f32[8,256,256]{2,1,0:T(8,128)} %param.26) | copy-start | bytes 6291460
  0.6 6.9 %copy-start.13 = (s32[32]{0:T(128)S(1)}, s32[32]{0:T(128)}, u32[]{:S(2)}) copy-start(s32[32]{0:T(128)} %constant.145) | copy-start | bytes 388
  0.7 6.9 %copy-start.9 = (s32[1,256]{1,0:T(1,128)S(1)}, s32[1,256]{1,0:T(1,128)}, u32[]{:S(2)}) copy-start(s32[1,256]{1,0:T(1,128)} %param.19) | copy-start | bytes 3076
  0.7 12.4 %collective-permute-start.3 = (f32[1,16,128]{2,1,0:T(8,128)}, f32[1,16,128]{2,1,0:T(8,128)S(1)}, u32[]{:S(2)}, u32[]{:S(2)}) collective-permute-start(f32[1,16,128]{2,1,0:T(8,128)} %bitcast.63), channel_id=1, source_target_pairs={{0,1},{1,0},{2,3},{3,2},{4,5},{5,4},{6,7},{7,6},{8,9},{9,8},{10,11... | collective-permute-start | bytes 24584 | tf_op jit(solution)/shard_map/ppermute | solution.py:13
  1.2 12.0 %collective-permute-start.4 = (f32[1,16,128]{2,1,0:T(8,128)}, f32[1,16,128]{2,1,0:T(8,128)S(1)}, u32[]{:S(2)}, u32[]{:S(2)}) collective-permute-start(f32[1,16,128]{2,1,0:T(8,128)} %bitcast.64), channel_id=1, source_target_pairs={{0,2},{1,3},{2,0},{3,1},{4,6},{5,7},{6,4},{7,5},{8,10},{9,11},{10,... | collective-permute-start | bytes 24584 | tf_op jit(solution)/shard_map/ppermute | solution.py:13
  3.8 9.4 %collective-permute-start.5 = (f32[1,16,128]{2,1,0:T(8,128)}, f32[1,16,128]{2,1,0:T(8,128)S(1)}, u32[]{:S(2)}, u32[]{:S(2)}) collective-permute-start(f32[1,16,128]{2,1,0:T(8,128)} %bitcast.65), channel_id=1, source_target_pairs={{0,3},{1,2},{2,1},{3,0},{4,7},{5,6},{6,5},{7,4},{8,11},{9,10},{10,... | collective-permute-start | bytes 24584 | tf_op jit(solution)/shard_map/ppermute | solution.py:13
  9.9 18.5 %collective-permute-start.2 = (f32[128,512]{0,1:T(8,128)S(1)}, f32[128,512]{0,1:T(8,128)}, u32[]{:S(2)}, u32[]{:S(2)}) collective-permute-start(f32[128,512]{0,1:T(8,128)S(1)} %bitcast.54), channel_id=1, source_target_pairs={{0,3},{1,2},{2,1},{3,0},{4,7},{5,6},{6,5},{7,4},{8,11},{9,10},{10,... | collective-permute-start | bytes 786440 | tf_op jit(solution)/shard_map/ppermute | solution.py:118
  12.2 16.1 %collective-permute-start.1 = (f32[128,512]{0,1:T(8,128)S(1)}, f32[128,512]{0,1:T(8,128)}, u32[]{:S(2)}, u32[]{:S(2)}) collective-permute-start(f32[128,512]{0,1:T(8,128)S(1)} %bitcast.55), channel_id=1, source_target_pairs={{0,2},{1,3},{2,0},{3,1},{4,6},{5,7},{6,4},{7,5},{8,10},{9,11},{10,... | collective-permute-start | bytes 786440 | tf_op jit(solution)/shard_map/ppermute | solution.py:118
  13.0 18.7 %copy-start.5 = (f32[8,256,128]{2,1,0:T(8,128)S(1)}, f32[8,256,128]{2,1,0:T(8,128)}, u32[]{:S(2)}) copy-start(f32[8,256,128]{2,1,0:T(8,128)} %param.25) | copy-start | bytes 3145732
  13.0 15.3 %collective-permute-start = (f32[128,512]{0,1:T(8,128)S(1)}, f32[128,512]{0,1:T(8,128)S(1)}, u32[]{:S(2)}, u32[]{:S(2)}) collective-permute-start(f32[128,512]{0,1:T(8,128)S(1)} %bitcast.56), channel_id=1, source_target_pairs={{0,1},{1,0},{2,3},{3,2},{4,5},{5,4},{6,7},{7,6},{8,9},{9,8},{10,11... | collective-permute-start | bytes 786440 | tf_op jit(solution)/shard_map/ppermute | solution.py:118
  13.2 5.0 %collective-permute-start.6 = (f32[4,16,128]{2,1,0:T(8,128)S(1)}, f32[4,16,128]{2,1,0:T(8,128)S(1)}, u32[]{:S(2)}, u32[]{:S(2)}) collective-permute-start(f32[4,16,128]{2,1,0:T(8,128)S(1)} %pad_maximum_fusion.1), channel_id=1, source_target_pairs={{0,16},{1,17},{2,18},{3,19},{4,20},{5,21},{6,22},{7,23},{8,24},{9,... | collective-permute-start | bytes 98312 | tf_op jit(solution)/shard_map/ppermute | solution.py:13
  18.2 5.0 %collective-permute-start.7 = (f32[8,16,128]{2,1,0:T(8,128)S(1)}, f32[8,16,128]{2,1,0:T(8,128)S(1)}, u32[]{:S(2)}, u32[]{:S(2)}) collective-permute-start(f32[8,16,128]{2,1,0:T(8,128)S(1)} %get-tuple-element.17), channel_id=1, source_target_pairs={{0,8},{1,9},{2,10},{3,11},{4,12},{5,13},{6,14},{7,15},{8,0},{9,1},... | collective-permute-start | bytes 196616 | tf_op jit(solution)/shard_map/ppermute | solution.py:13
  21.6 5.0 %collective-permute-start.8 = (f32[8,16,128]{2,1,0:T(8,128)S(1)}, f32[8,16,128]{2,1,0:T(8,128)S(1)}, u32[]{:S(2)}, u32[]{:S(2)}) collective-permute-start(f32[8,16,128]{2,1,0:T(8,128)S(1)} %get-tuple-element.17), channel_id=1, source_target_pairs={{0,4},{1,5},{2,6},{3,7},{4,0},{5,1},{6,2},{7,3},{8,12},{9,13},{10,... | collective-permute-start | bytes 196616 | tf_op jit(solution)/shard_map/ppermute | solution.py:13
  23.2 5.2 %collective-permute-start.9 = (f32[8,16,128]{2,1,0:T(8,128)S(1)}, f32[8,16,128]{2,1,0:T(8,128)S(1)}, u32[]{:S(2)}, u32[]{:S(2)}) collective-permute-start(f32[8,16,128]{2,1,0:T(8,128)S(1)} %get-tuple-element.17), channel_id=1, source_target_pairs={{0,12},{1,13},{2,14},{3,15},{4,8},{5,9},{6,10},{7,11},{8,4},{9,5},... | collective-permute-start | bytes 196616 | tf_op jit(solution)/shard_map/ppermute | solution.py:13
  30.1 6.1 %copy-start.6 = (f32[128,128]{1,0:T(8,128)}, f32[128,128]{1,0:T(8,128)S(1)}, u32[]{:S(2)}) copy-start(f32[128,128]{1,0:T(8,128)S(1)} %convolution_subtract_fusion) | copy-start | bytes 196612
  30.1 9.2 %copy-start.10 = (s32[2]{0:T(128)S(1)}, s32[2]{0:T(128)}, u32[]{:S(2)}) copy-start(s32[2]{0:T(128)} %constant.120.clone) | copy-start | bytes 28
  30.1 9.2 %copy-start.1 = (s32[8]{0:T(128)S(1)}, s32[8]{0:T(128)}, u32[]{:S(2)}) copy-start(s32[8]{0:T(128)} %param.21) | copy-start | bytes 100
  30.1 6.0 %collective-permute-start.10 = (f32[1,128,128]{2,1,0:T(8,128)S(1)}, f32[1,128,128]{2,1,0:T(8,128)S(1)}, u32[]{:S(2)}, u32[]{:S(2)}) collective-permute-start(f32[1,128,128]{2,1,0:T(8,128)S(1)} %bitcast.60), channel_id=1, source_target_pairs={{0,2},{1,3},{2,0},{3,1},{4,6},{5,7},{6,4},{7,5},{8,10},{9,11},{10,... | collective-permute-start | bytes 196616 | tf_op jit(solution)/shard_map/ppermute | solution.py:22
  36.2 7.5 %collective-permute-start.11 = (f32[2,128,128]{2,1,0:T(8,128)S(1)}, f32[2,128,128]{2,1,0:T(8,128)S(1)}, u32[]{:S(2)}, u32[]{:S(2)}) collective-permute-start(f32[2,128,128]{2,1,0:T(8,128)S(1)} %pad_maximum_fusion), channel_id=1, source_target_pairs={{0,16},{1,17},{2,18},{3,19},{4,20},{5,21},{6,22},{7,23},{8,24},{9,... | collective-permute-start | bytes 393224 | tf_op jit(solution)/shard_map/ppermute | solution.py:22
  40.6 19.4 %copy-start.7 = (s32[8,256]{1,0:T(8,128)S(1)}, s32[8,256]{1,0:T(8,128)}, u32[]{:S(2)}) copy-start(s32[8,256]{1,0:T(8,128)} %param.23) | copy-start | bytes 24580
  44.4 8.4 %collective-permute-start.12 = (f32[4,128,128]{2,1,0:T(8,128)S(1)}, f32[4,128,128]{2,1,0:T(8,128)S(1)}, u32[]{:S(2)}, u32[]{:S(2)}) collective-permute-start(f32[4,128,128]{2,1,0:T(8,128)S(1)} %get-tuple-element.13), channel_id=1, source_target_pairs={{0,8},{1,9},{2,10},{3,11},{4,12},{5,13},{6,14},{7,15},{8,0},{9,1},... | collective-permute-start | bytes 786440 | tf_op jit(solution)/shard_map/ppermute | solution.py:22
  45.0 10.6 %collective-permute-start.13 = (f32[4,128,128]{2,1,0:T(8,128)S(1)}, f32[4,128,128]{2,1,0:T(8,128)S(1)}, u32[]{:S(2)}, u32[]{:S(2)}) collective-permute-start(f32[4,128,128]{2,1,0:T(8,128)S(1)} %get-tuple-element.13), channel_id=1, source_target_pairs={{0,4},{1,5},{2,6},{3,7},{4,0},{5,1},{6,2},{7,3},{8,12},{9,13},{10,... | collective-permute-start | bytes 786440 | tf_op jit(solution)/shard_map/ppermute | solution.py:22
  45.9 10.4 %collective-permute-start.14 = (f32[4,128,128]{2,1,0:T(8,128)S(1)}, f32[4,128,128]{2,1,0:T(8,128)S(1)}, u32[]{:S(2)}, u32[]{:S(2)}) collective-permute-start(f32[4,128,128]{2,1,0:T(8,128)S(1)} %get-tuple-element.13), channel_id=1, source_target_pairs={{0,12},{1,13},{2,14},{3,15},{4,8},{5,9},{6,10},{7,11},{8,4},{9,5},... | collective-permute-start | bytes 786440 | tf_op jit(solution)/shard_map/ppermute | solution.py:22
  57.0 5.4 %collective-permute-start.15 = (f32[16,128,128]{2,1,0:T(8,128)}, f32[16,128,128]{2,1,0:T(8,128)}, u32[]{:S(2)}, u32[]{:S(2)}) collective-permute-start(f32[16,128,128]{2,1,0:T(8,128)} %constant_dynamic-update-slice_fusion.15), channel_id=1, source_target_pairs={{0,1},{1,0},{2,3},{3,2},{4,5},{5,4},{6,7},{7,6},{8,9},{9,8},{10,11... | collective-permute-start | bytes 3145736 | tf_op jit(solution)/shard_map/ppermute | solution.py:133
  (6 other events, 12.5 us)

commit v19 on v17

--- a/solution.py
+++ b/solution.py
@@ -104,9 +104,11 @@
     total = lax.dynamic_slice_in_dim(weights, begin, share, 0)
     for v in range(1, panels):
         outgoing = lax.dynamic_slice_in_dim(weights, (panel_index ^ v) * share, share, 0)
-        order = [static_position(static_offset(h, top_groups) ^ v, top_groups) for h in range(count)]
-        outgoing = outgoing.reshape(share, count, top_rows)[:, jnp.array(order), :]
-        outgoing = outgoing.reshape(share, count * top_rows)
+        assert top_groups[0] == panel_bits
+        width = len(panel_bits)
+        outgoing = outgoing.reshape((share, count // panels) + (2,) * width + (top_rows,))
+        flips = tuple(2 + width - 1 - t for t, b in enumerate(panel_bits) if (v >> b) & 1)
+        outgoing = jnp.flip(outgoing, flips).reshape(share, count * top_rows)
         total = total + lax.ppermute(outgoing, "panel", [(i, i ^ v) for i in range(panels)])
     own_inverse = lax.dynamic_slice_in_dim(upper_inverse[0], begin, share, 1)
     own_base = jnp.einsum("kw,kr->wr", own_inverse, upper_rhs[0], precision=highest)

time: 69.5 us -> 76 us (1.094)
  local copies, waits for them, and re-layouts: 12.7 us -> 19.9 us
  waiting for transfers between devices: 15.7 us -> 12.9 us
  matrix products: 16 us -> 17.8 us
  starting transfers between devices: 21.8 us -> 22.8 us
    rev x0 -> x3, local copies, waits for them, and re-layouts: none -> 4.08 us  [local(): outgoing = jnp.flip(outgoing, flips).reshape(share, count * top_rows)]
    unnamed x39 -> x33, local copies, waits for them, and re-layouts: 5.27 us -> 8.08 us
    ppermute x12, waiting for transfers between devices: 15.6 us -> 12.9 us  [xor_gather(): parts.append(lax.ppermute(held, axes, [(i, i ^ v) for i in range(count)]))]
    gather x3 -> x0, local copies, waits for them, and re-layouts: 1.75 us -> none  [local(): outgoing = outgoing.reshape(share, count, top_rows)[:, jnp.array(order), :]]
    ppermute x12, starting transfers between devices: 19.7 us -> 21 us  [xor_gather(): parts.append(lax.ppermute(held, axes, [(i, i ^ v) for i in range(count)]))]
    concatenate x3, local copies, waits for them, and re-layouts: 0.72 us -> 1.98 us  [xor_gather(): held = jnp.concatenate(parts, 0)]
    dot_general x1, matrix products: 0.7 us -> 1.75 us  [local(): weights = jnp.einsum('kj,kw->wj', pick_top, folded, precision=highest)]
    dot_general x1, matrix products: 2.44 us -> 3.24 us  [local(): jnp.einsum('kv,vw->kw', upper_panel[0], upper_inverse[0], precision=highest)]
  transfers between devices with their start and end apart: 16 -> 16, of which waited for: 7 -> 8; matrix products, arithmetic and copies ran while one was open for 23% -> 33% of each run, Pallas kernels for 0% -> 0%
where the time goes in v19:
time: 76 us; the launch traced here: 74.8 us
  starting transfers between devices  22.8 us (30%)
  local copies, waits for them, and re-layouts  19.9 us (26%)
  matrix products  17.8 us (23%)
  waiting for transfers between devices  12.9 us (17%)
  between operations  0.91 us (1%)
    ppermute x12, starting transfers between devices, xor_gather(): parts.append(lax.ppermute(held, axes, [(i, i ^ v) for i in range(count)]))  21 us
    ppermute x12, waiting for transfers between devices, xor_gather(): parts.append(lax.ppermute(held, axes, [(i, i ^ v) for i in range(count)]))  12.9 us
    unnamed x33, local copies, waits for them, and re-layouts  8.08 us
    rev x3, local copies, waits for them, and re-layouts, local(): outgoing = jnp.flip(outgoing, flips).reshape(share, count * top_rows)  4.08 us
    gather x2, local copies, waits for them, and re-layouts, local(): slabs = source[places].reshape(position.shape[0], -1, own_rows.shape[1])  3.67 us
    dot_general x1, matrix products, local(): jnp.einsum('swk,skr->swr', panel_t, parent_rows, precision=highest)  3.54 us
    dot_general x2, matrix products, local(): term = jnp.einsum('skj,sjr->skr', pick, slabs, precision=highest)  3.32 us
    dot_general x1, matrix products, local(): jnp.einsum('kv,vw->kw', upper_panel[0], upper_inverse[0], precision=highest)  3.24 us
  transfers between devices with their start and end apart: 16, of which 8 were waited for; matrix products, arithmetic and copies ran while one was open for 33% of the time, Pallas kernels for 0%

profile of v19, /device:TPU:0, one launch (start us, length us, event | category | flops | bytes accessed | tf_op | source)
XLA Modules:
  0.0 74.8 jit_solution(17049330978964488867)
XLA Ops:
  1.2 2.6 %collective-permute-start.4 = (f32[1,16,128]{2,1,0:T(8,128)}, f32[1,16,128]{2,1,0:T(8,128)S(1)}, u32[]{:S(2)}, u32[]{:S(2)}) collective-permute-start(f32[1,16,128]{2,1,0:T(8,128)} %bitcast.58), channel_id=1, source_target_pairs={{0,2},{1,3},{2,0},{3,1},{4,6},{5,7},{6,4},{7,5},{8,10},{9,11},{10,... | collective-permute-start | bytes 24584 | tf_op jit(solution)/shard_map/ppermute | solution.py:13
  4.4 3.2 %fusion.6 = f32[256,512]{1,0:T(8,128)} fusion(f32[1,512,512]{2,1,0:T(8,128)} %param.15, f32[1,256,512]{2,1,0:T(8,128)} %param.14), kind=kOutput, calls=%fused_computation.12 | convolution fusion | flops 805306368 | bytes 2097152 | tf_op jit(solution)/shard_map/kv,vw->kw/dot_general | solution.py:102
  7.7 1.7 %fusion.14 = f32[512,512]{0,1:T(8,128)S(1)} fusion(f32[256,512]{1,0:T(8,128)} %fusion.6, s32[512]{0:T(512)S(1)} %multiply_add_fusion, s32[256]{0:T(256)S(1)} %bitcast.61), kind=kOutput, calls=%fused_computation.20 | convolution fusion | flops 805437440 | bytes 1575936 | tf_op jit(solution)/shard_map/kj,kw->wj/dot_general | solution.py:103
  10.4 1.7 %rev.14 = f32[128,8,2,2,16]{0,4,3,2,1:T(8,128)} reverse(f32[128,8,2,2,16]{0,4,3,2,1:T(8,128)} %bitcast.52), dimensions={3,2} | reverse | bytes 524288 | tf_op jit(solution)/shard_map/jit(_flip)/rev | solution.py:111
  12.0 1.7 %collective-permute-start.2 = (f32[128,512]{0,1:T(8,128)}, f32[128,512]{0,1:T(8,128)}, u32[]{:S(2)}, u32[]{:S(2)}) collective-permute-start(f32[128,512]{0,1:T(8,128)} %bitcast.54), channel_id=1, source_target_pairs={{0,3},{1,2},{2,1},{3,0},{4,7},{5,6},{6,5},{7,4},{8,11},{9,10},{10,... | collective-permute-start | bytes 786440 | tf_op jit(solution)/shard_map/ppermute | solution.py:112
  13.7 1.7 %rev.13 = f32[128,8,2,2,16]{0,4,3,2,1:T(8,128)} reverse(f32[128,8,2,2,16]{0,4,3,2,1:T(8,128)} %bitcast.51), dimensions={2} | reverse | bytes 524288 | tf_op jit(solution)/shard_map/jit(_flip)/rev | solution.py:111
  16.1 1.6 %fusion.16 = f32[128,128]{1,0:T(8,128)S(1)} fusion(f32[1,512,128]{2,1,0:T(8,128)} %param.13, f32[1,512,512]{2,1,0:T(8,128)} %param.15, s32[]{:T(128)S(6)} %select_n.87), kind=kOutput, calls=%fused_computation.23 | convolution fusion | flops 100663296 | bytes 589828 | tf_op jit(solution)/shard_map/kw,kr->wr/dot_general | solution.py:114
  18.6 3.0 %collective-permute-start.6 = (f32[4,16,128]{2,1,0:T(8,128)S(1)}, f32[4,16,128]{2,1,0:T(8,128)S(1)}, u32[]{:S(2)}, u32[]{:S(2)}) collective-permute-start(f32[4,16,128]{2,1,0:T(8,128)S(1)} %pad_maximum_fusion.2), channel_id=1, source_target_pairs={{0,16},{1,17},{2,18},{3,19},{4,20},{5,21},{6,22},{7,23},{8,24},{9,... | collective-permute-start | bytes 98312 | tf_op jit(solution)/shard_map/ppermute | solution.py:13
  24.2 1.8 %collective-permute-start.7 = (f32[8,16,128]{2,1,0:T(8,128)}, f32[8,16,128]{2,1,0:T(8,128)S(1)}, u32[]{:S(2)}, u32[]{:S(2)}) collective-permute-start(f32[8,16,128]{2,1,0:T(8,128)} %get-tuple-element.11), channel_id=1, source_target_pairs={{0,8},{1,9},{2,10},{3,11},{4,12},{5,13},{6,14},{7,15},{8,0},{9,1},... | collective-permute-start | bytes 196616 | tf_op jit(solution)/shard_map/ppermute | solution.py:13
  26.0 1.5 %collective-permute-start.8 = (f32[8,16,128]{2,1,0:T(8,128)}, f32[8,16,128]{2,1,0:T(8,128)S(1)}, u32[]{:S(2)}, u32[]{:S(2)}) collective-permute-start(f32[8,16,128]{2,1,0:T(8,128)} %get-tuple-element.11), channel_id=1, source_target_pairs={{0,4},{1,5},{2,6},{3,7},{4,0},{5,1},{6,2},{7,3},{8,12},{9,13},{10,... | collective-permute-start | bytes 196616 | tf_op jit(solution)/shard_map/ppermute | solution.py:13
  28.7 2.7 %collective-permute-start.9 = (f32[8,16,128]{2,1,0:T(8,128)}, f32[8,16,128]{2,1,0:T(8,128)S(1)}, u32[]{:S(2)}, u32[]{:S(2)}) collective-permute-start(f32[8,16,128]{2,1,0:T(8,128)} %get-tuple-element.11), channel_id=1, source_target_pairs={{0,12},{1,13},{2,14},{3,15},{4,8},{5,9},{6,10},{7,11},{8,4},{9,5},... | collective-permute-start | bytes 196616 | tf_op jit(solution)/shard_map/ppermute | solution.py:13
  34.7 2.4 %constant_dynamic-update-slice_fusion.18 = (f32[16,128,128]{2,1,0:T(8,128)}, f32[1,128,128]{2,1,0:T(8,128)S(1)}) fusion(f32[128,128]{1,0:T(8,128)S(1)} %fusion.16, f32[512,128]{1,0:T(8,128)} %bitcast.53, f32[128,512]{0,1:T(8,128)} %collective-permute-done.2, f32[128,512]{0,1:T(8,128)} %collective-permute-done.1, f32[128,512]{0,1:T(8,128)S(1)} %collective-permute-done, ...), kind=kOutput, calls=%fused_computation.52 | convolution fusion | flops 100876288 | bytes 1507332 | tf_op jit(solution)/shard_map/wj,jr->wr/dot_general | solution.py:117
  37.1 1.7 %collective-permute-start.10 = (f32[1,128,128]{2,1,0:T(8,128)S(1)}, f32[1,128,128]{2,1,0:T(8,128)S(1)}, u32[]{:S(2)}, u32[]{:S(2)}) collective-permute-start(f32[1,128,128]{2,1,0:T(8,128)S(1)} %get-tuple-element.26), channel_id=1, source_target_pairs={{0,2},{1,3},{2,0},{3,1},{4,6},{5,7},{6,4},{7,5},{8,10},{9,11},{10,... | collective-permute-start | bytes 196616 | tf_op jit(solution)/shard_map/ppermute | solution.py:13
  39.5 1.9 %collective-permute-done.10 = f32[1,128,128]{2,1,0:T(8,128)S(1)} collective-permute-done((f32[1,128,128]{2,1,0:T(8,128)S(1)}, f32[1,128,128]{2,1,0:T(8,128)S(1)}, u32[]{:S(2)}, u32[]{:S(2)}) %collective-permute-start.10) | collective-permute-done | bytes 65568 | tf_op jit(solution)/shard_map/ppermute | solution.py:13
  41.4 2.9 %collective-permute-start.11 = (f32[2,128,128]{2,1,0:T(8,128)S(1)}, f32[2,128,128]{2,1,0:T(8,128)S(1)}, u32[]{:S(2)}, u32[]{:S(2)}) collective-permute-start(f32[2,128,128]{2,1,0:T(8,128)S(1)} %pad_maximum_fusion.1), channel_id=1, source_target_pairs={{0,16},{1,17},{2,18},{3,19},{4,20},{5,21},{6,22},{7,23},{8,24},{9,... | collective-permute-start | bytes 393224 | tf_op jit(solution)/shard_map/ppermute | solution.py:13
  44.3 3.5 %collective-permute-done.11 = f32[2,128,128]{2,1,0:T(8,128)S(1)} collective-permute-done((f32[2,128,128]{2,1,0:T(8,128)S(1)}, f32[2,128,128]{2,1,0:T(8,128)S(1)}, u32[]{:S(2)}, u32[]{:S(2)}) %collective-permute-start.11) | collective-permute-done | bytes 131104 | tf_op jit(solution)/shard_map/ppermute | solution.py:13
  47.8 2.0 %collective-permute-start.12 = (f32[4,128,128]{2,1,0:T(8,128)S(1)}, f32[4,128,128]{2,1,0:T(8,128)S(1)}, u32[]{:S(2)}, u32[]{:S(2)}) collective-permute-start(f32[4,128,128]{2,1,0:T(8,128)S(1)} %pad_maximum_fusion), channel_id=1, source_target_pairs={{0,8},{1,9},{2,10},{3,11},{4,12},{5,13},{6,14},{7,15},{8,0},{9,1},... | collective-permute-start | bytes 786440 | tf_op jit(solution)/shard_map/ppermute | solution.py:13
  53.6 2.2 %collective-permute-done.12 = f32[4,128,128]{2,1,0:T(8,128)S(1)} collective-permute-done((f32[4,128,128]{2,1,0:T(8,128)S(1)}, f32[4,128,128]{2,1,0:T(8,128)S(1)}, u32[]{:S(2)}, u32[]{:S(2)}) %collective-permute-start.12) | collective-permute-done | bytes 262176 | tf_op jit(solution)/shard_map/ppermute | solution.py:13
  56.5 2.1 %collective-permute-done.13 = f32[4,128,128]{2,1,0:T(8,128)S(1)} collective-permute-done((f32[4,128,128]{2,1,0:T(8,128)S(1)}, f32[4,128,128]{2,1,0:T(8,128)S(1)}, u32[]{:S(2)}, u32[]{:S(2)}) %collective-permute-start.13) | collective-permute-done | bytes 262176 | tf_op jit(solution)/shard_map/ppermute | solution.py:13
  60.6 1.8 %gather_fusion.1 = f32[16,128,128]{2,1,0:T(8,128)S(1)} fusion(f32[16,128,128]{2,1,0:T(8,128)} %constant_dynamic-update-slice_fusion.13, s32[1024]{0:T(1024)S(1)} %pad_clamp_fusion.1), kind=kCustom, calls=%fused_computation.1 | custom fusion | bytes 2097216 | tf_op jit(solution)/shard_map/gather | solution.py:129
  62.4 2.1 %fusion.2 = f32[8,256,128]{2,1,0:T(8,128)} fusion(f32[8,256,128]{2,1,0:T(8,128)S(1)} %bitcast.49, s32[256]{0:T(256)S(1)} %add_bitcast_fusion.1, s32[8,256]{1,0:T(8,128)S(1)} %copy-done.6), kind=kOutput, calls=%fused_computation.5 | convolution fusion | flops 805830656 | bytes 2106368 | tf_op jit(solution)/shard_map/skj,sjr->skr/dot_general | solution.py:133
  64.6 1.8 %gather_fusion.2 = f32[16,128,128]{2,1,0:T(8,128)S(1)} fusion(f32[16,128,128]{2,1,0:T(8,128)} %collective-permute-done.15, s32[1024]{0:T(1024)S(1)} %pad_clamp_fusion), kind=kCustom, calls=%fused_computation.2 | custom fusion | bytes 2097216 | tf_op jit(solution)/shard_map/gather | solution.py:129
  67.9 3.5 %fusion.4 = f32[8,256,128]{2,1,0:T(8,128)S(1)} fusion(f32[8,256,128]{2,1,0:T(8,128)S(1)} %copy-done.4, f32[8,256,256]{2,1,0:T(8,128)S(1)} %copy-done, f32[8,256,128]{2,1,0:T(8,128)S(1)} %copy-done.2, f32[8,256,128]{2,1,0:T(8,128)S(1)} %fusion), kind=kOutput, calls=%fused_computation.9 | convolution fusion | flops 805830656 | bytes 6291456 | tf_op jit(solution)/shard_map/swk,skr->swr/dot_general | solution.py:140
  71.5 2.0 %convolution_bitcast_fusion = f32[8,256,128]{1,2,0:T(8,128)S(1)} fusion(f32[8,256,128]{2,1,0:T(8,128)S(1)} %fusion.4, f32[8,256,256]{2,1,0:T(8,128)S(1)} %copy-done.3), kind=kOutput, calls=%fused_computation.7 | convolution fusion | flops 805306368 | bytes 4194304 | tf_op jit(solution)/shard_map/swk,skr->swr/dot_general | solution.py:141
  (86 shorter events, 20.7 us)
Async XLA Ops:
  0.6 67.0 %copy-start = (f32[8,256,256]{2,1,0:T(8,128)S(1)}, f32[8,256,256]{2,1,0:T(8,128)}, u32[]{:S(2)}) copy-start(f32[8,256,256]{2,1,0:T(8,128)} %param.21) | copy-start | bytes 6291460
  0.6 7.0 %copy-start.8 = (s32[1,256]{1,0:T(1,128)S(1)}, s32[1,256]{1,0:T(1,128)}, u32[]{:S(2)}) copy-start(s32[1,256]{1,0:T(1,128)} %param.16) | copy-start | bytes 3076
  0.7 17.8 %collective-permute-start.3 = (f32[1,16,128]{2,1,0:T(8,128)}, f32[1,16,128]{2,1,0:T(8,128)S(1)}, u32[]{:S(2)}, u32[]{:S(2)}) collective-permute-start(f32[1,16,128]{2,1,0:T(8,128)} %bitcast.57), channel_id=1, source_target_pairs={{0,1},{1,0},{2,3},{3,2},{4,5},{5,4},{6,7},{7,6},{8,9},{9,8},{10,11... | collective-permute-start | bytes 24584 | tf_op jit(solution)/shard_map/ppermute | solution.py:13
  1.2 17.4 %collective-permute-start.4 = (f32[1,16,128]{2,1,0:T(8,128)}, f32[1,16,128]{2,1,0:T(8,128)S(1)}, u32[]{:S(2)}, u32[]{:S(2)}) collective-permute-start(f32[1,16,128]{2,1,0:T(8,128)} %bitcast.58), channel_id=1, source_target_pairs={{0,2},{1,3},{2,0},{3,1},{4,6},{5,7},{6,4},{7,5},{8,10},{9,11},{10,... | collective-permute-start | bytes 24584 | tf_op jit(solution)/shard_map/ppermute | solution.py:13
  3.8 14.8 %collective-permute-start.5 = (f32[1,16,128]{2,1,0:T(8,128)}, f32[1,16,128]{2,1,0:T(8,128)S(1)}, u32[]{:S(2)}, u32[]{:S(2)}) collective-permute-start(f32[1,16,128]{2,1,0:T(8,128)} %bitcast.59), channel_id=1, source_target_pairs={{0,3},{1,2},{2,1},{3,0},{4,7},{5,6},{6,5},{7,4},{8,11},{9,10},{10,... | collective-permute-start | bytes 24584 | tf_op jit(solution)/shard_map/ppermute | solution.py:13
  7.7 7.9 %copy-start.7 = (f32[16,128]{1,0:T(8,128)S(1)}, f32[16,128]{1,0:T(8,128)}, u32[]{:S(2)}) copy-start(f32[16,128]{1,0:T(8,128)} %param.17) | copy-start | bytes 24580
  7.7 10.1 %copy-start.9 = (s32[2]{0:T(128)S(1)}, s32[2]{0:T(128)}, u32[]{:S(2)}) copy-start(s32[2]{0:T(128)} %constant.108.clone) | copy-start | bytes 28
  9.4 16.6 %copy-start.10 = (s32[8]{0:T(128)S(1)}, s32[8]{0:T(128)}, u32[]{:S(2)}) copy-start(s32[8]{0:T(128)} %param.19) | copy-start | bytes 100
  10.4 28.5 %copy-start.1 = (s32[8]{0:T(128)S(1)}, s32[8]{0:T(128)}, u32[]{:S(2)}) copy-start(s32[8]{0:T(128)} %param.18) | copy-start | bytes 100
  12.0 22.7 %collective-permute-start.2 = (f32[128,512]{0,1:T(8,128)}, f32[128,512]{0,1:T(8,128)}, u32[]{:S(2)}, u32[]{:S(2)}) collective-permute-start(f32[128,512]{0,1:T(8,128)} %bitcast.54), channel_id=1, source_target_pairs={{0,3},{1,2},{2,1},{3,0},{4,7},{5,6},{6,5},{7,4},{8,11},{9,10},{10,... | collective-permute-start | bytes 786440 | tf_op jit(solution)/shard_map/ppermute | solution.py:112
  15.4 19.3 %collective-permute-start.1 = (f32[128,512]{0,1:T(8,128)}, f32[128,512]{0,1:T(8,128)}, u32[]{:S(2)}, u32[]{:S(2)}) collective-permute-start(f32[128,512]{0,1:T(8,128)} %bitcast.55), channel_id=1, source_target_pairs={{0,2},{1,3},{2,0},{3,1},{4,6},{5,7},{6,4},{7,5},{8,10},{9,11},{10,... | collective-permute-start | bytes 786440 | tf_op jit(solution)/shard_map/ppermute | solution.py:112
  18.5 16.3 %collective-permute-start = (f32[128,512]{0,1:T(8,128)}, f32[128,512]{0,1:T(8,128)S(1)}, u32[]{:S(2)}, u32[]{:S(2)}) collective-permute-start(f32[128,512]{0,1:T(8,128)} %bitcast.56), channel_id=1, source_target_pairs={{0,1},{1,0},{2,3},{3,2},{4,5},{5,4},{6,7},{7,6},{8,9},{9,8},{10,11... | collective-permute-start | bytes 786440 | tf_op jit(solution)/shard_map/ppermute | solution.py:112
  18.6 5.0 %collective-permute-start.6 = (f32[4,16,128]{2,1,0:T(8,128)S(1)}, f32[4,16,128]{2,1,0:T(8,128)S(1)}, u32[]{:S(2)}, u32[]{:S(2)}) collective-permute-start(f32[4,16,128]{2,1,0:T(8,128)S(1)} %pad_maximum_fusion.2), channel_id=1, source_target_pairs={{0,16},{1,17},{2,18},{3,19},{4,20},{5,21},{6,22},{7,23},{8,24},{9,... | collective-permute-start | bytes 98312 | tf_op jit(solution)/shard_map/ppermute | solution.py:13
  24.2 4.5 %collective-permute-start.7 = (f32[8,16,128]{2,1,0:T(8,128)}, f32[8,16,128]{2,1,0:T(8,128)S(1)}, u32[]{:S(2)}, u32[]{:S(2)}) collective-permute-start(f32[8,16,128]{2,1,0:T(8,128)} %get-tuple-element.11), channel_id=1, source_target_pairs={{0,8},{1,9},{2,10},{3,11},{4,12},{5,13},{6,14},{7,15},{8,0},{9,1},... | collective-permute-start | bytes 196616 | tf_op jit(solution)/shard_map/ppermute | solution.py:13
  26.0 6.0 %collective-permute-start.8 = (f32[8,16,128]{2,1,0:T(8,128)}, f32[8,16,128]{2,1,0:T(8,128)S(1)}, u32[]{:S(2)}, u32[]{:S(2)}) collective-permute-start(f32[8,16,128]{2,1,0:T(8,128)} %get-tuple-element.11), channel_id=1, source_target_pairs={{0,4},{1,5},{2,6},{3,7},{4,0},{5,1},{6,2},{7,3},{8,12},{9,13},{10,... | collective-permute-start | bytes 196616 | tf_op jit(solution)/shard_map/ppermute | solution.py:13
  28.7 5.4 %collective-permute-start.9 = (f32[8,16,128]{2,1,0:T(8,128)}, f32[8,16,128]{2,1,0:T(8,128)S(1)}, u32[]{:S(2)}, u32[]{:S(2)}) collective-permute-start(f32[8,16,128]{2,1,0:T(8,128)} %get-tuple-element.11), channel_id=1, source_target_pairs={{0,12},{1,13},{2,14},{3,15},{4,8},{5,9},{6,10},{7,11},{8,4},{9,5},... | collective-permute-start | bytes 196616 | tf_op jit(solution)/shard_map/ppermute | solution.py:13
  37.1 25.3 %copy-start.5 = (f32[1,128,128]{2,1,0:T(8,128)}, f32[1,128,128]{2,1,0:T(8,128)S(1)}, u32[]{:S(2)}) copy-start(f32[1,128,128]{2,1,0:T(8,128)S(1)} %get-tuple-element.26) | copy-start | bytes 196612
  37.1 4.3 %collective-permute-start.10 = (f32[1,128,128]{2,1,0:T(8,128)S(1)}, f32[1,128,128]{2,1,0:T(8,128)S(1)}, u32[]{:S(2)}, u32[]{:S(2)}) collective-permute-start(f32[1,128,128]{2,1,0:T(8,128)S(1)} %get-tuple-element.26), channel_id=1, source_target_pairs={{0,2},{1,3},{2,0},{3,1},{4,6},{5,7},{6,4},{7,5},{8,10},{9,11},{10,... | collective-permute-start | bytes 196616 | tf_op jit(solution)/shard_map/ppermute | solution.py:13
  41.4 6.4 %collective-permute-start.11 = (f32[2,128,128]{2,1,0:T(8,128)S(1)}, f32[2,128,128]{2,1,0:T(8,128)S(1)}, u32[]{:S(2)}, u32[]{:S(2)}) collective-permute-start(f32[2,128,128]{2,1,0:T(8,128)S(1)} %pad_maximum_fusion.1), channel_id=1, source_target_pairs={{0,16},{1,17},{2,18},{3,19},{4,20},{5,21},{6,22},{7,23},{8,24},{9,... | collective-permute-start | bytes 393224 | tf_op jit(solution)/shard_map/ppermute | solution.py:13
  47.8 14.6 %copy-start.6 = (s32[8,256]{1,0:T(8,128)S(1)}, s32[8,256]{1,0:T(8,128)}, u32[]{:S(2)}) copy-start(s32[8,256]{1,0:T(8,128)} %param.20) | copy-start | bytes 24580
  47.8 8.0 %collective-permute-start.12 = (f32[4,128,128]{2,1,0:T(8,128)S(1)}, f32[4,128,128]{2,1,0:T(8,128)S(1)}, u32[]{:S(2)}, u32[]{:S(2)}) collective-permute-start(f32[4,128,128]{2,1,0:T(8,128)S(1)} %pad_maximum_fusion), channel_id=1, source_target_pairs={{0,8},{1,9},{2,10},{3,11},{4,12},{5,13},{6,14},{7,15},{8,0},{9,1},... | collective-permute-start | bytes 786440 | tf_op jit(solution)/shard_map/ppermute | solution.py:13
  50.1 8.6 %collective-permute-start.13 = (f32[4,128,128]{2,1,0:T(8,128)S(1)}, f32[4,128,128]{2,1,0:T(8,128)S(1)}, u32[]{:S(2)}, u32[]{:S(2)}) collective-permute-start(f32[4,128,128]{2,1,0:T(8,128)S(1)} %pad_maximum_fusion), channel_id=1, source_target_pairs={{0,4},{1,5},{2,6},{3,7},{4,0},{5,1},{6,2},{7,3},{8,12},{9,13},{10,... | collective-permute-start | bytes 786440 | tf_op jit(solution)/shard_map/ppermute | solution.py:13
  52.2 7.5 %collective-permute-start.14 = (f32[4,128,128]{2,1,0:T(8,128)S(1)}, f32[4,128,128]{2,1,0:T(8,128)S(1)}, u32[]{:S(2)}, u32[]{:S(2)}) collective-permute-start(f32[4,128,128]{2,1,0:T(8,128)S(1)} %pad_maximum_fusion), channel_id=1, source_target_pairs={{0,12},{1,13},{2,14},{3,15},{4,8},{5,9},{6,10},{7,11},{8,4},{9,5},... | collective-permute-start | bytes 786440 | tf_op jit(solution)/shard_map/ppermute | solution.py:13
  60.4 4.2 %collective-permute-start.15 = (f32[16,128,128]{2,1,0:T(8,128)}, f32[16,128,128]{2,1,0:T(8,128)}, u32[]{:S(2)}, u32[]{:S(2)}) collective-permute-start(f32[16,128,128]{2,1,0:T(8,128)} %constant_dynamic-update-slice_fusion.13), channel_id=1, source_target_pairs={{0,1},{1,0},{2,3},{3,2},{4,5},{5,4},{6,7},{7,6},{8,9},{9,8},{10,11... | collective-permute-start | bytes 3145736 | tf_op jit(solution)/shard_map/ppermute | solution.py:121
  (3 other events, 6.3 us)

commit v20 on v17

--- a/solution.py
+++ b/solution.py
@@ -133,6 +133,7 @@
             partner, term = lax.optimization_barrier((partner, term))
         parent_rows = term if parent_rows is None else parent_rows + term
 
+    parent_rows = lax.optimization_barrier(parent_rows)
     panel_t = jnp.swapaxes(lower_panel, 1, 2)
     inverse_t = jnp.swapaxes(lower_inverse, 1, 2)
     lower_update = jnp.einsum("swk,skr->swr", panel_t, parent_rows, precision=highest)

time: 69.5 us -> 73.8 us (1.062)
  local copies, waits for them, and re-layouts: 12.7 us -> 15.4 us
  matrix products: 16 us -> 17.4 us
    gather x2, local copies, waits for them, and re-layouts: 3.67 us -> 5.61 us  [local(): slabs = source[places].reshape(position.shape[0], -1, own_rows.shape[1])]
    dot_general x2, matrix products: 3.32 us -> 4.79 us  [local(): term = jnp.einsum('skj,sjr->skr', pick, slabs, precision=highest)]
    unnamed x39 -> x37, local copies, waits for them, and re-layouts: 5.27 us -> 6.04 us
where the time goes in v20:
time: 73.8 us; the launch traced here: 72.5 us
  starting transfers between devices  21.8 us (30%)
  matrix products  17.4 us (24%)
  waiting for transfers between devices  15.7 us (21%)
  local copies, waits for them, and re-layouts  15.4 us (21%)
  other arithmetic  1.27 us (2%)
  between operations  0.99 us (1%)
    ppermute x12, starting transfers between devices, xor_gather(): parts.append(lax.ppermute(held, axes, [(i, i ^ v) for i in range(count)]))  19.7 us
    ppermute x12, waiting for transfers between devices, xor_gather(): parts.append(lax.ppermute(held, axes, [(i, i ^ v) for i in range(count)]))  15.6 us
    unnamed x37, local copies, waits for them, and re-layouts  6.04 us
    gather x2, local copies, waits for them, and re-layouts, local(): slabs = source[places].reshape(position.shape[0], -1, own_rows.shape[1])  5.61 us
    dot_general x2, matrix products, local(): term = jnp.einsum('skj,sjr->skr', pick, slabs, precision=highest)  4.79 us
    dot_general x1, matrix products, local(): jnp.einsum('swk,skr->swr', panel_t, parent_rows, precision=highest)  3.51 us
    dot_general x1, matrix products, local(): jnp.einsum('kv,vw->kw', upper_panel[0], upper_inverse[0], precision=highest)  2.44 us
    dot_general x1, matrix products, local(): jnp.einsum('wj,jr->wr', total, top_held, precision=highest)  2.36 us
  transfers between devices with their start and end apart: 16, of which 7 were waited for; matrix products, arithmetic and copies ran while one was open for 23% of the time, Pallas kernels for 0%

profile of v20, /device:TPU:0, one launch (start us, length us, event | category | flops | bytes accessed | tf_op | source)
XLA Modules:
  0.0 72.5 jit_solution(1986733051385677120)
XLA Ops:
  1.2 2.6 %collective-permute-start.4 = (f32[1,16,128]{2,1,0:T(8,128)}, f32[1,16,128]{2,1,0:T(8,128)S(1)}, u32[]{:S(2)}, u32[]{:S(2)}) collective-permute-start(f32[1,16,128]{2,1,0:T(8,128)} %bitcast.65), channel_id=1, source_target_pairs={{0,2},{1,3},{2,0},{3,1},{4,6},{5,7},{6,4},{7,5},{8,10},{9,11},{10,... | collective-permute-start | bytes 24584 | tf_op jit(solution)/shard_map/ppermute | solution.py:13
  5.1 2.4 %fusion.6 = f32[256,512]{1,0:T(8,128)S(1)} fusion(f32[1,512,512]{2,1,0:T(8,128)} %param.18, f32[1,256,512]{2,1,0:T(8,128)} %param.17), kind=kOutput, calls=%fused_computation.15 | convolution fusion | flops 805306368 | bytes 2097152 | tf_op jit(solution)/shard_map/kv,vw->kw/dot_general | solution.py:102
  9.9 1.7 %collective-permute-start.2 = (f32[128,512]{0,1:T(8,128)S(1)}, f32[128,512]{0,1:T(8,128)}, u32[]{:S(2)}, u32[]{:S(2)}) collective-permute-start(f32[128,512]{0,1:T(8,128)S(1)} %bitcast.58), channel_id=1, source_target_pairs={{0,3},{1,2},{2,1},{3,0},{4,7},{5,6},{6,5},{7,4},{8,11},{9,10},{10,... | collective-permute-start | bytes 786440 | tf_op jit(solution)/shard_map/ppermute | solution.py:110
  13.2 3.0 %collective-permute-start.6 = (f32[4,16,128]{2,1,0:T(8,128)S(1)}, f32[4,16,128]{2,1,0:T(8,128)S(1)}, u32[]{:S(2)}, u32[]{:S(2)}) collective-permute-start(f32[4,16,128]{2,1,0:T(8,128)S(1)} %pad_maximum_fusion.2), channel_id=1, source_target_pairs={{0,16},{1,17},{2,18},{3,19},{4,20},{5,21},{6,22},{7,23},{8,24},{9,... | collective-permute-start | bytes 98312 | tf_op jit(solution)/shard_map/ppermute | solution.py:13
  16.2 2.0 %collective-permute-done.6 = f32[4,16,128]{2,1,0:T(8,128)S(1)} collective-permute-done((f32[4,16,128]{2,1,0:T(8,128)S(1)}, f32[4,16,128]{2,1,0:T(8,128)S(1)}, u32[]{:S(2)}, u32[]{:S(2)}) %collective-permute-start.6) | collective-permute-done | bytes 32800 | tf_op jit(solution)/shard_map/ppermute | solution.py:13
  18.2 1.8 %collective-permute-start.7 = (f32[8,16,128]{2,1,0:T(8,128)S(1)}, f32[8,16,128]{2,1,0:T(8,128)S(1)}, u32[]{:S(2)}, u32[]{:S(2)}) collective-permute-start(f32[8,16,128]{2,1,0:T(8,128)S(1)} %get-tuple-element.11), channel_id=1, source_target_pairs={{0,8},{1,9},{2,10},{3,11},{4,12},{5,13},{6,14},{7,15},{8,0},{9,1},... | collective-permute-start | bytes 196616 | tf_op jit(solution)/shard_map/ppermute | solution.py:13
  20.0 1.6 %fusion.15 = f32[128,128]{1,0:T(8,128)S(1)} fusion(f32[1,512,128]{2,1,0:T(8,128)} %param.16, f32[1,512,512]{2,1,0:T(8,128)} %param.18, s32[]{:T(128)S(6)} %select_n.96), kind=kOutput, calls=%fused_computation.25 | convolution fusion | flops 100663296 | bytes 589828 | tf_op jit(solution)/shard_map/kw,kr->wr/dot_general | solution.py:112
  21.6 1.6 %collective-permute-start.8 = (f32[8,16,128]{2,1,0:T(8,128)S(1)}, f32[8,16,128]{2,1,0:T(8,128)S(1)}, u32[]{:S(2)}, u32[]{:S(2)}) collective-permute-start(f32[8,16,128]{2,1,0:T(8,128)S(1)} %get-tuple-element.11), channel_id=1, source_target_pairs={{0,4},{1,5},{2,6},{3,7},{4,0},{5,1},{6,2},{7,3},{8,12},{9,13},{10,... | collective-permute-start | bytes 196616 | tf_op jit(solution)/shard_map/ppermute | solution.py:13
  23.2 2.0 %collective-permute-start.9 = (f32[8,16,128]{2,1,0:T(8,128)S(1)}, f32[8,16,128]{2,1,0:T(8,128)S(1)}, u32[]{:S(2)}, u32[]{:S(2)}) collective-permute-start(f32[8,16,128]{2,1,0:T(8,128)S(1)} %get-tuple-element.11), channel_id=1, source_target_pairs={{0,12},{1,13},{2,14},{3,15},{4,8},{5,9},{6,10},{7,11},{8,4},{9,5},... | collective-permute-start | bytes 196616 | tf_op jit(solution)/shard_map/ppermute | solution.py:13
  25.2 1.5 %collective-permute-done.8 = f32[8,16,128]{2,1,0:T(8,128)S(1)} collective-permute-done((f32[8,16,128]{2,1,0:T(8,128)S(1)}, f32[8,16,128]{2,1,0:T(8,128)S(1)}, u32[]{:S(2)}, u32[]{:S(2)}) %collective-permute-start.8) | collective-permute-done | bytes 65568 | tf_op jit(solution)/shard_map/ppermute | solution.py:13
  26.7 1.7 %collective-permute-done.9 = f32[8,16,128]{2,1,0:T(8,128)S(1)} collective-permute-done((f32[8,16,128]{2,1,0:T(8,128)S(1)}, f32[8,16,128]{2,1,0:T(8,128)S(1)}, u32[]{:S(2)}, u32[]{:S(2)}) %collective-permute-start.9) | collective-permute-done | bytes 65568 | tf_op jit(solution)/shard_map/ppermute | solution.py:13
  28.4 2.4 %constant_dynamic-update-slice_fusion.18 = (f32[16,128,128]{2,1,0:T(8,128)}, f32[1,128,128]{2,1,0:T(8,128)S(1)}) fusion(f32[128,128]{1,0:T(8,128)S(1)} %fusion.15, f32[512,128]{1,0:T(8,128)S(1)} %bitcast.63, f32[128,512]{0,1:T(8,128)} %collective-permute-done.2, f32[128,512]{0,1:T(8,128)} %collective-permute-done.1, ...), kind=kOutput, calls=%fused_computation.54 | convolution fusion | flops 100876288 | bytes 1507332 | tf_op jit(solution)/shard_map/wj,jr->wr/dot_general | solution.py:115
  30.8 1.5 %collective-permute-start.10 = (f32[1,128,128]{2,1,0:T(8,128)S(1)}, f32[1,128,128]{2,1,0:T(8,128)S(1)}, u32[]{:S(2)}, u32[]{:S(2)}) collective-permute-start(f32[1,128,128]{2,1,0:T(8,128)S(1)} %get-tuple-element.26), channel_id=1, source_target_pairs={{0,2},{1,3},{2,0},{3,1},{4,6},{5,7},{6,4},{7,5},{8,10},{9,11},{10,... | collective-permute-start | bytes 196616 | tf_op jit(solution)/shard_map/ppermute | solution.py:13
  32.9 2.1 %collective-permute-done.10 = f32[1,128,128]{2,1,0:T(8,128)S(1)} collective-permute-done((f32[1,128,128]{2,1,0:T(8,128)S(1)}, f32[1,128,128]{2,1,0:T(8,128)S(1)}, u32[]{:S(2)}, u32[]{:S(2)}) %collective-permute-start.10) | collective-permute-done | bytes 65568 | tf_op jit(solution)/shard_map/ppermute | solution.py:13
  35.0 3.1 %collective-permute-start.11 = (f32[2,128,128]{2,1,0:T(8,128)S(1)}, f32[2,128,128]{2,1,0:T(8,128)S(1)}, u32[]{:S(2)}, u32[]{:S(2)}) collective-permute-start(f32[2,128,128]{2,1,0:T(8,128)S(1)} %pad_maximum_fusion.1), channel_id=1, source_target_pairs={{0,16},{1,17},{2,18},{3,19},{4,20},{5,21},{6,22},{7,23},{8,24},{9,... | collective-permute-start | bytes 393224 | tf_op jit(solution)/shard_map/ppermute | solution.py:13
  38.1 4.5 %collective-permute-done.11 = f32[2,128,128]{2,1,0:T(8,128)S(1)} collective-permute-done((f32[2,128,128]{2,1,0:T(8,128)S(1)}, f32[2,128,128]{2,1,0:T(8,128)S(1)}, u32[]{:S(2)}, u32[]{:S(2)}) %collective-permute-start.11) | collective-permute-done | bytes 131104 | tf_op jit(solution)/shard_map/ppermute | solution.py:13
  45.0 2.0 %collective-permute-start.14 = (f32[4,128,128]{2,1,0:T(8,128)S(1)}, f32[4,128,128]{2,1,0:T(8,128)S(1)}, u32[]{:S(2)}, u32[]{:S(2)}) collective-permute-start(f32[4,128,128]{2,1,0:T(8,128)S(1)} %pad_maximum_fusion), channel_id=1, source_target_pairs={{0,12},{1,13},{2,14},{3,15},{4,8},{5,9},{6,10},{7,11},{8,4},{9,5},... | collective-permute-start | bytes 786440 | tf_op jit(solution)/shard_map/ppermute | solution.py:13
  47.7 2.9 %collective-permute-done.12 = f32[4,128,128]{2,1,0:T(8,128)S(1)} collective-permute-done((f32[4,128,128]{2,1,0:T(8,128)S(1)}, f32[4,128,128]{2,1,0:T(8,128)S(1)}, u32[]{:S(2)}, u32[]{:S(2)}) %collective-permute-start.12) | collective-permute-done | bytes 262176 | tf_op jit(solution)/shard_map/ppermute | solution.py:13
  54.0 2.8 %gather_fusion.4 = f32[16,128,128]{2,1,0:T(8,128)} fusion(f32[16,128,128]{2,1,0:T(8,128)} %constant_dynamic-update-slice_fusion.13, s32[1024]{0:T(1024)S(1)} %pad_clamp_fusion.1), kind=kCustom, calls=%fused_computation.4 | custom fusion | bytes 2097216 | tf_op jit(solution)/shard_map/gather | solution.py:127
  56.8 2.4 %fusion.2 = f32[8,256,128]{2,1,0:T(8,128)S(1)} fusion(f32[8,256,128]{2,1,0:T(8,128)} %bitcast.62, s32[256]{0:T(256)S(1)} %add_bitcast_fusion.1, s32[8,256]{1,0:T(8,128)S(1)} %copy-done.6), kind=kOutput, calls=%fused_computation.8 | convolution fusion | flops 805830656 | bytes 2106368 | tf_op jit(solution)/shard_map/skj,sjr->skr/dot_general | solution.py:131
  59.2 2.8 %gather_fusion.5 = f32[16,128,128]{2,1,0:T(8,128)} fusion(f32[16,128,128]{2,1,0:T(8,128)} %collective-permute-done.15, s32[1024]{0:T(1024)S(1)} %pad_clamp_fusion), kind=kCustom, calls=%fused_computation.5 | custom fusion | bytes 2097216 | tf_op jit(solution)/shard_map/gather | solution.py:127
  62.0 2.4 %fusion = f32[8,256,128]{2,1,0:T(8,128)S(1)} fusion(f32[8,256,128]{2,1,0:T(8,128)} %bitcast.61, s32[256]{0:T(256)S(1)} %add_bitcast_fusion, s32[8,256]{1,0:T(8,128)S(1)} %copy-done.6), kind=kOutput, calls=%fused_computation.6 | convolution fusion | flops 805830656 | bytes 2106368 | tf_op jit(solution)/shard_map/skj,sjr->skr/dot_general | solution.py:131
  65.6 3.5 %fusion.4 = f32[8,256,128]{2,1,0:T(8,128)S(1)} fusion(f32[8,256,128]{2,1,0:T(8,128)S(1)} %copy-done.4, f32[8,256,128]{2,1,0:T(8,128)S(1)} %add.287, f32[8,256,256]{2,1,0:T(8,128)S(1)} %copy-done), kind=kOutput, calls=%fused_computation.12 | convolution fusion | flops 805568512 | bytes 5242880 | tf_op jit(solution)/shard_map/swk,skr->swr/dot_general | solution.py:139
  69.2 2.0 %convolution_bitcast_fusion = f32[8,256,128]{1,2,0:T(8,128)S(1)} fusion(f32[8,256,128]{2,1,0:T(8,128)S(1)} %fusion.4, f32[8,256,256]{2,1,0:T(8,128)S(1)} %copy-done.3), kind=kOutput, calls=%fused_computation.10 | convolution fusion | flops 805306368 | bytes 4194304 | tf_op jit(solution)/shard_map/swk,skr->swr/dot_general | solution.py:140
  (92 shorter events, 15.2 us)
Async XLA Ops:
  0.6 63.9 %copy-start = (f32[8,256,256]{2,1,0:T(8,128)S(1)}, f32[8,256,256]{2,1,0:T(8,128)}, u32[]{:S(2)}) copy-start(f32[8,256,256]{2,1,0:T(8,128)} %param.24) | copy-start | bytes 6291460
  0.6 6.9 %copy-start.12 = (s32[32]{0:T(128)S(1)}, s32[32]{0:T(128)}, u32[]{:S(2)}) copy-start(s32[32]{0:T(128)} %constant.145) | copy-start | bytes 388
  0.7 6.9 %copy-start.8 = (s32[1,256]{1,0:T(1,128)S(1)}, s32[1,256]{1,0:T(1,128)}, u32[]{:S(2)}) copy-start(s32[1,256]{1,0:T(1,128)} %param.19) | copy-start | bytes 3076
  0.7 12.4 %collective-permute-start.3 = (f32[1,16,128]{2,1,0:T(8,128)}, f32[1,16,128]{2,1,0:T(8,128)S(1)}, u32[]{:S(2)}, u32[]{:S(2)}) collective-permute-start(f32[1,16,128]{2,1,0:T(8,128)} %bitcast.64), channel_id=1, source_target_pairs={{0,1},{1,0},{2,3},{3,2},{4,5},{5,4},{6,7},{7,6},{8,9},{9,8},{10,11... | collective-permute-start | bytes 24584 | tf_op jit(solution)/shard_map/ppermute | solution.py:13
  1.2 12.0 %collective-permute-start.4 = (f32[1,16,128]{2,1,0:T(8,128)}, f32[1,16,128]{2,1,0:T(8,128)S(1)}, u32[]{:S(2)}, u32[]{:S(2)}) collective-permute-start(f32[1,16,128]{2,1,0:T(8,128)} %bitcast.65), channel_id=1, source_target_pairs={{0,2},{1,3},{2,0},{3,1},{4,6},{5,7},{6,4},{7,5},{8,10},{9,11},{10,... | collective-permute-start | bytes 24584 | tf_op jit(solution)/shard_map/ppermute | solution.py:13
  3.8 9.4 %collective-permute-start.5 = (f32[1,16,128]{2,1,0:T(8,128)}, f32[1,16,128]{2,1,0:T(8,128)S(1)}, u32[]{:S(2)}, u32[]{:S(2)}) collective-permute-start(f32[1,16,128]{2,1,0:T(8,128)} %bitcast.66), channel_id=1, source_target_pairs={{0,3},{1,2},{2,1},{3,0},{4,7},{5,6},{6,5},{7,4},{8,11},{9,10},{10,... | collective-permute-start | bytes 24584 | tf_op jit(solution)/shard_map/ppermute | solution.py:13
  9.9 18.5 %collective-permute-start.2 = (f32[128,512]{0,1:T(8,128)S(1)}, f32[128,512]{0,1:T(8,128)}, u32[]{:S(2)}, u32[]{:S(2)}) collective-permute-start(f32[128,512]{0,1:T(8,128)S(1)} %bitcast.58), channel_id=1, source_target_pairs={{0,3},{1,2},{2,1},{3,0},{4,7},{5,6},{6,5},{7,4},{8,11},{9,10},{10,... | collective-permute-start | bytes 786440 | tf_op jit(solution)/shard_map/ppermute | solution.py:110
  12.2 16.1 %collective-permute-start.1 = (f32[128,512]{0,1:T(8,128)S(1)}, f32[128,512]{0,1:T(8,128)}, u32[]{:S(2)}, u32[]{:S(2)}) collective-permute-start(f32[128,512]{0,1:T(8,128)S(1)} %bitcast.59), channel_id=1, source_target_pairs={{0,2},{1,3},{2,0},{3,1},{4,6},{5,7},{6,4},{7,5},{8,10},{9,11},{10,... | collective-permute-start | bytes 786440 | tf_op jit(solution)/shard_map/ppermute | solution.py:110
  13.0 19.3 %copy-start.9 = (s32[2]{0:T(128)S(1)}, s32[2]{0:T(128)}, u32[]{:S(2)}) copy-start(s32[2]{0:T(128)} %constant.120.clone) | copy-start | bytes 28
  13.0 19.3 %copy-start.1 = (s32[8]{0:T(128)S(1)}, s32[8]{0:T(128)}, u32[]{:S(2)}) copy-start(s32[8]{0:T(128)} %param.21) | copy-start | bytes 100
  13.0 15.3 %collective-permute-start = (f32[128,512]{0,1:T(8,128)S(1)}, f32[128,512]{0,1:T(8,128)S(1)}, u32[]{:S(2)}, u32[]{:S(2)}) collective-permute-start(f32[128,512]{0,1:T(8,128)S(1)} %bitcast.60), channel_id=1, source_target_pairs={{0,1},{1,0},{2,3},{3,2},{4,5},{5,4},{6,7},{7,6},{8,9},{9,8},{10,11... | collective-permute-start | bytes 786440 | tf_op jit(solution)/shard_map/ppermute | solution.py:110
  13.2 5.0 %collective-permute-start.6 = (f32[4,16,128]{2,1,0:T(8,128)S(1)}, f32[4,16,128]{2,1,0:T(8,128)S(1)}, u32[]{:S(2)}, u32[]{:S(2)}) collective-permute-start(f32[4,16,128]{2,1,0:T(8,128)S(1)} %pad_maximum_fusion.2), channel_id=1, source_target_pairs={{0,16},{1,17},{2,18},{3,19},{4,20},{5,21},{6,22},{7,23},{8,24},{9,... | collective-permute-start | bytes 98312 | tf_op jit(solution)/shard_map/ppermute | solution.py:13
  18.2 5.0 %collective-permute-start.7 = (f32[8,16,128]{2,1,0:T(8,128)S(1)}, f32[8,16,128]{2,1,0:T(8,128)S(1)}, u32[]{:S(2)}, u32[]{:S(2)}) collective-permute-start(f32[8,16,128]{2,1,0:T(8,128)S(1)} %get-tuple-element.11), channel_id=1, source_target_pairs={{0,8},{1,9},{2,10},{3,11},{4,12},{5,13},{6,14},{7,15},{8,0},{9,1},... | collective-permute-start | bytes 196616 | tf_op jit(solution)/shard_map/ppermute | solution.py:13
  21.6 5.0 %collective-permute-start.8 = (f32[8,16,128]{2,1,0:T(8,128)S(1)}, f32[8,16,128]{2,1,0:T(8,128)S(1)}, u32[]{:S(2)}, u32[]{:S(2)}) collective-permute-start(f32[8,16,128]{2,1,0:T(8,128)S(1)} %get-tuple-element.11), channel_id=1, source_target_pairs={{0,4},{1,5},{2,6},{3,7},{4,0},{5,1},{6,2},{7,3},{8,12},{9,13},{10,... | collective-permute-start | bytes 196616 | tf_op jit(solution)/shard_map/ppermute | solution.py:13
  23.2 5.2 %collective-permute-start.9 = (f32[8,16,128]{2,1,0:T(8,128)S(1)}, f32[8,16,128]{2,1,0:T(8,128)S(1)}, u32[]{:S(2)}, u32[]{:S(2)}) collective-permute-start(f32[8,16,128]{2,1,0:T(8,128)S(1)} %get-tuple-element.11), channel_id=1, source_target_pairs={{0,12},{1,13},{2,14},{3,15},{4,8},{5,9},{6,10},{7,11},{8,4},{9,5},... | collective-permute-start | bytes 196616 | tf_op jit(solution)/shard_map/ppermute | solution.py:13
  30.8 26.0 %copy-start.5 = (f32[1,128,128]{2,1,0:T(8,128)}, f32[1,128,128]{2,1,0:T(8,128)S(1)}, u32[]{:S(2)}) copy-start(f32[1,128,128]{2,1,0:T(8,128)S(1)} %get-tuple-element.26) | copy-start | bytes 196612
  30.8 4.3 %collective-permute-start.10 = (f32[1,128,128]{2,1,0:T(8,128)S(1)}, f32[1,128,128]{2,1,0:T(8,128)S(1)}, u32[]{:S(2)}, u32[]{:S(2)}) collective-permute-start(f32[1,128,128]{2,1,0:T(8,128)S(1)} %get-tuple-element.26), channel_id=1, source_target_pairs={{0,2},{1,3},{2,0},{3,1},{4,6},{5,7},{6,4},{7,5},{8,10},{9,11},{10,... | collective-permute-start | bytes 196616 | tf_op jit(solution)/shard_map/ppermute | solution.py:13
  35.0 7.6 %collective-permute-start.11 = (f32[2,128,128]{2,1,0:T(8,128)S(1)}, f32[2,128,128]{2,1,0:T(8,128)S(1)}, u32[]{:S(2)}, u32[]{:S(2)}) collective-permute-start(f32[2,128,128]{2,1,0:T(8,128)S(1)} %pad_maximum_fusion.1), channel_id=1, source_target_pairs={{0,16},{1,17},{2,18},{3,19},{4,20},{5,21},{6,22},{7,23},{8,24},{9,... | collective-permute-start | bytes 393224 | tf_op jit(solution)/shard_map/ppermute | solution.py:13
  42.6 14.2 %copy-start.6 = (s32[8,256]{1,0:T(8,128)S(1)}, s32[8,256]{1,0:T(8,128)}, u32[]{:S(2)}) copy-start(s32[8,256]{1,0:T(8,128)} %param.23) | copy-start | bytes 24580
  42.6 8.0 %collective-permute-start.12 = (f32[4,128,128]{2,1,0:T(8,128)S(1)}, f32[4,128,128]{2,1,0:T(8,128)S(1)}, u32[]{:S(2)}, u32[]{:S(2)}) collective-permute-start(f32[4,128,128]{2,1,0:T(8,128)S(1)} %pad_maximum_fusion), channel_id=1, source_target_pairs={{0,8},{1,9},{2,10},{3,11},{4,12},{5,13},{6,14},{7,15},{8,0},{9,1},... | collective-permute-start | bytes 786440 | tf_op jit(solution)/shard_map/ppermute | solution.py:13
  43.1 8.3 %collective-permute-start.13 = (f32[4,128,128]{2,1,0:T(8,128)S(1)}, f32[4,128,128]{2,1,0:T(8,128)S(1)}, u32[]{:S(2)}, u32[]{:S(2)}) collective-permute-start(f32[4,128,128]{2,1,0:T(8,128)S(1)} %pad_maximum_fusion), channel_id=1, source_target_pairs={{0,4},{1,5},{2,6},{3,7},{4,0},{5,1},{6,2},{7,3},{8,12},{9,13},{10,... | collective-permute-start | bytes 786440 | tf_op jit(solution)/shard_map/ppermute | solution.py:13
  45.0 8.0 %collective-permute-start.14 = (f32[4,128,128]{2,1,0:T(8,128)S(1)}, f32[4,128,128]{2,1,0:T(8,128)S(1)}, u32[]{:S(2)}, u32[]{:S(2)}) collective-permute-start(f32[4,128,128]{2,1,0:T(8,128)S(1)} %pad_maximum_fusion), channel_id=1, source_target_pairs={{0,12},{1,13},{2,14},{3,15},{4,8},{5,9},{6,10},{7,11},{8,4},{9,5},... | collective-permute-start | bytes 786440 | tf_op jit(solution)/shard_map/ppermute | solution.py:13
  53.8 5.4 %collective-permute-start.15 = (f32[16,128,128]{2,1,0:T(8,128)}, f32[16,128,128]{2,1,0:T(8,128)}, u32[]{:S(2)}, u32[]{:S(2)}) collective-permute-start(f32[16,128,128]{2,1,0:T(8,128)} %constant_dynamic-update-slice_fusion.13), channel_id=1, source_target_pairs={{0,1},{1,0},{2,3},{3,2},{4,5},{5,4},{6,7},{7,6},{8,9},{9,8},{10,11... | collective-permute-start | bytes 3145736 | tf_op jit(solution)/shard_map/ppermute | solution.py:119
  65.6 3.5 %copy-start.3 = (f32[8,256,256]{2,1,0:T(8,128)S(1)}, f32[8,256,256]{2,1,0:T(8,128)}, u32[]{:S(2)}) copy-start(f32[8,256,256]{2,1,0:T(8,128)} %param.26) | copy-start | bytes 6291460
  (5 other events, 7.7 us)

commit v21 on v17

--- a/solution.py
+++ b/solution.py
@@ -13,6 +13,14 @@
             parts.append(lax.ppermute(held, axes, [(i, i ^ v) for i in range(count)]))
         held = jnp.concatenate(parts, 0)
     return held
+
+
+def xor_gather_step(held, axes, count, bits):
+    parts = [held]
+    for k in range(1, 1 << len(bits)):
+        v = sum(((k >> t) & 1) << b for t, b in enumerate(bits))
+        parts.append(lax.ppermute(held, axes, [(i, i ^ v) for i in range(count)]))
+    return jnp.concatenate(parts, 0)
 
 
 def xor_position(offset, groups):
@@ -102,6 +110,8 @@
     folded = jnp.einsum("kv,vw->kw", upper_panel[0], upper_inverse[0], precision=highest)
     weights = jnp.einsum("kj,kw->wj", pick_top, folded, precision=highest)
     total = lax.dynamic_slice_in_dim(weights, begin, share, 0)
+    top_first = xor_gather_step(top_solution[None], both, count, top_groups[0])
+    top_first, weights = lax.optimization_barrier((top_first, weights))
     for v in range(1, panels):
         outgoing = lax.dynamic_slice_in_dim(weights, (panel_index ^ v) * share, share, 0)
         order = [static_position(static_offset(h, top_groups) ^ v, top_groups) for h in range(count)]
@@ -111,7 +121,10 @@
     own_inverse = lax.dynamic_slice_in_dim(upper_inverse[0], begin, share, 1)
     own_base = jnp.einsum("kw,kr->wr", own_inverse, upper_rhs[0], precision=highest)
 
-    top_held = xor_gather(top_solution, both, count, top_groups).reshape(count * top_rows, rhs)
+    top_held = top_first
+    for bits in top_groups[1:]:
+        top_held = xor_gather_step(top_held, both, count, bits)
+    top_held = top_held.reshape(count * top_rows, rhs)
     own_rows = own_base - jnp.einsum("wj,jr->wr", total, top_held, precision=highest)
 
     held = xor_gather(own_rows, both, count, spread_groups[:-1])

time: 69.5 us -> 78.3 us (1.13); the launches traced: 68.2 us -> 77.9 us
  waiting for transfers between devices: 15.7 us -> 25.2 us
  local copies, waits for them, and re-layouts: 12.7 us -> 16.4 us
  starting transfers between devices: 21.8 us -> 18.3 us
    ppermute x12 -> x5, starting transfers between devices: 19.7 us -> 6.44 us  [xor_gather(): parts.append(lax.ppermute(held, axes, [(i, i ^ v) for i in range(count)]))]
    ppermute x0 -> x7, starting transfers between devices: none -> 9.98 us  [xor_gather_step(): parts.append(lax.ppermute(held, axes, [(i, i ^ v) for i in range(count)]))]
    ppermute x0 -> x7, waiting for transfers between devices: none -> 6.08 us  [xor_gather_step(): parts.append(lax.ppermute(held, axes, [(i, i ^ v) for i in range(count)]))]
    ppermute x3, waiting for transfers between devices: 0.01 us -> 3.06 us  [local(): lax.ppermute(outgoing, 'panel', [(i, i ^ v) for i in range(panels)])]
    dynamic_slice x1 -> x4, local copies, waits for them, and re-layouts: 0.11 us -> 2.19 us  [local(): lax.dynamic_slice_in_dim(weights, (panel_index ^ v) * share, share, 0)]
    reshape x0 -> x3, local copies, waits for them, and re-layouts: none -> 1.09 us  [local(): outgoing = outgoing.reshape(share, count * top_rows)]
    ppermute x12 -> x5, waiting for transfers between devices: 15.6 us -> 16 us  [xor_gather(): parts.append(lax.ppermute(held, axes, [(i, i ^ v) for i in range(count)]))]
    unnamed x39 -> x42, local copies, waits for them, and re-layouts: 5.27 us -> 5.19 us
  transfers between devices with their start and end apart: 16 -> 16, of which waited for: 7 -> 8; matrix products, arithmetic and copies ran while one was open for 23% -> 25% of each run, Pallas kernels for 0% -> 0%
where the time goes in v21:
time: 78.3 us; the launch traced here: 77.9 us
  waiting for transfers between devices  25.2 us (32%)
  starting transfers between devices  18.3 us (23%)
  local copies, waits for them, and re-layouts  16.4 us (21%)
  matrix products  15.7 us (20%)
  other arithmetic  1.16 us (1%)
  between operations  1.12 us (1%)
    ppermute x5, waiting for transfers between devices, xor_gather(): parts.append(lax.ppermute(held, axes, [(i, i ^ v) for i in range(count)]))  16 us
    ppermute x7, starting transfers between devices, xor_gather_step(): parts.append(lax.ppermute(held, axes, [(i, i ^ v) for i in range(count)]))  9.98 us
    ppermute x5, starting transfers between devices, xor_gather(): parts.append(lax.ppermute(held, axes, [(i, i ^ v) for i in range(count)]))  6.44 us
    ppermute x7, waiting for transfers between devices, xor_gather_step(): parts.append(lax.ppermute(held, axes, [(i, i ^ v) for i in range(count)]))  6.08 us
    unnamed x42, local copies, waits for them, and re-layouts  5.19 us
    gather x2, local copies, waits for them, and re-layouts, local(): slabs = source[places].reshape(position.shape[0], -1, own_rows.shape[1])  3.67 us
    dot_general x1, matrix products, local(): jnp.einsum('swk,skr->swr', panel_t, parent_rows, precision=highest)  3.54 us
    dot_general x2, matrix products, local(): term = jnp.einsum('skj,sjr->skr', pick, slabs, precision=highest)  3.32 us
  transfers between devices with their start and end apart: 16, of which 8 were waited for; matrix products, arithmetic and copies ran while one was open for 25% of the time, Pallas kernels for 0%

profile of v21, /device:TPU:0, one launch (start us, length us, event | category | flops | bytes accessed | tf_op | source)
XLA Modules:
  0.0 77.9 jit_solution(13569330850974085358)
XLA Ops:
  0.7 2.5 %collective-permute-start.2 = (f32[1,16,128]{2,1,0:T(8,128)}, f32[1,16,128]{2,1,0:T(8,128)S(1)}, u32[]{:S(2)}, u32[]{:S(2)}) collective-permute-start(f32[1,16,128]{2,1,0:T(8,128)} %bitcast.61), channel_id=1, source_target_pairs={{0,3},{1,2},{2,1},{3,0},{4,7},{5,6},{6,5},{7,4},{8,11},{9,10},{10,... | collective-permute-start | bytes 24584 | tf_op jit(solution)/shard_map/ppermute | solution.py:22
  5.0 2.5 %fusion.6 = f32[256,512]{1,0:T(8,128)S(1)} fusion(f32[1,512,512]{2,1,0:T(8,128)} %param.18, f32[1,256,512]{2,1,0:T(8,128)} %param.17), kind=kOutput, calls=%fused_computation.15 | convolution fusion | flops 805306368 | bytes 2097152 | tf_op jit(solution)/shard_map/kv,vw->kw/dot_general | solution.py:110
  7.5 1.5 %fusion.16 = f32[128,128]{1,0:T(8,128)S(1)} fusion(f32[1,512,128]{2,1,0:T(8,128)S(1)} %copy-done.9, f32[1,512,512]{2,1,0:T(8,128)} %param.18, s32[]{:T(128)S(6)} %select_n.96), kind=kOutput, calls=%fused_computation.26 | convolution fusion | flops 100663296 | bytes 589828 | tf_op jit(solution)/shard_map/kw,kr->wr/dot_general | solution.py:122
  10.0 2.9 %collective-permute-start.6 = (f32[4,16,128]{2,1,0:T(8,128)S(1)}, f32[4,16,128]{2,1,0:T(8,128)S(1)}, u32[]{:S(2)}, u32[]{:S(2)}) collective-permute-start(f32[4,16,128]{2,1,0:T(8,128)S(1)} %pad_maximum_fusion.2), channel_id=1, source_target_pairs={{0,16},{1,17},{2,18},{3,19},{4,20},{5,21},{6,22},{7,23},{8,24},{9,... | collective-permute-start | bytes 98312 | tf_op jit(solution)/shard_map/ppermute | solution.py:22
  13.5 1.4 %collective-permute-done.6 = f32[4,16,128]{2,1,0:T(8,128)S(1)} collective-permute-done((f32[4,16,128]{2,1,0:T(8,128)S(1)}, f32[4,16,128]{2,1,0:T(8,128)S(1)}, u32[]{:S(2)}, u32[]{:S(2)}) %collective-permute-start.6) | collective-permute-done | bytes 32800 | tf_op jit(solution)/shard_map/ppermute | solution.py:22
  15.5 1.8 %collective-permute-start.7 = (f32[8,16,128]{2,1,0:T(8,128)}, f32[8,16,128]{2,1,0:T(8,128)S(1)}, u32[]{:S(2)}, u32[]{:S(2)}) collective-permute-start(f32[8,16,128]{2,1,0:T(8,128)} %get-tuple-element.15), channel_id=1, source_target_pairs={{0,8},{1,9},{2,10},{3,11},{4,12},{5,13},{6,14},{7,15},{8,0},{9,1},... | collective-permute-start | bytes 196616 | tf_op jit(solution)/shard_map/ppermute | solution.py:22
  21.7 1.5 %collective-permute-start.4 = (f32[128,512]{1,0:T(8,128)}, f32[128,512]{1,0:T(8,128)}, u32[]{:S(2)}, u32[]{:S(2)}) collective-permute-start(f32[128,512]{1,0:T(8,128)} %copy.23), channel_id=1, source_target_pairs={{0,2},{1,3},{2,0},{3,1},{4,6},{5,7},{6,4},{7,5},{8,10},{9,11},{10,... | collective-permute-start | bytes 786440 | tf_op jit(solution)/shard_map/ppermute | solution.py:120
  24.4 1.5 %collective-permute-start.8 = (f32[8,16,128]{2,1,0:T(8,128)}, f32[8,16,128]{2,1,0:T(8,128)S(1)}, u32[]{:S(2)}, u32[]{:S(2)}) collective-permute-start(f32[8,16,128]{2,1,0:T(8,128)} %get-tuple-element.15), channel_id=1, source_target_pairs={{0,4},{1,5},{2,6},{3,7},{4,0},{5,1},{6,2},{7,3},{8,12},{9,13},{10,... | collective-permute-start | bytes 196616 | tf_op jit(solution)/shard_map/ppermute | solution.py:22
  26.6 2.4 %collective-permute-done.8 = f32[8,16,128]{2,1,0:T(8,128)S(1)} collective-permute-done((f32[8,16,128]{2,1,0:T(8,128)}, f32[8,16,128]{2,1,0:T(8,128)S(1)}, u32[]{:S(2)}, u32[]{:S(2)}) %collective-permute-start.8) | collective-permute-done | bytes 65568 | tf_op jit(solution)/shard_map/ppermute | solution.py:22
  28.9 2.3 %collective-permute-done.9 = f32[8,16,128]{2,1,0:T(8,128)S(1)} collective-permute-done((f32[8,16,128]{2,1,0:T(8,128)}, f32[8,16,128]{2,1,0:T(8,128)S(1)}, u32[]{:S(2)}, u32[]{:S(2)}) %collective-permute-start.9) | collective-permute-done | bytes 65568 | tf_op jit(solution)/shard_map/ppermute | solution.py:22
  31.3 3.1 %collective-permute-done.4 = f32[128,512]{1,0:T(8,128)} collective-permute-done((f32[128,512]{1,0:T(8,128)}, f32[128,512]{1,0:T(8,128)}, u32[]{:S(2)}, u32[]{:S(2)}) %collective-permute-start.4) | collective-permute-done | bytes 262176 | tf_op jit(solution)/shard_map/ppermute | solution.py:120
  34.4 2.2 %constant_dynamic-update-slice_fusion.12 = (f32[16,128,128]{2,1,0:T(8,128)}, f32[1,128,128]{2,1,0:T(8,128)S(1)}) fusion(f32[128,128]{1,0:T(8,128)S(1)} %fusion.16, f32[512,128]{1,0:T(8,128)S(1)} %bitcast.60, f32[128,512]{1,0:T(8,128)} %collective-permute-done.5, f32[128,512]{1,0:T(8,128)} %collective-permute-done.4, ...), kind=kOutput, calls=%fused_computation.50 | convolution fusion | flops 100876288 | bytes 1507332 | tf_op jit(solution)/shard_map/wj,jr->wr/dot_general | solution.py:128
  37.2 3.6 %collective-permute-done.10 = f32[1,128,128]{2,1,0:T(8,128)S(1)} collective-permute-done((f32[1,128,128]{2,1,0:T(8,128)S(1)}, f32[1,128,128]{2,1,0:T(8,128)S(1)}, u32[]{:S(2)}, u32[]{:S(2)}) %collective-permute-start.10) | collective-permute-done | bytes 65568 | tf_op jit(solution)/shard_map/ppermute | solution.py:13
  40.8 2.9 %collective-permute-start.11 = (f32[2,128,128]{2,1,0:T(8,128)S(1)}, f32[2,128,128]{2,1,0:T(8,128)S(1)}, u32[]{:S(2)}, u32[]{:S(2)}) collective-permute-start(f32[2,128,128]{2,1,0:T(8,128)S(1)} %pad_maximum_fusion.1), channel_id=1, source_target_pairs={{0,16},{1,17},{2,18},{3,19},{4,20},{5,21},{6,22},{7,23},{8,24},{9,... | collective-permute-start | bytes 393224 | tf_op jit(solution)/shard_map/ppermute | solution.py:13
  43.7 5.0 %collective-permute-done.11 = f32[2,128,128]{2,1,0:T(8,128)S(1)} collective-permute-done((f32[2,128,128]{2,1,0:T(8,128)S(1)}, f32[2,128,128]{2,1,0:T(8,128)S(1)}, u32[]{:S(2)}, u32[]{:S(2)}) %collective-permute-start.11) | collective-permute-done | bytes 131104 | tf_op jit(solution)/shard_map/ppermute | solution.py:13
  49.0 1.5 %collective-permute-start.13 = (f32[4,128,128]{2,1,0:T(8,128)S(1)}, f32[4,128,128]{2,1,0:T(8,128)S(1)}, u32[]{:S(2)}, u32[]{:S(2)}) collective-permute-start(f32[4,128,128]{2,1,0:T(8,128)S(1)} %pad_maximum_fusion), channel_id=1, source_target_pairs={{0,4},{1,5},{2,6},{3,7},{4,0},{5,1},{6,2},{7,3},{8,12},{9,13},{10,... | collective-permute-start | bytes 786440 | tf_op jit(solution)/shard_map/ppermute | solution.py:13
  51.1 2.0 %collective-permute-start.14 = (f32[4,128,128]{2,1,0:T(8,128)S(1)}, f32[4,128,128]{2,1,0:T(8,128)S(1)}, u32[]{:S(2)}, u32[]{:S(2)}) collective-permute-start(f32[4,128,128]{2,1,0:T(8,128)S(1)} %pad_maximum_fusion), channel_id=1, source_target_pairs={{0,12},{1,13},{2,14},{3,15},{4,8},{5,9},{6,10},{7,11},{8,4},{9,5},... | collective-permute-start | bytes 786440 | tf_op jit(solution)/shard_map/ppermute | solution.py:13
  53.8 4.2 %collective-permute-done.12 = f32[4,128,128]{2,1,0:T(8,128)S(1)} collective-permute-done((f32[4,128,128]{2,1,0:T(8,128)S(1)}, f32[4,128,128]{2,1,0:T(8,128)S(1)}, u32[]{:S(2)}, u32[]{:S(2)}) %collective-permute-start.12) | collective-permute-done | bytes 262176 | tf_op jit(solution)/shard_map/ppermute | solution.py:13
  59.5 3.3 %collective-permute-done.14 = f32[4,128,128]{2,1,0:T(8,128)S(1)} collective-permute-done((f32[4,128,128]{2,1,0:T(8,128)S(1)}, f32[4,128,128]{2,1,0:T(8,128)S(1)}, u32[]{:S(2)}, u32[]{:S(2)}) %collective-permute-start.14) | collective-permute-done | bytes 262176 | tf_op jit(solution)/shard_map/ppermute | solution.py:13
  63.6 1.8 %gather_fusion.4 = f32[16,128,128]{2,1,0:T(8,128)S(1)} fusion(f32[16,128,128]{2,1,0:T(8,128)} %constant_dynamic-update-slice_fusion.7, s32[1024]{0:T(1024)S(1)} %pad_clamp_fusion.1), kind=kCustom, calls=%fused_computation.4 | custom fusion | bytes 2097216 | tf_op jit(solution)/shard_map/gather | solution.py:140
  65.5 2.1 %fusion.2 = f32[8,256,128]{2,1,0:T(8,128)} fusion(f32[8,256,128]{2,1,0:T(8,128)S(1)} %bitcast.59, s32[256]{0:T(256)S(1)} %add_bitcast_fusion.1, s32[8,256]{1,0:T(8,128)S(1)} %copy-done.10), kind=kOutput, calls=%fused_computation.8 | convolution fusion | flops 805830656 | bytes 2106368 | tf_op jit(solution)/shard_map/skj,sjr->skr/dot_general | solution.py:144
  67.6 1.8 %gather_fusion.5 = f32[16,128,128]{2,1,0:T(8,128)S(1)} fusion(f32[16,128,128]{2,1,0:T(8,128)} %collective-permute-done.15, s32[1024]{0:T(1024)S(1)} %pad_clamp_fusion), kind=kCustom, calls=%fused_computation.5 | custom fusion | bytes 2097216 | tf_op jit(solution)/shard_map/gather | solution.py:140
  71.0 3.5 %fusion.4 = f32[8,256,128]{2,1,0:T(8,128)S(1)} fusion(f32[8,256,128]{2,1,0:T(8,128)S(1)} %copy-done.6, f32[8,256,256]{2,1,0:T(8,128)S(1)} %copy-done, f32[8,256,128]{2,1,0:T(8,128)S(1)} %copy-done.3, f32[8,256,128]{2,1,0:T(8,128)S(1)} %fusion), kind=kOutput, calls=%fused_computation.12 | convolution fusion | flops 805830656 | bytes 6291456 | tf_op jit(solution)/shard_map/swk,skr->swr/dot_general | solution.py:151
  74.5 2.0 %convolution_bitcast_fusion = f32[8,256,128]{1,2,0:T(8,128)S(1)} fusion(f32[8,256,128]{2,1,0:T(8,128)S(1)} %fusion.4, f32[8,256,256]{2,1,0:T(8,128)S(1)} %copy-done.4), kind=kOutput, calls=%fused_computation.10 | convolution fusion | flops 805306368 | bytes 4194304 | tf_op jit(solution)/shard_map/swk,skr->swr/dot_general | solution.py:152
  (102 shorter events, 17.5 us)
Async XLA Ops:
  0.6 70.0 %copy-start = (f32[8,256,256]{2,1,0:T(8,128)S(1)}, f32[8,256,256]{2,1,0:T(8,128)}, u32[]{:S(2)}) copy-start(f32[8,256,256]{2,1,0:T(8,128)} %param.24) | copy-start | bytes 6291460
  0.6 8.4 %copy-start.16 = (s32[32]{0:T(128)S(1)}, s32[32]{0:T(128)}, u32[]{:S(2)}) copy-start(s32[32]{0:T(128)} %constant.145) | copy-start | bytes 388
  0.7 8.5 %copy-start.12 = (s32[1,256]{1,0:T(1,128)S(1)}, s32[1,256]{1,0:T(1,128)}, u32[]{:S(2)}) copy-start(s32[1,256]{1,0:T(1,128)} %param.19) | copy-start | bytes 3076
  0.7 9.2 %collective-permute-start.2 = (f32[1,16,128]{2,1,0:T(8,128)}, f32[1,16,128]{2,1,0:T(8,128)S(1)}, u32[]{:S(2)}, u32[]{:S(2)}) collective-permute-start(f32[1,16,128]{2,1,0:T(8,128)} %bitcast.61), channel_id=1, source_target_pairs={{0,3},{1,2},{2,1},{3,0},{4,7},{5,6},{6,5},{7,4},{8,11},{9,10},{10,... | collective-permute-start | bytes 24584 | tf_op jit(solution)/shard_map/ppermute | solution.py:22
  3.1 6.8 %collective-permute-start.1 = (f32[1,16,128]{2,1,0:T(8,128)}, f32[1,16,128]{2,1,0:T(8,128)S(1)}, u32[]{:S(2)}, u32[]{:S(2)}) collective-permute-start(f32[1,16,128]{2,1,0:T(8,128)} %bitcast.62), channel_id=1, source_target_pairs={{0,2},{1,3},{2,0},{3,1},{4,6},{5,7},{6,4},{7,5},{8,10},{9,11},{10,... | collective-permute-start | bytes 24584 | tf_op jit(solution)/shard_map/ppermute | solution.py:22
  3.8 6.1 %collective-permute-start = (f32[1,16,128]{2,1,0:T(8,128)}, f32[1,16,128]{2,1,0:T(8,128)S(1)}, u32[]{:S(2)}, u32[]{:S(2)}) collective-permute-start(f32[1,16,128]{2,1,0:T(8,128)} %bitcast.63), channel_id=1, source_target_pairs={{0,1},{1,0},{2,3},{3,2},{4,5},{5,4},{6,7},{7,6},{8,9},{9,8},{10,11... | collective-permute-start | bytes 24584 | tf_op jit(solution)/shard_map/ppermute | solution.py:22
  9.9 8.3 %copy-start.2 = (f32[512,512]{1,0:T(8,128)}, f32[512,512]{1,0:T(8,128)S(1)}, u32[]{:S(2)}) copy-start(f32[512,512]{1,0:T(8,128)S(1)} %fusion.14) | copy-start | bytes 3145732
  10.0 4.9 %collective-permute-start.6 = (f32[4,16,128]{2,1,0:T(8,128)S(1)}, f32[4,16,128]{2,1,0:T(8,128)S(1)}, u32[]{:S(2)}, u32[]{:S(2)}) collective-permute-start(f32[4,16,128]{2,1,0:T(8,128)S(1)} %pad_maximum_fusion.2), channel_id=1, source_target_pairs={{0,16},{1,17},{2,18},{3,19},{4,20},{5,21},{6,22},{7,23},{8,24},{9,... | collective-permute-start | bytes 98312 | tf_op jit(solution)/shard_map/ppermute | solution.py:22
  15.5 10.5 %collective-permute-start.7 = (f32[8,16,128]{2,1,0:T(8,128)}, f32[8,16,128]{2,1,0:T(8,128)S(1)}, u32[]{:S(2)}, u32[]{:S(2)}) collective-permute-start(f32[8,16,128]{2,1,0:T(8,128)} %get-tuple-element.15), channel_id=1, source_target_pairs={{0,8},{1,9},{2,10},{3,11},{4,12},{5,13},{6,14},{7,15},{8,0},{9,1},... | collective-permute-start | bytes 196616 | tf_op jit(solution)/shard_map/ppermute | solution.py:22
  20.0 11.3 %collective-permute-start.5 = (f32[128,512]{1,0:T(8,128)S(1)}, f32[128,512]{1,0:T(8,128)}, u32[]{:S(2)}, u32[]{:S(2)}) collective-permute-start(f32[128,512]{1,0:T(8,128)S(1)} %copy.25), channel_id=1, source_target_pairs={{0,3},{1,2},{2,1},{3,0},{4,7},{5,6},{6,5},{7,4},{8,11},{9,10},{10,... | collective-permute-start | bytes 786440 | tf_op jit(solution)/shard_map/ppermute | solution.py:120
  21.7 12.6 %collective-permute-start.4 = (f32[128,512]{1,0:T(8,128)}, f32[128,512]{1,0:T(8,128)}, u32[]{:S(2)}, u32[]{:S(2)}) collective-permute-start(f32[128,512]{1,0:T(8,128)} %copy.23), channel_id=1, source_target_pairs={{0,2},{1,3},{2,0},{3,1},{4,6},{5,7},{6,4},{7,5},{8,10},{9,11},{10,... | collective-permute-start | bytes 786440 | tf_op jit(solution)/shard_map/ppermute | solution.py:120
  24.0 12.5 %copy-start.13 = (s32[2]{0:T(128)S(1)}, s32[2]{0:T(128)}, u32[]{:S(2)}) copy-start(s32[2]{0:T(128)} %constant.120.clone) | copy-start | bytes 28
  24.0 12.5 %copy-start.1 = (s32[8]{0:T(128)S(1)}, s32[8]{0:T(128)}, u32[]{:S(2)}) copy-start(s32[8]{0:T(128)} %param.21) | copy-start | bytes 100
  24.2 10.2 %collective-permute-start.3 = (f32[128,512]{1,0:T(8,128)S(1)}, f32[128,512]{1,0:T(8,128)S(1)}, u32[]{:S(2)}, u32[]{:S(2)}) collective-permute-start(f32[128,512]{1,0:T(8,128)S(1)} %copy.21), channel_id=1, source_target_pairs={{0,1},{1,0},{2,3},{3,2},{4,5},{5,4},{6,7},{7,6},{8,9},{9,8},{10,11... | collective-permute-start | bytes 786440 | tf_op jit(solution)/shard_map/ppermute | solution.py:120
  24.4 4.5 %collective-permute-start.8 = (f32[8,16,128]{2,1,0:T(8,128)}, f32[8,16,128]{2,1,0:T(8,128)S(1)}, u32[]{:S(2)}, u32[]{:S(2)}) collective-permute-start(f32[8,16,128]{2,1,0:T(8,128)} %get-tuple-element.15), channel_id=1, source_target_pairs={{0,4},{1,5},{2,6},{3,7},{4,0},{5,1},{6,2},{7,3},{8,12},{9,13},{10,... | collective-permute-start | bytes 196616 | tf_op jit(solution)/shard_map/ppermute | solution.py:22
  25.9 5.4 %collective-permute-start.9 = (f32[8,16,128]{2,1,0:T(8,128)}, f32[8,16,128]{2,1,0:T(8,128)S(1)}, u32[]{:S(2)}, u32[]{:S(2)}) collective-permute-start(f32[8,16,128]{2,1,0:T(8,128)} %get-tuple-element.15), channel_id=1, source_target_pairs={{0,12},{1,13},{2,14},{3,15},{4,8},{5,9},{6,10},{7,11},{8,4},{9,5},... | collective-permute-start | bytes 196616 | tf_op jit(solution)/shard_map/ppermute | solution.py:22
  36.5 28.9 %copy-start.7 = (f32[1,128,128]{2,1,0:T(8,128)}, f32[1,128,128]{2,1,0:T(8,128)S(1)}, u32[]{:S(2)}) copy-start(f32[1,128,128]{2,1,0:T(8,128)S(1)} %get-tuple-element.24) | copy-start | bytes 196612
  36.5 4.3 %collective-permute-start.10 = (f32[1,128,128]{2,1,0:T(8,128)S(1)}, f32[1,128,128]{2,1,0:T(8,128)S(1)}, u32[]{:S(2)}, u32[]{:S(2)}) collective-permute-start(f32[1,128,128]{2,1,0:T(8,128)S(1)} %get-tuple-element.24), channel_id=1, source_target_pairs={{0,2},{1,3},{2,0},{3,1},{4,6},{5,7},{6,4},{7,5},{8,10},{9,11},{10,... | collective-permute-start | bytes 196616 | tf_op jit(solution)/shard_map/ppermute | solution.py:13
  40.8 7.9 %collective-permute-start.11 = (f32[2,128,128]{2,1,0:T(8,128)S(1)}, f32[2,128,128]{2,1,0:T(8,128)S(1)}, u32[]{:S(2)}, u32[]{:S(2)}) collective-permute-start(f32[2,128,128]{2,1,0:T(8,128)S(1)} %pad_maximum_fusion.1), channel_id=1, source_target_pairs={{0,16},{1,17},{2,18},{3,19},{4,20},{5,21},{6,22},{7,23},{8,24},{9,... | collective-permute-start | bytes 393224 | tf_op jit(solution)/shard_map/ppermute | solution.py:13
  48.7 16.8 %copy-start.10 = (s32[8,256]{1,0:T(8,128)S(1)}, s32[8,256]{1,0:T(8,128)}, u32[]{:S(2)}) copy-start(s32[8,256]{1,0:T(8,128)} %param.23) | copy-start | bytes 24580
  48.7 9.3 %collective-permute-start.12 = (f32[4,128,128]{2,1,0:T(8,128)S(1)}, f32[4,128,128]{2,1,0:T(8,128)S(1)}, u32[]{:S(2)}, u32[]{:S(2)}) collective-permute-start(f32[4,128,128]{2,1,0:T(8,128)S(1)} %pad_maximum_fusion), channel_id=1, source_target_pairs={{0,8},{1,9},{2,10},{3,11},{4,12},{5,13},{6,14},{7,15},{8,0},{9,1},... | collective-permute-start | bytes 786440 | tf_op jit(solution)/shard_map/ppermute | solution.py:13
  49.0 9.7 %collective-permute-start.13 = (f32[4,128,128]{2,1,0:T(8,128)S(1)}, f32[4,128,128]{2,1,0:T(8,128)S(1)}, u32[]{:S(2)}, u32[]{:S(2)}) collective-permute-start(f32[4,128,128]{2,1,0:T(8,128)S(1)} %pad_maximum_fusion), channel_id=1, source_target_pairs={{0,4},{1,5},{2,6},{3,7},{4,0},{5,1},{6,2},{7,3},{8,12},{9,13},{10,... | collective-permute-start | bytes 786440 | tf_op jit(solution)/shard_map/ppermute | solution.py:13
  51.1 11.6 %collective-permute-start.14 = (f32[4,128,128]{2,1,0:T(8,128)S(1)}, f32[4,128,128]{2,1,0:T(8,128)S(1)}, u32[]{:S(2)}, u32[]{:S(2)}) collective-permute-start(f32[4,128,128]{2,1,0:T(8,128)S(1)} %pad_maximum_fusion), channel_id=1, source_target_pairs={{0,12},{1,13},{2,14},{3,15},{4,8},{5,9},{6,10},{7,11},{8,4},{9,5},... | collective-permute-start | bytes 786440 | tf_op jit(solution)/shard_map/ppermute | solution.py:13
  63.4 4.2 %collective-permute-start.15 = (f32[16,128,128]{2,1,0:T(8,128)}, f32[16,128,128]{2,1,0:T(8,128)}, u32[]{:S(2)}, u32[]{:S(2)}) collective-permute-start(f32[16,128,128]{2,1,0:T(8,128)} %constant_dynamic-update-slice_fusion.7), channel_id=1, source_target_pairs={{0,1},{1,0},{2,3},{3,2},{4,5},{5,4},{6,7},{7,6},{8,9},{9,8},{10,11... | collective-permute-start | bytes 3145736 | tf_op jit(solution)/shard_map/ppermute | solution.py:132
  (9 other events, 31.8 us)

commit v22 on v17

--- a/solution.py
+++ b/solution.py
@@ -111,8 +111,21 @@
     own_inverse = lax.dynamic_slice_in_dim(upper_inverse[0], begin, share, 1)
     own_base = jnp.einsum("kw,kr->wr", own_inverse, upper_rhs[0], precision=highest)
 
-    top_held = xor_gather(top_solution, both, count, top_groups).reshape(count * top_rows, rhs)
-    own_rows = own_base - jnp.einsum("wj,jr->wr", total, top_held, precision=highest)
+    top_held = xor_gather(top_solution, both, count, top_groups[:-1])
+    first = top_held.shape[0] * top_rows
+    partial = own_base - jnp.einsum(
+        "wj,jr->wr", total[:, :first], top_held.reshape(first, rhs), precision=highest
+    )
+    arrivals = []
+    bits = top_groups[-1]
+    for k in range(1, 1 << len(bits)):
+        v = sum(((k >> t) & 1) << b for t, b in enumerate(bits))
+        arrivals.append(lax.ppermute(top_held, both, [(i, i ^ v) for i in range(count)]))
+    arrivals, partial = lax.optimization_barrier((arrivals, partial))
+    own_rows = partial
+    for k, block in enumerate(arrivals):
+        columns = total[:, first * (k + 1) : first * (k + 2)]
+        own_rows = own_rows - jnp.einsum("wj,jr->wr", columns, block.reshape(first, rhs), precision=highest)
 
     held = xor_gather(own_rows, both, count, spread_groups[:-1])
     last = spread_groups[-1][0]

time: 69.5 us -> 69.7 us (level); the launches traced: 68.2 us -> 69.2 us
  local copies, waits for them, and re-layouts: 12.7 us -> 14.8 us
  starting transfers between devices: 21.8 us -> 19.9 us
  other arithmetic: 1.14 us -> 2.97 us
    ppermute x12 -> x9, starting transfers between devices: 19.7 us -> 14.3 us  [xor_gather(): parts.append(lax.ppermute(held, axes, [(i, i ^ v) for i in range(count)]))]
    ppermute x12 -> x9, waiting for transfers between devices: 15.6 us -> 11.7 us  [xor_gather(): parts.append(lax.ppermute(held, axes, [(i, i ^ v) for i in range(count)]))]
    ppermute x0 -> x3, starting transfers between devices: none -> 3.55 us  [local(): lax.ppermute(top_held, both, [(i, i ^ v) for i in range(count)])]
    ppermute x0 -> x3, waiting for transfers between devices: none -> 3.3 us  [local(): lax.ppermute(top_held, both, [(i, i ^ v) for i in range(count)])]
    unnamed x39 -> x37, local copies, waits for them, and re-layouts: 5.27 us -> 7.36 us
    add x0 -> x1, other arithmetic: none -> 1.1 us  [local(): total + lax.ppermute(outgoing, 'panel', [(i, i ^ v) for i in range(panels)])]
    concatenate x3, other arithmetic: 0.03 us -> 0.76 us  [xor_gather(): held = jnp.concatenate(parts, 0)]
    dot_general x1 -> x4, matrix products: 2.35 us -> 1.77 us  [the longest x3 1.49 us: local(): jnp.einsum('wj,jr->wr', columns, block.reshape(first, rhs), precision=hig...]
  transfers between devices with their start and end apart: 16 -> 16, of which waited for: 7 -> 7; matrix products, arithmetic and copies ran while one was open for 23% -> 29% of each run, Pallas kernels for 0% -> 0%
where the time goes in v22:
time: 69.7 us; the launch traced here: 69.2 us
  starting transfers between devices  19.9 us (29%)
  matrix products  15.4 us (22%)
  waiting for transfers between devices  15.1 us (22%)
  local copies, waits for them, and re-layouts  14.8 us (21%)
  other arithmetic  2.97 us (4%)
  between operations  1.05 us (2%)
    ppermute x9, starting transfers between devices, xor_gather(): parts.append(lax.ppermute(held, axes, [(i, i ^ v) for i in range(count)]))  14.3 us
    ppermute x9, waiting for transfers between devices, xor_gather(): parts.append(lax.ppermute(held, axes, [(i, i ^ v) for i in range(count)]))  11.7 us
    unnamed x37, local copies, waits for them, and re-layouts  7.36 us
    gather x2, local copies, waits for them, and re-layouts, local(): slabs = source[places].reshape(position.shape[0], -1, own_rows.shape[1])  3.67 us
    ppermute x3, starting transfers between devices, local(): lax.ppermute(top_held, both, [(i, i ^ v) for i in range(count)])  3.55 us
    dot_general x1, matrix products, local(): jnp.einsum('swk,skr->swr', panel_t, parent_rows, precision=highest)  3.54 us
    dot_general x2, matrix products, local(): term = jnp.einsum('skj,sjr->skr', pick, slabs, precision=highest)  3.32 us
    ppermute x3, waiting for transfers between devices, local(): lax.ppermute(top_held, both, [(i, i ^ v) for i in range(count)])  3.3 us
  transfers between devices with their start and end apart: 16, of which 7 were waited for; matrix products, arithmetic and copies ran while one was open for 29% of the time, Pallas kernels for 0%

profile of v22, /device:TPU:0, one launch (start us, length us, event | category | flops | bytes accessed | tf_op | source)
XLA Modules:
  0.0 69.2 jit_solution(14312830434724585113)
XLA Ops:
  1.2 2.6 %collective-permute-start.1 = (f32[1,16,128]{2,1,0:T(8,128)}, f32[1,16,128]{2,1,0:T(8,128)}, u32[]{:S(2)}, u32[]{:S(2)}) collective-permute-start(f32[1,16,128]{2,1,0:T(8,128)} %bitcast.73), channel_id=1, source_target_pairs={{0,2},{1,3},{2,0},{3,1},{4,6},{5,7},{6,4},{7,5},{8,10},{9,11},{10,... | collective-permute-start | bytes 24584 | tf_op jit(solution)/shard_map/ppermute | solution.py:13
  5.1 2.4 %fusion.5 = f32[256,512]{1,0:T(8,128)S(1)} fusion(f32[1,512,512]{2,1,0:T(8,128)} %param.18, f32[1,256,512]{2,1,0:T(8,128)} %param.17), kind=kOutput, calls=%fused_computation.14 | convolution fusion | flops 805306368 | bytes 2097152 | tf_op jit(solution)/shard_map/kv,vw->kw/dot_general | solution.py:102
  9.9 1.7 %collective-permute-start.9 = (f32[128,512]{0,1:T(8,128)S(1)}, f32[128,512]{0,1:T(8,128)S(1)}, u32[]{:S(2)}, u32[]{:S(2)}) collective-permute-start(f32[128,512]{0,1:T(8,128)S(1)} %bitcast.63), channel_id=1, source_target_pairs={{0,3},{1,2},{2,1},{3,0},{4,7},{5,6},{6,5},{7,4},{8,11},{9,10},{10,... | collective-permute-start | bytes 786440 | tf_op jit(solution)/shard_map/ppermute | solution.py:110
  12.4 1.6 %fusion.15 = f32[128,128]{1,0:T(8,128)S(1)} fusion(f32[1,512,128]{2,1,0:T(8,128)} %param.16, f32[1,512,512]{2,1,0:T(8,128)} %param.18, s32[]{:T(128)S(6)} %select_n.96), kind=kOutput, calls=%fused_computation.25 | convolution fusion | flops 100663296 | bytes 589828 | tf_op jit(solution)/shard_map/kw,kr->wr/dot_general | solution.py:112
  15.6 2.9 %collective-permute-start.3 = (f32[4,16,128]{2,1,0:T(8,128)S(1)}, f32[4,16,128]{2,1,0:T(8,128)S(1)}, u32[]{:S(2)}, u32[]{:S(2)}) collective-permute-start(f32[4,16,128]{2,1,0:T(8,128)S(1)} %pad_maximum_fusion.2), channel_id=1, source_target_pairs={{0,16},{1,17},{2,18},{3,19},{4,20},{5,21},{6,22},{7,23},{8,24},{9,... | collective-permute-start | bytes 98312 | tf_op jit(solution)/shard_map/ppermute | solution.py:13
  20.6 1.7 %collective-permute-start.4 = (f32[8,16,128]{2,1,0:T(8,128)S(1)}, f32[8,16,128]{2,1,0:T(8,128)S(1)}, u32[]{:S(2)}, u32[]{:S(2)}) collective-permute-start(f32[8,16,128]{2,1,0:T(8,128)S(1)} %constant_dynamic-update-slice_fusion), channel_id=1, source_target_pairs={{0,8},{1,9},{2,10},{3,11},{4,12},{5,13},{6,14},{7,15},{8,0},{9,1},... | collective-permute-start | bytes 196616 | tf_op jit(solution)/shard_map/ppermute | solution.py:123
  22.3 1.5 %collective-permute-start.5 = (f32[8,16,128]{2,1,0:T(8,128)S(1)}, f32[8,16,128]{2,1,0:T(8,128)S(1)}, u32[]{:S(2)}, u32[]{:S(2)}) collective-permute-start(f32[8,16,128]{2,1,0:T(8,128)S(1)} %constant_dynamic-update-slice_fusion), channel_id=1, source_target_pairs={{0,4},{1,5},{2,6},{3,7},{4,0},{5,1},{6,2},{7,3},{8,12},{9,13},{10,... | collective-permute-start | bytes 196616 | tf_op jit(solution)/shard_map/ppermute | solution.py:123
  24.3 1.1 %add_add_fusion = f32[128,512]{0,1:T(8,128)S(1)} fusion(f32[128,512]{0,1:T(8,128)S(1)} %collective-permute-done.9, f32[128,512]{0,1:T(8,128)} %collective-permute-done.8, f32[128,512]{0,1:T(8,128)S(1)} %collective-permute-done.7, f32[512,512]{0,1:T(8,128)} %copy-done.2, s32[]{:T(128)S(6)} %select_n.96), kind=kLoop, calls=%fused_computation.28 | loop fusion | flops 196608 | bytes 1310724 | tf_op jit(solution)/shard_map/add | solution.py:110
  26.6 2.4 %collective-permute-done.6 = f32[8,16,128]{2,1,0:T(8,128)S(1)} collective-permute-done((f32[8,16,128]{2,1,0:T(8,128)S(1)}, f32[8,16,128]{2,1,0:T(8,128)S(1)}, u32[]{:S(2)}, u32[]{:S(2)}) %collective-permute-start.6) | collective-permute-done | bytes 65568 | tf_op jit(solution)/shard_map/ppermute | solution.py:123
  29.6 0.9 %constant_dynamic-update-slice_fusion.10 = (f32[16,128,128]{2,1,0:T(8,128)}, f32[1,128,128]{2,1,0:T(8,128)S(1)}) fusion(f32[128,128]{1,0:T(8,128)S(1)} %fusion.23, f32[128,128]{1,0:T(8,128)S(1)} %convolution_subtract_fusion, f32[128,128]{1,0:T(8,128)S(1)} %fusion.25, f32[128,128]{1,0:T(8,128)S(1)} %bitcast.71, f32[128,512]{0,1:T(8,128)S(1)} %add_add_fusion), kind=kOutput, calls=%fused_computation.52 | convolution fusion | flops 25214976 | bytes 458752 | tf_op jit(solution)/shard_map/wj,jr->wr/dot_general | solution.py:128
  30.5 1.5 %collective-permute-start.10 = (f32[1,128,128]{2,1,0:T(8,128)S(1)}, f32[1,128,128]{2,1,0:T(8,128)S(1)}, u32[]{:S(2)}, u32[]{:S(2)}) collective-permute-start(f32[1,128,128]{2,1,0:T(8,128)S(1)} %get-tuple-element.17), channel_id=1, source_target_pairs={{0,2},{1,3},{2,0},{3,1},{4,6},{5,7},{6,4},{7,5},{8,10},{9,11},{10,... | collective-permute-start | bytes 196616 | tf_op jit(solution)/shard_map/ppermute | solution.py:13
  32.7 2.1 %collective-permute-done.10 = f32[1,128,128]{2,1,0:T(8,128)S(1)} collective-permute-done((f32[1,128,128]{2,1,0:T(8,128)S(1)}, f32[1,128,128]{2,1,0:T(8,128)S(1)}, u32[]{:S(2)}, u32[]{:S(2)}) %collective-permute-start.10) | collective-permute-done | bytes 65568 | tf_op jit(solution)/shard_map/ppermute | solution.py:13
  34.8 3.1 %collective-permute-start.11 = (f32[2,128,128]{2,1,0:T(8,128)S(1)}, f32[2,128,128]{2,1,0:T(8,128)S(1)}, u32[]{:S(2)}, u32[]{:S(2)}) collective-permute-start(f32[2,128,128]{2,1,0:T(8,128)S(1)} %pad_maximum_fusion.1), channel_id=1, source_target_pairs={{0,16},{1,17},{2,18},{3,19},{4,20},{5,21},{6,22},{7,23},{8,24},{9,... | collective-permute-start | bytes 393224 | tf_op jit(solution)/shard_map/ppermute | solution.py:13
  37.9 4.2 %collective-permute-done.11 = f32[2,128,128]{2,1,0:T(8,128)S(1)} collective-permute-done((f32[2,128,128]{2,1,0:T(8,128)S(1)}, f32[2,128,128]{2,1,0:T(8,128)S(1)}, u32[]{:S(2)}, u32[]{:S(2)}) %collective-permute-start.11) | collective-permute-done | bytes 131104 | tf_op jit(solution)/shard_map/ppermute | solution.py:13
  43.6 3.0 %collective-permute-start.14 = (f32[4,128,128]{2,1,0:T(8,128)S(1)}, f32[4,128,128]{2,1,0:T(8,128)S(1)}, u32[]{:S(2)}, u32[]{:S(2)}) collective-permute-start(f32[4,128,128]{2,1,0:T(8,128)S(1)} %pad_maximum_fusion), channel_id=1, source_target_pairs={{0,12},{1,13},{2,14},{3,15},{4,8},{5,9},{6,10},{7,11},{8,4},{9,5},... | collective-permute-start | bytes 786440 | tf_op jit(solution)/shard_map/ppermute | solution.py:13
  47.2 3.2 %collective-permute-done.12 = f32[4,128,128]{2,1,0:T(8,128)S(1)} collective-permute-done((f32[4,128,128]{2,1,0:T(8,128)S(1)}, f32[4,128,128]{2,1,0:T(8,128)S(1)}, u32[]{:S(2)}, u32[]{:S(2)}) %collective-permute-start.12) | collective-permute-done | bytes 262176 | tf_op jit(solution)/shard_map/ppermute | solution.py:13
  51.1 2.2 %collective-permute-done.13 = f32[4,128,128]{2,1,0:T(8,128)S(1)} collective-permute-done((f32[4,128,128]{2,1,0:T(8,128)S(1)}, f32[4,128,128]{2,1,0:T(8,128)S(1)}, u32[]{:S(2)}, u32[]{:S(2)}) %collective-permute-start.13) | collective-permute-done | bytes 262176 | tf_op jit(solution)/shard_map/ppermute | solution.py:13
  54.9 1.8 %gather_fusion.4 = f32[16,128,128]{2,1,0:T(8,128)S(1)} fusion(f32[16,128,128]{2,1,0:T(8,128)} %constant_dynamic-update-slice_fusion.5, s32[1024]{0:T(1024)S(1)} %pad_clamp_fusion.1), kind=kCustom, calls=%fused_computation.4 | custom fusion | bytes 2097216 | tf_op jit(solution)/shard_map/gather | solution.py:140
  56.8 2.1 %fusion.2 = f32[8,256,128]{2,1,0:T(8,128)} fusion(f32[8,256,128]{2,1,0:T(8,128)S(1)} %bitcast.67, s32[256]{0:T(256)S(1)} %add_bitcast_fusion.1, s32[8,256]{1,0:T(8,128)S(1)} %copy-done.7), kind=kOutput, calls=%fused_computation.8 | convolution fusion | flops 805830656 | bytes 2106368 | tf_op jit(solution)/shard_map/skj,sjr->skr/dot_general | solution.py:144
  58.9 1.8 %gather_fusion.5 = f32[16,128,128]{2,1,0:T(8,128)S(1)} fusion(f32[16,128,128]{2,1,0:T(8,128)} %collective-permute-done.15, s32[1024]{0:T(1024)S(1)} %pad_clamp_fusion), kind=kCustom, calls=%fused_computation.5 | custom fusion | bytes 2097216 | tf_op jit(solution)/shard_map/gather | solution.py:140
  60.8 1.2 %fusion = f32[8,256,128]{2,1,0:T(8,128)S(1)} fusion(f32[8,256,128]{2,1,0:T(8,128)S(1)} %bitcast.66, s32[256]{0:T(256)S(1)} %add_bitcast_fusion, s32[8,256]{1,0:T(8,128)S(1)} %copy-done.7), kind=kOutput, calls=%fused_computation.6 | convolution fusion | flops 805830656 | bytes 2106368 | tf_op jit(solution)/shard_map/skj,sjr->skr/dot_general | solution.py:144
  62.3 3.5 %fusion.4 = f32[8,256,128]{2,1,0:T(8,128)S(1)} fusion(f32[8,256,128]{2,1,0:T(8,128)S(1)} %copy-done.5, f32[8,256,256]{2,1,0:T(8,128)S(1)} %copy-done, f32[8,256,128]{2,1,0:T(8,128)S(1)} %copy-done.3, f32[8,256,128]{2,1,0:T(8,128)S(1)} %fusion), kind=kOutput, calls=%fused_computation.12 | convolution fusion | flops 805830656 | bytes 6291456 | tf_op jit(solution)/shard_map/swk,skr->swr/dot_general | solution.py:151
  65.9 2.0 %convolution_bitcast_fusion = f32[8,256,128]{1,2,0:T(8,128)S(1)} fusion(f32[8,256,128]{2,1,0:T(8,128)S(1)} %fusion.4, f32[8,256,256]{2,1,0:T(8,128)S(1)} %copy-done.4), kind=kOutput, calls=%fused_computation.10 | convolution fusion | flops 805306368 | bytes 4194304 | tf_op jit(solution)/shard_map/swk,skr->swr/dot_general | solution.py:152
  67.9 1.3 %copy.21 = f32[8,256,128]{2,1,0:T(8,128)} copy(f32[8,256,128]{1,2,0:T(8,128)S(1)} %convolution_bitcast_fusion) | data formatting | bytes 2097152
  (94 shorter events, 16.1 us)
Async XLA Ops:
  0.6 61.3 %copy-start = (f32[8,256,256]{2,1,0:T(8,128)S(1)}, f32[8,256,256]{2,1,0:T(8,128)}, u32[]{:S(2)}) copy-start(f32[8,256,256]{2,1,0:T(8,128)} %param.24) | copy-start | bytes 6291460
  0.6 6.9 %copy-start.13 = (s32[32]{0:T(128)S(1)}, s32[32]{0:T(128)}, u32[]{:S(2)}) copy-start(s32[32]{0:T(128)} %constant.145) | copy-start | bytes 388
  0.7 6.9 %copy-start.9 = (s32[1,256]{1,0:T(1,128)S(1)}, s32[1,256]{1,0:T(1,128)}, u32[]{:S(2)}) copy-start(s32[1,256]{1,0:T(1,128)} %param.19) | copy-start | bytes 3076
  0.7 14.0 %collective-permute-start = (f32[1,16,128]{2,1,0:T(8,128)}, f32[1,16,128]{2,1,0:T(8,128)}, u32[]{:S(2)}, u32[]{:S(2)}) collective-permute-start(f32[1,16,128]{2,1,0:T(8,128)} %bitcast.72), channel_id=1, source_target_pairs={{0,1},{1,0},{2,3},{3,2},{4,5},{5,4},{6,7},{7,6},{8,9},{9,8},{10,11... | collective-permute-start | bytes 24584 | tf_op jit(solution)/shard_map/ppermute | solution.py:13
  1.2 13.6 %collective-permute-start.1 = (f32[1,16,128]{2,1,0:T(8,128)}, f32[1,16,128]{2,1,0:T(8,128)}, u32[]{:S(2)}, u32[]{:S(2)}) collective-permute-start(f32[1,16,128]{2,1,0:T(8,128)} %bitcast.73), channel_id=1, source_target_pairs={{0,2},{1,3},{2,0},{3,1},{4,6},{5,7},{6,4},{7,5},{8,10},{9,11},{10,... | collective-permute-start | bytes 24584 | tf_op jit(solution)/shard_map/ppermute | solution.py:13
  3.8 11.0 %collective-permute-start.2 = (f32[1,16,128]{2,1,0:T(8,128)}, f32[1,16,128]{2,1,0:T(8,128)}, u32[]{:S(2)}, u32[]{:S(2)}) collective-permute-start(f32[1,16,128]{2,1,0:T(8,128)} %bitcast.74), channel_id=1, source_target_pairs={{0,3},{1,2},{2,1},{3,0},{4,7},{5,6},{6,5},{7,4},{8,11},{9,10},{10,... | collective-permute-start | bytes 24584 | tf_op jit(solution)/shard_map/ppermute | solution.py:13
  9.9 13.9 %collective-permute-start.9 = (f32[128,512]{0,1:T(8,128)S(1)}, f32[128,512]{0,1:T(8,128)S(1)}, u32[]{:S(2)}, u32[]{:S(2)}) collective-permute-start(f32[128,512]{0,1:T(8,128)S(1)} %bitcast.63), channel_id=1, source_target_pairs={{0,3},{1,2},{2,1},{3,0},{4,7},{5,6},{6,5},{7,4},{8,11},{9,10},{10,... | collective-permute-start | bytes 786440 | tf_op jit(solution)/shard_map/ppermute | solution.py:110
  12.2 12.0 %collective-permute-start.8 = (f32[128,512]{0,1:T(8,128)S(1)}, f32[128,512]{0,1:T(8,128)}, u32[]{:S(2)}, u32[]{:S(2)}) collective-permute-start(f32[128,512]{0,1:T(8,128)S(1)} %bitcast.64), channel_id=1, source_target_pairs={{0,2},{1,3},{2,0},{3,1},{4,6},{5,7},{6,4},{7,5},{8,10},{9,11},{10,... | collective-permute-start | bytes 786440 | tf_op jit(solution)/shard_map/ppermute | solution.py:110
  14.6 17.4 %copy-start.10 = (s32[2]{0:T(128)S(1)}, s32[2]{0:T(128)}, u32[]{:S(2)}) copy-start(s32[2]{0:T(128)} %constant.120.clone) | copy-start | bytes 28
  14.7 17.3 %copy-start.1 = (s32[8]{0:T(128)S(1)}, s32[8]{0:T(128)}, u32[]{:S(2)}) copy-start(s32[8]{0:T(128)} %param.21) | copy-start | bytes 100
  14.7 9.6 %collective-permute-start.7 = (f32[128,512]{0,1:T(8,128)S(1)}, f32[128,512]{0,1:T(8,128)S(1)}, u32[]{:S(2)}, u32[]{:S(2)}) collective-permute-start(f32[128,512]{0,1:T(8,128)S(1)} %bitcast.65), channel_id=1, source_target_pairs={{0,1},{1,0},{2,3},{3,2},{4,5},{5,4},{6,7},{7,6},{8,9},{9,8},{10,11... | collective-permute-start | bytes 786440 | tf_op jit(solution)/shard_map/ppermute | solution.py:110
  15.6 5.0 %collective-permute-start.3 = (f32[4,16,128]{2,1,0:T(8,128)S(1)}, f32[4,16,128]{2,1,0:T(8,128)S(1)}, u32[]{:S(2)}, u32[]{:S(2)}) collective-permute-start(f32[4,16,128]{2,1,0:T(8,128)S(1)} %pad_maximum_fusion.2), channel_id=1, source_target_pairs={{0,16},{1,17},{2,18},{3,19},{4,20},{5,21},{6,22},{7,23},{8,24},{9,... | collective-permute-start | bytes 98312 | tf_op jit(solution)/shard_map/ppermute | solution.py:13
  20.6 5.1 %collective-permute-start.4 = (f32[8,16,128]{2,1,0:T(8,128)S(1)}, f32[8,16,128]{2,1,0:T(8,128)S(1)}, u32[]{:S(2)}, u32[]{:S(2)}) collective-permute-start(f32[8,16,128]{2,1,0:T(8,128)S(1)} %constant_dynamic-update-slice_fusion), channel_id=1, source_target_pairs={{0,8},{1,9},{2,10},{3,11},{4,12},{5,13},{6,14},{7,15},{8,0},{9,1},... | collective-permute-start | bytes 196616 | tf_op jit(solution)/shard_map/ppermute | solution.py:123
  22.3 4.3 %collective-permute-start.5 = (f32[8,16,128]{2,1,0:T(8,128)S(1)}, f32[8,16,128]{2,1,0:T(8,128)S(1)}, u32[]{:S(2)}, u32[]{:S(2)}) collective-permute-start(f32[8,16,128]{2,1,0:T(8,128)S(1)} %constant_dynamic-update-slice_fusion), channel_id=1, source_target_pairs={{0,4},{1,5},{2,6},{3,7},{4,0},{5,1},{6,2},{7,3},{8,12},{9,13},{10,... | collective-permute-start | bytes 196616 | tf_op jit(solution)/shard_map/ppermute | solution.py:123
  23.8 5.2 %collective-permute-start.6 = (f32[8,16,128]{2,1,0:T(8,128)S(1)}, f32[8,16,128]{2,1,0:T(8,128)S(1)}, u32[]{:S(2)}, u32[]{:S(2)}) collective-permute-start(f32[8,16,128]{2,1,0:T(8,128)S(1)} %constant_dynamic-update-slice_fusion), channel_id=1, source_target_pairs={{0,12},{1,13},{2,14},{3,15},{4,8},{5,9},{6,10},{7,11},{8,4},{9,5},... | collective-permute-start | bytes 196616 | tf_op jit(solution)/shard_map/ppermute | solution.py:123
  30.5 26.3 %copy-start.6 = (f32[1,128,128]{2,1,0:T(8,128)}, f32[1,128,128]{2,1,0:T(8,128)S(1)}, u32[]{:S(2)}) copy-start(f32[1,128,128]{2,1,0:T(8,128)S(1)} %get-tuple-element.17) | copy-start | bytes 196612
  30.5 4.3 %collective-permute-start.10 = (f32[1,128,128]{2,1,0:T(8,128)S(1)}, f32[1,128,128]{2,1,0:T(8,128)S(1)}, u32[]{:S(2)}, u32[]{:S(2)}) collective-permute-start(f32[1,128,128]{2,1,0:T(8,128)S(1)} %get-tuple-element.17), channel_id=1, source_target_pairs={{0,2},{1,3},{2,0},{3,1},{4,6},{5,7},{6,4},{7,5},{8,10},{9,11},{10,... | collective-permute-start | bytes 196616 | tf_op jit(solution)/shard_map/ppermute | solution.py:13
  34.8 7.3 %collective-permute-start.11 = (f32[2,128,128]{2,1,0:T(8,128)S(1)}, f32[2,128,128]{2,1,0:T(8,128)S(1)}, u32[]{:S(2)}, u32[]{:S(2)}) collective-permute-start(f32[2,128,128]{2,1,0:T(8,128)S(1)} %pad_maximum_fusion.1), channel_id=1, source_target_pairs={{0,16},{1,17},{2,18},{3,19},{4,20},{5,21},{6,22},{7,23},{8,24},{9,... | collective-permute-start | bytes 393224 | tf_op jit(solution)/shard_map/ppermute | solution.py:13
  42.1 14.7 %copy-start.7 = (s32[8,256]{1,0:T(8,128)S(1)}, s32[8,256]{1,0:T(8,128)}, u32[]{:S(2)}) copy-start(s32[8,256]{1,0:T(8,128)} %param.23) | copy-start | bytes 24580
  42.1 8.3 %collective-permute-start.12 = (f32[4,128,128]{2,1,0:T(8,128)S(1)}, f32[4,128,128]{2,1,0:T(8,128)S(1)}, u32[]{:S(2)}, u32[]{:S(2)}) collective-permute-start(f32[4,128,128]{2,1,0:T(8,128)S(1)} %pad_maximum_fusion), channel_id=1, source_target_pairs={{0,8},{1,9},{2,10},{3,11},{4,12},{5,13},{6,14},{7,15},{8,0},{9,1},... | collective-permute-start | bytes 786440 | tf_op jit(solution)/shard_map/ppermute | solution.py:13
  42.4 10.9 %collective-permute-start.13 = (f32[4,128,128]{2,1,0:T(8,128)S(1)}, f32[4,128,128]{2,1,0:T(8,128)S(1)}, u32[]{:S(2)}, u32[]{:S(2)}) collective-permute-start(f32[4,128,128]{2,1,0:T(8,128)S(1)} %pad_maximum_fusion), channel_id=1, source_target_pairs={{0,4},{1,5},{2,6},{3,7},{4,0},{5,1},{6,2},{7,3},{8,12},{9,13},{10,... | collective-permute-start | bytes 786440 | tf_op jit(solution)/shard_map/ppermute | solution.py:13
  43.6 10.5 %collective-permute-start.14 = (f32[4,128,128]{2,1,0:T(8,128)S(1)}, f32[4,128,128]{2,1,0:T(8,128)S(1)}, u32[]{:S(2)}, u32[]{:S(2)}) collective-permute-start(f32[4,128,128]{2,1,0:T(8,128)S(1)} %pad_maximum_fusion), channel_id=1, source_target_pairs={{0,12},{1,13},{2,14},{3,15},{4,8},{5,9},{6,10},{7,11},{8,4},{9,5},... | collective-permute-start | bytes 786440 | tf_op jit(solution)/shard_map/ppermute | solution.py:13
  54.7 4.2 %collective-permute-start.15 = (f32[16,128,128]{2,1,0:T(8,128)}, f32[16,128,128]{2,1,0:T(8,128)}, u32[]{:S(2)}, u32[]{:S(2)}) collective-permute-start(f32[16,128,128]{2,1,0:T(8,128)} %constant_dynamic-update-slice_fusion.5), channel_id=1, source_target_pairs={{0,1},{1,0},{2,3},{3,2},{4,5},{5,4},{6,7},{7,6},{8,9},{9,8},{10,11... | collective-permute-start | bytes 3145736 | tf_op jit(solution)/shard_map/ppermute | solution.py:132
  62.3 3.6 %copy-start.4 = (f32[8,256,256]{2,1,0:T(8,128)S(1)}, f32[8,256,256]{2,1,0:T(8,128)}, u32[]{:S(2)}) copy-start(f32[8,256,256]{2,1,0:T(8,128)} %param.26) | copy-start | bytes 6291460
  (6 other events, 10.8 us)

commit v23 on v17

--- a/solution.py
+++ b/solution.py
@@ -91,7 +91,7 @@
         leaf_groups.append([high_first[0]])
         high_first = high_first[1:]
     leaf_groups += [high_first[i : i + 2] for i in range(0, len(high_first), 2)]
-    top_groups = [panel_bits] + leaf_groups
+    top_groups = [panel_bits] + leaf_groups[::-1]
     spread_groups = [[b] for b in panel_bits[1:]] + leaf_groups + [[0]]
 
     top_rows, rhs = top_solution.shape

time: 69.5 us -> 73.5 us (1.058)
  the two profiles are of different devices: /device:TPU:0 before, /device:TPU:17 now
where the time goes in v23:
time: 73.5 us; the launch traced here: 73.2 us
  starting transfers between devices  22.4 us (30%)
  local copies, waits for them, and re-layouts  16.9 us (23%)
  matrix products  16 us (22%)
  waiting for transfers between devices  15.8 us (21%)
  other arithmetic  1.14 us (2%)
  between operations  1.02 us (1%)
    ppermute x12, waiting for transfers between devices, xor_gather(): parts.append(lax.ppermute(held, axes, [(i, i ^ v) for i in range(count)]))  15.8 us
    ppermute x12, starting transfers between devices, xor_gather(): parts.append(lax.ppermute(held, axes, [(i, i ^ v) for i in range(count)]))  15.7 us
    unnamed x39, local copies, waits for them, and re-layouts  8.84 us
    ppermute x1, starting transfers between devices, local(): lax.ppermute(held, both, [(i, i ^ 1 << last) for i in range(count)])  4.37 us
    gather x2, local copies, waits for them, and re-layouts, local(): slabs = source[places].reshape(position.shape[0], -1, own_rows.shape[1])  3.67 us
    dot_general x1, matrix products, local(): jnp.einsum('swk,skr->swr', panel_t, parent_rows, precision=highest)  3.54 us
    dot_general x2, matrix products, local(): term = jnp.einsum('skj,sjr->skr', pick, slabs, precision=highest)  3.32 us
    dot_general x1, matrix products, local(): jnp.einsum('kv,vw->kw', upper_panel[0], upper_inverse[0], precision=highest)  2.44 us
  transfers between devices with their start and end apart: 16, of which 7 were waited for; matrix products, arithmetic and copies ran while one was open for 27% of the time, Pallas kernels for 0%

profile of v23, /device:TPU:17, one launch (start us, length us, event | category | flops | bytes accessed | tf_op | source)
XLA Modules:
  0.0 73.2 jit_solution(8862485045986715215)
XLA Ops:
  1.4 1.3 %collective-permute-start.4 = (f32[1,16,128]{2,1,0:T(8,128)}, f32[1,16,128]{2,1,0:T(8,128)S(1)}, u32[]{:S(2)}, u32[]{:S(2)}) collective-permute-start(f32[1,16,128]{2,1,0:T(8,128)} %bitcast.64), channel_id=1, source_target_pairs={{0,2},{1,3},{2,0},{3,1},{4,6},{5,7},{6,4},{7,5},{8,10},{9,11},{10,... | collective-permute-start | bytes 24584 | tf_op jit(solution)/shard_map/ppermute | solution.py:13
  4.3 2.4 %fusion.6 = f32[256,512]{1,0:T(8,128)S(1)} fusion(f32[1,512,512]{2,1,0:T(8,128)} %param.18, f32[1,256,512]{2,1,0:T(8,128)} %param.17), kind=kOutput, calls=%fused_computation.15 | convolution fusion | flops 805306368 | bytes 2097152 | tf_op jit(solution)/shard_map/kv,vw->kw/dot_general | solution.py:102
  9.1 1.4 %collective-permute-start.2 = (f32[128,512]{0,1:T(8,128)S(1)}, f32[128,512]{0,1:T(8,128)}, u32[]{:S(2)}, u32[]{:S(2)}) collective-permute-start(f32[128,512]{0,1:T(8,128)S(1)} %bitcast.57), channel_id=1, source_target_pairs={{0,3},{1,2},{2,1},{3,0},{4,7},{5,6},{6,5},{7,4},{8,11},{9,10},{10,... | collective-permute-start | bytes 786440 | tf_op jit(solution)/shard_map/ppermute | solution.py:110
  13.3 1.4 %collective-permute-start.6 = (f32[4,16,128]{2,1,0:T(8,128)S(1)}, f32[4,16,128]{2,1,0:T(8,128)S(1)}, u32[]{:S(2)}, u32[]{:S(2)}) collective-permute-start(f32[4,16,128]{2,1,0:T(8,128)S(1)} %pad_maximum_fusion.2), channel_id=1, source_target_pairs={{0,8},{1,9},{2,10},{3,11},{4,12},{5,13},{6,14},{7,15},{8,0},{9,1},... | collective-permute-start | bytes 98312 | tf_op jit(solution)/shard_map/ppermute | solution.py:13
  14.7 1.2 %collective-permute-start.7 = (f32[4,16,128]{2,1,0:T(8,128)S(1)}, f32[4,16,128]{2,1,0:T(8,128)S(1)}, u32[]{:S(2)}, u32[]{:S(2)}) collective-permute-start(f32[4,16,128]{2,1,0:T(8,128)S(1)} %pad_maximum_fusion.2), channel_id=1, source_target_pairs={{0,4},{1,5},{2,6},{3,7},{4,0},{5,1},{6,2},{7,3},{8,12},{9,13},{10,... | collective-permute-start | bytes 98312 | tf_op jit(solution)/shard_map/ppermute | solution.py:13
  20.0 1.3 %collective-permute-done.8 = f32[4,16,128]{2,1,0:T(8,128)S(1)} collective-permute-done((f32[4,16,128]{2,1,0:T(8,128)S(1)}, f32[4,16,128]{2,1,0:T(8,128)S(1)}, u32[]{:S(2)}, u32[]{:S(2)}) %collective-permute-start.8) | collective-permute-done | bytes 32800 | tf_op jit(solution)/shard_map/ppermute | solution.py:13
  22.0 1.6 %fusion.16 = f32[128,128]{1,0:T(8,128)S(1)} fusion(f32[1,512,128]{2,1,0:T(8,128)} %param.16, f32[1,512,512]{2,1,0:T(8,128)} %param.18, s32[]{:T(128)S(6)} %select_n.96), kind=kOutput, calls=%fused_computation.26 | convolution fusion | flops 100663296 | bytes 589828 | tf_op jit(solution)/shard_map/kw,kr->wr/dot_general | solution.py:112
  23.6 3.6 %collective-permute-done.9 = f32[16,16,128]{2,1,0:T(8,128)S(1)} collective-permute-done((f32[16,16,128]{2,1,0:T(8,128)}, f32[16,16,128]{2,1,0:T(8,128)S(1)}, u32[]{:S(2)}, u32[]{:S(2)}) %collective-permute-start.9) | collective-permute-done | bytes 131104 | tf_op jit(solution)/shard_map/ppermute | solution.py:13
  27.3 2.3 %constant_dynamic-update-slice_fusion.20 = (f32[16,128,128]{2,1,0:T(8,128)}, f32[1,128,128]{2,1,0:T(8,128)S(1)}) fusion(f32[128,128]{1,0:T(8,128)S(1)} %fusion.16, f32[512,128]{1,0:T(8,128)S(1)} %bitcast.62, f32[128,512]{0,1:T(8,128)} %collective-permute-done.2, f32[128,512]{0,1:T(8,128)} %collective-permute-done.1, ...), kind=kOutput, calls=%fused_computation.57 | convolution fusion | flops 100876288 | bytes 1507332 | tf_op jit(solution)/shard_map/wj,jr->wr/dot_general | solution.py:115
  29.6 1.2 %collective-permute-start.10 = (f32[1,128,128]{2,1,0:T(8,128)S(1)}, f32[1,128,128]{2,1,0:T(8,128)S(1)}, u32[]{:S(2)}, u32[]{:S(2)}) collective-permute-start(f32[1,128,128]{2,1,0:T(8,128)S(1)} %get-tuple-element.30), channel_id=1, source_target_pairs={{0,2},{1,3},{2,0},{3,1},{4,6},{5,7},{6,4},{7,5},{8,10},{9,11},{10,... | collective-permute-start | bytes 196616 | tf_op jit(solution)/shard_map/ppermute | solution.py:13
  31.5 1.2 %collective-permute-done.10 = f32[1,128,128]{2,1,0:T(8,128)S(1)} collective-permute-done((f32[1,128,128]{2,1,0:T(8,128)S(1)}, f32[1,128,128]{2,1,0:T(8,128)S(1)}, u32[]{:S(2)}, u32[]{:S(2)}) %collective-permute-start.10) | collective-permute-done | bytes 65568 | tf_op jit(solution)/shard_map/ppermute | solution.py:13
  32.7 3.2 %collective-permute-start.11 = (f32[2,128,128]{2,1,0:T(8,128)S(1)}, f32[2,128,128]{2,1,0:T(8,128)S(1)}, u32[]{:S(2)}, u32[]{:S(2)}) collective-permute-start(f32[2,128,128]{2,1,0:T(8,128)S(1)} %pad_maximum_fusion.1), channel_id=1, source_target_pairs={{0,16},{1,17},{2,18},{3,19},{4,20},{5,21},{6,22},{7,23},{8,24},{9,... | collective-permute-start | bytes 393224 | tf_op jit(solution)/shard_map/ppermute | solution.py:13
  35.9 2.5 %collective-permute-done.11 = f32[2,128,128]{2,1,0:T(8,128)S(1)} collective-permute-done((f32[2,128,128]{2,1,0:T(8,128)S(1)}, f32[2,128,128]{2,1,0:T(8,128)S(1)}, u32[]{:S(2)}, u32[]{:S(2)}) %collective-permute-start.11) | collective-permute-done | bytes 131104 | tf_op jit(solution)/shard_map/ppermute | solution.py:13
  38.4 2.4 %collective-permute-start.12 = (f32[4,128,128]{2,1,0:T(8,128)S(1)}, f32[4,128,128]{2,1,0:T(8,128)S(1)}, u32[]{:S(2)}, u32[]{:S(2)}) collective-permute-start(f32[4,128,128]{2,1,0:T(8,128)S(1)} %pad_maximum_fusion), channel_id=1, source_target_pairs={{0,8},{1,9},{2,10},{3,11},{4,12},{5,13},{6,14},{7,15},{8,0},{9,1},... | collective-permute-start | bytes 786440 | tf_op jit(solution)/shard_map/ppermute | solution.py:13
  41.0 2.7 %collective-permute-start.13 = (f32[4,128,128]{2,1,0:T(8,128)S(1)}, f32[4,128,128]{2,1,0:T(8,128)S(1)}, u32[]{:S(2)}, u32[]{:S(2)}) collective-permute-start(f32[4,128,128]{2,1,0:T(8,128)S(1)} %pad_maximum_fusion), channel_id=1, source_target_pairs={{0,4},{1,5},{2,6},{3,7},{4,0},{5,1},{6,2},{7,3},{8,12},{9,13},{10,... | collective-permute-start | bytes 786440 | tf_op jit(solution)/shard_map/ppermute | solution.py:13
  46.0 2.8 %collective-permute-done.13 = f32[4,128,128]{2,1,0:T(8,128)S(1)} collective-permute-done((f32[4,128,128]{2,1,0:T(8,128)S(1)}, f32[4,128,128]{2,1,0:T(8,128)S(1)}, u32[]{:S(2)}, u32[]{:S(2)}) %collective-permute-start.13) | collective-permute-done | bytes 262176 | tf_op jit(solution)/shard_map/ppermute | solution.py:13
  49.5 4.2 %collective-permute-done.14 = f32[4,128,128]{2,1,0:T(8,128)S(1)} collective-permute-done((f32[4,128,128]{2,1,0:T(8,128)S(1)}, f32[4,128,128]{2,1,0:T(8,128)S(1)}, u32[]{:S(2)}, u32[]{:S(2)}) %collective-permute-start.14) | collective-permute-done | bytes 262176 | tf_op jit(solution)/shard_map/ppermute | solution.py:13
  54.4 4.4 %collective-permute-start.15 = (f32[16,128,128]{2,1,0:T(8,128)}, f32[16,128,128]{2,1,0:T(8,128)}, u32[]{:S(2)}, u32[]{:S(2)}) collective-permute-start(f32[16,128,128]{2,1,0:T(8,128)} %constant_dynamic-update-slice_fusion.15), channel_id=1, source_target_pairs={{0,1},{1,0},{2,3},{3,2},{4,5},{5,4},{6,7},{7,6},{8,9},{9,8},{10,11... | collective-permute-start | bytes 3145736 | tf_op jit(solution)/shard_map/ppermute | solution.py:119
  58.9 1.8 %gather_fusion.4 = f32[16,128,128]{2,1,0:T(8,128)S(1)} fusion(f32[16,128,128]{2,1,0:T(8,128)} %constant_dynamic-update-slice_fusion.15, s32[1024]{0:T(1024)S(1)} %pad_clamp_fusion.1), kind=kCustom, calls=%fused_computation.4 | custom fusion | bytes 2097216 | tf_op jit(solution)/shard_map/gather | solution.py:127
  60.8 2.1 %fusion.2 = f32[8,256,128]{2,1,0:T(8,128)} fusion(f32[8,256,128]{2,1,0:T(8,128)S(1)} %bitcast.61, s32[256]{0:T(256)S(1)} %add_bitcast_fusion.1, s32[8,256]{1,0:T(8,128)S(1)} %copy-done.7), kind=kOutput, calls=%fused_computation.8 | convolution fusion | flops 805830656 | bytes 2106368 | tf_op jit(solution)/shard_map/skj,sjr->skr/dot_general | solution.py:131
  62.9 1.8 %gather_fusion.5 = f32[16,128,128]{2,1,0:T(8,128)S(1)} fusion(f32[16,128,128]{2,1,0:T(8,128)} %collective-permute-done.15, s32[1024]{0:T(1024)S(1)} %pad_clamp_fusion), kind=kCustom, calls=%fused_computation.5 | custom fusion | bytes 2097216 | tf_op jit(solution)/shard_map/gather | solution.py:127
  66.3 3.5 %fusion.4 = f32[8,256,128]{2,1,0:T(8,128)S(1)} fusion(f32[8,256,128]{2,1,0:T(8,128)S(1)} %copy-done.5, f32[8,256,256]{2,1,0:T(8,128)S(1)} %copy-done, f32[8,256,128]{2,1,0:T(8,128)S(1)} %copy-done.3, f32[8,256,128]{2,1,0:T(8,128)S(1)} %fusion), kind=kOutput, calls=%fused_computation.12 | convolution fusion | flops 805830656 | bytes 6291456 | tf_op jit(solution)/shard_map/swk,skr->swr/dot_general | solution.py:138
  69.9 2.0 %convolution_bitcast_fusion = f32[8,256,128]{1,2,0:T(8,128)S(1)} fusion(f32[8,256,128]{2,1,0:T(8,128)S(1)} %fusion.4, f32[8,256,256]{2,1,0:T(8,128)S(1)} %copy-done.4), kind=kOutput, calls=%fused_computation.10 | convolution fusion | flops 805306368 | bytes 4194304 | tf_op jit(solution)/shard_map/swk,skr->swr/dot_general | solution.py:139
  71.9 1.3 %copy.21 = f32[8,256,128]{2,1,0:T(8,128)} copy(f32[8,256,128]{1,2,0:T(8,128)S(1)} %convolution_bitcast_fusion) | data formatting | bytes 2097152
  (93 shorter events, 18.5 us)
Async XLA Ops:
  0.6 65.4 %copy-start = (f32[8,256,256]{2,1,0:T(8,128)S(1)}, f32[8,256,256]{2,1,0:T(8,128)}, u32[]{:S(2)}) copy-start(f32[8,256,256]{2,1,0:T(8,128)} %param.24) | copy-start | bytes 6291460
  0.6 6.2 %copy-start.13 = (s32[32]{0:T(128)S(1)}, s32[32]{0:T(128)}, u32[]{:S(2)}) copy-start(s32[32]{0:T(128)} %constant.145) | copy-start | bytes 388
  0.7 6.2 %copy-start.9 = (s32[1,256]{1,0:T(1,128)S(1)}, s32[1,256]{1,0:T(1,128)}, u32[]{:S(2)}) copy-start(s32[1,256]{1,0:T(1,128)} %param.19) | copy-start | bytes 3076
  0.7 11.9 %collective-permute-start.3 = (f32[1,16,128]{2,1,0:T(8,128)}, f32[1,16,128]{2,1,0:T(8,128)S(1)}, u32[]{:S(2)}, u32[]{:S(2)}) collective-permute-start(f32[1,16,128]{2,1,0:T(8,128)} %bitcast.63), channel_id=1, source_target_pairs={{0,1},{1,0},{2,3},{3,2},{4,5},{5,4},{6,7},{7,6},{8,9},{9,8},{10,11... | collective-permute-start | bytes 24584 | tf_op jit(solution)/shard_map/ppermute | solution.py:13
  1.4 11.9 %collective-permute-start.4 = (f32[1,16,128]{2,1,0:T(8,128)}, f32[1,16,128]{2,1,0:T(8,128)S(1)}, u32[]{:S(2)}, u32[]{:S(2)}) collective-permute-start(f32[1,16,128]{2,1,0:T(8,128)} %bitcast.64), channel_id=1, source_target_pairs={{0,2},{1,3},{2,0},{3,1},{4,6},{5,7},{6,4},{7,5},{8,10},{9,11},{10,... | collective-permute-start | bytes 24584 | tf_op jit(solution)/shard_map/ppermute | solution.py:13
  2.7 10.7 %collective-permute-start.5 = (f32[1,16,128]{2,1,0:T(8,128)}, f32[1,16,128]{2,1,0:T(8,128)S(1)}, u32[]{:S(2)}, u32[]{:S(2)}) collective-permute-start(f32[1,16,128]{2,1,0:T(8,128)} %bitcast.65), channel_id=1, source_target_pairs={{0,3},{1,2},{2,1},{3,0},{4,7},{5,6},{6,5},{7,4},{8,11},{9,10},{10,... | collective-permute-start | bytes 24584 | tf_op jit(solution)/shard_map/ppermute | solution.py:13
  9.1 18.1 %collective-permute-start.2 = (f32[128,512]{0,1:T(8,128)S(1)}, f32[128,512]{0,1:T(8,128)}, u32[]{:S(2)}, u32[]{:S(2)}) collective-permute-start(f32[128,512]{0,1:T(8,128)S(1)} %bitcast.57), channel_id=1, source_target_pairs={{0,3},{1,2},{2,1},{3,0},{4,7},{5,6},{6,5},{7,4},{8,11},{9,10},{10,... | collective-permute-start | bytes 786440 | tf_op jit(solution)/shard_map/ppermute | solution.py:110
  11.1 16.1 %collective-permute-start.1 = (f32[128,512]{0,1:T(8,128)S(1)}, f32[128,512]{0,1:T(8,128)}, u32[]{:S(2)}, u32[]{:S(2)}) collective-permute-start(f32[128,512]{0,1:T(8,128)S(1)} %bitcast.58), channel_id=1, source_target_pairs={{0,2},{1,3},{2,0},{3,1},{4,6},{5,7},{6,4},{7,5},{8,10},{9,11},{10,... | collective-permute-start | bytes 786440 | tf_op jit(solution)/shard_map/ppermute | solution.py:110
  12.6 18.3 %copy-start.10 = (s32[2]{0:T(128)S(1)}, s32[2]{0:T(128)}, u32[]{:S(2)}) copy-start(s32[2]{0:T(128)} %constant.120.clone) | copy-start | bytes 28
  12.6 18.3 %copy-start.1 = (s32[8]{0:T(128)S(1)}, s32[8]{0:T(128)}, u32[]{:S(2)}) copy-start(s32[8]{0:T(128)} %param.21) | copy-start | bytes 100
  12.6 14.6 %collective-permute-start = (f32[128,512]{0,1:T(8,128)S(1)}, f32[128,512]{0,1:T(8,128)S(1)}, u32[]{:S(2)}, u32[]{:S(2)}) collective-permute-start(f32[128,512]{0,1:T(8,128)S(1)} %bitcast.59), channel_id=1, source_target_pairs={{0,1},{1,0},{2,3},{3,2},{4,5},{5,4},{6,7},{7,6},{8,9},{9,8},{10,11... | collective-permute-start | bytes 786440 | tf_op jit(solution)/shard_map/ppermute | solution.py:110
  13.3 4.3 %collective-permute-start.6 = (f32[4,16,128]{2,1,0:T(8,128)S(1)}, f32[4,16,128]{2,1,0:T(8,128)S(1)}, u32[]{:S(2)}, u32[]{:S(2)}) collective-permute-start(f32[4,16,128]{2,1,0:T(8,128)S(1)} %pad_maximum_fusion.2), channel_id=1, source_target_pairs={{0,8},{1,9},{2,10},{3,11},{4,12},{5,13},{6,14},{7,15},{8,0},{9,1},... | collective-permute-start | bytes 98312 | tf_op jit(solution)/shard_map/ppermute | solution.py:13
  14.7 4.7 %collective-permute-start.7 = (f32[4,16,128]{2,1,0:T(8,128)S(1)}, f32[4,16,128]{2,1,0:T(8,128)S(1)}, u32[]{:S(2)}, u32[]{:S(2)}) collective-permute-start(f32[4,16,128]{2,1,0:T(8,128)S(1)} %pad_maximum_fusion.2), channel_id=1, source_target_pairs={{0,4},{1,5},{2,6},{3,7},{4,0},{5,1},{6,2},{7,3},{8,12},{9,13},{10,... | collective-permute-start | bytes 98312 | tf_op jit(solution)/shard_map/ppermute | solution.py:13
  17.7 3.7 %collective-permute-start.8 = (f32[4,16,128]{2,1,0:T(8,128)S(1)}, f32[4,16,128]{2,1,0:T(8,128)S(1)}, u32[]{:S(2)}, u32[]{:S(2)}) collective-permute-start(f32[4,16,128]{2,1,0:T(8,128)S(1)} %pad_maximum_fusion.2), channel_id=1, source_target_pairs={{0,12},{1,13},{2,14},{3,15},{4,8},{5,9},{6,10},{7,11},{8,4},{9,5},... | collective-permute-start | bytes 98312 | tf_op jit(solution)/shard_map/ppermute | solution.py:13
  21.9 5.3 %collective-permute-start.9 = (f32[16,16,128]{2,1,0:T(8,128)}, f32[16,16,128]{2,1,0:T(8,128)S(1)}, u32[]{:S(2)}, u32[]{:S(2)}) collective-permute-start(f32[16,16,128]{2,1,0:T(8,128)} %get-tuple-element.11), channel_id=1, source_target_pairs={{0,16},{1,17},{2,18},{3,19},{4,20},{5,21},{6,22},{7,23},{8,24},{9,... | collective-permute-start | bytes 393224 | tf_op jit(solution)/shard_map/ppermute | solution.py:13
  29.6 31.2 %copy-start.6 = (f32[1,128,128]{2,1,0:T(8,128)}, f32[1,128,128]{2,1,0:T(8,128)S(1)}, u32[]{:S(2)}) copy-start(f32[1,128,128]{2,1,0:T(8,128)S(1)} %get-tuple-element.30) | copy-start | bytes 196612
  29.6 3.1 %collective-permute-start.10 = (f32[1,128,128]{2,1,0:T(8,128)S(1)}, f32[1,128,128]{2,1,0:T(8,128)S(1)}, u32[]{:S(2)}, u32[]{:S(2)}) collective-permute-start(f32[1,128,128]{2,1,0:T(8,128)S(1)} %get-tuple-element.30), channel_id=1, source_target_pairs={{0,2},{1,3},{2,0},{3,1},{4,6},{5,7},{6,4},{7,5},{8,10},{9,11},{10,... | collective-permute-start | bytes 196616 | tf_op jit(solution)/shard_map/ppermute | solution.py:13
  32.7 5.7 %collective-permute-start.11 = (f32[2,128,128]{2,1,0:T(8,128)S(1)}, f32[2,128,128]{2,1,0:T(8,128)S(1)}, u32[]{:S(2)}, u32[]{:S(2)}) collective-permute-start(f32[2,128,128]{2,1,0:T(8,128)S(1)} %pad_maximum_fusion.1), channel_id=1, source_target_pairs={{0,16},{1,17},{2,18},{3,19},{4,20},{5,21},{6,22},{7,23},{8,24},{9,... | collective-permute-start | bytes 393224 | tf_op jit(solution)/shard_map/ppermute | solution.py:13
  38.4 22.4 %copy-start.7 = (s32[8,256]{1,0:T(8,128)S(1)}, s32[8,256]{1,0:T(8,128)}, u32[]{:S(2)}) copy-start(s32[8,256]{1,0:T(8,128)} %param.23) | copy-start | bytes 24580
  38.4 6.8 %collective-permute-start.12 = (f32[4,128,128]{2,1,0:T(8,128)S(1)}, f32[4,128,128]{2,1,0:T(8,128)S(1)}, u32[]{:S(2)}, u32[]{:S(2)}) collective-permute-start(f32[4,128,128]{2,1,0:T(8,128)S(1)} %pad_maximum_fusion), channel_id=1, source_target_pairs={{0,8},{1,9},{2,10},{3,11},{4,12},{5,13},{6,14},{7,15},{8,0},{9,1},... | collective-permute-start | bytes 786440 | tf_op jit(solution)/shard_map/ppermute | solution.py:13
  41.0 7.7 %collective-permute-start.13 = (f32[4,128,128]{2,1,0:T(8,128)S(1)}, f32[4,128,128]{2,1,0:T(8,128)S(1)}, u32[]{:S(2)}, u32[]{:S(2)}) collective-permute-start(f32[4,128,128]{2,1,0:T(8,128)S(1)} %pad_maximum_fusion), channel_id=1, source_target_pairs={{0,4},{1,5},{2,6},{3,7},{4,0},{5,1},{6,2},{7,3},{8,12},{9,13},{10,... | collective-permute-start | bytes 786440 | tf_op jit(solution)/shard_map/ppermute | solution.py:13
  44.4 9.3 %collective-permute-start.14 = (f32[4,128,128]{2,1,0:T(8,128)S(1)}, f32[4,128,128]{2,1,0:T(8,128)S(1)}, u32[]{:S(2)}, u32[]{:S(2)}) collective-permute-start(f32[4,128,128]{2,1,0:T(8,128)S(1)} %pad_maximum_fusion), channel_id=1, source_target_pairs={{0,12},{1,13},{2,14},{3,15},{4,8},{5,9},{6,10},{7,11},{8,4},{9,5},... | collective-permute-start | bytes 786440 | tf_op jit(solution)/shard_map/ppermute | solution.py:13
  54.4 8.5 %collective-permute-start.15 = (f32[16,128,128]{2,1,0:T(8,128)}, f32[16,128,128]{2,1,0:T(8,128)}, u32[]{:S(2)}, u32[]{:S(2)}) collective-permute-start(f32[16,128,128]{2,1,0:T(8,128)} %constant_dynamic-update-slice_fusion.15), channel_id=1, source_target_pairs={{0,1},{1,0},{2,3},{3,2},{4,5},{5,4},{6,7},{7,6},{8,9},{9,8},{10,11... | collective-permute-start | bytes 3145736 | tf_op jit(solution)/shard_map/ppermute | solution.py:119
  66.3 3.6 %copy-start.4 = (f32[8,256,256]{2,1,0:T(8,128)S(1)}, f32[8,256,256]{2,1,0:T(8,128)}, u32[]{:S(2)}) copy-start(f32[8,256,256]{2,1,0:T(8,128)} %param.26) | copy-start | bytes 6291460
  (6 other events, 8.5 us)
